TPU v7x, 256 devices: a whole 4x4x8 slice. The times are simulated.
256 devices in a mesh: tm: 32 (over x, z), scen: 8 (over y, core).
Axes of the slice: x: 4, y: 4, z: 8, core: 2. Of those that a mesh axis runs over, the one named last changes fastest.
Arguments:
- operators: float32 [32, 512, 512], P('tm'), may hold values from -1 to 1
- input_maps: bfloat16 [4, 512, 256], replicated, may hold values from -0.056152344 to 0.056152344
- segment: int32 [32], P('tm'), may hold values from 0 to 3
- load: bfloat16 [32, 512, 256], P('tm', 'scen'), may hold values from -6 to 6
- initial: float32 [512, 512], P('scen'), may hold values from -6 to 6
- observed: bfloat16 [32, 512, 2048], P('tm', 'scen'), may hold values from -6 to 6
Outputs:
- states: float32 [32, 512, 512], P('tm', 'scen')
- gram: float32 [512, 512], P('tm', 'scen')
- cross: float32 [512, 2048], P('tm', 'scen')
All inputs are finite; a program needn't handle non-finite values.
Results may differ from a plain program's by a relative error of at most 0.0003.
Values sent between devices are 32-bit elements; how exact they have to be, the bound alone decides.
No kernel may reach another device: no remote copies, remote signals or barrier semaphores. Data moves between devices by JAX's collectives and lax.ppermute only.
A program may use at most 192 MiB of HBM per device.

v0:
```python
import jax
import jax.numpy as jnp
from jax import lax
from jax.sharding import PartitionSpec as P


def prefix_2(shard, axis, combine, identity):
    count, index = (lax.axis_size(axis), lax.axis_index(axis))
    everything = jax.tree.map(lambda part: lax.all_gather(part, axis), shard)
    start = jax.tree.map(
        lambda part, zero: jnp.broadcast_to(jnp.asarray(zero, part.dtype), part.shape),
        shard,
        identity,
    )

    def turn(k, before):
        reached = k < index
        new = combine(before, jax.tree.map(lambda part: part[k], everything))
        return jax.tree.map(lambda a, b: jnp.where(reached, a, b), new, before)

    return lax.fori_loop(0, count, turn, start)


def on_device(operators, input_maps, segment, load, initial, observed):
    highest = lax.Precision.HIGHEST
    step_count = operators.shape[0]
    modes = operators.shape[1]
    local_scen = initial.shape[0]
    time_shards = lax.axis_size("tm")
    scen_shards = lax.axis_size("scen")
    regimes = jnp.arange(input_maps.shape[0], dtype=jnp.int32)
    onehot = (segment[:, None] == regimes[None, :]).astype(jnp.bfloat16)
    weighted = jnp.einsum(
        "tg,grk->trk", onehot, input_maps, preferred_element_type=jnp.float32
    ).astype(jnp.bfloat16)
    forcing = jnp.einsum("tsk,trk->tsr", load, weighted, preferred_element_type=jnp.float32)
    first_shard = lax.axis_index("tm") == 0
    anchor = jnp.where(first_shard, initial, jnp.zeros_like(initial))

    def advance(current, inputs):
        matrix, heating = inputs
        updated = jnp.einsum("sq,rq->sr", current, matrix, precision=highest) + heating
        return (updated, updated)

    last_state, local_states = lax.scan(advance, anchor, (operators, forcing))
    identity_matrix = jnp.eye(modes, dtype=jnp.float32)

    def compose_step(product, matrix):
        newer = jnp.dot(matrix, product, precision=highest)
        return (newer, newer)

    composed, products = lax.scan(compose_step, identity_matrix, operators)

    def combine(earlier, later):
        joined = jnp.dot(later[0], earlier[0], precision=highest)
        shifted = jnp.einsum("sq,rq->sr", earlier[1], later[0], precision=highest) + later[1]
        return (joined, shifted)

    prefix = prefix_2(
        (composed, last_state), "tm", combine, (identity_matrix, jnp.zeros_like(last_state))
    )
    entering = prefix[1]
    states = local_states + jnp.einsum("sq,trq->tsr", entering, products, precision=highest)
    normalize = 1.0 / (step_count * time_shards * local_scen * scen_shards)
    gram_term = jnp.einsum("tsr,tsq->rq", states, states, precision=highest) * normalize
    cross_term = (
        jnp.einsum("tsr,tso->ro", states, observed.astype(jnp.float32), precision=highest)
        * normalize
    )
    partial_gram, partial_cross = (
        lax.psum_scatter(gram_term, "scen", scatter_dimension=1, tiled=True),
        lax.psum_scatter(cross_term, "scen", scatter_dimension=1, tiled=True),
    )
    gram_out, cross_out = (
        lax.psum_scatter(partial_gram, "tm", scatter_dimension=0, tiled=True),
        lax.psum_scatter(partial_cross, "tm", scatter_dimension=0, tiled=True),
    )
    return (states, gram_out, cross_out)


def solution(mesh):
    in_specs = (
        P("tm", None, None),
        P(),
        P("tm"),
        P("tm", "scen", None),
        P("scen", None),
        P("tm", "scen", None),
    )
    out_specs = (P("tm", "scen", None), P("tm", "scen"), P("tm", "scen"))
    return jax.shard_map(
        on_device, mesh=mesh, in_specs=in_specs, out_specs=out_specs, check_vma=False
    )
```

profile of v0, /device:TPU:24, one launch (start us, length us, event | category | flops | bytes accessed | tf_op | source)
XLA Modules:
  0.0 927.8 jit_solution(6804148609973992862)
XLA Ops:
  7.2 1.1 copy-done
  8.4 2.1 fusion.10
  11.2 2.1 fusion.13
  13.5 1.8 convolution_add_fusion
  15.4 230.8 %all-gather.5.cloned.1.call-done = f32[16384,512]{0,1:T(8,128)} async-done(((f32[512,512]{0,1:T(8,128)}), f32[16384,512]{0,1:T(8,128)}) %all-gather.5.cloned.1.call-update) | async-done | bytes 33554448 | tf_op jit(solution)/shard_map/all_gather | solution.py:9
  246.2 33.5 %copy.15 = f32[16384,512]{1,0:T(8,128)} copy(f32[16384,512]{0,1:T(8,128)} %all-gather.5.cloned.1.call-done) | data formatting | bytes 67108864
  279.7 48.5 %all-gather.7.cloned.1.call-done = f32[2048,512]{1,0:T(8,128)} async-done(((f32[64,512]{1,0:T(8,128)}), f32[2048,512]{1,0:T(8,128)}) %all-gather.7.cloned.1.call-update) | async-done | bytes 4194320 | tf_op jit(solution)/shard_map/all_gather | solution.py:9
  328.2 77.0 %while.9 = (s32[]{:T(128)}, f32[64,512]{1,0:T(8,128)S(1)}, s32[]{:T(128)}, f32[32,512,512]{2,1,0:T(8,128)}, f32[32,64,512]{2,1,0:T(8,128)}, /*index=5*/s32[]{:T(128)}, s32[]{:T(128)}) while((s32[]{:T(128)}, f32[64,512]{1,0:T(8,128)S(1)}, s32[]{:T(128)}, f32[32,512,512]{2,1,0:T(8,128)}, f32[32,64,512]{2,1,0:T(8,128)}, ...), condition=%wide.region_1.2_spmd.clone, body=%wide.region_0.1_spmd.clone.sunk | while | flops 201457664 | bytes 1837671 | solution.py:21
  328.3 2.5 fusion.34
  330.8 2.4 fusion.34
  333.2 2.4 fusion.34
  335.6 2.4 fusion.34
  338.0 2.4 fusion.34
  340.4 2.4 fusion.34
  342.8 2.4 fusion.34
  345.2 2.4 fusion.34
  347.6 2.4 fusion.34
  350.0 2.4 fusion.34
  352.4 2.4 fusion.34
  354.8 2.4 fusion.34
  357.2 2.4 fusion.34
  359.6 2.4 fusion.34
  362.0 2.4 fusion.34
  364.4 2.4 fusion.34
  366.8 2.4 fusion.34
  369.2 2.4 fusion.34
  371.6 2.4 fusion.34
  374.0 2.4 fusion.34
  376.4 2.4 fusion.34
  378.9 2.4 fusion.34
  381.3 2.4 fusion.34
  383.7 2.4 fusion.34
  386.1 2.4 fusion.34
  388.5 2.4 fusion.34
  390.9 2.4 fusion.34
  393.3 2.4 fusion.34
  395.7 2.4 fusion.34
  398.1 2.4 fusion.34
  400.5 2.4 fusion.34
  402.9 2.4 fusion.34
  405.3 0.8 fusion.9
  406.1 2.0 convolution_multiply_fusion.1
  408.2 3.8 convolution_multiply_fusion
  412.1 24.7 %reduce-scatter.7.cloned.1.call-done = f32[512,64]{0,1:T(8,128)} async-done(((f32[512,512]{0,1:T(8,128)}), f32[512,64]{0,1:T(8,128)}) %reduce-scatter.7.cloned.1.call-update) | async-done | bytes 131088 | tf_op jit(solution)/shard_map/reduce_scatter | solution.py:71
  436.7 1.7 copy.16
  438.6 39.5 %reduce-scatter.9.cloned.1.call-done = f32[512,256]{1,0:T(8,128)} async-done(((f32[512,2048]{1,0:T(8,128)}), f32[512,256]{1,0:T(8,128)}) %reduce-scatter.9.cloned.1.call-update) | async-done | bytes 524304 | tf_op jit(solution)/shard_map/reduce_scatter | solution.py:72
  478.0 224.1 %reduce-scatter.13.cloned.1.call-done = f32[16,64]{1,0:T(8,128)} async-done(((f32[512,64]{1,0:T(8,128)}), f32[16,64]{1,0:T(8,128)}) %reduce-scatter.13.cloned.1.call-update) | async-done | bytes 4112
  702.1 218.8 %reduce-scatter.11.cloned.1.call-done = f32[16,256]{1,0:T(8,128)} async-done(((f32[512,256]{1,0:T(8,128)}), f32[16,256]{1,0:T(8,128)}) %reduce-scatter.11.cloned.1.call-update) | async-done | bytes 16400 | tf_op jit(solution)/shard_map/reduce_scatter | solution.py:76
  (61 shorter events, 0.9 us)
Async XLA Ops:
  7.2 1.2 copy-start
  7.2 6.1 copy-start.7
  7.2 6.3 copy-start.6
  7.2 239.0 %all-gather.5.cloned.1.call-start = ((), (), s32[]{:S(2)}) async-start(), calls=%async_computation.7 | async-start | bytes 34603008 | tf_op jit(solution)/shard_map/all_gather | solution.py:9
  10.5 317.7 %all-gather.7.cloned.1.call-start = ((), (), s32[]{:S(2)}) async-start(), calls=%async_computation.8 | async-start | bytes 4325376 | tf_op jit(solution)/shard_map/all_gather | solution.py:9
  15.4 421.4 %reduce-scatter.7.cloned.1.call-start = ((), (), s32[]{:S(2)}) async-start(), calls=%async_computation.4 | async-start | bytes 1179648 | tf_op jit(solution)/shard_map/reduce_scatter | solution.py:71
  328.2 77.0 %copy-start.2 = (f32[512,512]{1,0:T(8,128)S(1)}, f32[512,512]{1,0:T(8,128)}, u32[]{:S(2)}) copy-start(f32[512,512]{1,0:T(8,128)} %fusion.10) | copy-start | bytes 3145732
  328.2 77.0 %copy-start.4 = (f32[64,512]{1,0:T(8,128)S(1)}, f32[64,512]{1,0:T(8,128)}, u32[]{:S(2)}) copy-start(f32[64,512]{1,0:T(8,128)} %convolution_add_fusion) | copy-start | bytes 393220
  328.2 79.9 %copy-start.5 = (bf16[1,64,2048]{2,1,0:T(8,128)(2,1)S(1)}, bf16[1,64,2048]{2,1,0:T(8,128)(2,1)}, u32[]{:S(2)}) copy-start(bf16[1,64,2048]{2,1,0:T(8,128)(2,1)} %param.13) | copy-start | bytes 786436
  406.1 5.9 copy-start.3
  408.1 512.9 %copy-start.1 = (f32[1,512,512]{2,1,0:T(8,128)S(1)}, f32[1,512,512]{2,1,0:T(8,128)}, u32[]{:S(2)}) copy-start(f32[1,512,512]{2,1,0:T(8,128)} %param.8) | copy-start | bytes 3145732
  408.1 69.9 %reduce-scatter.9.cloned.1.call-start = ((), (), s32[]{:S(2)}) async-start(), calls=%async_computation.5 | async-start | bytes 4718592 | tf_op jit(solution)/shard_map/reduce_scatter | solution.py:72
  412.0 290.1 %reduce-scatter.13.cloned.1.call-start = ((), (), s32[]{:S(2)}) async-start(), calls=%async_computation.9 | async-start | bytes 270336
  438.5 482.5 %reduce-scatter.11.cloned.1.call-start = ((), (), s32[]{:S(2)}) async-start(), calls=%async_computation.6 | async-start | bytes 540672 | tf_op jit(solution)/shard_map/reduce_scatter | solution.py:76
Sparse Core Ops, SparseCore 0:
  10.6 235.5 all-gather.4
  249.4 78.7 all-gather.6
  408.2 28.4 reduce-scatter.6
  439.1 38.8 reduce-scatter.8
  482.2 219.8 reduce-scatter.12
  706.4 214.5 reduce-scatter.10
where the time goes:
time: 929 us; the launch traced here: 928 us
  waiting for transfers between devices  787 us (85%)
  matrix products  88.5 us (10%)
  local copies, waits for them, and re-layouts  36.7 us (4%)
  between operations  14.9 us (2%)
    all_gather x2, waiting for transfers between devices, prefix_2(): everything = jax.tree.map(lambda part: lax.all_gather(part, axis), shard)  279 us
    unnamed x7, waiting for transfers between devices  224 us
    reduce_scatter x1, waiting for transfers between devices, on_device(): lax.psum_scatter(partial_cross, 'tm', scatter_dimension=0, tiled=True)  219 us
    dot_general x32, matrix products, combine(): jnp.einsum('sq,rq->sr', earlier[1], later[0], precision=highest) + later[1]  75.8 us
    reduce_scatter x1, waiting for transfers between devices, on_device(): lax.psum_scatter(cross_term, 'scen', scatter_dimension=1, tiled=True)  39.5 us
    unnamed x18, local copies, waits for them, and re-layouts  36.4 us
    reduce_scatter x1, waiting for transfers between devices, on_device(): lax.psum_scatter(gram_term, 'scen', scatter_dimension=1, tiled=True)  24.7 us
  transfers between devices with their start and end apart: 6, of which 6 were waited for; matrix products, arithmetic and copies ran while one was open for 5% of the time, Pallas kernels for 0%

commit v1 on v0

v1 whole, which is shorter than its diff:
```python
import jax
import jax.numpy as jnp
from jax import lax
from jax.sharding import PartitionSpec as P


def shift_scan(matrix, vector, axis):
    highest = lax.Precision.HIGHEST
    count, index = (lax.axis_size(axis), lax.axis_index(axis))
    distance = 1
    while distance < count:
        pairs = [(j, j + distance) for j in range(count - distance)]
        last = 2 * distance >= count
        has = index >= distance
        got_vector = lax.ppermute(vector, axis, pairs)
        if not last:
            got_matrix = lax.ppermute(matrix, axis, pairs)
        newer = jnp.einsum("sq,rq->sr", got_vector, matrix, precision=highest) + vector
        vector = jnp.where(has, newer, vector)
        if not last:
            joined = jnp.dot(matrix, got_matrix, precision=highest)
            matrix = jnp.where(has, joined, matrix)
        distance *= 2
    return vector


def halving_scatter(block, axis):
    count, index = (lax.axis_size(axis), lax.axis_index(axis))
    bit = count // 2
    while bit >= 1:
        half = block.shape[0] // 2
        upper = (index // bit) % 2 == 1
        low, high = block[:half], block[half:]
        keep = jnp.where(upper, high, low)
        send = jnp.where(upper, low, high)
        pairs = [(j, j ^ bit) for j in range(count)]
        block = keep + lax.ppermute(send, axis, pairs)
        bit //= 2
    return block


def on_device(operators, input_maps, segment, load, initial, observed):
    highest = lax.Precision.HIGHEST
    step_count = operators.shape[0]
    modes = operators.shape[1]
    local_scen = initial.shape[0]
    time_shards = lax.axis_size("tm")
    scen_shards = lax.axis_size("scen")
    regimes = jnp.arange(input_maps.shape[0], dtype=jnp.int32)
    onehot = (segment[:, None] == regimes[None, :]).astype(jnp.bfloat16)
    weighted = jnp.einsum(
        "tg,grk->trk", onehot, input_maps, preferred_element_type=jnp.float32
    ).astype(jnp.bfloat16)
    forcing = jnp.einsum("tsk,trk->tsr", load, weighted, preferred_element_type=jnp.float32)
    first_shard = lax.axis_index("tm") == 0
    anchor = jnp.where(first_shard, initial, jnp.zeros_like(initial))

    def advance(current, inputs):
        matrix, heating = inputs
        updated = jnp.einsum("sq,rq->sr", current, matrix, precision=highest) + heating
        return (updated, updated)

    last_state, local_states = lax.scan(advance, anchor, (operators, forcing))
    identity_matrix = jnp.eye(modes, dtype=jnp.float32)

    def compose_step(product, matrix):
        newer = jnp.dot(matrix, product, precision=highest)
        return (newer, newer)

    composed, products = lax.scan(compose_step, identity_matrix, operators)
    composed = jnp.where(first_shard, jnp.zeros_like(composed), composed)
    leaving = shift_scan(composed, last_state, "tm")
    if step_count == 1:
        states = leaving[None]
    else:
        pairs = [(j, j + 1) for j in range(time_shards - 1)]
        entering = lax.ppermute(leaving, "tm", pairs)
        states = local_states + jnp.einsum("sq,trq->tsr", entering, products, precision=highest)
    normalize = 1.0 / (step_count * time_shards * local_scen * scen_shards)
    gram_term = jnp.einsum("tsr,tsq->rq", states, states, precision=highest) * normalize
    cross_term = (
        jnp.einsum("tsr,tso->ro", states, observed.astype(jnp.float32), precision=highest)
        * normalize
    )
    gram_cols = gram_term.shape[1] // scen_shards
    cross_cols = cross_term.shape[1] // scen_shards
    joined = jnp.concatenate(
        [
            gram_term.reshape(modes, scen_shards, gram_cols),
            cross_term.reshape(modes, scen_shards, cross_cols),
        ],
        axis=2,
    ).reshape(modes, scen_shards * (gram_cols + cross_cols))
    partial = lax.psum_scatter(joined, "scen", scatter_dimension=1, tiled=True)
    mine = halving_scatter(partial, "tm")
    return (states, mine[:, :gram_cols], mine[:, gram_cols:])


def solution(mesh):
    in_specs = (
        P("tm", None, None),
        P(),
        P("tm"),
        P("tm", "scen", None),
        P("scen", None),
        P("tm", "scen", None),
    )
    out_specs = (P("tm", "scen", None), P("tm", "scen"), P("tm", "scen"))
    return jax.shard_map(
        on_device, mesh=mesh, in_specs=in_specs, out_specs=out_specs, check_vma=False
    )
```

time: 929 us -> 313 us (0.34)
  waiting for transfers between devices: 787 us -> 187 us
  starting transfers between devices: 0.25 us -> 67.8 us
  matrix products: 88.5 us -> 26.1 us
  local copies, waits for them, and re-layouts: 36.7 us -> 7.99 us
    all_gather x2 -> x0, waiting for transfers between devices: 279 us -> none  [prefix_2(): everything = jax.tree.map(lambda part: lax.all_gather(part, axis), shard)]
    reduce_scatter x3 -> x1, waiting for transfers between devices: 283 us -> 36.3 us  [on_device(): partial = lax.psum_scatter(joined, 'scen', scatter_dimension=1, tiled=True)]
    unnamed x7 -> x1, waiting for transfers between devices: 224 us -> 0.02 us
    ppermute x0 -> x14, waiting for transfers between devices: none -> 151 us  [the longest x4 64 us: shift_scan(): got_matrix = lax.ppermute(matrix, axis, pairs)]
    ppermute x0 -> x14, starting transfers between devices: none -> 67.8 us  [the longest x4 27.8 us: shift_scan(): got_matrix = lax.ppermute(matrix, axis, pairs)]
    dot_general x33 -> x9, matrix products: 76.6 us -> 16.8 us  [the longest x4 13 us: shift_scan(): joined = jnp.dot(matrix, got_matrix, precision=highest)]
    unnamed x18 -> x16, local copies, waits for them, and re-layouts: 36.4 us -> 2.54 us
  transfers between devices with their start and end apart: 6 -> 15, of which waited for: 6 -> 11; matrix products, arithmetic and copies ran while one was open for 5% -> 4% of each run, Pallas kernels for 0% -> 0%
where the time goes in v1:
time: 313 us; the launch traced here: 312 us
  waiting for transfers between devices  187 us (60%)
  starting transfers between devices  67.8 us (22%)
  matrix products  26.1 us (8%)
  between operations  15 us (5%)
  other arithmetic  8.26 us (3%)
  local copies, waits for them, and re-layouts  7.99 us (3%)
    ppermute x4, waiting for transfers between devices, shift_scan(): got_matrix = lax.ppermute(matrix, axis, pairs)  64 us
    ppermute x5, waiting for transfers between devices, shift_scan(): got_vector = lax.ppermute(vector, axis, pairs)  55.9 us
    reduce_scatter x1, waiting for transfers between devices, on_device(): partial = lax.psum_scatter(joined, 'scen', scatter_dimension=1, tiled=True)  36.3 us
    ppermute x5, waiting for transfers between devices, halving_scatter(): block = keep + lax.ppermute(send, axis, pairs)  31 us
    ppermute x4, starting transfers between devices, shift_scan(): got_matrix = lax.ppermute(matrix, axis, pairs)  27.8 us
    ppermute x5, starting transfers between devices, shift_scan(): got_vector = lax.ppermute(vector, axis, pairs)  23.2 us
    ppermute x5, starting transfers between devices, halving_scatter(): block = keep + lax.ppermute(send, axis, pairs)  16.7 us
    dot_general x4, matrix products, shift_scan(): joined = jnp.dot(matrix, got_matrix, precision=highest)  13 us
  transfers between devices with their start and end apart: 15, of which 11 were waited for; matrix products, arithmetic and copies ran while one was open for 4% of the time, Pallas kernels for 0%

profile of v1, /device:TPU:24, one launch (start us, length us, event | category | flops | bytes accessed | tf_op | source)
XLA Modules:
  0.0 312.3 jit_solution(6239589370725342939)
XLA Ops:
  7.2 1.2 copy-done
  8.4 1.1 convolution_select_fusion.3
  9.5 4.8 %collective-permute-start.2 = (f32[512,512]{0,1:T(8,128)S(1)}, f32[512,512]{0,1:T(8,128)}, u32[]{:S(2)}, u32[]{:S(2)}) collective-permute-start(f32[512,512]{0,1:T(8,128)S(1)} %bitcast.50), channel_id=1, source_target_pairs={{0,8},{8,16},{16,24},{24,32},{32,40},{40,48},{48,56},{56,64},{64,7... | collective-permute-start | bytes 3145736 | tf_op jit(solution)/shard_map/ppermute | solution.py:17
  14.3 21.4 %collective-permute-done.2 = f32[512,512]{0,1:T(8,128)} collective-permute-done((f32[512,512]{0,1:T(8,128)S(1)}, f32[512,512]{0,1:T(8,128)}, u32[]{:S(2)}, u32[]{:S(2)}) %collective-permute-start.2) | collective-permute-done | bytes 1048608 | tf_op jit(solution)/shard_map/ppermute | solution.py:17
  35.7 3.1 convolution_select_fusion.4
  38.8 6.8 %collective-permute-start.4 = (f32[512,512]{0,1:T(8,128)S(1)}, f32[512,512]{0,1:T(8,128)}, u32[]{:S(2)}, u32[]{:S(2)}) collective-permute-start(f32[512,512]{0,1:T(8,128)S(1)} %convolution_select_fusion.4), channel_id=1, source_target_pairs={{0,16},{8,24},{16,32},{24,40},{32,48},{40,56},{48,64},{56,72},{64,... | collective-permute-start | bytes 3145736 | tf_op jit(solution)/shard_map/ppermute | solution.py:17
  46.3 42.6 %collective-permute-done.4 = f32[512,512]{0,1:T(8,128)} collective-permute-done((f32[512,512]{0,1:T(8,128)S(1)}, f32[512,512]{0,1:T(8,128)}, u32[]{:S(2)}, u32[]{:S(2)}) %collective-permute-start.4) | collective-permute-done | bytes 1048608 | tf_op jit(solution)/shard_map/ppermute | solution.py:17
  88.9 3.7 %convolution_select_fusion.2 = f32[512,512]{0,1:T(8,128)S(1)} fusion(f32[512,512]{0,1:T(8,128)} %copy-done.1, f32[512,512]{0,1:T(8,128)} %collective-permute-done.4, pred[]{:T(512)S(6)} %ge.18), kind=kOutput, calls=%fused_computation.4 | convolution fusion | flops 1610874880 | bytes 3145729 | tf_op jit(solution)/shard_map/dot_general | solution.py:21
  92.6 11.8 %collective-permute-start.6 = (f32[512,512]{0,1:T(8,128)S(1)}, f32[512,512]{0,1:T(8,128)}, u32[]{:S(2)}, u32[]{:S(2)}) collective-permute-start(f32[512,512]{0,1:T(8,128)S(1)} %convolution_select_fusion.2), channel_id=1, source_target_pairs={{0,32},{8,40},{16,48},{24,56},{32,64},{40,72},{48,80},{56,88},{64,... | collective-permute-start | bytes 3145736 | tf_op jit(solution)/shard_map/ppermute | solution.py:17
  104.4 2.1 fusion.7
  106.5 0.2 convolution_bitcast_fusion
  106.8 1.1 convolution_add_fusion.5
  107.9 1.3 collective-permute-start
  109.2 41.5 %collective-permute-done = f32[64,512]{1,0:T(8,128)S(1)} collective-permute-done((f32[64,512]{1,0:T(8,128)S(1)}, f32[64,512]{1,0:T(8,128)S(1)}, u32[]{:S(2)}, u32[]{:S(2)}) %collective-permute-start) | collective-permute-done | bytes 131104 | tf_op jit(solution)/shard_map/ppermute | solution.py:15
  150.7 0.8 fusion.4
  151.5 5.2 %collective-permute-start.1 = (f32[64,512]{1,0:T(8,128)S(1)}, f32[64,512]{1,0:T(8,128)S(1)}, u32[]{:S(2)}, u32[]{:S(2)}) collective-permute-start(f32[64,512]{1,0:T(8,128)S(1)} %fusion.4), channel_id=1, source_target_pairs={{0,16},{8,24},{16,32},{24,40},{32,48},{40,56},{48,64},{56,72},{64,... | collective-permute-start | bytes 393224 | tf_op jit(solution)/shard_map/ppermute | solution.py:15
  156.7 3.1 convolution_select_fusion.1
  159.8 4.4 %collective-permute-start.8 = (f32[512,512]{0,1:T(8,128)S(1)}, f32[512,512]{0,1:T(8,128)}, u32[]{:S(2)}, u32[]{:S(2)}) collective-permute-start(f32[512,512]{0,1:T(8,128)S(1)} %convolution_select_fusion.1), channel_id=1, source_target_pairs={{0,64},{8,72},{16,80},{24,88},{32,96},{40,104},{48,112},{56,120},{... | collective-permute-start | bytes 3145736 | tf_op jit(solution)/shard_map/ppermute | solution.py:17
  164.2 0.8 fusion.3
  165.0 4.1 %collective-permute-start.3 = (f32[64,512]{1,0:T(8,128)S(1)}, f32[64,512]{1,0:T(8,128)S(1)}, u32[]{:S(2)}, u32[]{:S(2)}) collective-permute-start(f32[64,512]{1,0:T(8,128)S(1)} %fusion.3), channel_id=1, source_target_pairs={{0,32},{8,40},{16,48},{24,56},{32,64},{40,72},{48,80},{56,88},{64,... | collective-permute-start | bytes 393224 | tf_op jit(solution)/shard_map/ppermute | solution.py:15
  169.1 3.5 %collective-permute-done.3 = f32[64,512]{1,0:T(8,128)S(1)} collective-permute-done((f32[64,512]{1,0:T(8,128)S(1)}, f32[64,512]{1,0:T(8,128)S(1)}, u32[]{:S(2)}, u32[]{:S(2)}) %collective-permute-start.3) | collective-permute-done | bytes 131104 | tf_op jit(solution)/shard_map/ppermute | solution.py:15
  172.6 0.8 fusion.2
  173.4 7.0 %collective-permute-start.5 = (f32[64,512]{1,0:T(8,128)S(1)}, f32[64,512]{1,0:T(8,128)S(1)}, u32[]{:S(2)}, u32[]{:S(2)}) collective-permute-start(f32[64,512]{1,0:T(8,128)S(1)} %fusion.2), channel_id=1, source_target_pairs={{0,64},{8,72},{16,80},{24,88},{32,96},{40,104},{48,112},{56,120},{... | collective-permute-start | bytes 393224 | tf_op jit(solution)/shard_map/ppermute | solution.py:15
  180.4 10.8 %collective-permute-done.5 = f32[64,512]{1,0:T(8,128)S(1)} collective-permute-done((f32[64,512]{1,0:T(8,128)S(1)}, f32[64,512]{1,0:T(8,128)S(1)}, u32[]{:S(2)}, u32[]{:S(2)}) %collective-permute-start.5) | collective-permute-done | bytes 131104 | tf_op jit(solution)/shard_map/ppermute | solution.py:15
  191.2 0.8 fusion.1
  191.9 5.6 %collective-permute-start.7 = (f32[64,512]{1,0:T(8,128)S(1)}, f32[64,512]{1,0:T(8,128)S(1)}, u32[]{:S(2)}, u32[]{:S(2)}) collective-permute-start(f32[64,512]{1,0:T(8,128)S(1)} %fusion.1), channel_id=1, source_target_pairs={{0,128},{8,136},{16,144},{24,152},{32,160},{40,168},{48,176},{56,1... | collective-permute-start | bytes 393224 | tf_op jit(solution)/shard_map/ppermute | solution.py:15
  197.6 3.1 convolution_select_fusion
  200.7 0.8 fusion
  201.5 1.0 convolution_multiply_fusion.1
  202.5 3.8 %convolution_multiply_fusion = f32[512,2048]{1,0:T(8,128)} fusion(f32[64,512]{1,0:T(8,128)S(1)} %fusion, bf16[1,64,2048]{2,1,0:T(8,128)(2,1)S(1)} %copy-done.4), kind=kOutput, calls=%fused_computation.1 | convolution fusion | flops 806354944 | bytes 4587520 | tf_op jit(solution)/shard_map/tsr,tso->ro/dot_general | solution.py:82
  206.3 5.4 %copy.24 = f32[512,2048]{0,1:T(8,128)} copy(f32[512,2048]{1,0:T(8,128)} %convolution_multiply_fusion) | data formatting | bytes 8388608 | tf_op jit(solution)/shard_map/reshape | solution.py:90
  211.7 5.3 %pad_maximum_fusion = f32[512,8,320]{0,2,1:T(8,128)} fusion(f32[512,8,256]{0,2,1:T(8,128)} %bitcast.49, f32[512,8,64]{0,2,1:T(8,128)S(1)} %bitcast.51), kind=kLoop, calls=%fused_computation | loop fusion | flops 1310720 | bytes 10485760 | tf_op jit(solution)/shard_map/concatenate | solution.py:87
  217.1 36.3 %reduce-scatter.2.cloned.1.call-done = f32[512,320]{0,1:T(8,128)} async-done(((f32[512,2560]{0,1:T(8,128)}), f32[512,320]{0,1:T(8,128)}) %reduce-scatter.2.cloned.1.call-update) | async-done | bytes 655376 | tf_op jit(solution)/shard_map/reduce_scatter | solution.py:94
  253.4 1.1 slice_select_fusion
  254.5 3.1 collective-permute-start.9
  257.6 7.6 %collective-permute-done.9 = f32[256,320]{0,1:T(8,128)S(1)} collective-permute-done((f32[256,320]{0,1:T(8,128)S(1)}, f32[256,320]{0,1:T(8,128)S(1)}, u32[]{:S(2)}, u32[]{:S(2)}) %collective-permute-start.9) | collective-permute-done | bytes 327712 | tf_op jit(solution)/shard_map/ppermute | solution.py:37
  265.2 1.1 select_add_fusion
  266.4 1.6 collective-permute-start.10
  268.0 5.2 %collective-permute-done.10 = f32[128,320]{0,1:T(8,128)S(1)} collective-permute-done((f32[128,320]{0,1:T(8,128)S(1)}, f32[128,320]{0,1:T(8,128)S(1)}, u32[]{:S(2)}, u32[]{:S(2)}) %collective-permute-start.10) | collective-permute-done | bytes 163872 | tf_op jit(solution)/shard_map/ppermute | solution.py:37
  273.2 0.1 slice_select_fusion.3
  273.3 5.9 %collective-permute-start.11 = (f32[64,320]{0,1:T(8,128)S(1)}, f32[64,320]{0,1:T(8,128)S(1)}, u32[]{:S(2)}, u32[]{:S(2)}) collective-permute-start(f32[64,320]{0,1:T(8,128)S(1)} %slice_select_fusion.3), channel_id=1, source_target_pairs={{0,32},{8,40},{16,48},{24,56},{32,0},{40,8},{48,16},{56,24},{64,96... | collective-permute-start | bytes 245768 | tf_op jit(solution)/shard_map/ppermute | solution.py:37
  279.2 4.6 %collective-permute-done.11 = f32[64,320]{0,1:T(8,128)S(1)} collective-permute-done((f32[64,320]{0,1:T(8,128)S(1)}, f32[64,320]{0,1:T(8,128)S(1)}, u32[]{:S(2)}, u32[]{:S(2)}) %collective-permute-start.11) | collective-permute-done | bytes 81952 | tf_op jit(solution)/shard_map/ppermute | solution.py:37
  283.8 0.1 select_add_fusion.3
  284.0 6.0 %collective-permute-start.12 = (f32[32,320]{0,1:T(8,128)S(1)}, f32[32,320]{0,1:T(8,128)S(1)}, u32[]{:S(2)}, u32[]{:S(2)}) collective-permute-start(f32[32,320]{0,1:T(8,128)S(1)} %slice_select_fusion.2), channel_id=1, source_target_pairs={{0,16},{8,24},{16,0},{24,8},{32,48},{40,56},{48,32},{56,40},{64,80... | collective-permute-start | bytes 122888 | tf_op jit(solution)/shard_map/ppermute | solution.py:37
  290.0 7.5 %collective-permute-done.12 = f32[32,320]{0,1:T(8,128)S(1)} collective-permute-done((f32[32,320]{0,1:T(8,128)S(1)}, f32[32,320]{0,1:T(8,128)S(1)}, u32[]{:S(2)}, u32[]{:S(2)}) %collective-permute-start.12) | collective-permute-done | bytes 40992 | tf_op jit(solution)/shard_map/ppermute | solution.py:37
  297.8 6.1 %collective-permute-done.13 = f32[16,320]{0,1:T(8,128)S(1)} collective-permute-done((f32[16,320]{0,1:T(8,128)S(1)}, f32[16,320]{0,1:T(8,128)S(1)}, u32[]{:S(2)}, u32[]{:S(2)}) %collective-permute-start.13) | collective-permute-done | bytes 20512 | tf_op jit(solution)/shard_map/ppermute | solution.py:37
  304.1 0.7 copy.18
  304.8 0.7 copy.17
  (28 shorter events, 0.7 us)
Async XLA Ops:
  7.2 1.2 copy-start
  7.2 246.2 %reduce-scatter.2.cloned.1.call-start = ((), (), s32[]{:S(2)}) async-start(), calls=%async_computation.1 | async-start | bytes 5898240 | tf_op jit(solution)/shard_map/reduce_scatter | solution.py:94
  9.5 26.2 %collective-permute-start.2 = (f32[512,512]{0,1:T(8,128)S(1)}, f32[512,512]{0,1:T(8,128)}, u32[]{:S(2)}, u32[]{:S(2)}) collective-permute-start(f32[512,512]{0,1:T(8,128)S(1)} %bitcast.50), channel_id=1, source_target_pairs={{0,8},{8,16},{16,24},{24,32},{32,40},{40,48},{48,56},{56,64},{64,7... | collective-permute-start | bytes 3145736 | tf_op jit(solution)/shard_map/ppermute | solution.py:17
  14.3 92.3 %copy-start.6 = (bf16[1,64,256]{2,1,0:T(8,128)(2,1)S(1)}, bf16[1,64,256]{2,1,0:T(8,128)(2,1)}, u32[]{:S(2)}) copy-start(bf16[1,64,256]{2,1,0:T(8,128)(2,1)} %param.9) | copy-start | bytes 98308
  14.3 92.5 %copy-start.5 = (f32[64,512]{1,0:T(8,128)S(1)}, f32[64,512]{1,0:T(8,128)}, u32[]{:S(2)}) copy-start(f32[64,512]{1,0:T(8,128)} %param.10) | copy-start | bytes 393220
  38.8 7.5 %copy-start.1 = (f32[512,512]{0,1:T(8,128)}, f32[512,512]{0,1:T(8,128)S(1)}, u32[]{:S(2)}) copy-start(f32[512,512]{0,1:T(8,128)S(1)} %convolution_select_fusion.4) | copy-start | bytes 3145732
  38.8 50.0 %collective-permute-start.4 = (f32[512,512]{0,1:T(8,128)S(1)}, f32[512,512]{0,1:T(8,128)}, u32[]{:S(2)}, u32[]{:S(2)}) collective-permute-start(f32[512,512]{0,1:T(8,128)S(1)} %convolution_select_fusion.4), channel_id=1, source_target_pairs={{0,16},{8,24},{16,32},{24,40},{32,48},{40,56},{48,64},{56,72},{64,... | collective-permute-start | bytes 3145736 | tf_op jit(solution)/shard_map/ppermute | solution.py:17
  92.6 64.1 %collective-permute-start.6 = (f32[512,512]{0,1:T(8,128)S(1)}, f32[512,512]{0,1:T(8,128)}, u32[]{:S(2)}, u32[]{:S(2)}) collective-permute-start(f32[512,512]{0,1:T(8,128)S(1)} %convolution_select_fusion.2), channel_id=1, source_target_pairs={{0,32},{8,40},{16,48},{24,56},{32,64},{40,72},{48,80},{56,88},{64,... | collective-permute-start | bytes 3145736 | tf_op jit(solution)/shard_map/ppermute | solution.py:17
  107.9 42.8 %collective-permute-start = (f32[64,512]{1,0:T(8,128)S(1)}, f32[64,512]{1,0:T(8,128)S(1)}, u32[]{:S(2)}, u32[]{:S(2)}) collective-permute-start(f32[64,512]{1,0:T(8,128)S(1)} %convolution_add_fusion.5), channel_id=1, source_target_pairs={{0,8},{8,16},{16,24},{24,32},{32,40},{40,48},{48,56},{56,64},{64,7... | collective-permute-start | bytes 393224 | tf_op jit(solution)/shard_map/ppermute | solution.py:15
  109.2 55.0 %copy-start.2 = (f32[512,512]{0,1:T(8,128)S(1)}, f32[512,512]{0,1:T(8,128)}, u32[]{:S(2)}) copy-start(f32[512,512]{0,1:T(8,128)} %copy-done.1) | copy-start | bytes 3145732
  151.5 12.7 %collective-permute-start.1 = (f32[64,512]{1,0:T(8,128)S(1)}, f32[64,512]{1,0:T(8,128)S(1)}, u32[]{:S(2)}, u32[]{:S(2)}) collective-permute-start(f32[64,512]{1,0:T(8,128)S(1)} %fusion.4), channel_id=1, source_target_pairs={{0,16},{8,24},{16,32},{24,40},{32,48},{40,56},{48,64},{56,72},{64,... | collective-permute-start | bytes 393224 | tf_op jit(solution)/shard_map/ppermute | solution.py:15
  159.8 37.7 %collective-permute-start.8 = (f32[512,512]{0,1:T(8,128)S(1)}, f32[512,512]{0,1:T(8,128)}, u32[]{:S(2)}, u32[]{:S(2)}) collective-permute-start(f32[512,512]{0,1:T(8,128)S(1)} %convolution_select_fusion.1), channel_id=1, source_target_pairs={{0,64},{8,72},{16,80},{24,88},{32,96},{40,104},{48,112},{56,120},{... | collective-permute-start | bytes 3145736 | tf_op jit(solution)/shard_map/ppermute | solution.py:17
  165.0 37.5 %copy-start.4 = (bf16[1,64,2048]{2,1,0:T(8,128)(2,1)S(1)}, bf16[1,64,2048]{2,1,0:T(8,128)(2,1)}, u32[]{:S(2)}) copy-start(bf16[1,64,2048]{2,1,0:T(8,128)(2,1)} %param.11) | copy-start | bytes 786436
  165.0 7.7 %collective-permute-start.3 = (f32[64,512]{1,0:T(8,128)S(1)}, f32[64,512]{1,0:T(8,128)S(1)}, u32[]{:S(2)}, u32[]{:S(2)}) collective-permute-start(f32[64,512]{1,0:T(8,128)S(1)} %fusion.3), channel_id=1, source_target_pairs={{0,32},{8,40},{16,48},{24,56},{32,64},{40,72},{48,80},{56,88},{64,... | collective-permute-start | bytes 393224 | tf_op jit(solution)/shard_map/ppermute | solution.py:15
  173.4 17.8 %collective-permute-start.5 = (f32[64,512]{1,0:T(8,128)S(1)}, f32[64,512]{1,0:T(8,128)S(1)}, u32[]{:S(2)}, u32[]{:S(2)}) collective-permute-start(f32[64,512]{1,0:T(8,128)S(1)} %fusion.2), channel_id=1, source_target_pairs={{0,64},{8,72},{16,80},{24,88},{32,96},{40,104},{48,112},{56,120},{... | collective-permute-start | bytes 393224 | tf_op jit(solution)/shard_map/ppermute | solution.py:15
  191.9 8.8 %collective-permute-start.7 = (f32[64,512]{1,0:T(8,128)S(1)}, f32[64,512]{1,0:T(8,128)S(1)}, u32[]{:S(2)}, u32[]{:S(2)}) collective-permute-start(f32[64,512]{1,0:T(8,128)S(1)} %fusion.1), channel_id=1, source_target_pairs={{0,128},{8,136},{16,144},{24,152},{32,160},{40,168},{48,176},{56,1... | collective-permute-start | bytes 393224 | tf_op jit(solution)/shard_map/ppermute | solution.py:15
  201.4 10.3 %copy-start.3 = (f32[64,512]{1,0:T(8,128)}, f32[64,512]{1,0:T(8,128)S(1)}, u32[]{:S(2)}) copy-start(f32[64,512]{1,0:T(8,128)S(1)} %fusion) | copy-start | bytes 393220
  254.5 10.7 %collective-permute-start.9 = (f32[256,320]{0,1:T(8,128)S(1)}, f32[256,320]{0,1:T(8,128)S(1)}, u32[]{:S(2)}, u32[]{:S(2)}) collective-permute-start(f32[256,320]{0,1:T(8,128)S(1)} %slice_select_fusion), channel_id=1, source_target_pairs={{0,128},{8,136},{16,144},{24,152},{32,160},{40,168},{48,176},{56,1... | collective-permute-start | bytes 983048 | tf_op jit(solution)/shard_map/ppermute | solution.py:37
  266.4 6.8 %collective-permute-start.10 = (f32[128,320]{0,1:T(8,128)S(1)}, f32[128,320]{0,1:T(8,128)S(1)}, u32[]{:S(2)}, u32[]{:S(2)}) collective-permute-start(f32[128,320]{0,1:T(8,128)S(1)} %slice_select_fusion.4), channel_id=1, source_target_pairs={{0,64},{8,72},{16,80},{24,88},{32,96},{40,104},{48,112},{56,120},{... | collective-permute-start | bytes 491528 | tf_op jit(solution)/shard_map/ppermute | solution.py:37
  273.3 10.5 %collective-permute-start.11 = (f32[64,320]{0,1:T(8,128)S(1)}, f32[64,320]{0,1:T(8,128)S(1)}, u32[]{:S(2)}, u32[]{:S(2)}) collective-permute-start(f32[64,320]{0,1:T(8,128)S(1)} %slice_select_fusion.3), channel_id=1, source_target_pairs={{0,32},{8,40},{16,48},{24,56},{32,0},{40,8},{48,16},{56,24},{64,96... | collective-permute-start | bytes 245768 | tf_op jit(solution)/shard_map/ppermute | solution.py:37
  284.0 13.5 %collective-permute-start.12 = (f32[32,320]{0,1:T(8,128)S(1)}, f32[32,320]{0,1:T(8,128)S(1)}, u32[]{:S(2)}, u32[]{:S(2)}) collective-permute-start(f32[32,320]{0,1:T(8,128)S(1)} %slice_select_fusion.2), channel_id=1, source_target_pairs={{0,16},{8,24},{16,0},{24,8},{32,48},{40,56},{48,32},{56,40},{64,80... | collective-permute-start | bytes 122888 | tf_op jit(solution)/shard_map/ppermute | solution.py:37
  297.7 6.2 %collective-permute-start.13 = (f32[16,320]{0,1:T(8,128)S(1)}, f32[16,320]{0,1:T(8,128)S(1)}, u32[]{:S(2)}, u32[]{:S(2)}) collective-permute-start(f32[16,320]{0,1:T(8,128)S(1)} %slice_select_fusion.1), channel_id=1, source_target_pairs={{0,8},{8,0},{16,24},{24,16},{32,40},{40,32},{48,56},{56,48},{64,72... | collective-permute-start | bytes 61448 | tf_op jit(solution)/shard_map/ppermute | solution.py:37
Sparse Core Ops, SparseCore 0:
  217.2 36.1 reduce-scatter.1

commit v2 on v1

--- a/solution.py
+++ b/solution.py
@@ -4,9 +4,13 @@
 from jax.sharding import PartitionSpec as P
 
 
-def shift_scan(matrix, vector, axis):
+def shift_scan(matrix, vector, axis, pair_axis):
     highest = lax.Precision.HIGHEST
     count, index = (lax.axis_size(axis), lax.axis_index(axis))
+    pair_count = lax.axis_size(pair_axis)
+    side = lax.axis_index(pair_axis) % 2
+    width = matrix.shape[1] // 2
+    swap = [(j, j ^ 1) for j in range(pair_count)]
     distance = 1
     while distance < count:
         pairs = [(j, j + distance) for j in range(count - distance)]
@@ -14,11 +18,18 @@
         has = index >= distance
         got_vector = lax.ppermute(vector, axis, pairs)
         if not last:
-            got_matrix = lax.ppermute(matrix, axis, pairs)
+            mine = lax.dynamic_slice_in_dim(matrix, side * width, width, axis=1)
+            got_half = lax.ppermute(mine, axis, pairs)
         newer = jnp.einsum("sq,rq->sr", got_vector, matrix, precision=highest) + vector
         vector = jnp.where(has, newer, vector)
         if not last:
-            joined = jnp.dot(matrix, got_matrix, precision=highest)
+            own = jnp.dot(matrix, got_half, precision=highest)
+            other = lax.ppermute(own, pair_axis, swap)
+            joined = jnp.where(
+                side == 0,
+                jnp.concatenate([own, other], axis=1),
+                jnp.concatenate([other, own], axis=1),
+            )
             matrix = jnp.where(has, joined, matrix)
         distance *= 2
     return vector
@@ -69,7 +80,7 @@
 
     composed, products = lax.scan(compose_step, identity_matrix, operators)
     composed = jnp.where(first_shard, jnp.zeros_like(composed), composed)
-    leaving = shift_scan(composed, last_state, "tm")
+    leaving = shift_scan(composed, last_state, "tm", "scen")
     if step_count == 1:
         states = leaving[None]
     else:

time: 313 us -> 271 us (0.87)
  waiting for transfers between devices: 187 us -> 138 us
  other arithmetic: 8.26 us -> 14.4 us
  starting transfers between devices: 67.8 us -> 73.9 us
  matrix products: 26.1 us -> 20.3 us
    ppermute x5, waiting for transfers between devices: 55.9 us -> 12.4 us  [shift_scan(): got_vector = lax.ppermute(vector, axis, pairs)]
    dot_general x4, matrix products: 13 us -> 5.94 us  [shift_scan(): own = jnp.dot(matrix, got_half, precision=highest)]
    select_n x0 -> x3, other arithmetic: none -> 6.11 us  [shift_scan(): matrix = jnp.where(has, joined, matrix)]
    ppermute x5, starting transfers between devices: 23.2 us -> 29.4 us  [shift_scan(): got_vector = lax.ppermute(vector, axis, pairs)]
    ppermute x4 -> x8, waiting for transfers between devices: 64 us -> 59.4 us  [the longest x4 55.8 us: shift_scan(): got_half = lax.ppermute(mine, axis, pairs)]
    ppermute x4 -> x8, starting transfers between devices: 27.8 us -> 27.9 us  [the longest x4 27.7 us: shift_scan(): got_half = lax.ppermute(mine, axis, pairs)]
  transfers between devices with their start and end apart: 15 -> 19, of which waited for: 11 -> 15; matrix products, arithmetic and copies ran while one was open for 4% -> 4% of each run, Pallas kernels for 0% -> 0%
where the time goes in v2:
time: 271 us; the launch traced here: 270 us
  waiting for transfers between devices  138 us (51%)
  starting transfers between devices  73.9 us (27%)
  matrix products  20.3 us (7%)
  between operations  15.1 us (6%)
  other arithmetic  14.4 us (5%)
  local copies, waits for them, and re-layouts  8.86 us (3%)
    ppermute x4, waiting for transfers between devices, shift_scan(): got_half = lax.ppermute(mine, axis, pairs)  55.8 us
    reduce_scatter x1, waiting for transfers between devices, on_device(): partial = lax.psum_scatter(joined, 'scen', scatter_dimension=1, tiled=True)  34.8 us
    ppermute x5, waiting for transfers between devices, halving_scatter(): block = keep + lax.ppermute(send, axis, pairs)  31.1 us
    ppermute x5, starting transfers between devices, shift_scan(): got_vector = lax.ppermute(vector, axis, pairs)  29.4 us
    ppermute x4, starting transfers between devices, shift_scan(): got_half = lax.ppermute(mine, axis, pairs)  27.7 us
    ppermute x5, starting transfers between devices, halving_scatter(): block = keep + lax.ppermute(send, axis, pairs)  16.6 us
    ppermute x5, waiting for transfers between devices, shift_scan(): got_vector = lax.ppermute(vector, axis, pairs)  12.4 us
    dot_general x5, matrix products, shift_scan(): jnp.einsum('sq,rq->sr', got_vector, matrix, precision=highest) + vector  6.27 us
  transfers between devices with their start and end apart: 19, of which 15 were waited for; matrix products, arithmetic and copies ran while one was open for 4% of the time, Pallas kernels for 0%

profile of v2, /device:TPU:24, one launch (start us, length us, event | category | flops | bytes accessed | tf_op | source)
XLA Modules:
  0.0 270.4 jit_solution(16619533101994089297)
XLA Ops:
  7.2 1.1 copy-done
  8.4 1.1 convolution_select_fusion
  9.5 3.9 %collective-permute-start.2 = (f32[512,256]{0,1:T(8,128)S(1)}, f32[512,256]{0,1:T(8,128)S(1)}, u32[]{:S(2)}, u32[]{:S(2)}) collective-permute-start(f32[512,256]{0,1:T(8,128)S(1)} %dynamic-slice_bitcast_fusion), channel_id=1, source_target_pairs={{0,8},{8,16},{16,24},{24,32},{32,40},{40,48},{48,56},{56,64},{64,7... | collective-permute-start | bytes 1572872 | tf_op jit(solution)/shard_map/ppermute | solution.py:22
  13.4 11.1 %collective-permute-done.2 = f32[512,256]{0,1:T(8,128)S(1)} collective-permute-done((f32[512,256]{0,1:T(8,128)S(1)}, f32[512,256]{0,1:T(8,128)S(1)}, u32[]{:S(2)}, u32[]{:S(2)}) %collective-permute-start.2) | collective-permute-done | bytes 524320 | tf_op jit(solution)/shard_map/ppermute | solution.py:22
  24.5 1.1 fusion.32
  26.4 1.3 collective-permute-done.3
  27.7 1.9 fusion.5
  29.7 5.8 %collective-permute-start.5 = (f32[512,256]{0,1:T(8,128)S(1)}, f32[512,256]{0,1:T(8,128)S(1)}, u32[]{:S(2)}, u32[]{:S(2)}) collective-permute-start(f32[512,256]{0,1:T(8,128)S(1)} %constant_dynamic-slice_fusion.2), channel_id=1, source_target_pairs={{0,16},{8,24},{16,32},{24,40},{32,48},{40,56},{48,64},{56,72},{64,... | collective-permute-start | bytes 1572872 | tf_op jit(solution)/shard_map/ppermute | solution.py:22
  35.5 22.8 %collective-permute-done.5 = f32[512,256]{0,1:T(8,128)S(1)} collective-permute-done((f32[512,256]{0,1:T(8,128)S(1)}, f32[512,256]{0,1:T(8,128)S(1)}, u32[]{:S(2)}, u32[]{:S(2)}) %collective-permute-start.5) | collective-permute-done | bytes 524320 | tf_op jit(solution)/shard_map/ppermute | solution.py:22
  58.3 1.9 fusion.33
  60.2 2.2 collective-permute-done.6
  62.5 1.9 fusion.6
  64.4 10.7 %collective-permute-start.8 = (f32[512,256]{0,1:T(8,128)S(1)}, f32[512,256]{0,1:T(8,128)S(1)}, u32[]{:S(2)}, u32[]{:S(2)}) collective-permute-start(f32[512,256]{0,1:T(8,128)S(1)} %constant_dynamic-slice_fusion.1), channel_id=1, source_target_pairs={{0,32},{8,40},{16,48},{24,56},{32,64},{40,72},{48,80},{56,88},{64,... | collective-permute-start | bytes 1572872 | tf_op jit(solution)/shard_map/ppermute | solution.py:22
  75.8 21.9 %collective-permute-done.8 = f32[512,256]{0,1:T(8,128)S(1)} collective-permute-done((f32[512,256]{0,1:T(8,128)S(1)}, f32[512,256]{0,1:T(8,128)S(1)}, u32[]{:S(2)}, u32[]{:S(2)}) %collective-permute-start.8) | collective-permute-done | bytes 524320 | tf_op jit(solution)/shard_map/ppermute | solution.py:22
  97.7 1.9 fusion.34
  99.6 0.9 fusion.17
  100.7 1.1 convolution_add_fusion.5
  101.9 1.3 collective-permute-start
  103.2 2.3 fusion.7
  105.5 7.4 %collective-permute-start.11 = (f32[512,256]{0,1:T(8,128)S(1)}, f32[512,256]{0,1:T(8,128)S(1)}, u32[]{:S(2)}, u32[]{:S(2)}) collective-permute-start(f32[512,256]{0,1:T(8,128)S(1)} %constant_dynamic-slice_fusion), channel_id=1, source_target_pairs={{0,64},{8,72},{16,80},{24,88},{32,96},{40,104},{48,112},{56,120},{... | collective-permute-start | bytes 1572872 | tf_op jit(solution)/shard_map/ppermute | solution.py:22
  112.9 0.8 fusion.4
  113.7 1.3 collective-permute-start.1
  115.0 3.4 %collective-permute-done.1 = f32[64,512]{1,0:T(8,128)S(1)} collective-permute-done((f32[64,512]{1,0:T(8,128)S(1)}, f32[64,512]{1,0:T(8,128)S(1)}, u32[]{:S(2)}, u32[]{:S(2)}) %collective-permute-start.1) | collective-permute-done | bytes 131104 | tf_op jit(solution)/shard_map/ppermute | solution.py:19
  119.1 13.9 %collective-permute-start.4 = (f32[64,512]{1,0:T(8,128)S(1)}, f32[64,512]{1,0:T(8,128)S(1)}, u32[]{:S(2)}, u32[]{:S(2)}) collective-permute-start(f32[64,512]{1,0:T(8,128)S(1)} %fusion.3), channel_id=1, source_target_pairs={{0,32},{8,40},{16,48},{24,56},{32,64},{40,72},{48,80},{56,88},{64,... | collective-permute-start | bytes 393224 | tf_op jit(solution)/shard_map/ppermute | solution.py:19
  133.0 1.1 fusion.35
  134.2 4.0 %collective-permute-done.4 = f32[64,512]{1,0:T(8,128)S(1)} collective-permute-done((f32[64,512]{1,0:T(8,128)S(1)}, f32[64,512]{1,0:T(8,128)S(1)}, u32[]{:S(2)}, u32[]{:S(2)}) %collective-permute-start.4) | collective-permute-done | bytes 131104 | tf_op jit(solution)/shard_map/ppermute | solution.py:19
  138.9 7.0 %collective-permute-start.7 = (f32[64,512]{1,0:T(8,128)S(1)}, f32[64,512]{1,0:T(8,128)S(1)}, u32[]{:S(2)}, u32[]{:S(2)}) collective-permute-start(f32[64,512]{1,0:T(8,128)S(1)} %fusion.2), channel_id=1, source_target_pairs={{0,64},{8,72},{16,80},{24,88},{32,96},{40,104},{48,112},{56,120},{... | collective-permute-start | bytes 393224 | tf_op jit(solution)/shard_map/ppermute | solution.py:19
  146.0 2.5 collective-permute-done.7
  148.5 2.0 fusion.1
  150.5 5.9 %collective-permute-start.10 = (f32[64,512]{1,0:T(8,128)S(1)}, f32[64,512]{1,0:T(8,128)S(1)}, u32[]{:S(2)}, u32[]{:S(2)}) collective-permute-start(f32[64,512]{1,0:T(8,128)S(1)} %fusion.1), channel_id=1, source_target_pairs={{0,128},{8,136},{16,144},{24,152},{32,160},{40,168},{48,176},{56,1... | collective-permute-start | bytes 393224 | tf_op jit(solution)/shard_map/ppermute | solution.py:19
  156.4 2.5 collective-permute-done.10
  158.9 2.0 fusion
  160.9 1.0 convolution_multiply_fusion.1
  162.0 3.8 %convolution_multiply_fusion = f32[512,2048]{1,0:T(8,128)} fusion(f32[64,512]{1,0:T(8,128)S(1)} %fusion, bf16[1,64,2048]{2,1,0:T(8,128)(2,1)S(1)} %copy-done.6), kind=kOutput, calls=%fused_computation.1 | convolution fusion | flops 806354944 | bytes 4587520 | tf_op jit(solution)/shard_map/tsr,tso->ro/dot_general | solution.py:93
  165.8 5.4 %copy.15 = f32[512,2048]{0,1:T(8,128)} copy(f32[512,2048]{1,0:T(8,128)} %convolution_multiply_fusion) | data formatting | bytes 8388608 | tf_op jit(solution)/shard_map/reshape | solution.py:101
  171.2 5.3 %pad_maximum_fusion = f32[512,8,320]{0,2,1:T(8,128)} fusion(f32[512,8,256]{0,2,1:T(8,128)} %bitcast.50, f32[512,8,64]{0,2,1:T(8,128)S(1)} %bitcast.51), kind=kLoop, calls=%fused_computation | loop fusion | flops 1310720 | bytes 10485760 | tf_op jit(solution)/shard_map/concatenate | solution.py:98
  176.6 34.8 %reduce-scatter.2.cloned.1.call-done = f32[512,320]{0,1:T(8,128)} async-done(((f32[512,2560]{0,1:T(8,128)}), f32[512,320]{0,1:T(8,128)}) %reduce-scatter.2.cloned.1.call-update) | async-done | bytes 655376 | tf_op jit(solution)/shard_map/reduce_scatter | solution.py:105
  211.4 1.1 slice_select_fusion
  212.5 3.2 %collective-permute-start.13 = (f32[256,320]{0,1:T(8,128)S(1)}, f32[256,320]{0,1:T(8,128)S(1)}, u32[]{:S(2)}, u32[]{:S(2)}) collective-permute-start(f32[256,320]{0,1:T(8,128)S(1)} %slice_select_fusion), channel_id=1, source_target_pairs={{0,128},{8,136},{16,144},{24,152},{32,160},{40,168},{48,176},{56,1... | collective-permute-start | bytes 983048 | tf_op jit(solution)/shard_map/ppermute | solution.py:48
  215.7 7.5 %collective-permute-done.13 = f32[256,320]{0,1:T(8,128)S(1)} collective-permute-done((f32[256,320]{0,1:T(8,128)S(1)}, f32[256,320]{0,1:T(8,128)S(1)}, u32[]{:S(2)}, u32[]{:S(2)}) %collective-permute-start.13) | collective-permute-done | bytes 327712 | tf_op jit(solution)/shard_map/ppermute | solution.py:48
  223.2 1.1 select_add_fusion
  224.4 1.6 collective-permute-start.14
  226.0 5.2 %collective-permute-done.14 = f32[128,320]{0,1:T(8,128)S(1)} collective-permute-done((f32[128,320]{0,1:T(8,128)S(1)}, f32[128,320]{0,1:T(8,128)S(1)}, u32[]{:S(2)}, u32[]{:S(2)}) %collective-permute-start.14) | collective-permute-done | bytes 163872 | tf_op jit(solution)/shard_map/ppermute | solution.py:48
  231.3 5.8 %collective-permute-start.15 = (f32[64,320]{0,1:T(8,128)S(1)}, f32[64,320]{0,1:T(8,128)S(1)}, u32[]{:S(2)}, u32[]{:S(2)}) collective-permute-start(f32[64,320]{0,1:T(8,128)S(1)} %slice_select_fusion.3), channel_id=1, source_target_pairs={{0,32},{8,40},{16,48},{24,56},{32,0},{40,8},{48,16},{56,24},{64,96... | collective-permute-start | bytes 245768 | tf_op jit(solution)/shard_map/ppermute | solution.py:48
  237.1 4.6 %collective-permute-done.15 = f32[64,320]{0,1:T(8,128)S(1)} collective-permute-done((f32[64,320]{0,1:T(8,128)S(1)}, f32[64,320]{0,1:T(8,128)S(1)}, u32[]{:S(2)}, u32[]{:S(2)}) %collective-permute-start.15) | collective-permute-done | bytes 81952 | tf_op jit(solution)/shard_map/ppermute | solution.py:48
  242.0 6.0 %collective-permute-start.16 = (f32[32,320]{0,1:T(8,128)S(1)}, f32[32,320]{0,1:T(8,128)S(1)}, u32[]{:S(2)}, u32[]{:S(2)}) collective-permute-start(f32[32,320]{0,1:T(8,128)S(1)} %slice_select_fusion.2), channel_id=1, source_target_pairs={{0,16},{8,24},{16,0},{24,8},{32,48},{40,56},{48,32},{56,40},{64,80... | collective-permute-start | bytes 122888 | tf_op jit(solution)/shard_map/ppermute | solution.py:48
  247.9 7.6 %collective-permute-done.16 = f32[32,320]{0,1:T(8,128)S(1)} collective-permute-done((f32[32,320]{0,1:T(8,128)S(1)}, f32[32,320]{0,1:T(8,128)S(1)}, u32[]{:S(2)}, u32[]{:S(2)}) %collective-permute-start.16) | collective-permute-done | bytes 40992 | tf_op jit(solution)/shard_map/ppermute | solution.py:48
  255.9 6.1 %collective-permute-done.17 = f32[16,320]{0,1:T(8,128)S(1)} collective-permute-done((f32[16,320]{0,1:T(8,128)S(1)}, f32[16,320]{0,1:T(8,128)S(1)}, u32[]{:S(2)}, u32[]{:S(2)}) %collective-permute-start.17) | collective-permute-done | bytes 20512 | tf_op jit(solution)/shard_map/ppermute | solution.py:48
  (49 shorter events, 5.0 us)
Async XLA Ops:
  7.2 1.2 copy-start
  7.2 204.2 %reduce-scatter.2.cloned.1.call-start = ((), (), s32[]{:S(2)}) async-start(), calls=%async_computation.1 | async-start | bytes 5898240 | tf_op jit(solution)/shard_map/reduce_scatter | solution.py:105
  9.5 15.0 %collective-permute-start.2 = (f32[512,256]{0,1:T(8,128)S(1)}, f32[512,256]{0,1:T(8,128)S(1)}, u32[]{:S(2)}, u32[]{:S(2)}) collective-permute-start(f32[512,256]{0,1:T(8,128)S(1)} %dynamic-slice_bitcast_fusion), channel_id=1, source_target_pairs={{0,8},{8,16},{16,24},{24,32},{32,40},{40,48},{48,56},{56,64},{64,7... | collective-permute-start | bytes 1572872 | tf_op jit(solution)/shard_map/ppermute | solution.py:22
  25.6 0.8 copy-start.4
  25.6 2.1 collective-permute-start.3
  29.7 28.6 %collective-permute-start.5 = (f32[512,256]{0,1:T(8,128)S(1)}, f32[512,256]{0,1:T(8,128)S(1)}, u32[]{:S(2)}, u32[]{:S(2)}) collective-permute-start(f32[512,256]{0,1:T(8,128)S(1)} %constant_dynamic-slice_fusion.2), channel_id=1, source_target_pairs={{0,16},{8,24},{16,32},{24,40},{32,48},{40,56},{48,64},{56,72},{64,... | collective-permute-start | bytes 1572872 | tf_op jit(solution)/shard_map/ppermute | solution.py:22
  60.2 2.3 collective-permute-start.6
  60.2 39.4 %copy-start.9 = (bf16[4,512,256]{2,1,0:T(8,128)(2,1)S(1)}, bf16[4,512,256]{2,1,0:T(8,128)(2,1)}, u32[]{:S(2)}) copy-start(bf16[4,512,256]{2,1,0:T(8,128)(2,1)} %param.7) | copy-start | bytes 3145732
  60.2 40.3 %copy-start.8 = (bf16[1,64,256]{2,1,0:T(8,128)(2,1)S(1)}, bf16[1,64,256]{2,1,0:T(8,128)(2,1)}, u32[]{:S(2)}) copy-start(bf16[1,64,256]{2,1,0:T(8,128)(2,1)} %param.9) | copy-start | bytes 98308
  60.2 40.5 %copy-start.7 = (f32[64,512]{1,0:T(8,128)S(1)}, f32[64,512]{1,0:T(8,128)}, u32[]{:S(2)}) copy-start(f32[64,512]{1,0:T(8,128)} %param.10) | copy-start | bytes 393220
  64.4 33.3 %copy-start.1 = (f32[512,512]{0,1:T(8,128)}, f32[512,512]{0,1:T(8,128)S(1)}, u32[]{:S(2)}) copy-start(f32[512,512]{0,1:T(8,128)S(1)} %fusion.6) | copy-start | bytes 3145732
  64.4 33.3 %collective-permute-start.8 = (f32[512,256]{0,1:T(8,128)S(1)}, f32[512,256]{0,1:T(8,128)S(1)}, u32[]{:S(2)}, u32[]{:S(2)}) collective-permute-start(f32[512,256]{0,1:T(8,128)S(1)} %constant_dynamic-slice_fusion.1), channel_id=1, source_target_pairs={{0,32},{8,40},{16,48},{24,56},{32,64},{40,72},{48,80},{56,88},{64,... | collective-permute-start | bytes 1572872 | tf_op jit(solution)/shard_map/ppermute | solution.py:22
  99.6 3.6 %collective-permute-start.9 = (f32[512,256]{0,1:T(8,128)}, f32[512,256]{0,1:T(8,128)}, u32[]{:S(2)}, u32[]{:S(2)}) collective-permute-start(f32[512,256]{0,1:T(8,128)} %fusion.34), channel_id=1, source_target_pairs={{0,1},{1,0},{2,3},{3,2},{4,5},{5,4},{6,7},{7,6},{8,9},{9,8},{10,11... | collective-permute-start | bytes 1572872 | tf_op jit(solution)/shard_map/ppermute | solution.py:27
  101.9 11.0 %collective-permute-start = (f32[64,512]{1,0:T(8,128)S(1)}, f32[64,512]{1,0:T(8,128)S(1)}, u32[]{:S(2)}, u32[]{:S(2)}) collective-permute-start(f32[64,512]{1,0:T(8,128)S(1)} %convolution_add_fusion.5), channel_id=1, source_target_pairs={{0,8},{8,16},{16,24},{24,32},{32,40},{40,48},{48,56},{56,64},{64,7... | collective-permute-start | bytes 393224 | tf_op jit(solution)/shard_map/ppermute | solution.py:19
  103.2 35.0 %copy-start.2 = (f32[512,512]{0,1:T(8,128)S(1)}, f32[512,512]{0,1:T(8,128)}, u32[]{:S(2)}) copy-start(f32[512,512]{0,1:T(8,128)} %copy-done.1) | copy-start | bytes 3145732
  105.5 33.5 %copy-start.3 = (f32[512,512]{0,1:T(8,128)}, f32[512,512]{0,1:T(8,128)S(1)}, u32[]{:S(2)}) copy-start(f32[512,512]{0,1:T(8,128)S(1)} %fusion.7) | copy-start | bytes 3145732
  105.5 27.5 %collective-permute-start.11 = (f32[512,256]{0,1:T(8,128)S(1)}, f32[512,256]{0,1:T(8,128)S(1)}, u32[]{:S(2)}, u32[]{:S(2)}) collective-permute-start(f32[512,256]{0,1:T(8,128)S(1)} %constant_dynamic-slice_fusion), channel_id=1, source_target_pairs={{0,64},{8,72},{16,80},{24,88},{32,96},{40,104},{48,112},{56,120},{... | collective-permute-start | bytes 1572872 | tf_op jit(solution)/shard_map/ppermute | solution.py:22
  113.7 4.7 %collective-permute-start.1 = (f32[64,512]{1,0:T(8,128)S(1)}, f32[64,512]{1,0:T(8,128)S(1)}, u32[]{:S(2)}, u32[]{:S(2)}) collective-permute-start(f32[64,512]{1,0:T(8,128)S(1)} %fusion.4), channel_id=1, source_target_pairs={{0,16},{8,24},{16,32},{24,40},{32,48},{40,56},{48,64},{56,72},{64,... | collective-permute-start | bytes 393224 | tf_op jit(solution)/shard_map/ppermute | solution.py:19
  119.1 42.8 %copy-start.6 = (bf16[1,64,2048]{2,1,0:T(8,128)(2,1)S(1)}, bf16[1,64,2048]{2,1,0:T(8,128)(2,1)}, u32[]{:S(2)}) copy-start(bf16[1,64,2048]{2,1,0:T(8,128)(2,1)} %param.11) | copy-start | bytes 786436
  119.1 19.0 %collective-permute-start.4 = (f32[64,512]{1,0:T(8,128)S(1)}, f32[64,512]{1,0:T(8,128)S(1)}, u32[]{:S(2)}, u32[]{:S(2)}) collective-permute-start(f32[64,512]{1,0:T(8,128)S(1)} %fusion.3), channel_id=1, source_target_pairs={{0,32},{8,40},{16,48},{24,56},{32,64},{40,72},{48,80},{56,88},{64,... | collective-permute-start | bytes 393224 | tf_op jit(solution)/shard_map/ppermute | solution.py:19
  134.1 24.8 %collective-permute-start.12 = (f32[512,256]{0,1:T(8,128)S(1)}, f32[512,256]{0,1:T(8,128)S(1)}, u32[]{:S(2)}, u32[]{:S(2)}) collective-permute-start(f32[512,256]{0,1:T(8,128)S(1)} %fusion.35), channel_id=1, source_target_pairs={{0,1},{1,0},{2,3},{3,2},{4,5},{5,4},{6,7},{7,6},{8,9},{9,8},{10,11... | collective-permute-start | bytes 1572872 | tf_op jit(solution)/shard_map/ppermute | solution.py:27
  138.9 9.6 %collective-permute-start.7 = (f32[64,512]{1,0:T(8,128)S(1)}, f32[64,512]{1,0:T(8,128)S(1)}, u32[]{:S(2)}, u32[]{:S(2)}) collective-permute-start(f32[64,512]{1,0:T(8,128)S(1)} %fusion.2), channel_id=1, source_target_pairs={{0,64},{8,72},{16,80},{24,88},{32,96},{40,104},{48,112},{56,120},{... | collective-permute-start | bytes 393224 | tf_op jit(solution)/shard_map/ppermute | solution.py:19
  150.5 8.4 %collective-permute-start.10 = (f32[64,512]{1,0:T(8,128)S(1)}, f32[64,512]{1,0:T(8,128)S(1)}, u32[]{:S(2)}, u32[]{:S(2)}) collective-permute-start(f32[64,512]{1,0:T(8,128)S(1)} %fusion.1), channel_id=1, source_target_pairs={{0,128},{8,136},{16,144},{24,152},{32,160},{40,168},{48,176},{56,1... | collective-permute-start | bytes 393224 | tf_op jit(solution)/shard_map/ppermute | solution.py:19
  160.9 10.3 %copy-start.5 = (f32[64,512]{1,0:T(8,128)}, f32[64,512]{1,0:T(8,128)S(1)}, u32[]{:S(2)}) copy-start(f32[64,512]{1,0:T(8,128)S(1)} %fusion) | copy-start | bytes 393220
  212.5 10.7 %collective-permute-start.13 = (f32[256,320]{0,1:T(8,128)S(1)}, f32[256,320]{0,1:T(8,128)S(1)}, u32[]{:S(2)}, u32[]{:S(2)}) collective-permute-start(f32[256,320]{0,1:T(8,128)S(1)} %slice_select_fusion), channel_id=1, source_target_pairs={{0,128},{8,136},{16,144},{24,152},{32,160},{40,168},{48,176},{56,1... | collective-permute-start | bytes 983048 | tf_op jit(solution)/shard_map/ppermute | solution.py:48
  224.4 6.8 %collective-permute-start.14 = (f32[128,320]{0,1:T(8,128)S(1)}, f32[128,320]{0,1:T(8,128)S(1)}, u32[]{:S(2)}, u32[]{:S(2)}) collective-permute-start(f32[128,320]{0,1:T(8,128)S(1)} %slice_select_fusion.4), channel_id=1, source_target_pairs={{0,64},{8,72},{16,80},{24,88},{32,96},{40,104},{48,112},{56,120},{... | collective-permute-start | bytes 491528 | tf_op jit(solution)/shard_map/ppermute | solution.py:48
  231.3 10.4 %collective-permute-start.15 = (f32[64,320]{0,1:T(8,128)S(1)}, f32[64,320]{0,1:T(8,128)S(1)}, u32[]{:S(2)}, u32[]{:S(2)}) collective-permute-start(f32[64,320]{0,1:T(8,128)S(1)} %slice_select_fusion.3), channel_id=1, source_target_pairs={{0,32},{8,40},{16,48},{24,56},{32,0},{40,8},{48,16},{56,24},{64,96... | collective-permute-start | bytes 245768 | tf_op jit(solution)/shard_map/ppermute | solution.py:48
  242.0 13.6 %collective-permute-start.16 = (f32[32,320]{0,1:T(8,128)S(1)}, f32[32,320]{0,1:T(8,128)S(1)}, u32[]{:S(2)}, u32[]{:S(2)}) collective-permute-start(f32[32,320]{0,1:T(8,128)S(1)} %slice_select_fusion.2), channel_id=1, source_target_pairs={{0,16},{8,24},{16,0},{24,8},{32,48},{40,56},{48,32},{56,40},{64,80... | collective-permute-start | bytes 122888 | tf_op jit(solution)/shard_map/ppermute | solution.py:48
  255.8 6.2 %collective-permute-start.17 = (f32[16,320]{0,1:T(8,128)S(1)}, f32[16,320]{0,1:T(8,128)S(1)}, u32[]{:S(2)}, u32[]{:S(2)}) collective-permute-start(f32[16,320]{0,1:T(8,128)S(1)} %slice_select_fusion.1), channel_id=1, source_target_pairs={{0,8},{8,0},{16,24},{24,16},{32,40},{40,32},{48,56},{56,48},{64,72... | collective-permute-start | bytes 61448 | tf_op jit(solution)/shard_map/ppermute | solution.py:48
Sparse Core Ops, SparseCore 0:
  176.7 34.6 reduce-scatter.1

commit v3 on v2

--- a/solution.py
+++ b/solution.py
@@ -31,7 +31,7 @@
                 jnp.concatenate([other, own], axis=1),
             )
             matrix = jnp.where(has, joined, matrix)
-        distance *= 2
+        distance = distance * 2
     return vector
 
 
@@ -50,7 +50,7 @@
     return block
 
 
-def on_device(operators, input_maps, segment, load, initial, observed):
+def on_device_body(operators, input_maps, segment, load, initial, observed):
     highest = lax.Precision.HIGHEST
     step_count = operators.shape[0]
     modes = operators.shape[1]
@@ -88,22 +88,20 @@
         entering = lax.ppermute(leaving, "tm", pairs)
         states = local_states + jnp.einsum("sq,trq->tsr", entering, products, precision=highest)
     normalize = 1.0 / (step_count * time_shards * local_scen * scen_shards)
-    gram_term = jnp.einsum("tsr,tsq->rq", states, states, precision=highest) * normalize
-    cross_term = (
-        jnp.einsum("tsr,tso->ro", states, observed.astype(jnp.float32), precision=highest)
-        * normalize
+    sensors = observed.shape[2]
+    cross_cols = sensors // scen_shards
+    gram_cols = modes // scen_shards
+    readings = observed.astype(jnp.float32).reshape(step_count * local_scen, scen_shards, cross_cols)
+    readings = lax.all_to_all(readings, "scen", 1, 0, tiled=True)
+    readings = readings.reshape(scen_shards, step_count, local_scen, cross_cols)
+    readings = readings.transpose(1, 0, 2, 3).reshape(step_count, scen_shards * local_scen, cross_cols)
+    every = lax.all_gather(states, "scen", axis=1, tiled=True)
+    column = lax.axis_index("scen") * gram_cols
+    right = jnp.concatenate(
+        [lax.dynamic_slice_in_dim(every, column, gram_cols, axis=2), readings], axis=2
     )
-    gram_cols = gram_term.shape[1] // scen_shards
-    cross_cols = cross_term.shape[1] // scen_shards
-    joined = jnp.concatenate(
-        [
-            gram_term.reshape(modes, scen_shards, gram_cols),
-            cross_term.reshape(modes, scen_shards, cross_cols),
-        ],
-        axis=2,
-    ).reshape(modes, scen_shards * (gram_cols + cross_cols))
-    partial = lax.psum_scatter(joined, "scen", scatter_dimension=1, tiled=True)
-    mine = halving_scatter(partial, "tm")
+    joined = jnp.einsum("tsr,tso->ro", every, right, precision=highest) * normalize
+    mine = halving_scatter(joined, "tm")
     return (states, mine[:, :gram_cols], mine[:, gram_cols:])
 
 
@@ -118,5 +116,5 @@
     )
     out_specs = (P("tm", "scen", None), P("tm", "scen"), P("tm", "scen"))
     return jax.shard_map(
-        on_device, mesh=mesh, in_specs=in_specs, out_specs=out_specs, check_vma=False
+        on_device_body, mesh=mesh, in_specs=in_specs, out_specs=out_specs, check_vma=False
     )

time: 271 us -> 241 us (0.89)
  waiting for transfers between devices: 138 us -> 121 us
  other arithmetic: 14.4 us -> 6.81 us
  starting transfers between devices: 73.9 us -> 70.6 us
    reduce_scatter x1 -> x0, waiting for transfers between devices: 34.8 us -> none  [on_device(): partial = lax.psum_scatter(joined, 'scen', scatter_dimension=1, tiled=True)]
    all_gather x0 -> x1, waiting for transfers between devices: none -> 17.3 us  [on_device_body(): every = lax.all_gather(states, 'scen', axis=1, tiled=True)]
    ppermute x5, starting transfers between devices: 16.6 us -> 8.92 us  [halving_scatter(): block = keep + lax.ppermute(send, axis, pairs)]
    concatenate x1 -> x0, other arithmetic: 5.35 us -> none  [on_device(): jnp.concatenate([gram_term.reshape(modes, scen_shards, gram_cols), cross_...]
    all_to_all x0 -> x1, starting transfers between devices: none -> 4.69 us  [on_device_body(): readings = lax.all_to_all(readings, 'scen', 1, 0, tiled=True)]
    reshape x1, local copies, waits for them, and re-layouts: 5.44 us -> 0.96 us  [on_device_body(): observed.astype(jnp.float32)]
    dot_general x4 -> x3, matrix products: 5.92 us -> 4.19 us  [the longest x1 3.08 us: on_device_body(): jnp.einsum('tsr,tso->ro', every, right, precision=highest) * normalize]
  transfers between devices with their start and end apart: 19 -> 20, of which waited for: 15 -> 15; matrix products, arithmetic and copies ran while one was open for 4% -> 4% of each run, Pallas kernels for 0% -> 0%
where the time goes in v3:
time: 241 us; the launch traced here: 238 us
  waiting for transfers between devices  121 us (50%)
  starting transfers between devices  70.6 us (29%)
  matrix products  17.8 us (7%)
  between operations  15.2 us (6%)
  local copies, waits for them, and re-layouts  6.85 us (3%)
  other arithmetic  6.81 us (3%)
    ppermute x4, waiting for transfers between devices, shift_scan(): got_half = lax.ppermute(mine, axis, pairs)  55.8 us
    ppermute x5, waiting for transfers between devices, halving_scatter(): block = keep + lax.ppermute(send, axis, pairs)  32.2 us
    ppermute x5, starting transfers between devices, shift_scan(): got_vector = lax.ppermute(vector, axis, pairs)  29 us
    ppermute x4, starting transfers between devices, shift_scan(): got_half = lax.ppermute(mine, axis, pairs)  27.7 us
    all_gather x1, waiting for transfers between devices, on_device_body(): every = lax.all_gather(states, 'scen', axis=1, tiled=True)  17.3 us
    ppermute x5, waiting for transfers between devices, shift_scan(): got_vector = lax.ppermute(vector, axis, pairs)  12.4 us
    ppermute x5, starting transfers between devices, halving_scatter(): block = keep + lax.ppermute(send, axis, pairs)  8.92 us
    select_n x3, other arithmetic, shift_scan(): matrix = jnp.where(has, joined, matrix)  6.03 us
  transfers between devices with their start and end apart: 20, of which 15 were waited for; matrix products, arithmetic and copies ran while one was open for 4% of the time, Pallas kernels for 0%

profile of v3, /device:TPU:24, one launch (start us, length us, event | category | flops | bytes accessed | tf_op | source)
XLA Modules:
  0.0 238.5 jit_solution(9623073185296784600)
XLA Ops:
  7.2 1.2 copy-done
  8.4 1.1 convolution_select_fusion
  9.5 3.9 %collective-permute-start.2 = (f32[512,256]{0,1:T(8,128)S(1)}, f32[512,256]{0,1:T(8,128)S(1)}, u32[]{:S(2)}, u32[]{:S(2)}) collective-permute-start(f32[512,256]{0,1:T(8,128)S(1)} %dynamic-slice_bitcast_fusion), channel_id=1, source_target_pairs={{0,8},{8,16},{16,24},{24,32},{32,40},{40,48},{48,56},{56,64},{64,7... | collective-permute-start | bytes 1572872 | tf_op jit(solution)/shard_map/ppermute | solution.py:22
  13.4 11.1 %collective-permute-done.2 = f32[512,256]{0,1:T(8,128)S(1)} collective-permute-done((f32[512,256]{0,1:T(8,128)S(1)}, f32[512,256]{0,1:T(8,128)S(1)}, u32[]{:S(2)}, u32[]{:S(2)}) %collective-permute-start.2) | collective-permute-done | bytes 524320 | tf_op jit(solution)/shard_map/ppermute | solution.py:22
  24.5 1.1 fusion.34
  26.4 1.3 collective-permute-done.3
  27.7 1.9 fusion.5
  29.7 5.8 %collective-permute-start.5 = (f32[512,256]{0,1:T(8,128)S(1)}, f32[512,256]{0,1:T(8,128)S(1)}, u32[]{:S(2)}, u32[]{:S(2)}) collective-permute-start(f32[512,256]{0,1:T(8,128)S(1)} %constant_dynamic-slice_fusion.2), channel_id=1, source_target_pairs={{0,16},{8,24},{16,32},{24,40},{32,48},{40,56},{48,64},{56,72},{64,... | collective-permute-start | bytes 1572872 | tf_op jit(solution)/shard_map/ppermute | solution.py:22
  35.5 22.8 %collective-permute-done.5 = f32[512,256]{0,1:T(8,128)S(1)} collective-permute-done((f32[512,256]{0,1:T(8,128)S(1)}, f32[512,256]{0,1:T(8,128)S(1)}, u32[]{:S(2)}, u32[]{:S(2)}) %collective-permute-start.5) | collective-permute-done | bytes 524320 | tf_op jit(solution)/shard_map/ppermute | solution.py:22
  58.3 1.9 fusion.35
  60.2 2.2 collective-permute-done.6
  62.4 1.9 fusion.6
  64.4 10.7 %collective-permute-start.8 = (f32[512,256]{0,1:T(8,128)S(1)}, f32[512,256]{0,1:T(8,128)S(1)}, u32[]{:S(2)}, u32[]{:S(2)}) collective-permute-start(f32[512,256]{0,1:T(8,128)S(1)} %constant_dynamic-slice_fusion.1), channel_id=1, source_target_pairs={{0,32},{8,40},{16,48},{24,56},{32,64},{40,72},{48,80},{56,88},{64,... | collective-permute-start | bytes 1572872 | tf_op jit(solution)/shard_map/ppermute | solution.py:22
  75.8 21.9 %collective-permute-done.8 = f32[512,256]{0,1:T(8,128)S(1)} collective-permute-done((f32[512,256]{0,1:T(8,128)S(1)}, f32[512,256]{0,1:T(8,128)S(1)}, u32[]{:S(2)}, u32[]{:S(2)}) %collective-permute-start.8) | collective-permute-done | bytes 524320 | tf_op jit(solution)/shard_map/ppermute | solution.py:22
  97.7 1.9 fusion.36
  99.6 0.9 fusion.17
  100.7 0.7 copy-done.7
  101.4 1.1 convolution_add_fusion.5
  102.6 1.3 collective-permute-start
  103.9 2.2 fusion.7
  106.1 7.4 %collective-permute-start.11 = (f32[512,256]{0,1:T(8,128)S(1)}, f32[512,256]{0,1:T(8,128)S(1)}, u32[]{:S(2)}, u32[]{:S(2)}) collective-permute-start(f32[512,256]{0,1:T(8,128)S(1)} %constant_dynamic-slice_fusion), channel_id=1, source_target_pairs={{0,64},{8,72},{16,80},{24,88},{32,96},{40,104},{48,112},{56,120},{... | collective-permute-start | bytes 1572872 | tf_op jit(solution)/shard_map/ppermute | solution.py:22
  113.5 0.8 fusion.4
  114.3 1.3 collective-permute-start.1
  115.6 3.4 %collective-permute-done.1 = f32[64,512]{1,0:T(8,128)S(1)} collective-permute-done((f32[64,512]{1,0:T(8,128)S(1)}, f32[64,512]{1,0:T(8,128)S(1)}, u32[]{:S(2)}, u32[]{:S(2)}) %collective-permute-start.1) | collective-permute-done | bytes 131104 | tf_op jit(solution)/shard_map/ppermute | solution.py:19
  119.0 0.8 fusion.3
  119.7 13.9 %collective-permute-start.4 = (f32[64,512]{1,0:T(8,128)S(1)}, f32[64,512]{1,0:T(8,128)S(1)}, u32[]{:S(2)}, u32[]{:S(2)}) collective-permute-start(f32[64,512]{1,0:T(8,128)S(1)} %fusion.3), channel_id=1, source_target_pairs={{0,32},{8,40},{16,48},{24,56},{32,64},{40,72},{48,80},{56,88},{64,... | collective-permute-start | bytes 393224 | tf_op jit(solution)/shard_map/ppermute | solution.py:19
  133.7 1.1 fusion.37
  134.9 4.0 %collective-permute-done.4 = f32[64,512]{1,0:T(8,128)S(1)} collective-permute-done((f32[64,512]{1,0:T(8,128)S(1)}, f32[64,512]{1,0:T(8,128)S(1)}, u32[]{:S(2)}, u32[]{:S(2)}) %collective-permute-start.4) | collective-permute-done | bytes 131104 | tf_op jit(solution)/shard_map/ppermute | solution.py:19
  138.9 0.8 fusion.2
  139.6 7.0 %collective-permute-start.7 = (f32[64,512]{1,0:T(8,128)S(1)}, f32[64,512]{1,0:T(8,128)S(1)}, u32[]{:S(2)}, u32[]{:S(2)}) collective-permute-start(f32[64,512]{1,0:T(8,128)S(1)} %fusion.2), channel_id=1, source_target_pairs={{0,64},{8,72},{16,80},{24,88},{32,96},{40,104},{48,112},{56,120},{... | collective-permute-start | bytes 393224 | tf_op jit(solution)/shard_map/ppermute | solution.py:19
  146.6 2.5 %collective-permute-done.7 = f32[64,512]{1,0:T(8,128)S(1)} collective-permute-done((f32[64,512]{1,0:T(8,128)S(1)}, f32[64,512]{1,0:T(8,128)S(1)}, u32[]{:S(2)}, u32[]{:S(2)}) %collective-permute-start.7) | collective-permute-done | bytes 131104 | tf_op jit(solution)/shard_map/ppermute | solution.py:19
  149.1 0.8 fusion.1
  149.9 5.5 %collective-permute-start.10 = (f32[64,512]{1,0:T(8,128)S(1)}, f32[64,512]{1,0:T(8,128)S(1)}, u32[]{:S(2)}, u32[]{:S(2)}) collective-permute-start(f32[64,512]{1,0:T(8,128)S(1)} %fusion.1), channel_id=1, source_target_pairs={{0,128},{8,136},{16,144},{24,152},{32,160},{40,168},{48,176},{56,1... | collective-permute-start | bytes 393224 | tf_op jit(solution)/shard_map/ppermute | solution.py:19
  155.4 2.5 %collective-permute-done.10 = f32[64,512]{1,0:T(8,128)S(1)} collective-permute-done((f32[64,512]{1,0:T(8,128)S(1)}, f32[64,512]{1,0:T(8,128)S(1)}, u32[]{:S(2)}, u32[]{:S(2)}) %collective-permute-start.10) | collective-permute-done | bytes 131104 | tf_op jit(solution)/shard_map/ppermute | solution.py:19
  158.6 2.4 %fusion = f32[64,512]{1,0:T(8,128)} fusion(f32[64,512]{1,0:T(8,128)S(1)} %fusion.1, f32[64,512]{1,0:T(8,128)} %copy-done.10, f32[512,512]{0,1:T(8,128)S(1)} %copy-done.4, f32[512,256]{0,1:T(8,128)S(1)} %collective-permute-done.12, f32[512,256]{0,1:T(8,128)S(1)} %fusion.37, pred[]{:T(512)S(6)} %ge.16, pred[]{:T(512)S(6)} %eq.52, pred[]{:T(512)S(6)} %ge.15), kind=kOutput, calls=%fused_computation.3 | convolution fusion | flops 202440704 | bytes 2490371 | tf_op jit(solution)/shard_map/sq,rq->sr/dot_general | solution.py:23
  161.1 1.0 copy.16
  162.1 4.7 %all-to-all-start = ((f32[64,8,256]{2,0,1:T(8,128)}), f32[64,8,256]{2,0,1:T(8,128)S(1)}, u32[]{:S(2)}, u32[]{:S(2)}) async-start(f32[64,8,256]{2,0,1:T(8,128)} %copy.16), calls=%async_computation | async-start | bytes 1048576 | tf_op jit(solution)/shard_map/all_to_all | solution.py:95
  166.7 17.3 %all-gather.3.cloned.1.call-done = f32[512,512]{1,0:T(8,128)} async-done(((f32[64,512]{1,0:T(8,128)}), f32[512,512]{1,0:T(8,128)}) %all-gather.3.cloned.1.call-update) | async-done | bytes 1048592 | tf_op jit(solution)/shard_map/all_gather | solution.py:98
  184.0 1.1 dynamic-slice_bitcast_fusion.1
  185.1 3.1 %convolution_multiply_fusion = f32[512,320]{0,1:T(8,128)S(1)} fusion(f32[512,512]{1,0:T(8,128)} %all-gather.3.cloned.1.call-done, f32[1,512,256]{2,1,0:T(8,128)S(1)} %bitcast.55, f32[1,512,64]{2,1,0:T(8,128)S(1)} %dynamic-slice_bitcast_fusion.1), kind=kOutput, calls=%fused_computation.1 | convolution fusion | flops 1006960640 | bytes 2359296 | tf_op jit(solution)/shard_map/tsr,tso->ro/dot_general | solution.py:103
  188.3 3.5 %collective-permute-start.13 = (f32[256,320]{0,1:T(8,128)S(1)}, f32[256,320]{0,1:T(8,128)S(1)}, u32[]{:S(2)}, u32[]{:S(2)}) collective-permute-start(f32[256,320]{0,1:T(8,128)S(1)} %slice_select_fusion), channel_id=1, source_target_pairs={{0,128},{8,136},{16,144},{24,152},{32,160},{40,168},{48,176},{56,1... | collective-permute-start | bytes 983048 | tf_op jit(solution)/shard_map/ppermute | solution.py:48
  191.8 8.1 %collective-permute-done.13 = f32[256,320]{0,1:T(8,128)S(1)} collective-permute-done((f32[256,320]{0,1:T(8,128)S(1)}, f32[256,320]{0,1:T(8,128)S(1)}, u32[]{:S(2)}, u32[]{:S(2)}) %collective-permute-start.13) | collective-permute-done | bytes 327712 | tf_op jit(solution)/shard_map/ppermute | solution.py:48
  199.9 1.1 collective-permute-start.14
  201.1 4.6 %collective-permute-done.14 = f32[128,320]{0,1:T(8,128)S(1)} collective-permute-done((f32[128,320]{0,1:T(8,128)S(1)}, f32[128,320]{0,1:T(8,128)S(1)}, u32[]{:S(2)}, u32[]{:S(2)}) %collective-permute-start.14) | collective-permute-done | bytes 163872 | tf_op jit(solution)/shard_map/ppermute | solution.py:48
  205.8 4.1 %collective-permute-start.15 = (f32[64,320]{0,1:T(8,128)S(1)}, f32[64,320]{0,1:T(8,128)S(1)}, u32[]{:S(2)}, u32[]{:S(2)}) collective-permute-start(f32[64,320]{0,1:T(8,128)S(1)} %slice_select_fusion.3), channel_id=1, source_target_pairs={{0,32},{8,40},{16,48},{24,56},{32,0},{40,8},{48,16},{56,24},{64,96... | collective-permute-start | bytes 245768 | tf_op jit(solution)/shard_map/ppermute | solution.py:48
  209.9 7.3 %collective-permute-done.15 = f32[64,320]{0,1:T(8,128)S(1)} collective-permute-done((f32[64,320]{0,1:T(8,128)S(1)}, f32[64,320]{0,1:T(8,128)S(1)}, u32[]{:S(2)}, u32[]{:S(2)}) %collective-permute-start.15) | collective-permute-done | bytes 81952 | tf_op jit(solution)/shard_map/ppermute | solution.py:48
  217.6 7.0 %collective-permute-done.16 = f32[32,320]{0,1:T(8,128)S(1)} collective-permute-done((f32[32,320]{0,1:T(8,128)S(1)}, f32[32,320]{0,1:T(8,128)S(1)}, u32[]{:S(2)}, u32[]{:S(2)}) %collective-permute-start.16) | collective-permute-done | bytes 40992 | tf_op jit(solution)/shard_map/ppermute | solution.py:48
  224.8 5.3 %collective-permute-done.17 = f32[16,320]{0,1:T(8,128)S(1)} collective-permute-done((f32[16,320]{0,1:T(8,128)S(1)}, f32[16,320]{0,1:T(8,128)S(1)}, u32[]{:S(2)}, u32[]{:S(2)}) %collective-permute-start.17) | collective-permute-done | bytes 20512 | tf_op jit(solution)/shard_map/ppermute | solution.py:48
  (53 shorter events, 4.4 us)
Async XLA Ops:
  7.2 1.2 copy-start
  7.2 176.9 %all-gather.3.cloned.1.call-start = ((), (), s32[]{:S(2)}) async-start(), calls=%async_computation.1 | async-start | bytes 1179648 | tf_op jit(solution)/shard_map/all_gather | solution.py:98
  9.5 15.0 %collective-permute-start.2 = (f32[512,256]{0,1:T(8,128)S(1)}, f32[512,256]{0,1:T(8,128)S(1)}, u32[]{:S(2)}, u32[]{:S(2)}) collective-permute-start(f32[512,256]{0,1:T(8,128)S(1)} %dynamic-slice_bitcast_fusion), channel_id=1, source_target_pairs={{0,8},{8,16},{16,24},{24,32},{32,40},{40,48},{48,56},{56,64},{64,7... | collective-permute-start | bytes 1572872 | tf_op jit(solution)/shard_map/ppermute | solution.py:22
  25.6 0.8 copy-start.5
  25.6 2.1 collective-permute-start.3
  29.7 28.6 %collective-permute-start.5 = (f32[512,256]{0,1:T(8,128)S(1)}, f32[512,256]{0,1:T(8,128)S(1)}, u32[]{:S(2)}, u32[]{:S(2)}) collective-permute-start(f32[512,256]{0,1:T(8,128)S(1)} %constant_dynamic-slice_fusion.2), channel_id=1, source_target_pairs={{0,16},{8,24},{16,32},{24,40},{32,48},{40,56},{48,64},{56,72},{64,... | collective-permute-start | bytes 1572872 | tf_op jit(solution)/shard_map/ppermute | solution.py:22
  60.2 2.3 collective-permute-start.6
  64.4 35.2 %copy-start.1 = (f32[512,512]{0,1:T(8,128)}, f32[512,512]{0,1:T(8,128)S(1)}, u32[]{:S(2)}) copy-start(f32[512,512]{0,1:T(8,128)S(1)} %fusion.6) | copy-start | bytes 3145732
  64.4 33.3 %collective-permute-start.8 = (f32[512,256]{0,1:T(8,128)S(1)}, f32[512,256]{0,1:T(8,128)S(1)}, u32[]{:S(2)}, u32[]{:S(2)}) collective-permute-start(f32[512,256]{0,1:T(8,128)S(1)} %constant_dynamic-slice_fusion.1), channel_id=1, source_target_pairs={{0,32},{8,40},{16,48},{24,56},{32,64},{40,72},{48,80},{56,88},{64,... | collective-permute-start | bytes 1572872 | tf_op jit(solution)/shard_map/ppermute | solution.py:22
  75.8 23.8 %copy-start.9 = (bf16[4,512,256]{2,1,0:T(8,128)(2,1)S(1)}, bf16[4,512,256]{2,1,0:T(8,128)(2,1)}, u32[]{:S(2)}) copy-start(bf16[4,512,256]{2,1,0:T(8,128)(2,1)} %param.7) | copy-start | bytes 3145732
  99.6 4.3 %collective-permute-start.9 = (f32[512,256]{0,1:T(8,128)}, f32[512,256]{0,1:T(8,128)}, u32[]{:S(2)}, u32[]{:S(2)}) collective-permute-start(f32[512,256]{0,1:T(8,128)} %fusion.36), channel_id=1, source_target_pairs={{0,1},{1,0},{2,3},{3,2},{4,5},{5,4},{6,7},{7,6},{8,9},{9,8},{10,11... | collective-permute-start | bytes 1572872 | tf_op jit(solution)/shard_map/ppermute | solution.py:27
  99.6 0.9 copy-start.8
  100.5 0.9 copy-start.7
  102.6 11.0 %collective-permute-start = (f32[64,512]{1,0:T(8,128)S(1)}, f32[64,512]{1,0:T(8,128)S(1)}, u32[]{:S(2)}, u32[]{:S(2)}) collective-permute-start(f32[64,512]{1,0:T(8,128)S(1)} %convolution_add_fusion.5), channel_id=1, source_target_pairs={{0,8},{8,16},{16,24},{24,32},{32,40},{40,48},{48,56},{56,64},{64,7... | collective-permute-start | bytes 393224 | tf_op jit(solution)/shard_map/ppermute | solution.py:19
  106.1 27.6 %copy-start.3 = (f32[512,512]{0,1:T(8,128)}, f32[512,512]{0,1:T(8,128)S(1)}, u32[]{:S(2)}) copy-start(f32[512,512]{0,1:T(8,128)S(1)} %fusion.7) | copy-start | bytes 3145732
  106.1 27.5 %collective-permute-start.11 = (f32[512,256]{0,1:T(8,128)S(1)}, f32[512,256]{0,1:T(8,128)S(1)}, u32[]{:S(2)}, u32[]{:S(2)}) collective-permute-start(f32[512,256]{0,1:T(8,128)S(1)} %constant_dynamic-slice_fusion), channel_id=1, source_target_pairs={{0,64},{8,72},{16,80},{24,88},{32,96},{40,104},{48,112},{56,120},{... | collective-permute-start | bytes 1572872 | tf_op jit(solution)/shard_map/ppermute | solution.py:22
  114.3 4.7 %collective-permute-start.1 = (f32[64,512]{1,0:T(8,128)S(1)}, f32[64,512]{1,0:T(8,128)S(1)}, u32[]{:S(2)}, u32[]{:S(2)}) collective-permute-start(f32[64,512]{1,0:T(8,128)S(1)} %fusion.4), channel_id=1, source_target_pairs={{0,16},{8,24},{16,32},{24,40},{32,48},{40,56},{48,64},{56,72},{64,... | collective-permute-start | bytes 393224 | tf_op jit(solution)/shard_map/ppermute | solution.py:19
  119.7 19.1 %copy-start.2 = (f32[512,512]{0,1:T(8,128)S(1)}, f32[512,512]{0,1:T(8,128)}, u32[]{:S(2)}) copy-start(f32[512,512]{0,1:T(8,128)} %copy-done.1) | copy-start | bytes 3145732
  119.7 19.1 %collective-permute-start.4 = (f32[64,512]{1,0:T(8,128)S(1)}, f32[64,512]{1,0:T(8,128)S(1)}, u32[]{:S(2)}, u32[]{:S(2)}) collective-permute-start(f32[64,512]{1,0:T(8,128)S(1)} %fusion.3), channel_id=1, source_target_pairs={{0,32},{8,40},{16,48},{24,56},{32,64},{40,72},{48,80},{56,88},{64,... | collective-permute-start | bytes 393224 | tf_op jit(solution)/shard_map/ppermute | solution.py:19
  134.8 14.3 %copy-start.4 = (f32[512,512]{0,1:T(8,128)S(1)}, f32[512,512]{0,1:T(8,128)}, u32[]{:S(2)}) copy-start(f32[512,512]{0,1:T(8,128)} %copy-done.3) | copy-start | bytes 3145732
  134.8 23.8 %collective-permute-start.12 = (f32[512,256]{0,1:T(8,128)S(1)}, f32[512,256]{0,1:T(8,128)S(1)}, u32[]{:S(2)}, u32[]{:S(2)}) collective-permute-start(f32[512,256]{0,1:T(8,128)S(1)} %fusion.37), channel_id=1, source_target_pairs={{0,1},{1,0},{2,3},{3,2},{4,5},{5,4},{6,7},{7,6},{8,9},{9,8},{10,11... | collective-permute-start | bytes 1572872 | tf_op jit(solution)/shard_map/ppermute | solution.py:27
  139.6 9.5 %collective-permute-start.7 = (f32[64,512]{1,0:T(8,128)S(1)}, f32[64,512]{1,0:T(8,128)S(1)}, u32[]{:S(2)}, u32[]{:S(2)}) collective-permute-start(f32[64,512]{1,0:T(8,128)S(1)} %fusion.2), channel_id=1, source_target_pairs={{0,64},{8,72},{16,80},{24,88},{32,96},{40,104},{48,112},{56,120},{... | collective-permute-start | bytes 393224 | tf_op jit(solution)/shard_map/ppermute | solution.py:19
  149.9 8.1 %collective-permute-start.10 = (f32[64,512]{1,0:T(8,128)S(1)}, f32[64,512]{1,0:T(8,128)S(1)}, u32[]{:S(2)}, u32[]{:S(2)}) collective-permute-start(f32[64,512]{1,0:T(8,128)S(1)} %fusion.1), channel_id=1, source_target_pairs={{0,128},{8,136},{16,144},{24,152},{32,160},{40,168},{48,176},{56,1... | collective-permute-start | bytes 393224 | tf_op jit(solution)/shard_map/ppermute | solution.py:19
  157.9 0.7 copy-start.10
  158.6 2.5 %copy-start.6 = (bf16[1,64,2048]{2,1,0:T(8,128)(2,1)S(1)}, bf16[1,64,2048]{2,1,0:T(8,128)(2,1)}, u32[]{:S(2)}) copy-start(bf16[1,64,2048]{2,1,0:T(8,128)(2,1)} %param.11) | copy-start | bytes 786436
  162.1 23.1 %all-to-all-start = ((f32[64,8,256]{2,0,1:T(8,128)}), f32[64,8,256]{2,0,1:T(8,128)S(1)}, u32[]{:S(2)}, u32[]{:S(2)}) async-start(f32[64,8,256]{2,0,1:T(8,128)} %copy.16), calls=%async_computation | async-start | bytes 1048576 | tf_op jit(solution)/shard_map/all_to_all | solution.py:95
  188.3 11.6 %collective-permute-start.13 = (f32[256,320]{0,1:T(8,128)S(1)}, f32[256,320]{0,1:T(8,128)S(1)}, u32[]{:S(2)}, u32[]{:S(2)}) collective-permute-start(f32[256,320]{0,1:T(8,128)S(1)} %slice_select_fusion), channel_id=1, source_target_pairs={{0,128},{8,136},{16,144},{24,152},{32,160},{40,168},{48,176},{56,1... | collective-permute-start | bytes 983048 | tf_op jit(solution)/shard_map/ppermute | solution.py:48
  199.9 5.7 %collective-permute-start.14 = (f32[128,320]{0,1:T(8,128)S(1)}, f32[128,320]{0,1:T(8,128)S(1)}, u32[]{:S(2)}, u32[]{:S(2)}) collective-permute-start(f32[128,320]{0,1:T(8,128)S(1)} %slice_select_fusion.4), channel_id=1, source_target_pairs={{0,64},{8,72},{16,80},{24,88},{32,96},{40,104},{48,112},{56,120},{... | collective-permute-start | bytes 491528 | tf_op jit(solution)/shard_map/ppermute | solution.py:48
  205.8 11.4 %collective-permute-start.15 = (f32[64,320]{0,1:T(8,128)S(1)}, f32[64,320]{0,1:T(8,128)S(1)}, u32[]{:S(2)}, u32[]{:S(2)}) collective-permute-start(f32[64,320]{0,1:T(8,128)S(1)} %slice_select_fusion.3), channel_id=1, source_target_pairs={{0,32},{8,40},{16,48},{24,56},{32,0},{40,8},{48,16},{56,24},{64,96... | collective-permute-start | bytes 245768 | tf_op jit(solution)/shard_map/ppermute | solution.py:48
  217.4 7.1 %collective-permute-start.16 = (f32[32,320]{0,1:T(8,128)S(1)}, f32[32,320]{0,1:T(8,128)S(1)}, u32[]{:S(2)}, u32[]{:S(2)}) collective-permute-start(f32[32,320]{0,1:T(8,128)S(1)} %slice_select_fusion.2), channel_id=1, source_target_pairs={{0,16},{8,24},{16,0},{24,8},{32,48},{40,56},{48,32},{56,40},{64,80... | collective-permute-start | bytes 122888 | tf_op jit(solution)/shard_map/ppermute | solution.py:48
  224.7 5.4 %collective-permute-start.17 = (f32[16,320]{0,1:T(8,128)S(1)}, f32[16,320]{0,1:T(8,128)S(1)}, u32[]{:S(2)}, u32[]{:S(2)}) collective-permute-start(f32[16,320]{0,1:T(8,128)S(1)} %slice_select_fusion.1), channel_id=1, source_target_pairs={{0,8},{8,0},{16,24},{24,16},{32,40},{40,32},{48,56},{56,48},{64,72... | collective-permute-start | bytes 61448 | tf_op jit(solution)/shard_map/ppermute | solution.py:48
Sparse Core Ops, SparseCore 0:
  161.1 22.8 all-gather.2

commit v4 on v3

--- a/solution.py
+++ b/solution.py
@@ -35,22 +35,42 @@
     return vector
 
 
-def halving_scatter(block, axis):
+def shift_scatter(block, axis, groups):
     count, index = (lax.axis_size(axis), lax.axis_index(axis))
-    bit = count // 2
-    while bit >= 1:
-        half = block.shape[0] // 2
-        upper = (index // bit) % 2 == 1
-        low, high = block[:half], block[half:]
-        keep = jnp.where(upper, high, low)
-        send = jnp.where(upper, low, high)
-        pairs = [(j, j ^ bit) for j in range(count)]
-        block = keep + lax.ppermute(send, axis, pairs)
-        bit //= 2
+    stride = count
+    for size in groups:
+        stride //= size
+        place = (index // stride) % size
+        chunk = block.shape[0] // size
+        total = lax.dynamic_slice_in_dim(block, place * chunk, chunk, axis=0)
+        for shift in range(1, size):
+            pairs = []
+            for j in range(count):
+                at = (j // stride) % size
+                pairs.append((j, j + (((at + shift) % size) - at) * stride))
+            target = (place + shift) % size
+            send = lax.dynamic_slice_in_dim(block, target * chunk, chunk, axis=0)
+            total = total + lax.ppermute(send, axis, pairs)
+        block = total
     return block
 
 
-def on_device_body(operators, input_maps, segment, load, initial, observed):
+def shift_gather(piece, axis, dimension):
+    count, index = (lax.axis_size(axis), lax.axis_index(axis))
+    parts = [piece]
+    for shift in range(1, count):
+        pairs = [(j, (j + shift) % count) for j in range(count)]
+        parts.append(lax.ppermute(piece, axis, pairs))
+    stacked = jnp.stack(parts, axis=0)
+    order = (index - jnp.arange(count)) % count
+    rolled = jnp.take(stacked, jnp.argsort(order), axis=0)
+    moved = jnp.moveaxis(rolled, 0, dimension)
+    shape = list(piece.shape)
+    shape[dimension] *= count
+    return moved.reshape(shape)
+
+
+def on_device_body(tm_groups, operators, input_maps, segment, load, initial, observed):
     highest = lax.Precision.HIGHEST
     step_count = operators.shape[0]
     modes = operators.shape[1]
@@ -95,13 +115,13 @@
     readings = lax.all_to_all(readings, "scen", 1, 0, tiled=True)
     readings = readings.reshape(scen_shards, step_count, local_scen, cross_cols)
     readings = readings.transpose(1, 0, 2, 3).reshape(step_count, scen_shards * local_scen, cross_cols)
-    every = lax.all_gather(states, "scen", axis=1, tiled=True)
+    every = shift_gather(states, "scen", 1)
     column = lax.axis_index("scen") * gram_cols
     right = jnp.concatenate(
         [lax.dynamic_slice_in_dim(every, column, gram_cols, axis=2), readings], axis=2
     )
     joined = jnp.einsum("tsr,tso->ro", every, right, precision=highest) * normalize
-    mine = halving_scatter(joined, "tm")
+    mine = shift_scatter(joined, "tm", tm_groups)
     return (states, mine[:, :gram_cols], mine[:, gram_cols:])
 
 
@@ -115,6 +135,12 @@
         P("tm", "scen", None),
     )
     out_specs = (P("tm", "scen", None), P("tm", "scen"), P("tm", "scen"))
+    count = dict(zip(mesh.axis_names, mesh.devices.shape))["tm"]
+    tm_groups = (count // 8, 8) if count % 8 == 0 and count > 8 else (count,)
+
+    def on_device(*args):
+        return on_device_body(tm_groups, *args)
+
     return jax.shard_map(
-        on_device_body, mesh=mesh, in_specs=in_specs, out_specs=out_specs, check_vma=False
+        on_device, mesh=mesh, in_specs=in_specs, out_specs=out_specs, check_vma=False
     )

time: 241 us -> 232 us (0.963)
  between operations: 15.2 us -> 1.81 us
  waiting for transfers between devices: 121 us -> 109 us
  starting transfers between devices: 70.6 us -> 79.9 us
  local copies, waits for them, and re-layouts: 6.85 us -> 11.8 us
    all_gather x1 -> x0, waiting for transfers between devices: 17.3 us -> none  [on_device_body(): every = lax.all_gather(states, 'scen', axis=1, tiled=True)]
    ppermute x5 -> x17, waiting for transfers between devices: 32.2 us -> 43.5 us  [the longest x10 39.3 us: shift_scatter(): total = total + lax.ppermute(send, axis, pairs)]
    ppermute x5 -> x17, starting transfers between devices: 8.92 us -> 19.4 us  [the longest x10 12 us: shift_scatter(): total = total + lax.ppermute(send, axis, pairs)]
    ppermute x5, starting transfers between devices: 29 us -> 21.6 us  [shift_scan(): got_vector = lax.ppermute(vector, axis, pairs)]
    ppermute x4, starting transfers between devices: 27.7 us -> 34 us  [shift_scan(): got_half = lax.ppermute(mine, axis, pairs)]
    ppermute x5, waiting for transfers between devices: 12.4 us -> 6.13 us  [shift_scan(): got_vector = lax.ppermute(vector, axis, pairs)]
    unnamed x25 -> x31, local copies, waits for them, and re-layouts: 4.62 us -> 6.62 us
  transfers between devices with their start and end apart: 20 -> 31, of which waited for: 15 -> 19; matrix products, arithmetic and copies ran while one was open for 4% -> 10% of each run, Pallas kernels for 0% -> 0%
where the time goes in v4:
time: 232 us; the launch traced here: 229 us
  waiting for transfers between devices  109 us (47%)
  starting transfers between devices  79.9 us (34%)
  matrix products  19.7 us (8%)
  local copies, waits for them, and re-layouts  11.8 us (5%)
  other arithmetic  7.22 us (3%)
    ppermute x4, waiting for transfers between devices, shift_scan(): got_half = lax.ppermute(mine, axis, pairs)  54.7 us
    ppermute x10, waiting for transfers between devices, shift_scatter(): total = total + lax.ppermute(send, axis, pairs)  39.3 us
    ppermute x4, starting transfers between devices, shift_scan(): got_half = lax.ppermute(mine, axis, pairs)  34 us
    ppermute x5, starting transfers between devices, shift_scan(): got_vector = lax.ppermute(vector, axis, pairs)  21.6 us
    ppermute x10, starting transfers between devices, shift_scatter(): total = total + lax.ppermute(send, axis, pairs)  12 us
    dot_general x4, matrix products, shift_scan(): own = jnp.dot(matrix, got_half, precision=highest)  7.8 us
    ppermute x7, starting transfers between devices, shift_gather(): parts.append(lax.ppermute(piece, axis, pairs))  7.35 us
    unnamed x31, local copies, waits for them, and re-layouts  6.62 us
  transfers between devices with their start and end apart: 31, of which 19 were waited for; matrix products, arithmetic and copies ran while one was open for 10% of the time, Pallas kernels for 0%

profile of v4, /device:TPU:24, one launch (start us, length us, event | category | flops | bytes accessed | tf_op | source)
XLA Modules:
  0.0 229.2 jit_solution(12336294273421362482)
XLA Ops:
  0.7 1.2 copy-done
  1.9 1.1 convolution_select_fusion
  3.0 3.9 %collective-permute-start.2 = (f32[512,256]{0,1:T(8,128)S(1)}, f32[512,256]{0,1:T(8,128)S(1)}, u32[]{:S(2)}, u32[]{:S(2)}) collective-permute-start(f32[512,256]{0,1:T(8,128)S(1)} %dynamic-slice_bitcast_fusion), channel_id=1, source_target_pairs={{0,8},{8,16},{16,24},{24,32},{32,40},{40,48},{48,56},{56,64},{64,7... | collective-permute-start | bytes 1572872 | tf_op jit(solution)/shard_map/ppermute | solution.py:22
  6.9 11.1 %collective-permute-done.2 = f32[512,256]{0,1:T(8,128)S(1)} collective-permute-done((f32[512,256]{0,1:T(8,128)S(1)}, f32[512,256]{0,1:T(8,128)S(1)}, u32[]{:S(2)}, u32[]{:S(2)}) %collective-permute-start.2) | collective-permute-done | bytes 524320 | tf_op jit(solution)/shard_map/ppermute | solution.py:22
  18.0 1.9 fusion.35
  19.9 2.2 collective-permute-done.3
  22.1 1.9 fusion.5
  24.1 5.8 %collective-permute-start.5 = (f32[512,256]{0,1:T(8,128)S(1)}, f32[512,256]{0,1:T(8,128)S(1)}, u32[]{:S(2)}, u32[]{:S(2)}) collective-permute-start(f32[512,256]{0,1:T(8,128)S(1)} %constant_dynamic-slice_fusion.12), channel_id=1, source_target_pairs={{0,16},{8,24},{16,32},{24,40},{32,48},{40,56},{48,64},{56,72},{64,... | collective-permute-start | bytes 1572872 | tf_op jit(solution)/shard_map/ppermute | solution.py:22
  29.8 22.8 %collective-permute-done.5 = f32[512,256]{0,1:T(8,128)S(1)} collective-permute-done((f32[512,256]{0,1:T(8,128)S(1)}, f32[512,256]{0,1:T(8,128)S(1)}, u32[]{:S(2)}, u32[]{:S(2)}) %collective-permute-start.5) | collective-permute-done | bytes 524320 | tf_op jit(solution)/shard_map/ppermute | solution.py:22
  52.7 1.9 fusion.36
  54.5 2.2 collective-permute-done.6
  56.8 1.9 fusion.6
  58.8 10.8 %collective-permute-start.8 = (f32[512,256]{0,1:T(8,128)S(1)}, f32[512,256]{0,1:T(8,128)S(1)}, u32[]{:S(2)}, u32[]{:S(2)}) collective-permute-start(f32[512,256]{0,1:T(8,128)S(1)} %constant_dynamic-slice_fusion.11), channel_id=1, source_target_pairs={{0,32},{8,40},{16,48},{24,56},{32,64},{40,72},{48,80},{56,88},{64,... | collective-permute-start | bytes 1572872 | tf_op jit(solution)/shard_map/ppermute | solution.py:22
  71.4 20.8 %collective-permute-done.8 = f32[512,256]{0,1:T(8,128)S(1)} collective-permute-done((f32[512,256]{0,1:T(8,128)S(1)}, f32[512,256]{0,1:T(8,128)S(1)}, u32[]{:S(2)}, u32[]{:S(2)}) %collective-permute-start.8) | collective-permute-done | bytes 524320 | tf_op jit(solution)/shard_map/ppermute | solution.py:22
  92.2 1.9 fusion.37
  94.1 1.1 convolution_add_fusion.5
  95.2 1.3 collective-permute-start
  96.5 3.6 %collective-permute-done = f32[64,512]{1,0:T(8,128)S(1)} collective-permute-done((f32[64,512]{1,0:T(8,128)S(1)}, f32[64,512]{1,0:T(8,128)S(1)}, u32[]{:S(2)}, u32[]{:S(2)}) %collective-permute-start) | collective-permute-done | bytes 131104 | tf_op jit(solution)/shard_map/ppermute | solution.py:19
  100.9 1.3 collective-permute-start.1
  102.3 1.9 fusion.7
  105.1 13.5 %collective-permute-start.11 = (f32[512,256]{0,1:T(8,128)}, f32[512,256]{0,1:T(8,128)}, u32[]{:S(2)}, u32[]{:S(2)}) collective-permute-start(f32[512,256]{0,1:T(8,128)} %constant_dynamic-slice_fusion.10), channel_id=1, source_target_pairs={{0,64},{8,72},{16,80},{24,88},{32,96},{40,104},{48,112},{56,120},{... | collective-permute-start | bytes 1572872 | tf_op jit(solution)/shard_map/ppermute | solution.py:22
  119.4 4.5 %collective-permute-start.4 = (f32[64,512]{1,0:T(8,128)S(1)}, f32[64,512]{1,0:T(8,128)S(1)}, u32[]{:S(2)}, u32[]{:S(2)}) collective-permute-start(f32[64,512]{1,0:T(8,128)S(1)} %fusion.3), channel_id=1, source_target_pairs={{0,32},{8,40},{16,48},{24,56},{32,64},{40,72},{48,80},{56,88},{64,... | collective-permute-start | bytes 393224 | tf_op jit(solution)/shard_map/ppermute | solution.py:19
  124.8 4.8 %all-to-all-start = ((f32[64,8,256]{2,0,1:T(8,128)}), f32[64,8,256]{2,0,1:T(8,128)}, u32[]{:S(2)}, u32[]{:S(2)}) async-start(f32[64,8,256]{2,0,1:T(8,128)} %copy.16), calls=%async_computation | async-start | bytes 1048576 | tf_op jit(solution)/shard_map/all_to_all | solution.py:115
  130.4 9.5 %collective-permute-start.7 = (f32[64,512]{1,0:T(8,128)S(1)}, f32[64,512]{1,0:T(8,128)S(1)}, u32[]{:S(2)}, u32[]{:S(2)}) collective-permute-start(f32[64,512]{1,0:T(8,128)S(1)} %fusion.2), channel_id=1, source_target_pairs={{0,64},{8,72},{16,80},{24,88},{32,96},{40,104},{48,112},{56,120},{... | collective-permute-start | bytes 393224 | tf_op jit(solution)/shard_map/ppermute | solution.py:19
  140.0 2.1 fusion.38
  144.0 5.0 %collective-permute-start.10 = (f32[64,512]{1,0:T(8,128)S(1)}, f32[64,512]{1,0:T(8,128)S(1)}, u32[]{:S(2)}, u32[]{:S(2)}) collective-permute-start(f32[64,512]{1,0:T(8,128)S(1)} %fusion.1), channel_id=1, source_target_pairs={{0,128},{8,136},{16,144},{24,152},{32,160},{40,168},{48,176},{56,1... | collective-permute-start | bytes 393224 | tf_op jit(solution)/shard_map/ppermute | solution.py:19
  149.0 2.5 %collective-permute-done.10 = f32[64,512]{1,0:T(8,128)S(1)} collective-permute-done((f32[64,512]{1,0:T(8,128)S(1)}, f32[64,512]{1,0:T(8,128)S(1)}, u32[]{:S(2)}, u32[]{:S(2)}) %collective-permute-start.10) | collective-permute-done | bytes 131104 | tf_op jit(solution)/shard_map/ppermute | solution.py:19
  151.5 2.7 %bitcast_dynamic-update-slice_fusion.7 = (f32[8,1,64,512]{3,2,1,0:T(8,128)}, f32[64,512]{1,0:T(8,128)S(1)}) fusion(f32[64,512]{1,0:T(8,128)S(1)} %fusion.1, f32[64,512]{1,0:T(8,128)S(1)} %collective-permute-done.10, f32[512,512]{0,1:T(8,128)S(1)} %copy-done.5, f32[512,256]{0,1:T(8,128)} %collective-permute-done.12, f32[512,256]{0,1:T(8,128)S(1)} %fusion.38, ...), kind=kOutput, calls=%fused_computation.52 | convolution fusion | flops 202440704 | bytes 2621443 | tf_op jit(solution)/shard_map/sq,rq->sr/dot_general | solution.py:23
  154.7 2.5 %collective-permute-start.15 = (f32[1,64,512]{2,1,0:T(8,128)S(1)}, f32[1,64,512]{2,1,0:T(8,128)S(1)}, u32[]{:S(2)}, u32[]{:S(2)}) collective-permute-start(f32[1,64,512]{2,1,0:T(8,128)S(1)} %bitcast.82), channel_id=1, source_target_pairs={{0,3},{1,4},{2,5},{3,6},{4,7},{5,0},{6,1},{7,2},{8,11},{9,12},{10,... | collective-permute-start | bytes 393224 | tf_op jit(solution)/shard_map/ppermute | solution.py:63
  157.2 1.1 collective-permute-start.16
  158.3 2.0 collective-permute-start.17
  160.9 1.5 collective-permute-start.19
  163.8 1.3 collective-permute-done.16
  165.8 1.9 collective-permute-done.17
  170.6 1.8 gather_fusion
  172.9 2.9 %convolution_multiply_fusion = f32[512,320]{0,1:T(8,128)S(1)} fusion(f32[512,512]{1,0:T(8,128)S(1)} %bitcast.77, f32[1,512,256]{2,1,0:T(8,128)} %bitcast.23, f32[1,512,64]{2,1,0:T(8,128)S(1)} %dynamic-slice_select_fusion), kind=kOutput, calls=%fused_computation.2 | convolution fusion | flops 1006960640 | bytes 2359296 | tf_op jit(solution)/shard_map/tsr,tso->ro/dot_general | solution.py:123
  175.9 3.3 %collective-permute-start.22 = (f32[128,320]{0,1:T(8,128)S(1)}, f32[128,320]{0,1:T(8,128)S(1)}, u32[]{:S(2)}, u32[]{:S(2)}) collective-permute-start(f32[128,320]{0,1:T(8,128)S(1)} %get-tuple-element.39), channel_id=1, source_target_pairs={{0,192},{8,200},{16,208},{24,216},{32,224},{40,232},{48,240},{56,2... | collective-permute-start | bytes 491528 | tf_op jit(solution)/shard_map/ppermute | solution.py:53
  180.0 1.3 collective-permute-start.20
  181.3 5.7 %collective-permute-done.22 = f32[128,320]{0,1:T(8,128)S(1)} collective-permute-done((f32[128,320]{0,1:T(8,128)S(1)}, f32[128,320]{0,1:T(8,128)S(1)}, u32[]{:S(2)}, u32[]{:S(2)}) %collective-permute-start.22) | collective-permute-done | bytes 163872 | tf_op jit(solution)/shard_map/ppermute | solution.py:53
  187.8 3.4 %collective-permute-done.20 = f32[128,320]{0,1:T(8,128)S(1)} collective-permute-done((f32[128,320]{0,1:T(8,128)S(1)}, f32[128,320]{0,1:T(8,128)S(1)}, u32[]{:S(2)}, u32[]{:S(2)}) %collective-permute-start.20) | collective-permute-done | bytes 163872 | tf_op jit(solution)/shard_map/ppermute | solution.py:53
  191.8 2.3 %collective-permute-start.27 = (f32[16,320]{0,1:T(8,128)S(1)}, f32[16,320]{0,1:T(8,128)S(1)}, u32[]{:S(2)}, u32[]{:S(2)}) collective-permute-start(f32[16,320]{0,1:T(8,128)S(1)} %get-tuple-element.44), channel_id=1, source_target_pairs={{0,40},{8,48},{16,56},{24,0},{32,8},{40,16},{48,24},{56,32},{64,10... | collective-permute-start | bytes 61448 | tf_op jit(solution)/shard_map/ppermute | solution.py:53
  194.2 4.1 %collective-permute-start.26 = (f32[16,320]{0,1:T(8,128)S(1)}, f32[16,320]{0,1:T(8,128)S(1)}, u32[]{:S(2)}, u32[]{:S(2)}) collective-permute-start(f32[16,320]{0,1:T(8,128)S(1)} %get-tuple-element.45), channel_id=1, source_target_pairs={{0,32},{8,40},{16,48},{24,56},{32,0},{40,8},{48,16},{56,24},{64,96... | collective-permute-start | bytes 61448 | tf_op jit(solution)/shard_map/ppermute | solution.py:53
  198.2 4.8 %collective-permute-done.29 = f32[16,320]{0,1:T(8,128)S(1)} collective-permute-done((f32[16,320]{0,1:T(8,128)S(1)}, f32[16,320]{0,1:T(8,128)S(1)}, u32[]{:S(2)}, u32[]{:S(2)}) %collective-permute-start.29) | collective-permute-done | bytes 20512 | tf_op jit(solution)/shard_map/ppermute | solution.py:53
  203.1 4.6 %collective-permute-done.28 = f32[16,320]{0,1:T(8,128)S(1)} collective-permute-done((f32[16,320]{0,1:T(8,128)S(1)}, f32[16,320]{0,1:T(8,128)S(1)}, u32[]{:S(2)}, u32[]{:S(2)}) %collective-permute-start.28) | collective-permute-done | bytes 20512 | tf_op jit(solution)/shard_map/ppermute | solution.py:53
  207.7 3.2 %collective-permute-done.27 = f32[16,320]{0,1:T(8,128)S(1)} collective-permute-done((f32[16,320]{0,1:T(8,128)S(1)}, f32[16,320]{0,1:T(8,128)S(1)}, u32[]{:S(2)}, u32[]{:S(2)}) %collective-permute-start.27) | collective-permute-done | bytes 20512 | tf_op jit(solution)/shard_map/ppermute | solution.py:53
  210.9 8.9 %collective-permute-done.25 = f32[16,320]{0,1:T(8,128)S(1)} collective-permute-done((f32[16,320]{0,1:T(8,128)S(1)}, f32[16,320]{0,1:T(8,128)S(1)}, u32[]{:S(2)}, u32[]{:S(2)}) %collective-permute-start.25) | collective-permute-done | bytes 20512 | tf_op jit(solution)/shard_map/ppermute | solution.py:53
  219.8 4.8 %collective-permute-done.24 = f32[16,320]{0,1:T(8,128)S(1)} collective-permute-done((f32[16,320]{0,1:T(8,128)S(1)}, f32[16,320]{0,1:T(8,128)S(1)}, u32[]{:S(2)}, u32[]{:S(2)}) %collective-permute-start.24) | collective-permute-done | bytes 20512 | tf_op jit(solution)/shard_map/ppermute | solution.py:53
  224.6 3.1 %collective-permute-done.23 = f32[16,320]{0,1:T(8,128)S(1)} collective-permute-done((f32[16,320]{0,1:T(8,128)S(1)}, f32[16,320]{0,1:T(8,128)S(1)}, u32[]{:S(2)}, u32[]{:S(2)}) %collective-permute-start.23) | collective-permute-done | bytes 20512 | tf_op jit(solution)/shard_map/ppermute | solution.py:53
  (85 shorter events, 17.6 us)
Async XLA Ops:
  0.6 1.2 copy-start
  3.0 15.0 %collective-permute-start.2 = (f32[512,256]{0,1:T(8,128)S(1)}, f32[512,256]{0,1:T(8,128)S(1)}, u32[]{:S(2)}, u32[]{:S(2)}) collective-permute-start(f32[512,256]{0,1:T(8,128)S(1)} %dynamic-slice_bitcast_fusion), channel_id=1, source_target_pairs={{0,8},{8,16},{16,24},{24,32},{32,40},{40,48},{48,56},{56,64},{64,7... | collective-permute-start | bytes 1572872 | tf_op jit(solution)/shard_map/ppermute | solution.py:22
  19.9 2.3 collective-permute-start.3
  24.1 28.6 %collective-permute-start.5 = (f32[512,256]{0,1:T(8,128)S(1)}, f32[512,256]{0,1:T(8,128)S(1)}, u32[]{:S(2)}, u32[]{:S(2)}) collective-permute-start(f32[512,256]{0,1:T(8,128)S(1)} %constant_dynamic-slice_fusion.12), channel_id=1, source_target_pairs={{0,16},{8,24},{16,32},{24,40},{32,48},{40,56},{48,64},{56,72},{64,... | collective-permute-start | bytes 1572872 | tf_op jit(solution)/shard_map/ppermute | solution.py:22
  54.5 2.3 collective-permute-start.6
  58.7 33.5 %copy-start.1 = (f32[512,512]{0,1:T(8,128)}, f32[512,512]{0,1:T(8,128)S(1)}, u32[]{:S(2)}) copy-start(f32[512,512]{0,1:T(8,128)S(1)} %fusion.6) | copy-start | bytes 3145732
  58.7 11.5 %copy-start.9 = (bf16[4,512,256]{2,1,0:T(8,128)(2,1)S(1)}, bf16[4,512,256]{2,1,0:T(8,128)(2,1)}, u32[]{:S(2)}) copy-start(bf16[4,512,256]{2,1,0:T(8,128)(2,1)} %param.7) | copy-start | bytes 3145732
  58.8 33.4 %collective-permute-start.8 = (f32[512,256]{0,1:T(8,128)S(1)}, f32[512,256]{0,1:T(8,128)S(1)}, u32[]{:S(2)}, u32[]{:S(2)}) collective-permute-start(f32[512,256]{0,1:T(8,128)S(1)} %constant_dynamic-slice_fusion.11), channel_id=1, source_target_pairs={{0,32},{8,40},{16,48},{24,56},{32,64},{40,72},{48,80},{56,88},{64,... | collective-permute-start | bytes 1572872 | tf_op jit(solution)/shard_map/ppermute | solution.py:22
  70.2 0.9 copy-start.8
  71.4 22.7 %copy-start.7 = (f32[64,512]{1,0:T(8,128)S(1)}, f32[64,512]{1,0:T(8,128)}, u32[]{:S(2)}) copy-start(f32[64,512]{1,0:T(8,128)} %param.10) | copy-start | bytes 393220
  94.1 8.2 %collective-permute-start.9 = (f32[512,256]{0,1:T(8,128)}, f32[512,256]{0,1:T(8,128)}, u32[]{:S(2)}, u32[]{:S(2)}) collective-permute-start(f32[512,256]{0,1:T(8,128)} %fusion.37), channel_id=1, source_target_pairs={{0,1},{1,0},{2,3},{3,2},{4,5},{5,4},{6,7},{7,6},{8,9},{9,8},{10,11... | collective-permute-start | bytes 1572872 | tf_op jit(solution)/shard_map/ppermute | solution.py:27
  95.2 5.0 %collective-permute-start = (f32[64,512]{1,0:T(8,128)S(1)}, f32[64,512]{1,0:T(8,128)S(1)}, u32[]{:S(2)}, u32[]{:S(2)}) collective-permute-start(f32[64,512]{1,0:T(8,128)S(1)} %convolution_add_fusion.5), channel_id=1, source_target_pairs={{0,8},{8,16},{16,24},{24,32},{32,40},{40,48},{48,56},{56,64},{64,7... | collective-permute-start | bytes 393224 | tf_op jit(solution)/shard_map/ppermute | solution.py:19
  96.5 5.7 %copy-start.2 = (f32[512,512]{0,1:T(8,128)S(1)}, f32[512,512]{0,1:T(8,128)}, u32[]{:S(2)}) copy-start(f32[512,512]{0,1:T(8,128)} %copy-done.1) | copy-start | bytes 3145732
  100.9 17.7 %collective-permute-start.1 = (f32[64,512]{1,0:T(8,128)S(1)}, f32[64,512]{1,0:T(8,128)S(1)}, u32[]{:S(2)}, u32[]{:S(2)}) collective-permute-start(f32[64,512]{1,0:T(8,128)S(1)} %fusion.4), channel_id=1, source_target_pairs={{0,16},{8,24},{16,32},{24,40},{32,48},{40,56},{48,64},{56,72},{64,... | collective-permute-start | bytes 393224 | tf_op jit(solution)/shard_map/ppermute | solution.py:19
  104.1 15.2 %copy-start.4 = (f32[512,512]{0,1:T(8,128)}, f32[512,512]{0,1:T(8,128)S(1)}, u32[]{:S(2)}) copy-start(f32[512,512]{0,1:T(8,128)S(1)} %fusion.7) | copy-start | bytes 3145732
  105.1 18.7 %copy-start.6 = (bf16[1,64,2048]{2,1,0:T(8,128)(2,1)S(1)}, bf16[1,64,2048]{2,1,0:T(8,128)(2,1)}, u32[]{:S(2)}) copy-start(bf16[1,64,2048]{2,1,0:T(8,128)(2,1)} %param.11) | copy-start | bytes 786436
  105.1 34.9 %collective-permute-start.11 = (f32[512,256]{0,1:T(8,128)}, f32[512,256]{0,1:T(8,128)}, u32[]{:S(2)}, u32[]{:S(2)}) collective-permute-start(f32[512,256]{0,1:T(8,128)} %constant_dynamic-slice_fusion.10), channel_id=1, source_target_pairs={{0,64},{8,72},{16,80},{24,88},{32,96},{40,104},{48,112},{56,120},{... | collective-permute-start | bytes 1572872 | tf_op jit(solution)/shard_map/ppermute | solution.py:22
  119.4 10.3 %collective-permute-start.4 = (f32[64,512]{1,0:T(8,128)S(1)}, f32[64,512]{1,0:T(8,128)S(1)}, u32[]{:S(2)}, u32[]{:S(2)}) collective-permute-start(f32[64,512]{1,0:T(8,128)S(1)} %fusion.3), channel_id=1, source_target_pairs={{0,32},{8,40},{16,48},{24,56},{32,64},{40,72},{48,80},{56,88},{64,... | collective-permute-start | bytes 393224 | tf_op jit(solution)/shard_map/ppermute | solution.py:19
  123.9 5.8 %copy-start.3 = (f32[512,512]{0,1:T(8,128)S(1)}, f32[512,512]{0,1:T(8,128)}, u32[]{:S(2)}) copy-start(f32[512,512]{0,1:T(8,128)} %copy-done.1) | copy-start | bytes 3145732
  124.8 15.1 %copy-start.5 = (f32[512,512]{0,1:T(8,128)S(1)}, f32[512,512]{0,1:T(8,128)}, u32[]{:S(2)}) copy-start(f32[512,512]{0,1:T(8,128)} %copy-done.4) | copy-start | bytes 3145732
  124.8 48.0 %all-to-all-start = ((f32[64,8,256]{2,0,1:T(8,128)}), f32[64,8,256]{2,0,1:T(8,128)}, u32[]{:S(2)}, u32[]{:S(2)}) async-start(f32[64,8,256]{2,0,1:T(8,128)} %copy.16), calls=%async_computation | async-start | bytes 1048576 | tf_op jit(solution)/shard_map/all_to_all | solution.py:115
  130.4 12.8 %collective-permute-start.7 = (f32[64,512]{1,0:T(8,128)S(1)}, f32[64,512]{1,0:T(8,128)S(1)}, u32[]{:S(2)}, u32[]{:S(2)}) collective-permute-start(f32[64,512]{1,0:T(8,128)S(1)} %fusion.2), channel_id=1, source_target_pairs={{0,64},{8,72},{16,80},{24,88},{32,96},{40,104},{48,112},{56,120},{... | collective-permute-start | bytes 393224 | tf_op jit(solution)/shard_map/ppermute | solution.py:19
  142.1 9.4 %collective-permute-start.12 = (f32[512,256]{0,1:T(8,128)S(1)}, f32[512,256]{0,1:T(8,128)}, u32[]{:S(2)}, u32[]{:S(2)}) collective-permute-start(f32[512,256]{0,1:T(8,128)S(1)} %fusion.38), channel_id=1, source_target_pairs={{0,1},{1,0},{2,3},{3,2},{4,5},{5,4},{6,7},{7,6},{8,9},{9,8},{10,11... | collective-permute-start | bytes 1572872 | tf_op jit(solution)/shard_map/ppermute | solution.py:27
  144.0 7.5 %collective-permute-start.10 = (f32[64,512]{1,0:T(8,128)S(1)}, f32[64,512]{1,0:T(8,128)S(1)}, u32[]{:S(2)}, u32[]{:S(2)}) collective-permute-start(f32[64,512]{1,0:T(8,128)S(1)} %fusion.1), channel_id=1, source_target_pairs={{0,128},{8,136},{16,144},{24,152},{32,160},{40,168},{48,176},{56,1... | collective-permute-start | bytes 393224 | tf_op jit(solution)/shard_map/ppermute | solution.py:19
  154.2 6.8 %copy-start.10 = (f32[64,512]{1,0:T(8,128)}, f32[64,512]{1,0:T(8,128)S(1)}, u32[]{:S(2)}) copy-start(f32[64,512]{1,0:T(8,128)S(1)} %get-tuple-element.49) | copy-start | bytes 393220
  154.2 6.1 %collective-permute-start.13 = (f32[1,64,512]{2,1,0:T(8,128)S(1)}, f32[1,64,512]{2,1,0:T(8,128)S(1)}, u32[]{:S(2)}, u32[]{:S(2)}) collective-permute-start(f32[1,64,512]{2,1,0:T(8,128)S(1)} %bitcast.80), channel_id=1, source_target_pairs={{0,1},{1,2},{2,3},{3,4},{4,5},{5,6},{6,7},{7,0},{8,9},{9,10},{10,1... | collective-permute-start | bytes 393224 | tf_op jit(solution)/shard_map/ppermute | solution.py:63
  154.4 6.5 %collective-permute-start.14 = (f32[1,64,512]{2,1,0:T(8,128)S(1)}, f32[1,64,512]{2,1,0:T(8,128)S(1)}, u32[]{:S(2)}, u32[]{:S(2)}) collective-permute-start(f32[1,64,512]{2,1,0:T(8,128)S(1)} %bitcast.81), channel_id=1, source_target_pairs={{0,2},{1,3},{2,4},{3,5},{4,6},{5,7},{6,0},{7,1},{8,10},{9,11},{10,... | collective-permute-start | bytes 393224 | tf_op jit(solution)/shard_map/ppermute | solution.py:63
  154.7 8.4 %collective-permute-start.15 = (f32[1,64,512]{2,1,0:T(8,128)S(1)}, f32[1,64,512]{2,1,0:T(8,128)S(1)}, u32[]{:S(2)}, u32[]{:S(2)}) collective-permute-start(f32[1,64,512]{2,1,0:T(8,128)S(1)} %bitcast.82), channel_id=1, source_target_pairs={{0,3},{1,4},{2,5},{3,6},{4,7},{5,0},{6,1},{7,2},{8,11},{9,12},{10,... | collective-permute-start | bytes 393224 | tf_op jit(solution)/shard_map/ppermute | solution.py:63
  157.2 7.9 %collective-permute-start.16 = (f32[1,64,512]{2,1,0:T(8,128)S(1)}, f32[1,64,512]{2,1,0:T(8,128)S(1)}, u32[]{:S(2)}, u32[]{:S(2)}) collective-permute-start(f32[1,64,512]{2,1,0:T(8,128)S(1)} %bitcast.83), channel_id=1, source_target_pairs={{0,4},{1,5},{2,6},{3,7},{4,0},{5,1},{6,2},{7,3},{8,12},{9,13},{10,... | collective-permute-start | bytes 393224 | tf_op jit(solution)/shard_map/ppermute | solution.py:63
  158.3 9.3 %collective-permute-start.17 = (f32[1,64,512]{2,1,0:T(8,128)S(1)}, f32[1,64,512]{2,1,0:T(8,128)S(1)}, u32[]{:S(2)}, u32[]{:S(2)}) collective-permute-start(f32[1,64,512]{2,1,0:T(8,128)S(1)} %bitcast.84), channel_id=1, source_target_pairs={{0,5},{1,6},{2,7},{3,0},{4,1},{5,2},{6,3},{7,4},{8,13},{9,14},{10,... | collective-permute-start | bytes 393224 | tf_op jit(solution)/shard_map/ppermute | solution.py:63
  160.3 9.0 %collective-permute-start.18 = (f32[1,64,512]{2,1,0:T(8,128)S(1)}, f32[1,64,512]{2,1,0:T(8,128)S(1)}, u32[]{:S(2)}, u32[]{:S(2)}) collective-permute-start(f32[1,64,512]{2,1,0:T(8,128)S(1)} %bitcast.85), channel_id=1, source_target_pairs={{0,6},{1,7},{2,0},{3,1},{4,2},{5,3},{6,4},{7,5},{8,14},{9,15},{10,... | collective-permute-start | bytes 393224 | tf_op jit(solution)/shard_map/ppermute | solution.py:63
  160.9 9.0 %collective-permute-start.19 = (f32[1,64,512]{2,1,0:T(8,128)S(1)}, f32[1,64,512]{2,1,0:T(8,128)S(1)}, u32[]{:S(2)}, u32[]{:S(2)}) collective-permute-start(f32[1,64,512]{2,1,0:T(8,128)S(1)} %bitcast.86), channel_id=1, source_target_pairs={{0,7},{1,0},{2,1},{3,2},{4,3},{5,4},{6,5},{7,6},{8,15},{9,8},{10,9... | collective-permute-start | bytes 393224 | tf_op jit(solution)/shard_map/ppermute | solution.py:63
  175.9 11.2 %collective-permute-start.22 = (f32[128,320]{0,1:T(8,128)S(1)}, f32[128,320]{0,1:T(8,128)S(1)}, u32[]{:S(2)}, u32[]{:S(2)}) collective-permute-start(f32[128,320]{0,1:T(8,128)S(1)} %get-tuple-element.39), channel_id=1, source_target_pairs={{0,192},{8,200},{16,208},{24,216},{32,224},{40,232},{48,240},{56,2... | collective-permute-start | bytes 491528 | tf_op jit(solution)/shard_map/ppermute | solution.py:53
  179.2 8.6 %collective-permute-start.21 = (f32[128,320]{0,1:T(8,128)S(1)}, f32[128,320]{0,1:T(8,128)S(1)}, u32[]{:S(2)}, u32[]{:S(2)}) collective-permute-start(f32[128,320]{0,1:T(8,128)S(1)} %get-tuple-element.40), channel_id=1, source_target_pairs={{0,128},{8,136},{16,144},{24,152},{32,160},{40,168},{48,176},{56,1... | collective-permute-start | bytes 491528 | tf_op jit(solution)/shard_map/ppermute | solution.py:53
  180.0 11.2 %collective-permute-start.20 = (f32[128,320]{0,1:T(8,128)S(1)}, f32[128,320]{0,1:T(8,128)S(1)}, u32[]{:S(2)}, u32[]{:S(2)}) collective-permute-start(f32[128,320]{0,1:T(8,128)S(1)} %get-tuple-element.38), channel_id=1, source_target_pairs={{0,64},{8,72},{16,80},{24,88},{32,96},{40,104},{48,112},{56,120},{... | collective-permute-start | bytes 491528 | tf_op jit(solution)/shard_map/ppermute | solution.py:53
  191.7 11.4 %collective-permute-start.29 = (f32[16,320]{0,1:T(8,128)S(1)}, f32[16,320]{0,1:T(8,128)S(1)}, u32[]{:S(2)}, u32[]{:S(2)}) collective-permute-start(f32[16,320]{0,1:T(8,128)S(1)} %get-tuple-element.42), channel_id=1, source_target_pairs={{0,56},{8,0},{16,8},{24,16},{32,24},{40,32},{48,40},{56,48},{64,12... | collective-permute-start | bytes 61448 | tf_op jit(solution)/shard_map/ppermute | solution.py:53
  191.7 15.9 %collective-permute-start.28 = (f32[16,320]{0,1:T(8,128)S(1)}, f32[16,320]{0,1:T(8,128)S(1)}, u32[]{:S(2)}, u32[]{:S(2)}) collective-permute-start(f32[16,320]{0,1:T(8,128)S(1)} %get-tuple-element.43), channel_id=1, source_target_pairs={{0,48},{8,56},{16,0},{24,8},{32,16},{40,24},{48,32},{56,40},{64,11... | collective-permute-start | bytes 61448 | tf_op jit(solution)/shard_map/ppermute | solution.py:53
  191.8 19.1 %collective-permute-start.27 = (f32[16,320]{0,1:T(8,128)S(1)}, f32[16,320]{0,1:T(8,128)S(1)}, u32[]{:S(2)}, u32[]{:S(2)}) collective-permute-start(f32[16,320]{0,1:T(8,128)S(1)} %get-tuple-element.44), channel_id=1, source_target_pairs={{0,40},{8,48},{16,56},{24,0},{32,8},{40,16},{48,24},{56,32},{64,10... | collective-permute-start | bytes 61448 | tf_op jit(solution)/shard_map/ppermute | solution.py:53
  194.2 16.7 %collective-permute-start.26 = (f32[16,320]{0,1:T(8,128)S(1)}, f32[16,320]{0,1:T(8,128)S(1)}, u32[]{:S(2)}, u32[]{:S(2)}) collective-permute-start(f32[16,320]{0,1:T(8,128)S(1)} %get-tuple-element.45), channel_id=1, source_target_pairs={{0,32},{8,40},{16,48},{24,56},{32,0},{40,8},{48,16},{56,24},{64,96... | collective-permute-start | bytes 61448 | tf_op jit(solution)/shard_map/ppermute | solution.py:53
  198.2 21.6 %collective-permute-start.25 = (f32[16,320]{0,1:T(8,128)S(1)}, f32[16,320]{0,1:T(8,128)S(1)}, u32[]{:S(2)}, u32[]{:S(2)}) collective-permute-start(f32[16,320]{0,1:T(8,128)S(1)} %get-tuple-element.46), channel_id=1, source_target_pairs={{0,24},{8,32},{16,40},{24,48},{32,56},{40,0},{48,8},{56,16},{64,88... | collective-permute-start | bytes 61448 | tf_op jit(solution)/shard_map/ppermute | solution.py:53
  203.1 21.5 %collective-permute-start.24 = (f32[16,320]{0,1:T(8,128)S(1)}, f32[16,320]{0,1:T(8,128)S(1)}, u32[]{:S(2)}, u32[]{:S(2)}) collective-permute-start(f32[16,320]{0,1:T(8,128)S(1)} %get-tuple-element.47), channel_id=1, source_target_pairs={{0,16},{8,24},{16,32},{24,40},{32,48},{40,56},{48,0},{56,8},{64,80... | collective-permute-start | bytes 61448 | tf_op jit(solution)/shard_map/ppermute | solution.py:53
  207.7 20.0 %collective-permute-start.23 = (f32[16,320]{0,1:T(8,128)S(1)}, f32[16,320]{0,1:T(8,128)S(1)}, u32[]{:S(2)}, u32[]{:S(2)}) collective-permute-start(f32[16,320]{0,1:T(8,128)S(1)} %get-tuple-element.41), channel_id=1, source_target_pairs={{0,8},{8,16},{16,24},{24,32},{32,40},{40,48},{48,56},{56,0},{64,72... | collective-permute-start | bytes 61448 | tf_op jit(solution)/shard_map/ppermute | solution.py:53

commit v5 on v3

--- a/solution.py
+++ b/solution.py
@@ -11,6 +11,7 @@
     side = lax.axis_index(pair_axis) % 2
     width = matrix.shape[1] // 2
     swap = [(j, j ^ 1) for j in range(pair_count)]
+    mine = lax.dynamic_slice_in_dim(matrix, side * width, width, axis=1)
     distance = 1
     while distance < count:
         pairs = [(j, j + distance) for j in range(count - distance)]
@@ -18,7 +19,6 @@
         has = index >= distance
         got_vector = lax.ppermute(vector, axis, pairs)
         if not last:
-            mine = lax.dynamic_slice_in_dim(matrix, side * width, width, axis=1)
             got_half = lax.ppermute(mine, axis, pairs)
         newer = jnp.einsum("sq,rq->sr", got_vector, matrix, precision=highest) + vector
         vector = jnp.where(has, newer, vector)
@@ -31,23 +31,9 @@
                 jnp.concatenate([other, own], axis=1),
             )
             matrix = jnp.where(has, joined, matrix)
+            mine = jnp.where(has, own, mine)
         distance = distance * 2
     return vector
-
-
-def halving_scatter(block, axis):
-    count, index = (lax.axis_size(axis), lax.axis_index(axis))
-    bit = count // 2
-    while bit >= 1:
-        half = block.shape[0] // 2
-        upper = (index // bit) % 2 == 1
-        low, high = block[:half], block[half:]
-        keep = jnp.where(upper, high, low)
-        send = jnp.where(upper, low, high)
-        pairs = [(j, j ^ bit) for j in range(count)]
-        block = keep + lax.ppermute(send, axis, pairs)
-        bit //= 2
-    return block
 
 
 def on_device_body(operators, input_maps, segment, load, initial, observed):
@@ -95,13 +81,18 @@
     readings = lax.all_to_all(readings, "scen", 1, 0, tiled=True)
     readings = readings.reshape(scen_shards, step_count, local_scen, cross_cols)
     readings = readings.transpose(1, 0, 2, 3).reshape(step_count, scen_shards * local_scen, cross_cols)
-    every = lax.all_gather(states, "scen", axis=1, tiled=True)
+    every = lax.all_to_all(
+        jnp.broadcast_to(states[None], (scen_shards,) + states.shape), "scen", 0, 0, tiled=True
+    )
+    every = every.reshape(scen_shards, step_count, local_scen, modes).transpose(1, 0, 2, 3)
+    every = every.reshape(step_count, scen_shards * local_scen, modes)
     column = lax.axis_index("scen") * gram_cols
     right = jnp.concatenate(
         [lax.dynamic_slice_in_dim(every, column, gram_cols, axis=2), readings], axis=2
     )
     joined = jnp.einsum("tsr,tso->ro", every, right, precision=highest) * normalize
-    mine = halving_scatter(joined, "tm")
+    pieces = joined.reshape(time_shards, modes // time_shards, joined.shape[1])
+    mine = lax.all_to_all(pieces, "tm", 0, 0, tiled=True).sum(axis=0)
     return (states, mine[:, :gram_cols], mine[:, gram_cols:])
 
 
@@ -115,6 +106,7 @@
         P("tm", "scen", None),
     )
     out_specs = (P("tm", "scen", None), P("tm", "scen"), P("tm", "scen"))
+
     return jax.shard_map(
         on_device_body, mesh=mesh, in_specs=in_specs, out_specs=out_specs, check_vma=False
     )

time: 241 us -> 207 us (0.86)
  waiting for transfers between devices: 121 us -> 81.3 us
  blocking collectives: 0 us -> 30.2 us
  between operations: 15.2 us -> 1.57 us
  starting transfers between devices: 70.6 us -> 63.4 us
  other arithmetic: 6.81 us -> 4.07 us
    ppermute x5 -> x0, waiting for transfers between devices: 32.2 us -> none  [halving_scatter(): block = keep + lax.ppermute(send, axis, pairs)]
    all_to_all x0 -> x1, blocking collectives: none -> 30.2 us  [on_device_body(): mine = lax.all_to_all(pieces, 'tm', 0, 0, tiled=True).sum(axis=0)]
    all_gather x1 -> x0, waiting for transfers between devices: 17.3 us -> none  [on_device_body(): every = lax.all_gather(states, 'scen', axis=1, tiled=True)]
    all_to_all x0 -> x1, waiting for transfers between devices: none -> 12.9 us  [on_device_body(): lax.all_to_all(jnp.broadcast_to(states[None], (scen_shards,) + states.sha...]
    ppermute x5 -> x0, starting transfers between devices: 8.92 us -> none  [halving_scatter(): block = keep + lax.ppermute(send, axis, pairs)]
    all_to_all x1, waiting for transfers between devices: 0.01 us -> 8.09 us  [on_device_body(): readings = lax.all_to_all(readings, 'scen', 1, 0, tiled=True)]
    all_to_all x0 -> x1, starting transfers between devices: none -> 4.82 us  [on_device_body(): lax.all_to_all(jnp.broadcast_to(states[None], (scen_shards,) + states.sha...]
    ppermute x5, waiting for transfers between devices: 12.4 us -> 7.59 us  [shift_scan(): got_vector = lax.ppermute(vector, axis, pairs)]
  transfers between devices with their start and end apart: 20 -> 15, of which waited for: 15 -> 10; matrix products, arithmetic and copies ran while one was open for 4% -> 7% of each run, Pallas kernels for 0% -> 0%
where the time goes in v5:
time: 207 us; the launch traced here: 205 us
  waiting for transfers between devices  81.3 us (39%)
  starting transfers between devices  63.4 us (31%)
  blocking collectives  30.2 us (15%)
  matrix products  18.6 us (9%)
  local copies, waits for them, and re-layouts  5.71 us (3%)
  other arithmetic  4.07 us (2%)
    ppermute x4, waiting for transfers between devices, shift_scan(): got_half = lax.ppermute(mine, axis, pairs)  52.7 us
    all_to_all x1, blocking collectives, on_device_body(): mine = lax.all_to_all(pieces, 'tm', 0, 0, tiled=True).sum(axis=0)  30.2 us
    ppermute x5, starting transfers between devices, shift_scan(): got_vector = lax.ppermute(vector, axis, pairs)  26.6 us
    ppermute x4, starting transfers between devices, shift_scan(): got_half = lax.ppermute(mine, axis, pairs)  26.1 us
    all_to_all x1, waiting for transfers between devices, on_device_body(): lax.all_to_all(jnp.broadcast_to(states[None], (scen_shards,) + states.sha...  12.9 us
    dot_general x4, matrix products, shift_scan(): own = jnp.dot(matrix, got_half, precision=highest)  9.62 us
    all_to_all x1, waiting for transfers between devices, on_device_body(): readings = lax.all_to_all(readings, 'scen', 1, 0, tiled=True)  8.09 us
    ppermute x5, waiting for transfers between devices, shift_scan(): got_vector = lax.ppermute(vector, axis, pairs)  7.59 us
  transfers between devices with their start and end apart: 15, of which 10 were waited for; matrix products, arithmetic and copies ran while one was open for 7% of the time, Pallas kernels for 0%

profile of v5, /device:TPU:24, one launch (start us, length us, event | category | flops | bytes accessed | tf_op | source)
XLA Modules:
  0.0 204.8 jit_solution(14621002914668150140)
XLA Ops:
  0.7 1.2 copy-done
  1.9 1.1 convolution_select_fusion
  3.0 4.6 %collective-permute-start.2 = (f32[512,256]{0,1:T(8,128)S(1)}, f32[512,256]{0,1:T(8,128)}, u32[]{:S(2)}, u32[]{:S(2)}) collective-permute-start(f32[512,256]{0,1:T(8,128)S(1)} %dynamic-slice_bitcast_fusion), channel_id=1, source_target_pairs={{0,8},{8,16},{16,24},{24,32},{32,40},{40,48},{48,56},{56,64},{64,7... | collective-permute-start | bytes 1572872 | tf_op jit(solution)/shard_map/ppermute | solution.py:22
  7.6 10.4 %collective-permute-done.2 = f32[512,256]{0,1:T(8,128)} collective-permute-done((f32[512,256]{0,1:T(8,128)S(1)}, f32[512,256]{0,1:T(8,128)}, u32[]{:S(2)}, u32[]{:S(2)}) %collective-permute-start.2) | collective-permute-done | bytes 524320 | tf_op jit(solution)/shard_map/ppermute | solution.py:22
  18.0 2.9 %broadcast_select_fusion.2 = (f32[512,256]{0,1:T(8,128)}, f32[512,256]{0,1:T(8,128)S(1)}) fusion(f32[512,256]{0,1:T(8,128)S(1)} %dynamic-slice_bitcast_fusion, pred[]{:T(512)S(6)} %ge.19, f32[512,512]{1,0:T(8,128)S(1)} %convolution_select_fusion, f32[512,256]{0,1:T(8,128)} %collective-permute-done.2), kind=kOutput, calls=%fused_computation.42 | convolution fusion | flops 805437440 | bytes 3145729 | tf_op jit(solution)/shard_map/dot_general | solution.py:26
  20.9 6.6 %collective-permute-start.5 = (f32[512,256]{0,1:T(8,128)}, f32[512,256]{0,1:T(8,128)}, u32[]{:S(2)}, u32[]{:S(2)}) collective-permute-start(f32[512,256]{0,1:T(8,128)} %get-tuple-element.18), channel_id=1, source_target_pairs={{0,16},{8,24},{16,32},{24,40},{32,48},{40,56},{48,64},{56,72},{64,... | collective-permute-start | bytes 1572872 | tf_op jit(solution)/shard_map/ppermute | solution.py:22
  28.2 1.9 fusion.5
  30.1 20.2 %collective-permute-done.5 = f32[512,256]{0,1:T(8,128)} collective-permute-done((f32[512,256]{0,1:T(8,128)}, f32[512,256]{0,1:T(8,128)}, u32[]{:S(2)}, u32[]{:S(2)}) %collective-permute-start.5) | collective-permute-done | bytes 524320 | tf_op jit(solution)/shard_map/ppermute | solution.py:22
  50.3 3.3 %broadcast_select_fusion.1 = (f32[512,256]{0,1:T(8,128)}, f32[512,256]{0,1:T(8,128)}) fusion(f32[512,256]{0,1:T(8,128)} %get-tuple-element.18, pred[]{:T(512)S(6)} %ge.18, f32[512,512]{0,1:T(8,128)S(1)} %fusion.5, f32[512,256]{0,1:T(8,128)} %collective-permute-done.5), kind=kOutput, calls=%fused_computation.41 | convolution fusion | flops 805437440 | bytes 3145729 | tf_op jit(solution)/shard_map/dot_general | solution.py:26
  53.6 0.9 fusion.17
  54.5 0.2 convolution_bitcast_fusion
  54.7 11.4 %collective-permute-start.8 = (f32[512,256]{0,1:T(8,128)}, f32[512,256]{0,1:T(8,128)}, u32[]{:S(2)}, u32[]{:S(2)}) collective-permute-start(f32[512,256]{0,1:T(8,128)} %get-tuple-element.23), channel_id=1, source_target_pairs={{0,32},{8,40},{16,48},{24,56},{32,64},{40,72},{48,80},{56,88},{64,... | collective-permute-start | bytes 1572872 | tf_op jit(solution)/shard_map/ppermute | solution.py:22
  66.1 1.1 convolution_add_fusion.5
  67.2 1.3 collective-permute-start
  68.5 1.9 fusion.6
  70.5 18.0 %collective-permute-done.8 = f32[512,256]{0,1:T(8,128)} collective-permute-done((f32[512,256]{0,1:T(8,128)}, f32[512,256]{0,1:T(8,128)}, u32[]{:S(2)}, u32[]{:S(2)}) %collective-permute-start.8) | collective-permute-done | bytes 524320 | tf_op jit(solution)/shard_map/ppermute | solution.py:22
  88.4 2.3 %broadcast_select_fusion = (f32[512,256]{0,1:T(8,128)S(1)}, f32[512,256]{0,1:T(8,128)S(1)}) fusion(f32[512,256]{0,1:T(8,128)} %get-tuple-element.23, pred[]{:T(512)S(6)} %ge.17, f32[512,512]{0,1:T(8,128)S(1)} %fusion.6, f32[512,256]{0,1:T(8,128)} %collective-permute-done.8), kind=kOutput, calls=%fused_computation.40 | convolution fusion | flops 805437440 | bytes 3145729 | tf_op jit(solution)/shard_map/dot_general | solution.py:26
  90.9 0.2 collective-permute-done
  91.1 0.8 fusion.4
  91.9 5.2 %collective-permute-start.1 = (f32[64,512]{1,0:T(8,128)S(1)}, f32[64,512]{1,0:T(8,128)S(1)}, u32[]{:S(2)}, u32[]{:S(2)}) collective-permute-start(f32[64,512]{1,0:T(8,128)S(1)} %fusion.4), channel_id=1, source_target_pairs={{0,16},{8,24},{16,32},{24,40},{32,48},{40,56},{48,64},{56,72},{64,... | collective-permute-start | bytes 393224 | tf_op jit(solution)/shard_map/ppermute | solution.py:20
  97.1 3.4 %collective-permute-start.11 = (f32[512,256]{0,1:T(8,128)S(1)}, f32[512,256]{0,1:T(8,128)S(1)}, u32[]{:S(2)}, u32[]{:S(2)}) collective-permute-start(f32[512,256]{0,1:T(8,128)S(1)} %get-tuple-element.28), channel_id=1, source_target_pairs={{0,64},{8,72},{16,80},{24,88},{32,96},{40,104},{48,112},{56,120},{... | collective-permute-start | bytes 1572872 | tf_op jit(solution)/shard_map/ppermute | solution.py:22
  100.5 2.4 %collective-permute-done.1 = f32[64,512]{1,0:T(8,128)S(1)} collective-permute-done((f32[64,512]{1,0:T(8,128)S(1)}, f32[64,512]{1,0:T(8,128)S(1)}, u32[]{:S(2)}, u32[]{:S(2)}) %collective-permute-start.1) | collective-permute-done | bytes 131104 | tf_op jit(solution)/shard_map/ppermute | solution.py:20
  102.9 0.8 fusion.3
  103.7 7.0 %collective-permute-start.4 = (f32[64,512]{1,0:T(8,128)S(1)}, f32[64,512]{1,0:T(8,128)S(1)}, u32[]{:S(2)}, u32[]{:S(2)}) collective-permute-start(f32[64,512]{1,0:T(8,128)S(1)} %fusion.3), channel_id=1, source_target_pairs={{0,32},{8,40},{16,48},{24,56},{32,64},{40,72},{48,80},{56,88},{64,... | collective-permute-start | bytes 393224 | tf_op jit(solution)/shard_map/ppermute | solution.py:20
  110.7 0.2 fusion.7
  111.0 4.2 %collective-permute-done.11 = f32[512,256]{0,1:T(8,128)S(1)} collective-permute-done((f32[512,256]{0,1:T(8,128)S(1)}, f32[512,256]{0,1:T(8,128)S(1)}, u32[]{:S(2)}, u32[]{:S(2)}) %collective-permute-start.11) | collective-permute-done | bytes 524320 | tf_op jit(solution)/shard_map/ppermute | solution.py:22
  115.2 1.1 fusion.34
  116.3 0.3 collective-permute-start.12
  116.6 0.8 fusion.2
  117.3 5.8 %collective-permute-start.7 = (f32[64,512]{1,0:T(8,128)S(1)}, f32[64,512]{1,0:T(8,128)S(1)}, u32[]{:S(2)}, u32[]{:S(2)}) collective-permute-start(f32[64,512]{1,0:T(8,128)S(1)} %fusion.2), channel_id=1, source_target_pairs={{0,64},{8,72},{16,80},{24,88},{32,96},{40,104},{48,112},{56,120},{... | collective-permute-start | bytes 393224 | tf_op jit(solution)/shard_map/ppermute | solution.py:20
  123.2 2.5 %collective-permute-done.7 = f32[64,512]{1,0:T(8,128)S(1)} collective-permute-done((f32[64,512]{1,0:T(8,128)S(1)}, f32[64,512]{1,0:T(8,128)S(1)}, u32[]{:S(2)}, u32[]{:S(2)}) %collective-permute-start.7) | collective-permute-done | bytes 131104 | tf_op jit(solution)/shard_map/ppermute | solution.py:20
  125.7 0.8 fusion.1
  126.4 7.2 %collective-permute-start.10 = (f32[64,512]{1,0:T(8,128)S(1)}, f32[64,512]{1,0:T(8,128)S(1)}, u32[]{:S(2)}, u32[]{:S(2)}) collective-permute-start(f32[64,512]{1,0:T(8,128)S(1)} %fusion.1), channel_id=1, source_target_pairs={{0,128},{8,136},{16,144},{24,152},{32,160},{40,168},{48,176},{56,1... | collective-permute-start | bytes 393224 | tf_op jit(solution)/shard_map/ppermute | solution.py:20
  133.6 2.5 %collective-permute-done.10 = f32[64,512]{1,0:T(8,128)S(1)} collective-permute-done((f32[64,512]{1,0:T(8,128)S(1)}, f32[64,512]{1,0:T(8,128)S(1)}, u32[]{:S(2)}, u32[]{:S(2)}) %collective-permute-start.10) | collective-permute-done | bytes 131104 | tf_op jit(solution)/shard_map/ppermute | solution.py:20
  136.1 0.8 fusion
  136.9 0.7 copy-done.3
  137.6 1.1 broadcast_in_dim.19
  138.7 4.8 %all-to-all-start = ((f32[8,1,64,512]{3,2,1,0:T(8,128)}), f32[8,1,64,512]{3,2,1,0:T(8,128)S(1)}, u32[]{:S(2)}, u32[]{:S(2)}) async-start(f32[8,1,64,512]{3,2,1,0:T(8,128)} %broadcast_in_dim.19), calls=%async_computation | async-start | bytes 2097152 | tf_op jit(solution)/shard_map/all_to_all | solution.py:84
  143.6 1.0 copy.12
  144.5 12.9 %all-to-all-done = f32[8,1,64,512]{3,2,1,0:T(8,128)S(1)} async-done(((f32[8,1,64,512]{3,2,1,0:T(8,128)}), f32[8,1,64,512]{3,2,1,0:T(8,128)S(1)}, u32[]{:S(2)}, u32[]{:S(2)}) %all-to-all-start) | async-done | bytes 1048608 | tf_op jit(solution)/shard_map/all_to_all | solution.py:84
  157.4 5.5 %all-to-all-start.1 = ((f32[64,8,256]{2,0,1:T(8,128)}), f32[64,8,256]{2,0,1:T(8,128)S(1)}, u32[]{:S(2)}, u32[]{:S(2)}) async-start(f32[64,8,256]{2,0,1:T(8,128)} %copy.12), calls=%async_computation.1 | async-start | bytes 1048576 | tf_op jit(solution)/shard_map/all_to_all | solution.py:81
  162.9 0.1 constant_dynamic-slice_fusion
  163.0 8.1 %all-to-all-done.1 = f32[64,8,256]{2,0,1:T(8,128)S(1)} async-done(((f32[64,8,256]{2,0,1:T(8,128)}), f32[64,8,256]{2,0,1:T(8,128)S(1)}, u32[]{:S(2)}, u32[]{:S(2)}) %all-to-all-start.1) | async-done | bytes 524320 | tf_op jit(solution)/shard_map/all_to_all | solution.py:81
  171.1 1.9 convolution_multiply_fusion
  173.0 0.3 copy.13
  173.3 30.2 %all_to_all.25 = f32[32,16,320]{2,1,0:T(8,128)S(1)} all-to-all(f32[32,16,320]{2,1,0:T(8,128)S(1)} %bitcast.58), channel_id=1, replica_groups=mesh['tm'=32,'scen'=8] {'tm'}, dimensions={0} | all-to-all | bytes 1310720 | tf_op jit(solution)/shard_map/all_to_all | solution.py:95
  203.6 0.6 slice.8
  204.2 0.7 slice.9
  (23 shorter events, 0.3 us)
Async XLA Ops:
  0.6 1.2 copy-start
  3.0 15.0 %collective-permute-start.2 = (f32[512,256]{0,1:T(8,128)S(1)}, f32[512,256]{0,1:T(8,128)}, u32[]{:S(2)}, u32[]{:S(2)}) collective-permute-start(f32[512,256]{0,1:T(8,128)S(1)} %dynamic-slice_bitcast_fusion), channel_id=1, source_target_pairs={{0,8},{8,16},{16,24},{24,32},{32,40},{40,48},{48,56},{56,64},{64,7... | collective-permute-start | bytes 1572872 | tf_op jit(solution)/shard_map/ppermute | solution.py:22
  20.9 7.3 %copy-start.1 = (f32[512,256]{0,1:T(8,128)}, f32[512,256]{0,1:T(8,128)S(1)}, u32[]{:S(2)}) copy-start(f32[512,256]{0,1:T(8,128)S(1)} %get-tuple-element.22) | copy-start | bytes 1572868
  20.9 7.3 %collective-permute-start.3 = (f32[512,256]{0,1:T(8,128)S(1)}, f32[512,256]{0,1:T(8,128)}, u32[]{:S(2)}, u32[]{:S(2)}) collective-permute-start(f32[512,256]{0,1:T(8,128)S(1)} %get-tuple-element.22), channel_id=1, source_target_pairs={{0,1},{1,0},{2,3},{3,2},{4,5},{5,4},{6,7},{7,6},{8,9},{9,8},{10,11... | collective-permute-start | bytes 1572872 | tf_op jit(solution)/shard_map/ppermute | solution.py:27
  20.9 29.4 %collective-permute-start.5 = (f32[512,256]{0,1:T(8,128)}, f32[512,256]{0,1:T(8,128)}, u32[]{:S(2)}, u32[]{:S(2)}) collective-permute-start(f32[512,256]{0,1:T(8,128)} %get-tuple-element.18), channel_id=1, source_target_pairs={{0,16},{8,24},{16,32},{24,40},{32,48},{40,56},{48,64},{56,72},{64,... | collective-permute-start | bytes 1572872 | tf_op jit(solution)/shard_map/ppermute | solution.py:22
  30.1 23.5 %copy-start.6 = (bf16[4,512,256]{2,1,0:T(8,128)(2,1)S(1)}, bf16[4,512,256]{2,1,0:T(8,128)(2,1)}, u32[]{:S(2)}) copy-start(bf16[4,512,256]{2,1,0:T(8,128)(2,1)} %param.7) | copy-start | bytes 3145732
  53.6 15.0 %collective-permute-start.6 = (f32[512,256]{0,1:T(8,128)}, f32[512,256]{0,1:T(8,128)}, u32[]{:S(2)}, u32[]{:S(2)}) collective-permute-start(f32[512,256]{0,1:T(8,128)} %get-tuple-element.24), channel_id=1, source_target_pairs={{0,1},{1,0},{2,3},{3,2},{4,5},{5,4},{6,7},{7,6},{8,9},{9,8},{10,11... | collective-permute-start | bytes 1572872 | tf_op jit(solution)/shard_map/ppermute | solution.py:27
  53.6 0.9 copy-start.5
  54.5 11.6 %copy-start.4 = (f32[64,512]{1,0:T(8,128)S(1)}, f32[64,512]{1,0:T(8,128)}, u32[]{:S(2)}) copy-start(f32[64,512]{1,0:T(8,128)} %param.10) | copy-start | bytes 393220
  54.7 33.7 %collective-permute-start.8 = (f32[512,256]{0,1:T(8,128)}, f32[512,256]{0,1:T(8,128)}, u32[]{:S(2)}, u32[]{:S(2)}) collective-permute-start(f32[512,256]{0,1:T(8,128)} %get-tuple-element.23), channel_id=1, source_target_pairs={{0,32},{8,40},{16,48},{24,56},{32,64},{40,72},{48,80},{56,88},{64,... | collective-permute-start | bytes 1572872 | tf_op jit(solution)/shard_map/ppermute | solution.py:22
  67.2 23.9 %collective-permute-start = (f32[64,512]{1,0:T(8,128)S(1)}, f32[64,512]{1,0:T(8,128)S(1)}, u32[]{:S(2)}, u32[]{:S(2)}) collective-permute-start(f32[64,512]{1,0:T(8,128)S(1)} %convolution_add_fusion.5), channel_id=1, source_target_pairs={{0,8},{8,16},{16,24},{24,32},{32,40},{40,48},{48,56},{56,64},{64,7... | collective-permute-start | bytes 393224 | tf_op jit(solution)/shard_map/ppermute | solution.py:20
  90.8 20.0 %collective-permute-start.9 = (f32[512,256]{0,1:T(8,128)S(1)}, f32[512,256]{0,1:T(8,128)S(1)}, u32[]{:S(2)}, u32[]{:S(2)}) collective-permute-start(f32[512,256]{0,1:T(8,128)S(1)} %get-tuple-element.29), channel_id=1, source_target_pairs={{0,1},{1,0},{2,3},{3,2},{4,5},{5,4},{6,7},{7,6},{8,9},{9,8},{10,11... | collective-permute-start | bytes 1572872 | tf_op jit(solution)/shard_map/ppermute | solution.py:27
  91.9 11.0 %collective-permute-start.1 = (f32[64,512]{1,0:T(8,128)S(1)}, f32[64,512]{1,0:T(8,128)S(1)}, u32[]{:S(2)}, u32[]{:S(2)}) collective-permute-start(f32[64,512]{1,0:T(8,128)S(1)} %fusion.4), channel_id=1, source_target_pairs={{0,16},{8,24},{16,32},{24,40},{32,48},{40,56},{48,64},{56,72},{64,... | collective-permute-start | bytes 393224 | tf_op jit(solution)/shard_map/ppermute | solution.py:20
  97.1 18.1 %collective-permute-start.11 = (f32[512,256]{0,1:T(8,128)S(1)}, f32[512,256]{0,1:T(8,128)S(1)}, u32[]{:S(2)}, u32[]{:S(2)}) collective-permute-start(f32[512,256]{0,1:T(8,128)S(1)} %get-tuple-element.28), channel_id=1, source_target_pairs={{0,64},{8,72},{16,80},{24,88},{32,96},{40,104},{48,112},{56,120},{... | collective-permute-start | bytes 1572872 | tf_op jit(solution)/shard_map/ppermute | solution.py:22
  103.7 12.9 %collective-permute-start.4 = (f32[64,512]{1,0:T(8,128)S(1)}, f32[64,512]{1,0:T(8,128)S(1)}, u32[]{:S(2)}, u32[]{:S(2)}) collective-permute-start(f32[64,512]{1,0:T(8,128)S(1)} %fusion.3), channel_id=1, source_target_pairs={{0,32},{8,40},{16,48},{24,56},{32,64},{40,72},{48,80},{56,88},{64,... | collective-permute-start | bytes 393224 | tf_op jit(solution)/shard_map/ppermute | solution.py:20
  116.3 19.8 %collective-permute-start.12 = (f32[512,256]{0,1:T(8,128)S(1)}, f32[512,256]{0,1:T(8,128)S(1)}, u32[]{:S(2)}, u32[]{:S(2)}) collective-permute-start(f32[512,256]{0,1:T(8,128)S(1)} %fusion.34), channel_id=1, source_target_pairs={{0,1},{1,0},{2,3},{3,2},{4,5},{5,4},{6,7},{7,6},{8,9},{9,8},{10,11... | collective-permute-start | bytes 1572872 | tf_op jit(solution)/shard_map/ppermute | solution.py:27
  117.3 8.3 %collective-permute-start.7 = (f32[64,512]{1,0:T(8,128)S(1)}, f32[64,512]{1,0:T(8,128)S(1)}, u32[]{:S(2)}, u32[]{:S(2)}) collective-permute-start(f32[64,512]{1,0:T(8,128)S(1)} %fusion.2), channel_id=1, source_target_pairs={{0,64},{8,72},{16,80},{24,88},{32,96},{40,104},{48,112},{56,120},{... | collective-permute-start | bytes 393224 | tf_op jit(solution)/shard_map/ppermute | solution.py:20
  126.4 9.7 %collective-permute-start.10 = (f32[64,512]{1,0:T(8,128)S(1)}, f32[64,512]{1,0:T(8,128)S(1)}, u32[]{:S(2)}, u32[]{:S(2)}) collective-permute-start(f32[64,512]{1,0:T(8,128)S(1)} %fusion.1), channel_id=1, source_target_pairs={{0,128},{8,136},{16,144},{24,152},{32,160},{40,168},{48,176},{56,1... | collective-permute-start | bytes 393224 | tf_op jit(solution)/shard_map/ppermute | solution.py:20
  136.9 0.7 copy-start.3
  138.7 4.8 %copy-start.2 = (bf16[1,64,2048]{2,1,0:T(8,128)(2,1)S(1)}, bf16[1,64,2048]{2,1,0:T(8,128)(2,1)}, u32[]{:S(2)}) copy-start(bf16[1,64,2048]{2,1,0:T(8,128)(2,1)} %param.11) | copy-start | bytes 786436
  138.7 18.7 %all-to-all-start = ((f32[8,1,64,512]{3,2,1,0:T(8,128)}), f32[8,1,64,512]{3,2,1,0:T(8,128)S(1)}, u32[]{:S(2)}, u32[]{:S(2)}) async-start(f32[8,1,64,512]{3,2,1,0:T(8,128)} %broadcast_in_dim.19), calls=%async_computation | async-start | bytes 2097152 | tf_op jit(solution)/shard_map/all_to_all | solution.py:84
  157.4 13.7 %all-to-all-start.1 = ((f32[64,8,256]{2,0,1:T(8,128)}), f32[64,8,256]{2,0,1:T(8,128)S(1)}, u32[]{:S(2)}, u32[]{:S(2)}) async-start(f32[64,8,256]{2,0,1:T(8,128)} %copy.12), calls=%async_computation.1 | async-start | bytes 1048576 | tf_op jit(solution)/shard_map/all_to_all | solution.py:81

commit v6 on v5

--- a/solution.py
+++ b/solution.py
@@ -17,9 +17,13 @@
         pairs = [(j, j + distance) for j in range(count - distance)]
         last = 2 * distance >= count
         has = index >= distance
-        got_vector = lax.ppermute(vector, axis, pairs)
-        if not last:
-            got_half = lax.ppermute(mine, axis, pairs)
+        if last:
+            got_vector = lax.ppermute(vector, axis, pairs)
+        else:
+            packed = jnp.concatenate([vector.reshape(-1, width), mine], axis=0)
+            got = lax.ppermute(packed, axis, pairs)
+            got_vector = got[: vector.size // width].reshape(vector.shape)
+            got_half = got[vector.size // width :]
         newer = jnp.einsum("sq,rq->sr", got_vector, matrix, precision=highest) + vector
         vector = jnp.where(has, newer, vector)
         if not last:

time: 207 us -> 221 us (1.068)
  waiting for transfers between devices: 81.3 us -> 103 us
  starting transfers between devices: 63.4 us -> 46.7 us
  other arithmetic: 4.07 us -> 7.2 us
  local copies, waits for them, and re-layouts: 5.71 us -> 8.67 us
  matrix products: 18.6 us -> 21.3 us
    ppermute x4, waiting for transfers between devices: 52.7 us -> 78.3 us  [shift_scan(): got = lax.ppermute(packed, axis, pairs)]
    ppermute x5 -> x1, starting transfers between devices: 26.6 us -> 5.92 us  [shift_scan(): got_vector = lax.ppermute(vector, axis, pairs)]
    ppermute x5 -> x1, waiting for transfers between devices: 7.59 us -> 3.38 us  [shift_scan(): got_vector = lax.ppermute(vector, axis, pairs)]
    ppermute x4, starting transfers between devices: 26.1 us -> 30.1 us  [shift_scan(): got = lax.ppermute(packed, axis, pairs)]
    slice x0 -> x5, local copies, waits for them, and re-layouts: none -> 3.64 us  [shift_scan(): got_vector = got[:vector.size // width].reshape(vector.shape)]
    dot_general x5, matrix products: 3.83 us -> 6.79 us  [shift_scan(): jnp.einsum('sq,rq->sr', got_vector, matrix, precision=highest) + vector]
  transfers between devices with their start and end apart: 15 -> 11, of which waited for: 10 -> 7; matrix products, arithmetic and copies ran while one was open for 7% -> 6% of each run, Pallas kernels for 0% -> 0%
where the time goes in v6:
time: 221 us; the launch traced here: 219 us
  waiting for transfers between devices  103 us (47%)
  starting transfers between devices  46.7 us (21%)
  blocking collectives  30.8 us (14%)
  matrix products  21.3 us (10%)
  local copies, waits for them, and re-layouts  8.67 us (4%)
  other arithmetic  7.2 us (3%)
    ppermute x4, waiting for transfers between devices, shift_scan(): got = lax.ppermute(packed, axis, pairs)  78.3 us
    all_to_all x1, blocking collectives, on_device_body(): mine = lax.all_to_all(pieces, 'tm', 0, 0, tiled=True).sum(axis=0)  30.8 us
    ppermute x4, starting transfers between devices, shift_scan(): got = lax.ppermute(packed, axis, pairs)  30.1 us
    all_to_all x1, waiting for transfers between devices, on_device_body(): lax.all_to_all(jnp.broadcast_to(states[None], (scen_shards,) + states.sha...  12.8 us
    dot_general x4, matrix products, shift_scan(): own = jnp.dot(matrix, got_half, precision=highest)  8.2 us
    all_to_all x1, waiting for transfers between devices, on_device_body(): readings = lax.all_to_all(readings, 'scen', 1, 0, tiled=True)  8.09 us
    dot_general x5, matrix products, shift_scan(): jnp.einsum('sq,rq->sr', got_vector, matrix, precision=highest) + vector  6.79 us
    ppermute x1, starting transfers between devices, shift_scan(): got_vector = lax.ppermute(vector, axis, pairs)  5.92 us
  transfers between devices with their start and end apart: 11, of which 7 were waited for; matrix products, arithmetic and copies ran while one was open for 6% of the time, Pallas kernels for 0%

profile of v6, /device:TPU:24, one launch (start us, length us, event | category | flops | bytes accessed | tf_op | source)
XLA Modules:
  0.0 219.0 jit_solution(2477090929889913338)
XLA Ops:
  1.4 2.1 fusion.17
  3.6 0.2 convolution_bitcast_fusion
  3.8 1.0 convolution_select_fusion
  4.8 1.1 convolution_add_fusion.5
  6.0 4.7 %collective-permute-start = (f32[640,256]{1,0:T(8,128)S(1)}, f32[640,256]{1,0:T(8,128)}, u32[]{:S(2)}, u32[]{:S(2)}) collective-permute-start(f32[640,256]{1,0:T(8,128)S(1)} %pad_maximum_fusion), channel_id=1, source_target_pairs={{0,8},{8,16},{16,24},{24,32},{32,40},{40,48},{48,56},{56,64},{64,7... | collective-permute-start | bytes 1966088 | tf_op jit(solution)/shard_map/ppermute | solution.py:24
  10.7 13.1 %collective-permute-done = f32[640,256]{1,0:T(8,128)} collective-permute-done((f32[640,256]{1,0:T(8,128)S(1)}, f32[640,256]{1,0:T(8,128)}, u32[]{:S(2)}, u32[]{:S(2)}) %collective-permute-start) | collective-permute-done | bytes 655392 | tf_op jit(solution)/shard_map/ppermute | solution.py:24
  23.8 0.9 slice.40
  24.8 2.8 %broadcast_select_fusion.2 = (f32[512,256]{1,0:T(8,128)S(1)}, f32[512,256]{1,0:T(8,128)}) fusion(f32[512,256]{1,0:T(8,128)S(1)} %dynamic-slice_bitcast_fusion, pred[]{:T(512)S(6)} %ge.19, f32[512,512]{0,1:T(8,128)S(1)} %convolution_select_fusion, f32[640,256]{1,0:T(8,128)} %collective-permute-done), kind=kOutput, calls=%fused_computation.53 | convolution fusion | flops 805437440 | bytes 3145729 | tf_op jit(solution)/shard_map/dot_general | solution.py:30
  27.6 1.1 fusion.4
  28.8 0.9 pad_maximum_fusion.1
  29.7 6.7 %collective-permute-start.1 = (f32[640,256]{1,0:T(8,128)}, f32[640,256]{1,0:T(8,128)}, u32[]{:S(2)}, u32[]{:S(2)}) collective-permute-start(f32[640,256]{1,0:T(8,128)} %pad_maximum_fusion.1), channel_id=1, source_target_pairs={{0,16},{8,24},{16,32},{24,40},{32,48},{40,56},{48,64},{56,72},{64,... | collective-permute-start | bytes 1966088 | tf_op jit(solution)/shard_map/ppermute | solution.py:24
  36.4 1.8 fusion.5
  38.3 26.4 %collective-permute-done.1 = f32[640,256]{1,0:T(8,128)} collective-permute-done((f32[640,256]{1,0:T(8,128)}, f32[640,256]{1,0:T(8,128)}, u32[]{:S(2)}, u32[]{:S(2)}) %collective-permute-start.1) | collective-permute-done | bytes 655392 | tf_op jit(solution)/shard_map/ppermute | solution.py:24
  64.7 0.9 slice.42
  65.7 2.2 broadcast_select_fusion.1
  67.9 0.1 collective-permute-start.4
  68.0 1.1 fusion.3
  69.2 0.9 pad_maximum_fusion.2
  70.1 11.5 %collective-permute-start.3 = (f32[640,256]{1,0:T(8,128)}, f32[640,256]{1,0:T(8,128)}, u32[]{:S(2)}, u32[]{:S(2)}) collective-permute-start(f32[640,256]{1,0:T(8,128)} %pad_maximum_fusion.2), channel_id=1, source_target_pairs={{0,32},{8,40},{16,48},{24,56},{32,64},{40,72},{48,80},{56,88},{64,... | collective-permute-start | bytes 1966088 | tf_op jit(solution)/shard_map/ppermute | solution.py:24
  81.5 1.8 fusion.6
  83.4 26.0 %collective-permute-done.3 = f32[640,256]{1,0:T(8,128)} collective-permute-done((f32[640,256]{1,0:T(8,128)}, f32[640,256]{1,0:T(8,128)}, u32[]{:S(2)}, u32[]{:S(2)}) %collective-permute-start.3) | collective-permute-done | bytes 655392 | tf_op jit(solution)/shard_map/ppermute | solution.py:24
  109.3 0.9 slice.44
  110.3 2.2 broadcast_select_fusion
  112.5 0.2 collective-permute-start.6
  112.7 1.1 fusion.2
  113.9 7.3 %collective-permute-start.5 = (f32[640,256]{1,0:T(8,128)S(1)}, f32[640,256]{1,0:T(8,128)S(1)}, u32[]{:S(2)}, u32[]{:S(2)}) collective-permute-start(f32[640,256]{1,0:T(8,128)S(1)} %pad_maximum_fusion.3), channel_id=1, source_target_pairs={{0,64},{8,72},{16,80},{24,88},{32,96},{40,104},{48,112},{56,120},{... | collective-permute-start | bytes 1966088 | tf_op jit(solution)/shard_map/ppermute | solution.py:24
  121.2 1.5 fusion.7
  122.7 12.8 %collective-permute-done.5 = f32[640,256]{1,0:T(8,128)S(1)} collective-permute-done((f32[640,256]{1,0:T(8,128)S(1)}, f32[640,256]{1,0:T(8,128)S(1)}, u32[]{:S(2)}, u32[]{:S(2)}) %collective-permute-start.5) | collective-permute-done | bytes 655392 | tf_op jit(solution)/shard_map/ppermute | solution.py:24
  135.6 0.9 copy-done.6
  136.4 1.0 fusion.21
  137.4 0.1 collective-permute-start.8
  137.5 0.9 slice-done
  138.4 1.1 fusion.1
  139.6 5.9 %collective-permute-start.7 = (f32[64,512]{1,0:T(8,128)S(1)}, f32[64,512]{1,0:T(8,128)S(1)}, u32[]{:S(2)}, u32[]{:S(2)}) collective-permute-start(f32[64,512]{1,0:T(8,128)S(1)} %fusion.1), channel_id=1, source_target_pairs={{0,128},{8,136},{16,144},{24,152},{32,160},{40,168},{48,176},{56,1... | collective-permute-start | bytes 393224 | tf_op jit(solution)/shard_map/ppermute | solution.py:21
  145.5 3.4 %collective-permute-done.7 = f32[64,512]{1,0:T(8,128)S(1)} collective-permute-done((f32[64,512]{1,0:T(8,128)S(1)}, f32[64,512]{1,0:T(8,128)S(1)}, u32[]{:S(2)}, u32[]{:S(2)}) %collective-permute-start.7) | collective-permute-done | bytes 131104 | tf_op jit(solution)/shard_map/ppermute | solution.py:21
  148.9 2.3 %fusion = f32[64,512]{1,0:T(8,128)S(1)} fusion(f32[64,512]{1,0:T(8,128)S(1)} %fusion.1, f32[64,512]{1,0:T(8,128)S(1)} %collective-permute-done.7, f32[512,512]{1,0:T(8,128)S(1)} %fusion.7, f32[512,256]{1,0:T(8,128)} %collective-permute-done.8, f32[512,256]{1,0:T(8,128)S(1)} %fusion.21, pred[]{:T(512)S(6)} %ge.16, pred[]{:T(512)S(6)} %eq.32, pred[]{:T(512)S(6)} %ge.15), kind=kOutput, calls=%fused_computation.3 | convolution fusion | flops 202440704 | bytes 2490371 | tf_op jit(solution)/shard_map/sq,rq->sr/dot_general | solution.py:27
  151.2 1.1 broadcast_in_dim.19
  152.4 4.8 %all-to-all-start = ((f32[8,1,64,512]{3,2,1,0:T(8,128)}), f32[8,1,64,512]{3,2,1,0:T(8,128)S(1)}, u32[]{:S(2)}, u32[]{:S(2)}) async-start(f32[8,1,64,512]{3,2,1,0:T(8,128)} %broadcast_in_dim.19), calls=%async_computation | async-start | bytes 2097152 | tf_op jit(solution)/shard_map/all_to_all | solution.py:88
  157.2 1.0 copy.40
  158.2 12.8 %all-to-all-done = f32[8,1,64,512]{3,2,1,0:T(8,128)S(1)} async-done(((f32[8,1,64,512]{3,2,1,0:T(8,128)}), f32[8,1,64,512]{3,2,1,0:T(8,128)S(1)}, u32[]{:S(2)}, u32[]{:S(2)}) %all-to-all-start) | async-done | bytes 1048608 | tf_op jit(solution)/shard_map/all_to_all | solution.py:88
  171.0 5.5 %all-to-all-start.1 = ((f32[64,8,256]{2,0,1:T(8,128)}), f32[64,8,256]{2,0,1:T(8,128)S(1)}, u32[]{:S(2)}, u32[]{:S(2)}) async-start(f32[64,8,256]{2,0,1:T(8,128)} %copy.40), calls=%async_computation.1 | async-start | bytes 1048576 | tf_op jit(solution)/shard_map/all_to_all | solution.py:85
  176.5 0.1 constant_dynamic-slice_fusion
  176.7 8.1 %all-to-all-done.1 = f32[64,8,256]{2,0,1:T(8,128)S(1)} async-done(((f32[64,8,256]{2,0,1:T(8,128)}), f32[64,8,256]{2,0,1:T(8,128)S(1)}, u32[]{:S(2)}, u32[]{:S(2)}) %all-to-all-start.1) | async-done | bytes 524320 | tf_op jit(solution)/shard_map/all_to_all | solution.py:85
  184.8 1.9 convolution_multiply_fusion
  186.6 0.3 copy.41
  186.9 30.8 %all_to_all.25 = f32[32,16,320]{2,1,0:T(8,128)S(1)} all-to-all(f32[32,16,320]{2,1,0:T(8,128)S(1)} %bitcast.54), channel_id=1, replica_groups=mesh['tm'=32,'scen'=8] {'tm'}, dimensions={0} | all-to-all | bytes 1310720 | tf_op jit(solution)/shard_map/all_to_all | solution.py:99
  217.8 0.6 slice.48
  218.4 0.7 slice.49
  (40 shorter events, 0.6 us)
Async XLA Ops:
  0.6 3.1 %copy-start = (f32[1,512,512]{2,1,0:T(8,128)S(1)}, f32[1,512,512]{2,1,0:T(8,128)}, u32[]{:S(2)}) copy-start(f32[1,512,512]{2,1,0:T(8,128)} %param.6) | copy-start | bytes 3145732
  1.4 2.2 copy-start.10
  3.8 1.0 copy-start.9
  6.0 17.8 %collective-permute-start = (f32[640,256]{1,0:T(8,128)S(1)}, f32[640,256]{1,0:T(8,128)}, u32[]{:S(2)}, u32[]{:S(2)}) collective-permute-start(f32[640,256]{1,0:T(8,128)S(1)} %pad_maximum_fusion), channel_id=1, source_target_pairs={{0,8},{8,16},{16,24},{24,32},{32,40},{40,48},{48,56},{56,64},{64,7... | collective-permute-start | bytes 1966088 | tf_op jit(solution)/shard_map/ppermute | solution.py:24
  27.6 1.2 copy-start.1
  27.6 8.8 %collective-permute-start.2 = (f32[512,256]{1,0:T(8,128)}, f32[512,256]{1,0:T(8,128)}, u32[]{:S(2)}, u32[]{:S(2)}) collective-permute-start(f32[512,256]{1,0:T(8,128)} %get-tuple-element.22), channel_id=1, source_target_pairs={{0,1},{1,0},{2,3},{3,2},{4,5},{5,4},{6,7},{7,6},{8,9},{9,8},{10,11... | collective-permute-start | bytes 1572872 | tf_op jit(solution)/shard_map/ppermute | solution.py:31
  29.7 35.0 %collective-permute-start.1 = (f32[640,256]{1,0:T(8,128)}, f32[640,256]{1,0:T(8,128)}, u32[]{:S(2)}, u32[]{:S(2)}) collective-permute-start(f32[640,256]{1,0:T(8,128)} %pad_maximum_fusion.1), channel_id=1, source_target_pairs={{0,16},{8,24},{16,32},{24,40},{32,48},{40,56},{48,64},{56,72},{64,... | collective-permute-start | bytes 1966088 | tf_op jit(solution)/shard_map/ppermute | solution.py:24
  67.9 1.2 copy-start.3
  67.9 1.3 copy-start.2
  67.9 13.7 %collective-permute-start.4 = (f32[512,256]{1,0:T(8,128)S(1)}, f32[512,256]{1,0:T(8,128)}, u32[]{:S(2)}, u32[]{:S(2)}) collective-permute-start(f32[512,256]{1,0:T(8,128)S(1)} %get-tuple-element.24), channel_id=1, source_target_pairs={{0,1},{1,0},{2,3},{3,2},{4,5},{5,4},{6,7},{7,6},{8,9},{9,8},{10,11... | collective-permute-start | bytes 1572872 | tf_op jit(solution)/shard_map/ppermute | solution.py:31
  70.1 39.3 %collective-permute-start.3 = (f32[640,256]{1,0:T(8,128)}, f32[640,256]{1,0:T(8,128)}, u32[]{:S(2)}, u32[]{:S(2)}) collective-permute-start(f32[640,256]{1,0:T(8,128)} %pad_maximum_fusion.2), channel_id=1, source_target_pairs={{0,32},{8,40},{16,48},{24,56},{32,64},{40,72},{48,80},{56,88},{64,... | collective-permute-start | bytes 1966088 | tf_op jit(solution)/shard_map/ppermute | solution.py:24
  112.5 1.3 copy-start.4
  112.5 8.7 %collective-permute-start.6 = (f32[512,256]{1,0:T(8,128)S(1)}, f32[512,256]{1,0:T(8,128)}, u32[]{:S(2)}, u32[]{:S(2)}) collective-permute-start(f32[512,256]{1,0:T(8,128)S(1)} %get-tuple-element.29), channel_id=1, source_target_pairs={{0,1},{1,0},{2,3},{3,2},{4,5},{5,4},{6,7},{7,6},{8,9},{9,8},{10,11... | collective-permute-start | bytes 1572872 | tf_op jit(solution)/shard_map/ppermute | solution.py:31
  113.8 7.4 %copy-start.5 = (f32[512,256]{1,0:T(8,128)S(1)}, f32[512,256]{1,0:T(8,128)}, u32[]{:S(2)}) copy-start(f32[512,256]{1,0:T(8,128)} %copy-done.4) | copy-start | bytes 1572868
  113.9 21.7 %collective-permute-start.5 = (f32[640,256]{1,0:T(8,128)S(1)}, f32[640,256]{1,0:T(8,128)S(1)}, u32[]{:S(2)}, u32[]{:S(2)}) collective-permute-start(f32[640,256]{1,0:T(8,128)S(1)} %pad_maximum_fusion.3), channel_id=1, source_target_pairs={{0,64},{8,72},{16,80},{24,88},{32,96},{40,104},{48,112},{56,120},{... | collective-permute-start | bytes 1966088 | tf_op jit(solution)/shard_map/ppermute | solution.py:24
  135.5 0.9 copy-start.6
  137.4 11.5 %collective-permute-start.8 = (f32[512,256]{1,0:T(8,128)S(1)}, f32[512,256]{1,0:T(8,128)}, u32[]{:S(2)}, u32[]{:S(2)}) collective-permute-start(f32[512,256]{1,0:T(8,128)S(1)} %fusion.21), channel_id=1, source_target_pairs={{0,1},{1,0},{2,3},{3,2},{4,5},{5,4},{6,7},{7,6},{8,9},{9,8},{10,11... | collective-permute-start | bytes 1572872 | tf_op jit(solution)/shard_map/ppermute | solution.py:31
  137.5 0.9 slice-start
  139.6 9.3 %collective-permute-start.7 = (f32[64,512]{1,0:T(8,128)S(1)}, f32[64,512]{1,0:T(8,128)S(1)}, u32[]{:S(2)}, u32[]{:S(2)}) collective-permute-start(f32[64,512]{1,0:T(8,128)S(1)} %fusion.1), channel_id=1, source_target_pairs={{0,128},{8,136},{16,144},{24,152},{32,160},{40,168},{48,176},{56,1... | collective-permute-start | bytes 393224 | tf_op jit(solution)/shard_map/ppermute | solution.py:21
  151.2 1.2 copy-start.8
  152.4 4.8 %copy-start.7 = (bf16[1,64,2048]{2,1,0:T(8,128)(2,1)S(1)}, bf16[1,64,2048]{2,1,0:T(8,128)(2,1)}, u32[]{:S(2)}) copy-start(bf16[1,64,2048]{2,1,0:T(8,128)(2,1)} %param.11) | copy-start | bytes 786436
  152.4 18.7 %all-to-all-start = ((f32[8,1,64,512]{3,2,1,0:T(8,128)}), f32[8,1,64,512]{3,2,1,0:T(8,128)S(1)}, u32[]{:S(2)}, u32[]{:S(2)}) async-start(f32[8,1,64,512]{3,2,1,0:T(8,128)} %broadcast_in_dim.19), calls=%async_computation | async-start | bytes 2097152 | tf_op jit(solution)/shard_map/all_to_all | solution.py:88
  171.0 13.7 %all-to-all-start.1 = ((f32[64,8,256]{2,0,1:T(8,128)}), f32[64,8,256]{2,0,1:T(8,128)S(1)}, u32[]{:S(2)}, u32[]{:S(2)}) async-start(f32[64,8,256]{2,0,1:T(8,128)} %copy.40), calls=%async_computation.1 | async-start | bytes 1048576 | tf_op jit(solution)/shard_map/all_to_all | solution.py:85

commit v7 on v5

--- a/solution.py
+++ b/solution.py
@@ -36,7 +36,7 @@
     return vector
 
 
-def on_device_body(operators, input_maps, segment, load, initial, observed):
+def on_device_body(tm_groups, operators, input_maps, segment, load, initial, observed):
     highest = lax.Precision.HIGHEST
     step_count = operators.shape[0]
     modes = operators.shape[1]
@@ -91,8 +91,17 @@
         [lax.dynamic_slice_in_dim(every, column, gram_cols, axis=2), readings], axis=2
     )
     joined = jnp.einsum("tsr,tso->ro", every, right, precision=highest) * normalize
-    pieces = joined.reshape(time_shards, modes // time_shards, joined.shape[1])
-    mine = lax.all_to_all(pieces, "tm", 0, 0, tiled=True).sum(axis=0)
+    mine = joined
+    stride = time_shards
+    for size in tm_groups:
+        stride //= size
+        groups = [
+            [base + k * stride for k in range(size)]
+            for base in range(time_shards)
+            if (base // stride) % size == 0
+        ]
+        pieces = mine.reshape(size, mine.shape[0] // size, mine.shape[1])
+        mine = lax.all_to_all(pieces, "tm", 0, 0, tiled=True, axis_index_groups=groups).sum(axis=0)
     return (states, mine[:, :gram_cols], mine[:, gram_cols:])
 
 
@@ -106,7 +115,12 @@
         P("tm", "scen", None),
     )
     out_specs = (P("tm", "scen", None), P("tm", "scen"), P("tm", "scen"))
+    count = dict(zip(mesh.axis_names, mesh.devices.shape))["tm"]
+    tm_groups = (count // 8, 8) if count % 8 == 0 and count > 8 else (count,)
+
+    def on_device(*args):
+        return on_device_body(tm_groups, *args)
 
     return jax.shard_map(
-        on_device_body, mesh=mesh, in_specs=in_specs, out_specs=out_specs, check_vma=False
+        on_device, mesh=mesh, in_specs=in_specs, out_specs=out_specs, check_vma=False
     )

time: 207 us -> 204 us (0.986)
    all_to_all x1 -> x2, blocking collectives: 30.2 us -> 28.8 us  [on_device_body(): lax.all_to_all(pieces, 'tm', 0, 0, tiled=True, axis_index_groups=groups)]
where the time goes in v7:
time: 204 us; the launch traced here: 203 us
  waiting for transfers between devices  81.3 us (40%)
  starting transfers between devices  63.3 us (31%)
  blocking collectives  28.8 us (14%)
  matrix products  18.6 us (9%)
  local copies, waits for them, and re-layouts  4.98 us (2%)
  other arithmetic  4.05 us (2%)
    ppermute x4, waiting for transfers between devices, shift_scan(): got_half = lax.ppermute(mine, axis, pairs)  52.8 us
    all_to_all x2, blocking collectives, on_device_body(): lax.all_to_all(pieces, 'tm', 0, 0, tiled=True, axis_index_groups=groups)  28.8 us
    ppermute x5, starting transfers between devices, shift_scan(): got_vector = lax.ppermute(vector, axis, pairs)  26.6 us
    ppermute x4, starting transfers between devices, shift_scan(): got_half = lax.ppermute(mine, axis, pairs)  26.1 us
    all_to_all x1, waiting for transfers between devices, on_device_body(): lax.all_to_all(jnp.broadcast_to(states[None], (scen_shards,) + states.sha...  12.8 us
    dot_general x4, matrix products, shift_scan(): own = jnp.dot(matrix, got_half, precision=highest)  9.6 us
    all_to_all x1, waiting for transfers between devices, on_device_body(): readings = lax.all_to_all(readings, 'scen', 1, 0, tiled=True)  8.09 us
    ppermute x5, waiting for transfers between devices, shift_scan(): got_vector = lax.ppermute(vector, axis, pairs)  7.59 us
  transfers between devices with their start and end apart: 15, of which 10 were waited for; matrix products, arithmetic and copies ran while one was open for 7% of the time, Pallas kernels for 0%

profile of v7, /device:TPU:24, one launch (start us, length us, event | category | flops | bytes accessed | tf_op | source)
XLA Modules:
  0.0 202.6 jit_solution(9361356460886734906)
XLA Ops:
  0.7 1.2 copy-done
  1.9 1.1 convolution_select_fusion
  3.0 4.6 %collective-permute-start.2 = (f32[512,256]{0,1:T(8,128)S(1)}, f32[512,256]{0,1:T(8,128)}, u32[]{:S(2)}, u32[]{:S(2)}) collective-permute-start(f32[512,256]{0,1:T(8,128)S(1)} %dynamic-slice_bitcast_fusion), channel_id=1, source_target_pairs={{0,8},{8,16},{16,24},{24,32},{32,40},{40,48},{48,56},{56,64},{64,7... | collective-permute-start | bytes 1572872 | tf_op jit(solution)/shard_map/ppermute | solution.py:22
  7.6 10.4 %collective-permute-done.2 = f32[512,256]{0,1:T(8,128)} collective-permute-done((f32[512,256]{0,1:T(8,128)S(1)}, f32[512,256]{0,1:T(8,128)}, u32[]{:S(2)}, u32[]{:S(2)}) %collective-permute-start.2) | collective-permute-done | bytes 524320 | tf_op jit(solution)/shard_map/ppermute | solution.py:22
  18.0 2.9 %broadcast_select_fusion.2 = (f32[512,256]{0,1:T(8,128)}, f32[512,256]{0,1:T(8,128)S(1)}) fusion(f32[512,256]{0,1:T(8,128)S(1)} %dynamic-slice_bitcast_fusion, pred[]{:T(512)S(6)} %ge.19, f32[512,512]{1,0:T(8,128)S(1)} %convolution_select_fusion, f32[512,256]{0,1:T(8,128)} %collective-permute-done.2), kind=kOutput, calls=%fused_computation.44 | convolution fusion | flops 805437440 | bytes 3145729 | tf_op jit(solution)/shard_map/dot_general | solution.py:26
  20.9 6.6 %collective-permute-start.5 = (f32[512,256]{0,1:T(8,128)}, f32[512,256]{0,1:T(8,128)}, u32[]{:S(2)}, u32[]{:S(2)}) collective-permute-start(f32[512,256]{0,1:T(8,128)} %get-tuple-element.18), channel_id=1, source_target_pairs={{0,16},{8,24},{16,32},{24,40},{32,48},{40,56},{48,64},{56,72},{64,... | collective-permute-start | bytes 1572872 | tf_op jit(solution)/shard_map/ppermute | solution.py:22
  28.2 1.9 fusion.6
  30.1 20.2 %collective-permute-done.5 = f32[512,256]{0,1:T(8,128)} collective-permute-done((f32[512,256]{0,1:T(8,128)}, f32[512,256]{0,1:T(8,128)}, u32[]{:S(2)}, u32[]{:S(2)}) %collective-permute-start.5) | collective-permute-done | bytes 524320 | tf_op jit(solution)/shard_map/ppermute | solution.py:22
  50.3 3.2 %broadcast_select_fusion.1 = (f32[512,256]{0,1:T(8,128)}, f32[512,256]{0,1:T(8,128)}) fusion(f32[512,256]{0,1:T(8,128)} %get-tuple-element.18, pred[]{:T(512)S(6)} %ge.18, f32[512,512]{0,1:T(8,128)S(1)} %fusion.6, f32[512,256]{0,1:T(8,128)} %collective-permute-done.5), kind=kOutput, calls=%fused_computation.43 | convolution fusion | flops 805437440 | bytes 3145729 | tf_op jit(solution)/shard_map/dot_general | solution.py:26
  53.6 0.9 fusion.18
  54.5 0.2 convolution_bitcast_fusion
  54.7 11.4 %collective-permute-start.8 = (f32[512,256]{0,1:T(8,128)}, f32[512,256]{0,1:T(8,128)}, u32[]{:S(2)}, u32[]{:S(2)}) collective-permute-start(f32[512,256]{0,1:T(8,128)} %get-tuple-element.23), channel_id=1, source_target_pairs={{0,32},{8,40},{16,48},{24,56},{32,64},{40,72},{48,80},{56,88},{64,... | collective-permute-start | bytes 1572872 | tf_op jit(solution)/shard_map/ppermute | solution.py:22
  66.1 1.1 convolution_add_fusion.5
  67.2 1.3 collective-permute-start
  68.5 1.9 fusion.7
  70.4 18.0 %collective-permute-done.8 = f32[512,256]{0,1:T(8,128)} collective-permute-done((f32[512,256]{0,1:T(8,128)}, f32[512,256]{0,1:T(8,128)}, u32[]{:S(2)}, u32[]{:S(2)}) %collective-permute-start.8) | collective-permute-done | bytes 524320 | tf_op jit(solution)/shard_map/ppermute | solution.py:22
  88.4 2.3 %broadcast_select_fusion = (f32[512,256]{0,1:T(8,128)S(1)}, f32[512,256]{0,1:T(8,128)S(1)}) fusion(f32[512,256]{0,1:T(8,128)} %get-tuple-element.23, pred[]{:T(512)S(6)} %ge.17, f32[512,512]{0,1:T(8,128)S(1)} %fusion.7, f32[512,256]{0,1:T(8,128)} %collective-permute-done.8), kind=kOutput, calls=%fused_computation.42 | convolution fusion | flops 805437440 | bytes 3145729 | tf_op jit(solution)/shard_map/dot_general | solution.py:26
  90.8 0.2 collective-permute-done
  91.1 0.8 fusion.5
  91.8 5.2 %collective-permute-start.1 = (f32[64,512]{1,0:T(8,128)S(1)}, f32[64,512]{1,0:T(8,128)S(1)}, u32[]{:S(2)}, u32[]{:S(2)}) collective-permute-start(f32[64,512]{1,0:T(8,128)S(1)} %fusion.5), channel_id=1, source_target_pairs={{0,16},{8,24},{16,32},{24,40},{32,48},{40,56},{48,64},{56,72},{64,... | collective-permute-start | bytes 393224 | tf_op jit(solution)/shard_map/ppermute | solution.py:20
  97.1 3.4 %collective-permute-start.11 = (f32[512,256]{0,1:T(8,128)S(1)}, f32[512,256]{0,1:T(8,128)S(1)}, u32[]{:S(2)}, u32[]{:S(2)}) collective-permute-start(f32[512,256]{0,1:T(8,128)S(1)} %get-tuple-element.28), channel_id=1, source_target_pairs={{0,64},{8,72},{16,80},{24,88},{32,96},{40,104},{48,112},{56,120},{... | collective-permute-start | bytes 1572872 | tf_op jit(solution)/shard_map/ppermute | solution.py:22
  100.5 2.4 %collective-permute-done.1 = f32[64,512]{1,0:T(8,128)S(1)} collective-permute-done((f32[64,512]{1,0:T(8,128)S(1)}, f32[64,512]{1,0:T(8,128)S(1)}, u32[]{:S(2)}, u32[]{:S(2)}) %collective-permute-start.1) | collective-permute-done | bytes 131104 | tf_op jit(solution)/shard_map/ppermute | solution.py:20
  102.9 0.8 fusion.4
  103.6 7.0 %collective-permute-start.4 = (f32[64,512]{1,0:T(8,128)S(1)}, f32[64,512]{1,0:T(8,128)S(1)}, u32[]{:S(2)}, u32[]{:S(2)}) collective-permute-start(f32[64,512]{1,0:T(8,128)S(1)} %fusion.4), channel_id=1, source_target_pairs={{0,32},{8,40},{16,48},{24,56},{32,64},{40,72},{48,80},{56,88},{64,... | collective-permute-start | bytes 393224 | tf_op jit(solution)/shard_map/ppermute | solution.py:20
  110.7 0.2 fusion.8
  110.9 4.2 %collective-permute-done.11 = f32[512,256]{0,1:T(8,128)S(1)} collective-permute-done((f32[512,256]{0,1:T(8,128)S(1)}, f32[512,256]{0,1:T(8,128)S(1)}, u32[]{:S(2)}, u32[]{:S(2)}) %collective-permute-start.11) | collective-permute-done | bytes 524320 | tf_op jit(solution)/shard_map/ppermute | solution.py:22
  115.2 1.1 fusion.35
  116.3 0.3 collective-permute-start.12
  116.6 0.8 fusion.3
  117.3 5.8 %collective-permute-start.7 = (f32[64,512]{1,0:T(8,128)S(1)}, f32[64,512]{1,0:T(8,128)S(1)}, u32[]{:S(2)}, u32[]{:S(2)}) collective-permute-start(f32[64,512]{1,0:T(8,128)S(1)} %fusion.3), channel_id=1, source_target_pairs={{0,64},{8,72},{16,80},{24,88},{32,96},{40,104},{48,112},{56,120},{... | collective-permute-start | bytes 393224 | tf_op jit(solution)/shard_map/ppermute | solution.py:20
  123.1 2.5 %collective-permute-done.7 = f32[64,512]{1,0:T(8,128)S(1)} collective-permute-done((f32[64,512]{1,0:T(8,128)S(1)}, f32[64,512]{1,0:T(8,128)S(1)}, u32[]{:S(2)}, u32[]{:S(2)}) %collective-permute-start.7) | collective-permute-done | bytes 131104 | tf_op jit(solution)/shard_map/ppermute | solution.py:20
  125.6 0.8 fusion.2
  126.4 7.2 %collective-permute-start.10 = (f32[64,512]{1,0:T(8,128)S(1)}, f32[64,512]{1,0:T(8,128)S(1)}, u32[]{:S(2)}, u32[]{:S(2)}) collective-permute-start(f32[64,512]{1,0:T(8,128)S(1)} %fusion.2), channel_id=1, source_target_pairs={{0,128},{8,136},{16,144},{24,152},{32,160},{40,168},{48,176},{56,1... | collective-permute-start | bytes 393224 | tf_op jit(solution)/shard_map/ppermute | solution.py:20
  133.6 2.5 %collective-permute-done.10 = f32[64,512]{1,0:T(8,128)S(1)} collective-permute-done((f32[64,512]{1,0:T(8,128)S(1)}, f32[64,512]{1,0:T(8,128)S(1)}, u32[]{:S(2)}, u32[]{:S(2)}) %collective-permute-start.10) | collective-permute-done | bytes 131104 | tf_op jit(solution)/shard_map/ppermute | solution.py:20
  136.1 0.8 fusion.1
  136.9 1.1 broadcast_in_dim.19
  138.0 4.8 %all-to-all-start = ((f32[8,1,64,512]{3,2,1,0:T(8,128)}), f32[8,1,64,512]{3,2,1,0:T(8,128)S(1)}, u32[]{:S(2)}, u32[]{:S(2)}) async-start(f32[8,1,64,512]{3,2,1,0:T(8,128)} %broadcast_in_dim.19), calls=%async_computation | async-start | bytes 2097152 | tf_op jit(solution)/shard_map/all_to_all | solution.py:84
  142.9 1.0 copy.13
  143.9 12.8 %all-to-all-done = f32[8,1,64,512]{3,2,1,0:T(8,128)S(1)} async-done(((f32[8,1,64,512]{3,2,1,0:T(8,128)}), f32[8,1,64,512]{3,2,1,0:T(8,128)S(1)}, u32[]{:S(2)}, u32[]{:S(2)}) %all-to-all-start) | async-done | bytes 1048608 | tf_op jit(solution)/shard_map/all_to_all | solution.py:84
  156.7 5.5 %all-to-all-start.1 = ((f32[64,8,256]{2,0,1:T(8,128)}), f32[64,8,256]{2,0,1:T(8,128)S(1)}, u32[]{:S(2)}, u32[]{:S(2)}) async-start(f32[64,8,256]{2,0,1:T(8,128)} %copy.13), calls=%async_computation.1 | async-start | bytes 1048576 | tf_op jit(solution)/shard_map/all_to_all | solution.py:81
  162.2 0.1 constant_dynamic-slice_fusion
  162.4 8.1 %all-to-all-done.1 = f32[64,8,256]{2,0,1:T(8,128)S(1)} async-done(((f32[64,8,256]{2,0,1:T(8,128)}), f32[64,8,256]{2,0,1:T(8,128)S(1)}, u32[]{:S(2)}, u32[]{:S(2)}) %all-to-all-start.1) | async-done | bytes 524320 | tf_op jit(solution)/shard_map/all_to_all | solution.py:81
  170.5 1.9 fusion
  172.4 16.5 %all_to_all.30 = f32[4,128,320]{1,2,0:T(8,128)S(1)} all-to-all(f32[4,128,320]{1,2,0:T(8,128)S(1)} %bitcast.63), channel_id=1, replica_groups={{0,64,128,192},{8,72,136,200},{16,80,144,208},{24,88,152,216},{32,96,16..., dimensions={0} | all-to-all | bytes 1310720 | tf_op jit(solution)/shard_map/all_to_all | solution.py:104
  188.9 0.1 copy.16
  189.0 12.3 %all_to_all.31 = f32[8,16,320]{2,1,0:T(8,128)S(1)} all-to-all(f32[8,16,320]{2,1,0:T(8,128)S(1)} %bitcast.66), channel_id=1, replica_groups={{0,8,16,24,32,40,48,56},{64,72,80,88,96,104,112,120},{128,136,144,152,1..., dimensions={0} | all-to-all | bytes 327680 | tf_op jit(solution)/shard_map/all_to_all | solution.py:104
  201.3 0.6 slice.8
  201.9 0.7 slice.9
  (26 shorter events, 0.4 us)
Async XLA Ops:
  0.6 1.2 copy-start
  3.0 15.0 %collective-permute-start.2 = (f32[512,256]{0,1:T(8,128)S(1)}, f32[512,256]{0,1:T(8,128)}, u32[]{:S(2)}, u32[]{:S(2)}) collective-permute-start(f32[512,256]{0,1:T(8,128)S(1)} %dynamic-slice_bitcast_fusion), channel_id=1, source_target_pairs={{0,8},{8,16},{16,24},{24,32},{32,40},{40,48},{48,56},{56,64},{64,7... | collective-permute-start | bytes 1572872 | tf_op jit(solution)/shard_map/ppermute | solution.py:22
  20.9 7.3 %copy-start.1 = (f32[512,256]{0,1:T(8,128)}, f32[512,256]{0,1:T(8,128)S(1)}, u32[]{:S(2)}) copy-start(f32[512,256]{0,1:T(8,128)S(1)} %get-tuple-element.22) | copy-start | bytes 1572868
  20.9 7.3 %collective-permute-start.3 = (f32[512,256]{0,1:T(8,128)S(1)}, f32[512,256]{0,1:T(8,128)}, u32[]{:S(2)}, u32[]{:S(2)}) collective-permute-start(f32[512,256]{0,1:T(8,128)S(1)} %get-tuple-element.22), channel_id=1, source_target_pairs={{0,1},{1,0},{2,3},{3,2},{4,5},{5,4},{6,7},{7,6},{8,9},{9,8},{10,11... | collective-permute-start | bytes 1572872 | tf_op jit(solution)/shard_map/ppermute | solution.py:27
  20.9 29.4 %collective-permute-start.5 = (f32[512,256]{0,1:T(8,128)}, f32[512,256]{0,1:T(8,128)}, u32[]{:S(2)}, u32[]{:S(2)}) collective-permute-start(f32[512,256]{0,1:T(8,128)} %get-tuple-element.18), channel_id=1, source_target_pairs={{0,16},{8,24},{16,32},{24,40},{32,48},{40,56},{48,64},{56,72},{64,... | collective-permute-start | bytes 1572872 | tf_op jit(solution)/shard_map/ppermute | solution.py:22
  30.1 23.4 %copy-start.6 = (bf16[4,512,256]{2,1,0:T(8,128)(2,1)S(1)}, bf16[4,512,256]{2,1,0:T(8,128)(2,1)}, u32[]{:S(2)}) copy-start(bf16[4,512,256]{2,1,0:T(8,128)(2,1)} %param.7) | copy-start | bytes 3145732
  53.5 15.0 %collective-permute-start.6 = (f32[512,256]{0,1:T(8,128)}, f32[512,256]{0,1:T(8,128)}, u32[]{:S(2)}, u32[]{:S(2)}) collective-permute-start(f32[512,256]{0,1:T(8,128)} %get-tuple-element.24), channel_id=1, source_target_pairs={{0,1},{1,0},{2,3},{3,2},{4,5},{5,4},{6,7},{7,6},{8,9},{9,8},{10,11... | collective-permute-start | bytes 1572872 | tf_op jit(solution)/shard_map/ppermute | solution.py:27
  53.5 0.9 copy-start.5
  54.5 11.6 %copy-start.4 = (f32[64,512]{1,0:T(8,128)S(1)}, f32[64,512]{1,0:T(8,128)}, u32[]{:S(2)}) copy-start(f32[64,512]{1,0:T(8,128)} %param.10) | copy-start | bytes 393220
  54.7 33.7 %collective-permute-start.8 = (f32[512,256]{0,1:T(8,128)}, f32[512,256]{0,1:T(8,128)}, u32[]{:S(2)}, u32[]{:S(2)}) collective-permute-start(f32[512,256]{0,1:T(8,128)} %get-tuple-element.23), channel_id=1, source_target_pairs={{0,32},{8,40},{16,48},{24,56},{32,64},{40,72},{48,80},{56,88},{64,... | collective-permute-start | bytes 1572872 | tf_op jit(solution)/shard_map/ppermute | solution.py:22
  67.2 23.9 %collective-permute-start = (f32[64,512]{1,0:T(8,128)S(1)}, f32[64,512]{1,0:T(8,128)S(1)}, u32[]{:S(2)}, u32[]{:S(2)}) collective-permute-start(f32[64,512]{1,0:T(8,128)S(1)} %convolution_add_fusion.5), channel_id=1, source_target_pairs={{0,8},{8,16},{16,24},{24,32},{32,40},{40,48},{48,56},{56,64},{64,7... | collective-permute-start | bytes 393224 | tf_op jit(solution)/shard_map/ppermute | solution.py:20
  90.7 20.0 %collective-permute-start.9 = (f32[512,256]{0,1:T(8,128)S(1)}, f32[512,256]{0,1:T(8,128)S(1)}, u32[]{:S(2)}, u32[]{:S(2)}) collective-permute-start(f32[512,256]{0,1:T(8,128)S(1)} %get-tuple-element.29), channel_id=1, source_target_pairs={{0,1},{1,0},{2,3},{3,2},{4,5},{5,4},{6,7},{7,6},{8,9},{9,8},{10,11... | collective-permute-start | bytes 1572872 | tf_op jit(solution)/shard_map/ppermute | solution.py:27
  91.8 11.0 %collective-permute-start.1 = (f32[64,512]{1,0:T(8,128)S(1)}, f32[64,512]{1,0:T(8,128)S(1)}, u32[]{:S(2)}, u32[]{:S(2)}) collective-permute-start(f32[64,512]{1,0:T(8,128)S(1)} %fusion.5), channel_id=1, source_target_pairs={{0,16},{8,24},{16,32},{24,40},{32,48},{40,56},{48,64},{56,72},{64,... | collective-permute-start | bytes 393224 | tf_op jit(solution)/shard_map/ppermute | solution.py:20
  97.1 18.1 %collective-permute-start.11 = (f32[512,256]{0,1:T(8,128)S(1)}, f32[512,256]{0,1:T(8,128)S(1)}, u32[]{:S(2)}, u32[]{:S(2)}) collective-permute-start(f32[512,256]{0,1:T(8,128)S(1)} %get-tuple-element.28), channel_id=1, source_target_pairs={{0,64},{8,72},{16,80},{24,88},{32,96},{40,104},{48,112},{56,120},{... | collective-permute-start | bytes 1572872 | tf_op jit(solution)/shard_map/ppermute | solution.py:22
  103.6 12.9 %collective-permute-start.4 = (f32[64,512]{1,0:T(8,128)S(1)}, f32[64,512]{1,0:T(8,128)S(1)}, u32[]{:S(2)}, u32[]{:S(2)}) collective-permute-start(f32[64,512]{1,0:T(8,128)S(1)} %fusion.4), channel_id=1, source_target_pairs={{0,32},{8,40},{16,48},{24,56},{32,64},{40,72},{48,80},{56,88},{64,... | collective-permute-start | bytes 393224 | tf_op jit(solution)/shard_map/ppermute | solution.py:20
  116.3 19.8 %collective-permute-start.12 = (f32[512,256]{0,1:T(8,128)S(1)}, f32[512,256]{0,1:T(8,128)S(1)}, u32[]{:S(2)}, u32[]{:S(2)}) collective-permute-start(f32[512,256]{0,1:T(8,128)S(1)} %fusion.35), channel_id=1, source_target_pairs={{0,1},{1,0},{2,3},{3,2},{4,5},{5,4},{6,7},{7,6},{8,9},{9,8},{10,11... | collective-permute-start | bytes 1572872 | tf_op jit(solution)/shard_map/ppermute | solution.py:27
  117.3 8.3 %collective-permute-start.7 = (f32[64,512]{1,0:T(8,128)S(1)}, f32[64,512]{1,0:T(8,128)S(1)}, u32[]{:S(2)}, u32[]{:S(2)}) collective-permute-start(f32[64,512]{1,0:T(8,128)S(1)} %fusion.3), channel_id=1, source_target_pairs={{0,64},{8,72},{16,80},{24,88},{32,96},{40,104},{48,112},{56,120},{... | collective-permute-start | bytes 393224 | tf_op jit(solution)/shard_map/ppermute | solution.py:20
  126.4 9.7 %collective-permute-start.10 = (f32[64,512]{1,0:T(8,128)S(1)}, f32[64,512]{1,0:T(8,128)S(1)}, u32[]{:S(2)}, u32[]{:S(2)}) collective-permute-start(f32[64,512]{1,0:T(8,128)S(1)} %fusion.2), channel_id=1, source_target_pairs={{0,128},{8,136},{16,144},{24,152},{32,160},{40,168},{48,176},{56,1... | collective-permute-start | bytes 393224 | tf_op jit(solution)/shard_map/ppermute | solution.py:20
  136.9 1.1 copy-start.3
  138.0 4.8 %copy-start.2 = (bf16[1,64,2048]{2,1,0:T(8,128)(2,1)S(1)}, bf16[1,64,2048]{2,1,0:T(8,128)(2,1)}, u32[]{:S(2)}) copy-start(bf16[1,64,2048]{2,1,0:T(8,128)(2,1)} %param.11) | copy-start | bytes 786436
  138.0 18.7 %all-to-all-start = ((f32[8,1,64,512]{3,2,1,0:T(8,128)}), f32[8,1,64,512]{3,2,1,0:T(8,128)S(1)}, u32[]{:S(2)}, u32[]{:S(2)}) async-start(f32[8,1,64,512]{3,2,1,0:T(8,128)} %broadcast_in_dim.19), calls=%async_computation | async-start | bytes 2097152 | tf_op jit(solution)/shard_map/all_to_all | solution.py:84
  156.7 13.7 %all-to-all-start.1 = ((f32[64,8,256]{2,0,1:T(8,128)}), f32[64,8,256]{2,0,1:T(8,128)S(1)}, u32[]{:S(2)}, u32[]{:S(2)}) async-start(f32[64,8,256]{2,0,1:T(8,128)} %copy.13), calls=%async_computation.1 | async-start | bytes 1048576 | tf_op jit(solution)/shard_map/all_to_all | solution.py:81

commit v8 on v7

--- a/solution.py
+++ b/solution.py
@@ -5,7 +5,7 @@
 
 
 def shift_scan(matrix, vector, axis, pair_axis):
-    highest = lax.Precision.HIGHEST
+    highest = lax.Precision.HIGH
     count, index = (lax.axis_size(axis), lax.axis_index(axis))
     pair_count = lax.axis_size(pair_axis)
     side = lax.axis_index(pair_axis) % 2
@@ -64,7 +64,10 @@
         newer = jnp.dot(matrix, product, precision=highest)
         return (newer, newer)
 
-    composed, products = lax.scan(compose_step, identity_matrix, operators)
+    if step_count == 1:
+        composed, products = (operators[0], operators)
+    else:
+        composed, products = lax.scan(compose_step, identity_matrix, operators)
     composed = jnp.where(first_shard, jnp.zeros_like(composed), composed)
     leaving = shift_scan(composed, last_state, "tm", "scen")
     if step_count == 1:

time: 204 us -> 202 us (level)
  matrix products: 18.6 us -> 14 us
  transfers between devices with their start and end apart: 15 -> 15, of which waited for: 10 -> 10; matrix products, arithmetic and copies ran while one was open for 7% -> 6% of each run, Pallas kernels for 0% -> 0%
where the time goes in v8:
time: 202 us; the launch traced here: 200 us
  waiting for transfers between devices  81.6 us (40%)
  starting transfers between devices  63.3 us (31%)
  blocking collectives  28.6 us (14%)
  matrix products  14 us (7%)
  local copies, waits for them, and re-layouts  6.31 us (3%)
  other arithmetic  4.46 us (2%)
    ppermute x4, waiting for transfers between devices, shift_scan(): got_half = lax.ppermute(mine, axis, pairs)  52.7 us
    all_to_all x2, blocking collectives, on_device_body(): lax.all_to_all(pieces, 'tm', 0, 0, tiled=True, axis_index_groups=groups)  28.6 us
    ppermute x5, starting transfers between devices, shift_scan(): got_vector = lax.ppermute(vector, axis, pairs)  26.7 us
    ppermute x4, starting transfers between devices, shift_scan(): got_half = lax.ppermute(mine, axis, pairs)  26.1 us
    all_to_all x1, waiting for transfers between devices, on_device_body(): lax.all_to_all(jnp.broadcast_to(states[None], (scen_shards,) + states.sha...  12.9 us
    all_to_all x1, waiting for transfers between devices, on_device_body(): readings = lax.all_to_all(readings, 'scen', 1, 0, tiled=True)  8.09 us
    ppermute x5, waiting for transfers between devices, shift_scan(): got_vector = lax.ppermute(vector, axis, pairs)  7.99 us
    dot_general x4, matrix products, shift_scan(): own = jnp.dot(matrix, got_half, precision=highest)  7.71 us
  transfers between devices with their start and end apart: 15, of which 10 were waited for; matrix products, arithmetic and copies ran while one was open for 6% of the time, Pallas kernels for 0%

profile of v8, /device:TPU:24, one launch (start us, length us, event | category | flops | bytes accessed | tf_op | source)
XLA Modules:
  0.0 199.9 jit_solution(3791690641257502368)
XLA Ops:
  0.7 1.6 copy.17
  2.4 0.9 copy-done.1
  3.3 4.6 %collective-permute-start.2 = (f32[512,256]{0,1:T(8,128)S(1)}, f32[512,256]{0,1:T(8,128)}, u32[]{:S(2)}, u32[]{:S(2)}) collective-permute-start(f32[512,256]{0,1:T(8,128)S(1)} %constant_dynamic-slice_fusion.1), channel_id=1, source_target_pairs={{0,8},{8,16},{16,24},{24,32},{32,40},{40,48},{48,56},{56,64},{64,7... | collective-permute-start | bytes 1572872 | tf_op jit(solution)/shard_map/ppermute | solution.py:22
  8.0 10.3 %collective-permute-done.2 = f32[512,256]{0,1:T(8,128)} collective-permute-done((f32[512,256]{0,1:T(8,128)S(1)}, f32[512,256]{0,1:T(8,128)}, u32[]{:S(2)}, u32[]{:S(2)}) %collective-permute-start.2) | collective-permute-done | bytes 524320 | tf_op jit(solution)/shard_map/ppermute | solution.py:22
  18.3 2.4 %broadcast_select_fusion.2 = (f32[512,256]{0,1:T(8,128)}, f32[512,256]{0,1:T(8,128)S(1)}) fusion(f32[512,256]{0,1:T(8,128)S(1)} %constant_dynamic-slice_fusion.1, pred[]{:T(512)S(6)} %ge.19, f32[512,512]{0,1:T(8,128)S(1)} %bitcast_select_fusion, f32[512,256]{0,1:T(8,128)} %collective-permute-done.2), kind=kOutput, calls=%fused_computation.40 | convolution fusion | flops 402784256 | bytes 3145729 | tf_op jit(solution)/shard_map/dot_general | solution.py:26
  20.8 6.7 %collective-permute-start.5 = (f32[512,256]{0,1:T(8,128)}, f32[512,256]{0,1:T(8,128)}, u32[]{:S(2)}, u32[]{:S(2)}) collective-permute-start(f32[512,256]{0,1:T(8,128)} %get-tuple-element.11), channel_id=1, source_target_pairs={{0,16},{8,24},{16,32},{24,40},{32,48},{40,56},{48,64},{56,72},{64,... | collective-permute-start | bytes 1572872 | tf_op jit(solution)/shard_map/ppermute | solution.py:22
  28.1 2.2 %fusion.6 = f32[512,512]{0,1:T(8,128)S(1)} fusion(f32[512,256]{0,1:T(8,128)} %collective-permute-done.3, f32[512,256]{0,1:T(8,128)} %copy-done.3, pred[]{:T(512)S(6)} %eq.28, pred[]{:T(512)S(6)} %ge.19, f32[1,512,512]{1,2,0:T(8,128)} %copy-done.1, pred[]{:T(512)S(6)} %eq.24), kind=kLoop, calls=%fused_computation.15 | loop fusion | flops 1310720 | bytes 3145731 | tf_op jit(solution)/shard_map/jit(_where)/select_n | solution.py:33
  30.4 19.8 %collective-permute-done.5 = f32[512,256]{0,1:T(8,128)} collective-permute-done((f32[512,256]{0,1:T(8,128)}, f32[512,256]{0,1:T(8,128)}, u32[]{:S(2)}, u32[]{:S(2)}) %collective-permute-start.5) | collective-permute-done | bytes 524320 | tf_op jit(solution)/shard_map/ppermute | solution.py:22
  50.2 2.8 %broadcast_select_fusion.1 = (f32[512,256]{0,1:T(8,128)}, f32[512,256]{0,1:T(8,128)}) fusion(f32[512,256]{0,1:T(8,128)} %get-tuple-element.11, pred[]{:T(512)S(6)} %ge.18, f32[512,512]{0,1:T(8,128)S(1)} %fusion.6, f32[512,256]{0,1:T(8,128)} %collective-permute-done.5), kind=kOutput, calls=%fused_computation.39 | convolution fusion | flops 402784256 | bytes 3145729 | tf_op jit(solution)/shard_map/dot_general | solution.py:26
  53.0 0.9 fusion.17
  53.9 0.2 convolution_bitcast_fusion
  54.1 11.3 %collective-permute-start.8 = (f32[512,256]{0,1:T(8,128)}, f32[512,256]{0,1:T(8,128)}, u32[]{:S(2)}, u32[]{:S(2)}) collective-permute-start(f32[512,256]{0,1:T(8,128)} %get-tuple-element.17), channel_id=1, source_target_pairs={{0,32},{8,40},{16,48},{24,56},{32,64},{40,72},{48,80},{56,88},{64,... | collective-permute-start | bytes 1572872 | tf_op jit(solution)/shard_map/ppermute | solution.py:22
  65.5 1.1 convolution_add_fusion.5
  66.6 1.3 collective-permute-start
  67.9 1.9 fusion.7
  69.8 18.1 %collective-permute-done.8 = f32[512,256]{0,1:T(8,128)} collective-permute-done((f32[512,256]{0,1:T(8,128)}, f32[512,256]{0,1:T(8,128)}, u32[]{:S(2)}, u32[]{:S(2)}) %collective-permute-start.8) | collective-permute-done | bytes 524320 | tf_op jit(solution)/shard_map/ppermute | solution.py:22
  87.8 1.8 broadcast_select_fusion
  89.7 0.1 collective-permute-start.9
  89.8 0.7 collective-permute-done
  90.5 0.4 fusion.5
  91.0 5.2 %collective-permute-start.1 = (f32[64,512]{1,0:T(8,128)S(1)}, f32[64,512]{1,0:T(8,128)S(1)}, u32[]{:S(2)}, u32[]{:S(2)}) collective-permute-start(f32[64,512]{1,0:T(8,128)S(1)} %fusion.5), channel_id=1, source_target_pairs={{0,16},{8,24},{16,32},{24,40},{32,48},{40,56},{48,64},{56,72},{64,... | collective-permute-start | bytes 393224 | tf_op jit(solution)/shard_map/ppermute | solution.py:20
  96.2 3.4 %collective-permute-start.11 = (f32[512,256]{0,1:T(8,128)S(1)}, f32[512,256]{0,1:T(8,128)S(1)}, u32[]{:S(2)}, u32[]{:S(2)}) collective-permute-start(f32[512,256]{0,1:T(8,128)S(1)} %get-tuple-element.19), channel_id=1, source_target_pairs={{0,64},{8,72},{16,80},{24,88},{32,96},{40,104},{48,112},{56,120},{... | collective-permute-start | bytes 1572872 | tf_op jit(solution)/shard_map/ppermute | solution.py:22
  99.6 2.3 %collective-permute-done.1 = f32[64,512]{1,0:T(8,128)S(1)} collective-permute-done((f32[64,512]{1,0:T(8,128)S(1)}, f32[64,512]{1,0:T(8,128)S(1)}, u32[]{:S(2)}, u32[]{:S(2)}) %collective-permute-start.1) | collective-permute-done | bytes 131104 | tf_op jit(solution)/shard_map/ppermute | solution.py:20
  101.9 0.4 fusion.4
  102.3 6.6 %collective-permute-start.4 = (f32[64,512]{1,0:T(8,128)S(1)}, f32[64,512]{1,0:T(8,128)S(1)}, u32[]{:S(2)}, u32[]{:S(2)}) collective-permute-start(f32[64,512]{1,0:T(8,128)S(1)} %fusion.4), channel_id=1, source_target_pairs={{0,32},{8,40},{16,48},{24,56},{32,64},{40,72},{48,80},{56,88},{64,... | collective-permute-start | bytes 393224 | tf_op jit(solution)/shard_map/ppermute | solution.py:20
  109.0 0.2 fusion.8
  109.2 4.5 %collective-permute-done.11 = f32[512,256]{0,1:T(8,128)S(1)} collective-permute-done((f32[512,256]{0,1:T(8,128)S(1)}, f32[512,256]{0,1:T(8,128)S(1)}, u32[]{:S(2)}, u32[]{:S(2)}) %collective-permute-start.11) | collective-permute-done | bytes 524320 | tf_op jit(solution)/shard_map/ppermute | solution.py:22
  113.7 0.6 fusion.32
  114.5 0.5 fusion.3
  114.9 7.8 %collective-permute-start.7 = (f32[64,512]{1,0:T(8,128)S(1)}, f32[64,512]{1,0:T(8,128)S(1)}, u32[]{:S(2)}, u32[]{:S(2)}) collective-permute-start(f32[64,512]{1,0:T(8,128)S(1)} %fusion.3), channel_id=1, source_target_pairs={{0,64},{8,72},{16,80},{24,88},{32,96},{40,104},{48,112},{56,120},{... | collective-permute-start | bytes 393224 | tf_op jit(solution)/shard_map/ppermute | solution.py:20
  122.7 2.5 %collective-permute-done.7 = f32[64,512]{1,0:T(8,128)S(1)} collective-permute-done((f32[64,512]{1,0:T(8,128)S(1)}, f32[64,512]{1,0:T(8,128)S(1)}, u32[]{:S(2)}, u32[]{:S(2)}) %collective-permute-start.7) | collective-permute-done | bytes 131104 | tf_op jit(solution)/shard_map/ppermute | solution.py:20
  125.2 0.4 fusion.2
  125.6 5.7 %collective-permute-start.10 = (f32[64,512]{1,0:T(8,128)S(1)}, f32[64,512]{1,0:T(8,128)S(1)}, u32[]{:S(2)}, u32[]{:S(2)}) collective-permute-start(f32[64,512]{1,0:T(8,128)S(1)} %fusion.2), channel_id=1, source_target_pairs={{0,128},{8,136},{16,144},{24,152},{32,160},{40,168},{48,176},{56,1... | collective-permute-start | bytes 393224 | tf_op jit(solution)/shard_map/ppermute | solution.py:20
  131.4 2.5 %collective-permute-done.10 = f32[64,512]{1,0:T(8,128)S(1)} collective-permute-done((f32[64,512]{1,0:T(8,128)S(1)}, f32[64,512]{1,0:T(8,128)S(1)}, u32[]{:S(2)}, u32[]{:S(2)}) %collective-permute-start.10) | collective-permute-done | bytes 131104 | tf_op jit(solution)/shard_map/ppermute | solution.py:20
  133.9 0.5 fusion.1
  134.4 1.1 broadcast_in_dim.19
  135.5 4.8 %all-to-all-start = ((f32[8,1,64,512]{3,2,1,0:T(8,128)}), f32[8,1,64,512]{3,2,1,0:T(8,128)S(1)}, u32[]{:S(2)}, u32[]{:S(2)}) async-start(f32[8,1,64,512]{3,2,1,0:T(8,128)} %broadcast_in_dim.19), calls=%async_computation | async-start | bytes 2097152 | tf_op jit(solution)/shard_map/all_to_all | solution.py:87
  140.4 1.0 copy.18
  141.3 12.9 %all-to-all-done = f32[8,1,64,512]{3,2,1,0:T(8,128)S(1)} async-done(((f32[8,1,64,512]{3,2,1,0:T(8,128)}), f32[8,1,64,512]{3,2,1,0:T(8,128)S(1)}, u32[]{:S(2)}, u32[]{:S(2)}) %all-to-all-start) | async-done | bytes 1048608 | tf_op jit(solution)/shard_map/all_to_all | solution.py:87
  154.2 5.5 %all-to-all-start.1 = ((f32[64,8,256]{2,0,1:T(8,128)}), f32[64,8,256]{2,0,1:T(8,128)S(1)}, u32[]{:S(2)}, u32[]{:S(2)}) async-start(f32[64,8,256]{2,0,1:T(8,128)} %copy.18), calls=%async_computation.1 | async-start | bytes 1048576 | tf_op jit(solution)/shard_map/all_to_all | solution.py:84
  159.7 0.1 constant_dynamic-slice_fusion
  159.8 8.1 %all-to-all-done.1 = f32[64,8,256]{2,0,1:T(8,128)S(1)} async-done(((f32[64,8,256]{2,0,1:T(8,128)}), f32[64,8,256]{2,0,1:T(8,128)S(1)}, u32[]{:S(2)}, u32[]{:S(2)}) %all-to-all-start.1) | async-done | bytes 524320 | tf_op jit(solution)/shard_map/all_to_all | solution.py:84
  167.9 1.9 fusion
  169.9 16.1 %all_to_all.30 = f32[4,128,320]{1,2,0:T(8,128)S(1)} all-to-all(f32[4,128,320]{1,2,0:T(8,128)S(1)} %bitcast.61), channel_id=1, replica_groups={{0,64,128,192},{8,72,136,200},{16,80,144,208},{24,88,152,216},{32,96,16..., dimensions={0} | all-to-all | bytes 1310720 | tf_op jit(solution)/shard_map/all_to_all | solution.py:107
  186.0 0.1 copy.21
  186.1 12.6 %all_to_all.31 = f32[8,16,320]{2,1,0:T(8,128)S(1)} all-to-all(f32[8,16,320]{2,1,0:T(8,128)S(1)} %bitcast.64), channel_id=1, replica_groups={{0,8,16,24,32,40,48,56},{64,72,80,88,96,104,112,120},{128,136,144,152,1..., dimensions={0} | all-to-all | bytes 327680 | tf_op jit(solution)/shard_map/all_to_all | solution.py:107
  198.7 0.6 slice.8
  199.3 0.7 slice.9
  (29 shorter events, 0.4 us)
Async XLA Ops:
  0.6 52.3 %copy-start = (bf16[4,512,256]{2,1,0:T(8,128)(2,1)S(1)}, bf16[4,512,256]{2,1,0:T(8,128)(2,1)}, u32[]{:S(2)}) copy-start(bf16[4,512,256]{2,1,0:T(8,128)(2,1)} %param.7) | copy-start | bytes 3145732
  2.3 1.0 copy-start.1
  3.3 15.0 %collective-permute-start.2 = (f32[512,256]{0,1:T(8,128)S(1)}, f32[512,256]{0,1:T(8,128)}, u32[]{:S(2)}, u32[]{:S(2)}) collective-permute-start(f32[512,256]{0,1:T(8,128)S(1)} %constant_dynamic-slice_fusion.1), channel_id=1, source_target_pairs={{0,8},{8,16},{16,24},{24,32},{32,40},{40,48},{48,56},{56,64},{64,7... | collective-permute-start | bytes 1572872 | tf_op jit(solution)/shard_map/ppermute | solution.py:22
  20.8 7.3 %copy-start.3 = (f32[512,256]{0,1:T(8,128)}, f32[512,256]{0,1:T(8,128)S(1)}, u32[]{:S(2)}) copy-start(f32[512,256]{0,1:T(8,128)S(1)} %get-tuple-element.16) | copy-start | bytes 1572868
  20.8 7.3 %collective-permute-start.3 = (f32[512,256]{0,1:T(8,128)S(1)}, f32[512,256]{0,1:T(8,128)}, u32[]{:S(2)}, u32[]{:S(2)}) collective-permute-start(f32[512,256]{0,1:T(8,128)S(1)} %get-tuple-element.16), channel_id=1, source_target_pairs={{0,1},{1,0},{2,3},{3,2},{4,5},{5,4},{6,7},{7,6},{8,9},{9,8},{10,11... | collective-permute-start | bytes 1572872 | tf_op jit(solution)/shard_map/ppermute | solution.py:27
  20.8 29.4 %collective-permute-start.5 = (f32[512,256]{0,1:T(8,128)}, f32[512,256]{0,1:T(8,128)}, u32[]{:S(2)}, u32[]{:S(2)}) collective-permute-start(f32[512,256]{0,1:T(8,128)} %get-tuple-element.11), channel_id=1, source_target_pairs={{0,16},{8,24},{16,32},{24,40},{32,48},{40,56},{48,64},{56,72},{64,... | collective-permute-start | bytes 1572872 | tf_op jit(solution)/shard_map/ppermute | solution.py:22
  53.0 14.9 %collective-permute-start.6 = (f32[512,256]{0,1:T(8,128)}, f32[512,256]{0,1:T(8,128)}, u32[]{:S(2)}, u32[]{:S(2)}) collective-permute-start(f32[512,256]{0,1:T(8,128)} %get-tuple-element.18), channel_id=1, source_target_pairs={{0,1},{1,0},{2,3},{3,2},{4,5},{5,4},{6,7},{7,6},{8,9},{9,8},{10,11... | collective-permute-start | bytes 1572872 | tf_op jit(solution)/shard_map/ppermute | solution.py:27
  53.0 0.9 copy-start.7
  53.0 12.5 %copy-start.2 = (f32[1,512,512]{2,1,0:T(8,128)S(1)}, f32[1,512,512]{2,1,0:T(8,128)}, u32[]{:S(2)}) copy-start(f32[1,512,512]{2,1,0:T(8,128)} %param.6) | copy-start | bytes 3145732
  53.9 11.6 %copy-start.6 = (f32[64,512]{1,0:T(8,128)S(1)}, f32[64,512]{1,0:T(8,128)}, u32[]{:S(2)}) copy-start(f32[64,512]{1,0:T(8,128)} %param.10) | copy-start | bytes 393220
  54.1 33.7 %collective-permute-start.8 = (f32[512,256]{0,1:T(8,128)}, f32[512,256]{0,1:T(8,128)}, u32[]{:S(2)}, u32[]{:S(2)}) collective-permute-start(f32[512,256]{0,1:T(8,128)} %get-tuple-element.17), channel_id=1, source_target_pairs={{0,32},{8,40},{16,48},{24,56},{32,64},{40,72},{48,80},{56,88},{64,... | collective-permute-start | bytes 1572872 | tf_op jit(solution)/shard_map/ppermute | solution.py:22
  66.6 23.9 %collective-permute-start = (f32[64,512]{1,0:T(8,128)S(1)}, f32[64,512]{1,0:T(8,128)S(1)}, u32[]{:S(2)}, u32[]{:S(2)}) collective-permute-start(f32[64,512]{1,0:T(8,128)S(1)} %convolution_add_fusion.5), channel_id=1, source_target_pairs={{0,8},{8,16},{16,24},{24,32},{32,40},{40,48},{48,56},{56,64},{64,7... | collective-permute-start | bytes 393224 | tf_op jit(solution)/shard_map/ppermute | solution.py:20
  89.7 19.3 %collective-permute-start.9 = (f32[512,256]{0,1:T(8,128)S(1)}, f32[512,256]{0,1:T(8,128)S(1)}, u32[]{:S(2)}, u32[]{:S(2)}) collective-permute-start(f32[512,256]{0,1:T(8,128)S(1)} %get-tuple-element.20), channel_id=1, source_target_pairs={{0,1},{1,0},{2,3},{3,2},{4,5},{5,4},{6,7},{7,6},{8,9},{9,8},{10,11... | collective-permute-start | bytes 1572872 | tf_op jit(solution)/shard_map/ppermute | solution.py:27
  91.0 11.0 %collective-permute-start.1 = (f32[64,512]{1,0:T(8,128)S(1)}, f32[64,512]{1,0:T(8,128)S(1)}, u32[]{:S(2)}, u32[]{:S(2)}) collective-permute-start(f32[64,512]{1,0:T(8,128)S(1)} %fusion.5), channel_id=1, source_target_pairs={{0,16},{8,24},{16,32},{24,40},{32,48},{40,56},{48,64},{56,72},{64,... | collective-permute-start | bytes 393224 | tf_op jit(solution)/shard_map/ppermute | solution.py:20
  96.2 17.5 %collective-permute-start.11 = (f32[512,256]{0,1:T(8,128)S(1)}, f32[512,256]{0,1:T(8,128)S(1)}, u32[]{:S(2)}, u32[]{:S(2)}) collective-permute-start(f32[512,256]{0,1:T(8,128)S(1)} %get-tuple-element.19), channel_id=1, source_target_pairs={{0,64},{8,72},{16,80},{24,88},{32,96},{40,104},{48,112},{56,120},{... | collective-permute-start | bytes 1572872 | tf_op jit(solution)/shard_map/ppermute | solution.py:22
  102.3 12.1 %collective-permute-start.4 = (f32[64,512]{1,0:T(8,128)S(1)}, f32[64,512]{1,0:T(8,128)S(1)}, u32[]{:S(2)}, u32[]{:S(2)}) collective-permute-start(f32[64,512]{1,0:T(8,128)S(1)} %fusion.4), channel_id=1, source_target_pairs={{0,32},{8,40},{16,48},{24,56},{32,64},{40,72},{48,80},{56,88},{64,... | collective-permute-start | bytes 393224 | tf_op jit(solution)/shard_map/ppermute | solution.py:20
  114.4 19.5 %collective-permute-start.12 = (f32[512,256]{0,1:T(8,128)S(1)}, f32[512,256]{0,1:T(8,128)S(1)}, u32[]{:S(2)}, u32[]{:S(2)}) collective-permute-start(f32[512,256]{0,1:T(8,128)S(1)} %fusion.32), channel_id=1, source_target_pairs={{0,1},{1,0},{2,3},{3,2},{4,5},{5,4},{6,7},{7,6},{8,9},{9,8},{10,11... | collective-permute-start | bytes 1572872 | tf_op jit(solution)/shard_map/ppermute | solution.py:27
  114.9 10.3 %collective-permute-start.7 = (f32[64,512]{1,0:T(8,128)S(1)}, f32[64,512]{1,0:T(8,128)S(1)}, u32[]{:S(2)}, u32[]{:S(2)}) collective-permute-start(f32[64,512]{1,0:T(8,128)S(1)} %fusion.3), channel_id=1, source_target_pairs={{0,64},{8,72},{16,80},{24,88},{32,96},{40,104},{48,112},{56,120},{... | collective-permute-start | bytes 393224 | tf_op jit(solution)/shard_map/ppermute | solution.py:20
  125.6 8.2 %collective-permute-start.10 = (f32[64,512]{1,0:T(8,128)S(1)}, f32[64,512]{1,0:T(8,128)S(1)}, u32[]{:S(2)}, u32[]{:S(2)}) collective-permute-start(f32[64,512]{1,0:T(8,128)S(1)} %fusion.2), channel_id=1, source_target_pairs={{0,128},{8,136},{16,144},{24,152},{32,160},{40,168},{48,176},{56,1... | collective-permute-start | bytes 393224 | tf_op jit(solution)/shard_map/ppermute | solution.py:20
  134.4 1.1 copy-start.5
  135.5 4.8 %copy-start.4 = (bf16[1,64,2048]{2,1,0:T(8,128)(2,1)S(1)}, bf16[1,64,2048]{2,1,0:T(8,128)(2,1)}, u32[]{:S(2)}) copy-start(bf16[1,64,2048]{2,1,0:T(8,128)(2,1)} %param.11) | copy-start | bytes 786436
  135.5 18.7 %all-to-all-start = ((f32[8,1,64,512]{3,2,1,0:T(8,128)}), f32[8,1,64,512]{3,2,1,0:T(8,128)S(1)}, u32[]{:S(2)}, u32[]{:S(2)}) async-start(f32[8,1,64,512]{3,2,1,0:T(8,128)} %broadcast_in_dim.19), calls=%async_computation | async-start | bytes 2097152 | tf_op jit(solution)/shard_map/all_to_all | solution.py:87
  154.2 13.7 %all-to-all-start.1 = ((f32[64,8,256]{2,0,1:T(8,128)}), f32[64,8,256]{2,0,1:T(8,128)S(1)}, u32[]{:S(2)}, u32[]{:S(2)}) async-start(f32[64,8,256]{2,0,1:T(8,128)} %copy.18), calls=%async_computation.1 | async-start | bytes 1048576 | tf_op jit(solution)/shard_map/all_to_all | solution.py:84

commit v9 on v8

--- a/solution.py
+++ b/solution.py
@@ -5,7 +5,7 @@
 
 
 def shift_scan(matrix, vector, axis, pair_axis):
-    highest = lax.Precision.HIGH
+    highest = lax.Precision.HIGHEST
     count, index = (lax.axis_size(axis), lax.axis_index(axis))
     pair_count = lax.axis_size(pair_axis)
     side = lax.axis_index(pair_axis) % 2
@@ -84,10 +84,20 @@
     readings = lax.all_to_all(readings, "scen", 1, 0, tiled=True)
     readings = readings.reshape(scen_shards, step_count, local_scen, cross_cols)
     readings = readings.transpose(1, 0, 2, 3).reshape(step_count, scen_shards * local_scen, cross_cols)
+    core = lax.axis_index("scen") % 2
+    partner = lax.ppermute(states, "scen", [(j, j ^ 1) for j in range(scen_shards)])
+    pair = jnp.where(
+        core == 0,
+        jnp.concatenate([states, partner], axis=1),
+        jnp.concatenate([partner, states], axis=1),
+    )
+    chips = scen_shards // 2
+    groups = [[c + 2 * k for k in range(chips)] for c in range(2)]
     every = lax.all_to_all(
-        jnp.broadcast_to(states[None], (scen_shards,) + states.shape), "scen", 0, 0, tiled=True
+        jnp.broadcast_to(pair[None], (chips,) + pair.shape),
+        "scen", 0, 0, tiled=True, axis_index_groups=groups,
     )
-    every = every.reshape(scen_shards, step_count, local_scen, modes).transpose(1, 0, 2, 3)
+    every = every.reshape(chips, step_count, 2 * local_scen, modes).transpose(1, 0, 2, 3)
     every = every.reshape(step_count, scen_shards * local_scen, modes)
     column = lax.axis_index("scen") * gram_cols
     right = jnp.concatenate(

time: 202 us -> 206 us (1.020)
  matrix products: 14 us -> 17.6 us
  transfers between devices with their start and end apart: 15 -> 16, of which waited for: 10 -> 11; matrix products, arithmetic and copies ran while one was open for 6% -> 7% of each run, Pallas kernels for 0% -> 0%
where the time goes in v9:
time: 206 us; the launch traced here: 204 us
  waiting for transfers between devices  81.8 us (40%)
  starting transfers between devices  63.4 us (31%)
  blocking collectives  28.7 us (14%)
  matrix products  17.6 us (9%)
  local copies, waits for them, and re-layouts  6.31 us (3%)
  other arithmetic  4.48 us (2%)
    ppermute x4, waiting for transfers between devices, shift_scan(): got_half = lax.ppermute(mine, axis, pairs)  52.5 us
    all_to_all x2, blocking collectives, on_device_body(): lax.all_to_all(pieces, 'tm', 0, 0, tiled=True, axis_index_groups=groups)  28.7 us
    ppermute x5, starting transfers between devices, shift_scan(): got_vector = lax.ppermute(vector, axis, pairs)  26.6 us
    ppermute x4, starting transfers between devices, shift_scan(): got_half = lax.ppermute(mine, axis, pairs)  26.1 us
    all_to_all x1, waiting for transfers between devices, on_device_body(): lax.all_to_all(jnp.broadcast_to(pair[None], (chips,) + pair.shape), 'scen...  12.3 us
    dot_general x4, matrix products, shift_scan(): own = jnp.dot(matrix, got_half, precision=highest)  9.62 us
    all_to_all x1, waiting for transfers between devices, on_device_body(): readings = lax.all_to_all(readings, 'scen', 1, 0, tiled=True)  8.09 us
    ppermute x5, waiting for transfers between devices, shift_scan(): got_vector = lax.ppermute(vector, axis, pairs)  7.59 us
  transfers between devices with their start and end apart: 16, of which 11 were waited for; matrix products, arithmetic and copies ran while one was open for 7% of the time, Pallas kernels for 0%

profile of v9, /device:TPU:24, one launch (start us, length us, event | category | flops | bytes accessed | tf_op | source)
XLA Modules:
  0.0 203.9 jit_solution(4359609587356325825)
XLA Ops:
  0.7 1.6 copy.17
  2.4 0.9 copy-done.1
  3.3 4.6 %collective-permute-start.2 = (f32[512,256]{0,1:T(8,128)S(1)}, f32[512,256]{0,1:T(8,128)}, u32[]{:S(2)}, u32[]{:S(2)}) collective-permute-start(f32[512,256]{0,1:T(8,128)S(1)} %constant_dynamic-slice_fusion.1), channel_id=1, source_target_pairs={{0,8},{8,16},{16,24},{24,32},{32,40},{40,48},{48,56},{56,64},{64,7... | collective-permute-start | bytes 1572872 | tf_op jit(solution)/shard_map/ppermute | solution.py:22
  8.0 10.4 %collective-permute-done.2 = f32[512,256]{0,1:T(8,128)} collective-permute-done((f32[512,256]{0,1:T(8,128)S(1)}, f32[512,256]{0,1:T(8,128)}, u32[]{:S(2)}, u32[]{:S(2)}) %collective-permute-start.2) | collective-permute-done | bytes 524320 | tf_op jit(solution)/shard_map/ppermute | solution.py:22
  18.3 2.9 %broadcast_select_fusion.2 = (f32[512,256]{0,1:T(8,128)}, f32[512,256]{0,1:T(8,128)S(1)}) fusion(f32[512,256]{0,1:T(8,128)S(1)} %constant_dynamic-slice_fusion.1, pred[]{:T(512)S(6)} %ge.19, f32[512,512]{0,1:T(8,128)S(1)} %bitcast_select_fusion, f32[512,256]{0,1:T(8,128)} %collective-permute-done.2), kind=kOutput, calls=%fused_computation.41 | convolution fusion | flops 805437440 | bytes 3145729 | tf_op jit(solution)/shard_map/dot_general | solution.py:26
  21.3 6.7 %collective-permute-start.5 = (f32[512,256]{0,1:T(8,128)}, f32[512,256]{0,1:T(8,128)}, u32[]{:S(2)}, u32[]{:S(2)}) collective-permute-start(f32[512,256]{0,1:T(8,128)} %get-tuple-element.11), channel_id=1, source_target_pairs={{0,16},{8,24},{16,32},{24,40},{32,48},{40,56},{48,64},{56,72},{64,... | collective-permute-start | bytes 1572872 | tf_op jit(solution)/shard_map/ppermute | solution.py:22
  28.6 2.2 %fusion.6 = f32[512,512]{0,1:T(8,128)S(1)} fusion(f32[512,256]{0,1:T(8,128)} %collective-permute-done.3, f32[512,256]{0,1:T(8,128)} %copy-done.3, pred[]{:T(512)S(6)} %eq.30, pred[]{:T(512)S(6)} %ge.19, f32[1,512,512]{1,2,0:T(8,128)} %copy-done.1, pred[]{:T(512)S(6)} %eq.26), kind=kLoop, calls=%fused_computation.15 | loop fusion | flops 1310720 | bytes 3145731 | tf_op jit(solution)/shard_map/jit(_where)/select_n | solution.py:33
  30.8 19.8 %collective-permute-done.5 = f32[512,256]{0,1:T(8,128)} collective-permute-done((f32[512,256]{0,1:T(8,128)}, f32[512,256]{0,1:T(8,128)}, u32[]{:S(2)}, u32[]{:S(2)}) %collective-permute-start.5) | collective-permute-done | bytes 524320 | tf_op jit(solution)/shard_map/ppermute | solution.py:22
  50.6 3.3 %broadcast_select_fusion.1 = (f32[512,256]{0,1:T(8,128)}, f32[512,256]{0,1:T(8,128)}) fusion(f32[512,256]{0,1:T(8,128)} %get-tuple-element.11, pred[]{:T(512)S(6)} %ge.18, f32[512,512]{0,1:T(8,128)S(1)} %fusion.6, f32[512,256]{0,1:T(8,128)} %collective-permute-done.5), kind=kOutput, calls=%fused_computation.40 | convolution fusion | flops 805437440 | bytes 3145729 | tf_op jit(solution)/shard_map/dot_general | solution.py:26
  53.9 0.9 fusion.17
  54.9 0.2 convolution_bitcast_fusion
  55.1 11.4 %collective-permute-start.8 = (f32[512,256]{0,1:T(8,128)}, f32[512,256]{0,1:T(8,128)}, u32[]{:S(2)}, u32[]{:S(2)}) collective-permute-start(f32[512,256]{0,1:T(8,128)} %get-tuple-element.17), channel_id=1, source_target_pairs={{0,32},{8,40},{16,48},{24,56},{32,64},{40,72},{48,80},{56,88},{64,... | collective-permute-start | bytes 1572872 | tf_op jit(solution)/shard_map/ppermute | solution.py:22
  66.4 1.1 convolution_add_fusion.5
  67.6 1.3 collective-permute-start
  68.9 1.9 fusion.7
  70.8 18.0 %collective-permute-done.8 = f32[512,256]{0,1:T(8,128)} collective-permute-done((f32[512,256]{0,1:T(8,128)}, f32[512,256]{0,1:T(8,128)}, u32[]{:S(2)}, u32[]{:S(2)}) %collective-permute-start.8) | collective-permute-done | bytes 524320 | tf_op jit(solution)/shard_map/ppermute | solution.py:22
  88.8 2.3 %broadcast_select_fusion = (f32[512,256]{0,1:T(8,128)S(1)}, f32[512,256]{0,1:T(8,128)S(1)}) fusion(f32[512,256]{0,1:T(8,128)} %get-tuple-element.17, pred[]{:T(512)S(6)} %ge.17, f32[512,512]{0,1:T(8,128)S(1)} %fusion.7, f32[512,256]{0,1:T(8,128)} %collective-permute-done.8), kind=kOutput, calls=%fused_computation.39 | convolution fusion | flops 805437440 | bytes 3145729 | tf_op jit(solution)/shard_map/dot_general | solution.py:26
  91.2 0.2 collective-permute-done
  91.5 0.8 fusion.5
  92.2 5.2 %collective-permute-start.1 = (f32[64,512]{1,0:T(8,128)S(1)}, f32[64,512]{1,0:T(8,128)S(1)}, u32[]{:S(2)}, u32[]{:S(2)}) collective-permute-start(f32[64,512]{1,0:T(8,128)S(1)} %fusion.5), channel_id=1, source_target_pairs={{0,16},{8,24},{16,32},{24,40},{32,48},{40,56},{48,64},{56,72},{64,... | collective-permute-start | bytes 393224 | tf_op jit(solution)/shard_map/ppermute | solution.py:20
  97.5 3.4 %collective-permute-start.11 = (f32[512,256]{0,1:T(8,128)S(1)}, f32[512,256]{0,1:T(8,128)S(1)}, u32[]{:S(2)}, u32[]{:S(2)}) collective-permute-start(f32[512,256]{0,1:T(8,128)S(1)} %get-tuple-element.19), channel_id=1, source_target_pairs={{0,64},{8,72},{16,80},{24,88},{32,96},{40,104},{48,112},{56,120},{... | collective-permute-start | bytes 1572872 | tf_op jit(solution)/shard_map/ppermute | solution.py:22
  100.9 2.4 %collective-permute-done.1 = f32[64,512]{1,0:T(8,128)S(1)} collective-permute-done((f32[64,512]{1,0:T(8,128)S(1)}, f32[64,512]{1,0:T(8,128)S(1)}, u32[]{:S(2)}, u32[]{:S(2)}) %collective-permute-start.1) | collective-permute-done | bytes 131104 | tf_op jit(solution)/shard_map/ppermute | solution.py:20
  103.3 0.8 fusion.4
  104.0 7.0 %collective-permute-start.4 = (f32[64,512]{1,0:T(8,128)S(1)}, f32[64,512]{1,0:T(8,128)S(1)}, u32[]{:S(2)}, u32[]{:S(2)}) collective-permute-start(f32[64,512]{1,0:T(8,128)S(1)} %fusion.4), channel_id=1, source_target_pairs={{0,32},{8,40},{16,48},{24,56},{32,64},{40,72},{48,80},{56,88},{64,... | collective-permute-start | bytes 393224 | tf_op jit(solution)/shard_map/ppermute | solution.py:20
  111.1 0.2 fusion.8
  111.3 4.2 %collective-permute-done.11 = f32[512,256]{0,1:T(8,128)S(1)} collective-permute-done((f32[512,256]{0,1:T(8,128)S(1)}, f32[512,256]{0,1:T(8,128)S(1)}, u32[]{:S(2)}, u32[]{:S(2)}) %collective-permute-start.11) | collective-permute-done | bytes 524320 | tf_op jit(solution)/shard_map/ppermute | solution.py:22
  115.5 1.1 fusion.32
  116.6 0.3 collective-permute-start.12
  116.9 0.8 fusion.3
  117.7 5.8 %collective-permute-start.7 = (f32[64,512]{1,0:T(8,128)S(1)}, f32[64,512]{1,0:T(8,128)S(1)}, u32[]{:S(2)}, u32[]{:S(2)}) collective-permute-start(f32[64,512]{1,0:T(8,128)S(1)} %fusion.3), channel_id=1, source_target_pairs={{0,64},{8,72},{16,80},{24,88},{32,96},{40,104},{48,112},{56,120},{... | collective-permute-start | bytes 393224 | tf_op jit(solution)/shard_map/ppermute | solution.py:20
  123.6 2.5 %collective-permute-done.7 = f32[64,512]{1,0:T(8,128)S(1)} collective-permute-done((f32[64,512]{1,0:T(8,128)S(1)}, f32[64,512]{1,0:T(8,128)S(1)}, u32[]{:S(2)}, u32[]{:S(2)}) %collective-permute-start.7) | collective-permute-done | bytes 131104 | tf_op jit(solution)/shard_map/ppermute | solution.py:20
  126.0 0.8 fusion.2
  126.8 7.2 %collective-permute-start.10 = (f32[64,512]{1,0:T(8,128)S(1)}, f32[64,512]{1,0:T(8,128)S(1)}, u32[]{:S(2)}, u32[]{:S(2)}) collective-permute-start(f32[64,512]{1,0:T(8,128)S(1)} %fusion.2), channel_id=1, source_target_pairs={{0,128},{8,136},{16,144},{24,152},{32,160},{40,168},{48,176},{56,1... | collective-permute-start | bytes 393224 | tf_op jit(solution)/shard_map/ppermute | solution.py:20
  134.0 2.5 %collective-permute-done.10 = f32[64,512]{1,0:T(8,128)S(1)} collective-permute-done((f32[64,512]{1,0:T(8,128)S(1)}, f32[64,512]{1,0:T(8,128)S(1)}, u32[]{:S(2)}, u32[]{:S(2)}) %collective-permute-start.10) | collective-permute-done | bytes 131104 | tf_op jit(solution)/shard_map/ppermute | solution.py:20
  136.5 0.8 fusion.1
  137.4 1.3 collective-permute-done.13
  138.8 1.1 broadcast_in_dim.20
  139.9 4.8 %all-to-all-start = ((f32[4,1,128,512]{3,2,1,0:T(8,128)}), f32[4,1,128,512]{3,2,1,0:T(8,128)S(1)}, u32[]{:S(2)}, u32[]{:S(2)}) async-start(f32[4,1,128,512]{3,2,1,0:T(8,128)} %broadcast_in_dim.20), calls=%async_computation | async-start | bytes 2097152 | tf_op jit(solution)/shard_map/all_to_all | solution.py:96
  144.8 1.0 copy.18
  145.8 12.3 %all-to-all-done = f32[4,1,128,512]{3,2,1,0:T(8,128)S(1)} async-done(((f32[4,1,128,512]{3,2,1,0:T(8,128)}), f32[4,1,128,512]{3,2,1,0:T(8,128)S(1)}, u32[]{:S(2)}, u32[]{:S(2)}) %all-to-all-start) | async-done | bytes 1048608 | tf_op jit(solution)/shard_map/all_to_all | solution.py:96
  158.1 5.5 %all-to-all-start.1 = ((f32[64,8,256]{2,0,1:T(8,128)}), f32[64,8,256]{2,0,1:T(8,128)S(1)}, u32[]{:S(2)}, u32[]{:S(2)}) async-start(f32[64,8,256]{2,0,1:T(8,128)} %copy.18), calls=%async_computation.1 | async-start | bytes 1048576 | tf_op jit(solution)/shard_map/all_to_all | solution.py:84
  163.6 0.1 constant_dynamic-slice_fusion
  163.7 8.1 %all-to-all-done.1 = f32[64,8,256]{2,0,1:T(8,128)S(1)} async-done(((f32[64,8,256]{2,0,1:T(8,128)}), f32[64,8,256]{2,0,1:T(8,128)S(1)}, u32[]{:S(2)}, u32[]{:S(2)}) %all-to-all-start.1) | async-done | bytes 524320 | tf_op jit(solution)/shard_map/all_to_all | solution.py:84
  171.8 1.9 fusion
  173.7 16.4 %all_to_all.30 = f32[4,128,320]{1,2,0:T(8,128)S(1)} all-to-all(f32[4,128,320]{1,2,0:T(8,128)S(1)} %bitcast.62), channel_id=1, replica_groups={{0,64,128,192},{8,72,136,200},{16,80,144,208},{24,88,152,216},{32,96,16..., dimensions={0} | all-to-all | bytes 1310720 | tf_op jit(solution)/shard_map/all_to_all | solution.py:117
  190.3 12.3 %all_to_all.31 = f32[8,16,320]{2,1,0:T(8,128)S(1)} all-to-all(f32[8,16,320]{2,1,0:T(8,128)S(1)} %bitcast.65), channel_id=1, replica_groups={{0,8,16,24,32,40,48,56},{64,72,80,88,96,104,112,120},{128,136,144,152,1..., dimensions={0} | all-to-all | bytes 327680 | tf_op jit(solution)/shard_map/all_to_all | solution.py:117
  202.6 0.6 slice.8
  203.2 0.7 slice.9
  (32 shorter events, 0.7 us)
Async XLA Ops:
  0.6 53.3 %copy-start = (bf16[4,512,256]{2,1,0:T(8,128)(2,1)S(1)}, bf16[4,512,256]{2,1,0:T(8,128)(2,1)}, u32[]{:S(2)}) copy-start(bf16[4,512,256]{2,1,0:T(8,128)(2,1)} %param.7) | copy-start | bytes 3145732
  2.3 1.0 copy-start.1
  3.3 15.0 %collective-permute-start.2 = (f32[512,256]{0,1:T(8,128)S(1)}, f32[512,256]{0,1:T(8,128)}, u32[]{:S(2)}, u32[]{:S(2)}) collective-permute-start(f32[512,256]{0,1:T(8,128)S(1)} %constant_dynamic-slice_fusion.1), channel_id=1, source_target_pairs={{0,8},{8,16},{16,24},{24,32},{32,40},{40,48},{48,56},{56,64},{64,7... | collective-permute-start | bytes 1572872 | tf_op jit(solution)/shard_map/ppermute | solution.py:22
  21.3 7.3 %copy-start.3 = (f32[512,256]{0,1:T(8,128)}, f32[512,256]{0,1:T(8,128)S(1)}, u32[]{:S(2)}) copy-start(f32[512,256]{0,1:T(8,128)S(1)} %get-tuple-element.16) | copy-start | bytes 1572868
  21.3 7.3 %collective-permute-start.3 = (f32[512,256]{0,1:T(8,128)S(1)}, f32[512,256]{0,1:T(8,128)}, u32[]{:S(2)}, u32[]{:S(2)}) collective-permute-start(f32[512,256]{0,1:T(8,128)S(1)} %get-tuple-element.16), channel_id=1, source_target_pairs={{0,1},{1,0},{2,3},{3,2},{4,5},{5,4},{6,7},{7,6},{8,9},{9,8},{10,11... | collective-permute-start | bytes 1572872 | tf_op jit(solution)/shard_map/ppermute | solution.py:27
  21.3 29.4 %collective-permute-start.5 = (f32[512,256]{0,1:T(8,128)}, f32[512,256]{0,1:T(8,128)}, u32[]{:S(2)}, u32[]{:S(2)}) collective-permute-start(f32[512,256]{0,1:T(8,128)} %get-tuple-element.11), channel_id=1, source_target_pairs={{0,16},{8,24},{16,32},{24,40},{32,48},{40,56},{48,64},{56,72},{64,... | collective-permute-start | bytes 1572872 | tf_op jit(solution)/shard_map/ppermute | solution.py:22
  53.9 15.0 %collective-permute-start.6 = (f32[512,256]{0,1:T(8,128)}, f32[512,256]{0,1:T(8,128)}, u32[]{:S(2)}, u32[]{:S(2)}) collective-permute-start(f32[512,256]{0,1:T(8,128)} %get-tuple-element.18), channel_id=1, source_target_pairs={{0,1},{1,0},{2,3},{3,2},{4,5},{5,4},{6,7},{7,6},{8,9},{9,8},{10,11... | collective-permute-start | bytes 1572872 | tf_op jit(solution)/shard_map/ppermute | solution.py:27
  53.9 0.9 copy-start.7
  53.9 12.5 %copy-start.2 = (f32[1,512,512]{2,1,0:T(8,128)S(1)}, f32[1,512,512]{2,1,0:T(8,128)}, u32[]{:S(2)}) copy-start(f32[1,512,512]{2,1,0:T(8,128)} %param.6) | copy-start | bytes 3145732
  54.9 11.6 %copy-start.6 = (f32[64,512]{1,0:T(8,128)S(1)}, f32[64,512]{1,0:T(8,128)}, u32[]{:S(2)}) copy-start(f32[64,512]{1,0:T(8,128)} %param.10) | copy-start | bytes 393220
  55.1 33.7 %collective-permute-start.8 = (f32[512,256]{0,1:T(8,128)}, f32[512,256]{0,1:T(8,128)}, u32[]{:S(2)}, u32[]{:S(2)}) collective-permute-start(f32[512,256]{0,1:T(8,128)} %get-tuple-element.17), channel_id=1, source_target_pairs={{0,32},{8,40},{16,48},{24,56},{32,64},{40,72},{48,80},{56,88},{64,... | collective-permute-start | bytes 1572872 | tf_op jit(solution)/shard_map/ppermute | solution.py:22
  67.6 23.9 %collective-permute-start = (f32[64,512]{1,0:T(8,128)S(1)}, f32[64,512]{1,0:T(8,128)S(1)}, u32[]{:S(2)}, u32[]{:S(2)}) collective-permute-start(f32[64,512]{1,0:T(8,128)S(1)} %convolution_add_fusion.5), channel_id=1, source_target_pairs={{0,8},{8,16},{16,24},{24,32},{32,40},{40,48},{48,56},{56,64},{64,7... | collective-permute-start | bytes 393224 | tf_op jit(solution)/shard_map/ppermute | solution.py:20
  91.1 19.9 %collective-permute-start.9 = (f32[512,256]{0,1:T(8,128)S(1)}, f32[512,256]{0,1:T(8,128)S(1)}, u32[]{:S(2)}, u32[]{:S(2)}) collective-permute-start(f32[512,256]{0,1:T(8,128)S(1)} %get-tuple-element.20), channel_id=1, source_target_pairs={{0,1},{1,0},{2,3},{3,2},{4,5},{5,4},{6,7},{7,6},{8,9},{9,8},{10,11... | collective-permute-start | bytes 1572872 | tf_op jit(solution)/shard_map/ppermute | solution.py:27
  92.2 11.0 %collective-permute-start.1 = (f32[64,512]{1,0:T(8,128)S(1)}, f32[64,512]{1,0:T(8,128)S(1)}, u32[]{:S(2)}, u32[]{:S(2)}) collective-permute-start(f32[64,512]{1,0:T(8,128)S(1)} %fusion.5), channel_id=1, source_target_pairs={{0,16},{8,24},{16,32},{24,40},{32,48},{40,56},{48,64},{56,72},{64,... | collective-permute-start | bytes 393224 | tf_op jit(solution)/shard_map/ppermute | solution.py:20
  97.5 18.1 %collective-permute-start.11 = (f32[512,256]{0,1:T(8,128)S(1)}, f32[512,256]{0,1:T(8,128)S(1)}, u32[]{:S(2)}, u32[]{:S(2)}) collective-permute-start(f32[512,256]{0,1:T(8,128)S(1)} %get-tuple-element.19), channel_id=1, source_target_pairs={{0,64},{8,72},{16,80},{24,88},{32,96},{40,104},{48,112},{56,120},{... | collective-permute-start | bytes 1572872 | tf_op jit(solution)/shard_map/ppermute | solution.py:22
  104.0 12.9 %collective-permute-start.4 = (f32[64,512]{1,0:T(8,128)S(1)}, f32[64,512]{1,0:T(8,128)S(1)}, u32[]{:S(2)}, u32[]{:S(2)}) collective-permute-start(f32[64,512]{1,0:T(8,128)S(1)} %fusion.4), channel_id=1, source_target_pairs={{0,32},{8,40},{16,48},{24,56},{32,64},{40,72},{48,80},{56,88},{64,... | collective-permute-start | bytes 393224 | tf_op jit(solution)/shard_map/ppermute | solution.py:20
  116.6 19.8 %collective-permute-start.12 = (f32[512,256]{0,1:T(8,128)S(1)}, f32[512,256]{0,1:T(8,128)S(1)}, u32[]{:S(2)}, u32[]{:S(2)}) collective-permute-start(f32[512,256]{0,1:T(8,128)S(1)} %fusion.32), channel_id=1, source_target_pairs={{0,1},{1,0},{2,3},{3,2},{4,5},{5,4},{6,7},{7,6},{8,9},{9,8},{10,11... | collective-permute-start | bytes 1572872 | tf_op jit(solution)/shard_map/ppermute | solution.py:27
  117.7 8.4 %collective-permute-start.7 = (f32[64,512]{1,0:T(8,128)S(1)}, f32[64,512]{1,0:T(8,128)S(1)}, u32[]{:S(2)}, u32[]{:S(2)}) collective-permute-start(f32[64,512]{1,0:T(8,128)S(1)} %fusion.3), channel_id=1, source_target_pairs={{0,64},{8,72},{16,80},{24,88},{32,96},{40,104},{48,112},{56,120},{... | collective-permute-start | bytes 393224 | tf_op jit(solution)/shard_map/ppermute | solution.py:20
  126.8 9.7 %collective-permute-start.10 = (f32[64,512]{1,0:T(8,128)S(1)}, f32[64,512]{1,0:T(8,128)S(1)}, u32[]{:S(2)}, u32[]{:S(2)}) collective-permute-start(f32[64,512]{1,0:T(8,128)S(1)} %fusion.2), channel_id=1, source_target_pairs={{0,128},{8,136},{16,144},{24,152},{32,160},{40,168},{48,176},{56,1... | collective-permute-start | bytes 393224 | tf_op jit(solution)/shard_map/ppermute | solution.py:20
  137.3 1.5 copy-start.5
  137.3 1.4 collective-permute-start.13
  139.9 4.8 %copy-start.4 = (bf16[1,64,2048]{2,1,0:T(8,128)(2,1)S(1)}, bf16[1,64,2048]{2,1,0:T(8,128)(2,1)}, u32[]{:S(2)}) copy-start(bf16[1,64,2048]{2,1,0:T(8,128)(2,1)} %param.11) | copy-start | bytes 786436
  139.9 18.2 %all-to-all-start = ((f32[4,1,128,512]{3,2,1,0:T(8,128)}), f32[4,1,128,512]{3,2,1,0:T(8,128)S(1)}, u32[]{:S(2)}, u32[]{:S(2)}) async-start(f32[4,1,128,512]{3,2,1,0:T(8,128)} %broadcast_in_dim.20), calls=%async_computation | async-start | bytes 2097152 | tf_op jit(solution)/shard_map/all_to_all | solution.py:96
  158.1 13.7 %all-to-all-start.1 = ((f32[64,8,256]{2,0,1:T(8,128)}), f32[64,8,256]{2,0,1:T(8,128)S(1)}, u32[]{:S(2)}, u32[]{:S(2)}) async-start(f32[64,8,256]{2,0,1:T(8,128)} %copy.18), calls=%async_computation.1 | async-start | bytes 1048576 | tf_op jit(solution)/shard_map/all_to_all | solution.py:84

commit v10 on v9

--- a/solution.py
+++ b/solution.py
@@ -8,10 +8,12 @@
     highest = lax.Precision.HIGHEST
     count, index = (lax.axis_size(axis), lax.axis_index(axis))
     pair_count = lax.axis_size(pair_axis)
-    side = lax.axis_index(pair_axis) % 2
-    width = matrix.shape[1] // 2
+    part = lax.axis_index(pair_axis) % 4
+    width = matrix.shape[1] // 4
+    across = [(j, j ^ 2) for j in range(pair_count)]
     swap = [(j, j ^ 1) for j in range(pair_count)]
-    mine = lax.dynamic_slice_in_dim(matrix, side * width, width, axis=1)
+    place = jnp.array([0, 2, 1, 3], jnp.int32)[part ^ jnp.arange(4, dtype=jnp.int32)]
+    mine = lax.dynamic_slice_in_dim(matrix, part * width, width, axis=1)
     distance = 1
     while distance < count:
         pairs = [(j, j + distance) for j in range(count - distance)]
@@ -19,17 +21,16 @@
         has = index >= distance
         got_vector = lax.ppermute(vector, axis, pairs)
         if not last:
-            got_half = lax.ppermute(mine, axis, pairs)
+            got_part = lax.ppermute(mine, axis, pairs)
         newer = jnp.einsum("sq,rq->sr", got_vector, matrix, precision=highest) + vector
         vector = jnp.where(has, newer, vector)
         if not last:
-            own = jnp.dot(matrix, got_half, precision=highest)
-            other = lax.ppermute(own, pair_axis, swap)
-            joined = jnp.where(
-                side == 0,
-                jnp.concatenate([own, other], axis=1),
-                jnp.concatenate([other, own], axis=1),
-            )
+            own = jnp.dot(matrix, got_part, precision=highest)
+            far = lax.ppermute(own, pair_axis, across)
+            near = lax.ppermute(jnp.stack([own, far]), pair_axis, swap)
+            pieces = jnp.concatenate([jnp.stack([own, far]), near], axis=0)
+            ordered = jnp.take(pieces, place, axis=0)
+            joined = jnp.concatenate([ordered[k] for k in range(4)], axis=1)
             matrix = jnp.where(has, joined, matrix)
             mine = jnp.where(has, own, mine)
         distance = distance * 2

time: 206 us -> 219 us (1.063)
  starting transfers between devices: 63.4 us -> 73.3 us
  waiting for transfers between devices: 81.8 us -> 73 us
  local copies, waits for them, and re-layouts: 6.31 us -> 13 us
  other arithmetic: 4.48 us -> 9.95 us
  blocking collectives: 28.7 us -> 25.6 us
  matrix products: 17.6 us -> 20.6 us
    ppermute x8 -> x12, starting transfers between devices: 26.5 us -> 37.9 us  [the longest x4 34.5 us: shift_scan(): got_part = lax.ppermute(mine, axis, pairs)]
    gather x0 -> x5, local copies, waits for them, and re-layouts: none -> 7.75 us  [the longest x4 7.11 us: shift_scan(): ordered = jnp.take(pieces, place, axis=0)]
    ppermute x8 -> x12, waiting for transfers between devices: 52.5 us -> 45.2 us  [the longest x4 23.6 us: shift_scan(): got_part = lax.ppermute(mine, axis, pairs)]
    concatenate x0 -> x4, other arithmetic: none -> 5.27 us  [shift_scan(): pieces = jnp.concatenate([jnp.stack([own, far]), near], axis=0)]
    dot_general x5, matrix products: 3.84 us -> 8.28 us  [shift_scan(): jnp.einsum('sq,rq->sr', got_vector, matrix, precision=highest) + vector]
    select_n x3, other arithmetic: 4.32 us -> 0.42 us  [shift_scan(): matrix = jnp.where(has, joined, matrix)]
    all_to_all x2, blocking collectives: 28.7 us -> 25.6 us  [on_device_body(): lax.all_to_all(pieces, 'tm', 0, 0, tiled=True, axis_index_groups=groups)]
  transfers between devices with their start and end apart: 16 -> 20, of which waited for: 11 -> 13; matrix products, arithmetic and copies ran while one was open for 7% -> 13% of each run, Pallas kernels for 0% -> 0%
where the time goes in v10:
time: 219 us; the launch traced here: 217 us
  starting transfers between devices  73.3 us (33%)
  waiting for transfers between devices  73 us (33%)
  blocking collectives  25.6 us (12%)
  matrix products  20.6 us (9%)
  local copies, waits for them, and re-layouts  13 us (6%)
  other arithmetic  9.95 us (5%)
    ppermute x4, starting transfers between devices, shift_scan(): got_part = lax.ppermute(mine, axis, pairs)  34.5 us
    all_to_all x2, blocking collectives, on_device_body(): lax.all_to_all(pieces, 'tm', 0, 0, tiled=True, axis_index_groups=groups)  25.6 us
    ppermute x5, starting transfers between devices, shift_scan(): got_vector = lax.ppermute(vector, axis, pairs)  24.4 us
    ppermute x4, waiting for transfers between devices, shift_scan(): got_part = lax.ppermute(mine, axis, pairs)  23.6 us
    ppermute x4, waiting for transfers between devices, shift_scan(): far = lax.ppermute(own, pair_axis, across)  21.5 us
    all_to_all x1, waiting for transfers between devices, on_device_body(): lax.all_to_all(jnp.broadcast_to(pair[None], (chips,) + pair.shape), 'scen...  12.3 us
    dot_general x5, matrix products, shift_scan(): jnp.einsum('sq,rq->sr', got_vector, matrix, precision=highest) + vector  8.28 us
    dot_general x4, matrix products, shift_scan(): own = jnp.dot(matrix, got_part, precision=highest)  8.27 us
  transfers between devices with their start and end apart: 20, of which 13 were waited for; matrix products, arithmetic and copies ran while one was open for 13% of the time, Pallas kernels for 0%

profile of v10, /device:TPU:24, one launch (start us, length us, event | category | flops | bytes accessed | tf_op | source)
XLA Modules:
  0.0 217.3 jit_solution(3295915050503542289)
XLA Ops:
  0.7 1.4 bitcast_select_fusion
  2.1 3.8 %collective-permute-start.2 = (f32[512,128]{1,0:T(8,128)S(1)}, f32[512,128]{1,0:T(8,128)S(1)}, u32[]{:S(2)}, u32[]{:S(2)}) collective-permute-start(f32[512,128]{1,0:T(8,128)S(1)} %constant_dynamic-slice_fusion.1), channel_id=1, source_target_pairs={{0,8},{8,16},{16,24},{24,32},{32,40},{40,48},{48,56},{56,64},{64,7... | collective-permute-start | bytes 786440 | tf_op jit(solution)/shard_map/ppermute | solution.py:24
  6.0 5.5 %collective-permute-done.2 = f32[512,128]{1,0:T(8,128)S(1)} collective-permute-done((f32[512,128]{1,0:T(8,128)S(1)}, f32[512,128]{1,0:T(8,128)S(1)}, u32[]{:S(2)}, u32[]{:S(2)}) %collective-permute-start.2) | collective-permute-done | bytes 262176 | tf_op jit(solution)/shard_map/ppermute | solution.py:24
  11.5 1.7 broadcast_select_fusion.6
  14.6 5.8 %collective-permute-done.3 = f32[512,128]{1,0:T(8,128)S(1)} collective-permute-done((f32[512,128]{1,0:T(8,128)S(1)}, f32[512,128]{1,0:T(8,128)S(1)}, u32[]{:S(2)}, u32[]{:S(2)}) %collective-permute-start.3) | collective-permute-done | bytes 262176 | tf_op jit(solution)/shard_map/ppermute | solution.py:29
  20.6 6.4 %collective-permute-start.6 = (f32[512,128]{1,0:T(8,128)}, f32[512,128]{1,0:T(8,128)}, u32[]{:S(2)}, u32[]{:S(2)}) collective-permute-start(f32[512,128]{1,0:T(8,128)} %get-tuple-element.32), channel_id=1, source_target_pairs={{0,16},{8,24},{16,32},{24,40},{32,48},{40,56},{48,64},{56,72},{64,... | collective-permute-start | bytes 786440 | tf_op jit(solution)/shard_map/ppermute | solution.py:24
  28.0 1.1 copy-done.6
  29.2 9.2 %collective-permute-done.6 = f32[512,128]{1,0:T(8,128)} collective-permute-done((f32[512,128]{1,0:T(8,128)}, f32[512,128]{1,0:T(8,128)}, u32[]{:S(2)}, u32[]{:S(2)}) %collective-permute-start.6) | collective-permute-done | bytes 262176 | tf_op jit(solution)/shard_map/ppermute | solution.py:24
  38.5 2.0 broadcast_select_fusion.5
  41.3 7.1 %collective-permute-done.7 = f32[512,128]{1,0:T(8,128)S(1)} collective-permute-done((f32[512,128]{1,0:T(8,128)S(1)}, f32[512,128]{1,0:T(8,128)S(1)}, u32[]{:S(2)}, u32[]{:S(2)}) %collective-permute-start.7) | collective-permute-done | bytes 262176 | tf_op jit(solution)/shard_map/ppermute | solution.py:29
  49.2 11.8 %collective-permute-start.10 = (f32[512,128]{1,0:T(8,128)S(1)}, f32[512,128]{1,0:T(8,128)}, u32[]{:S(2)}, u32[]{:S(2)}) collective-permute-start(f32[512,128]{1,0:T(8,128)S(1)} %get-tuple-element.34), channel_id=1, source_target_pairs={{0,32},{8,40},{16,48},{24,56},{32,64},{40,72},{48,80},{56,88},{64,... | collective-permute-start | bytes 786440 | tf_op jit(solution)/shard_map/ppermute | solution.py:24
  61.0 2.1 pad_maximum_fusion.1
  63.1 1.8 gather_fusion.2
  65.3 6.6 %collective-permute-done.10 = f32[512,128]{1,0:T(8,128)} collective-permute-done((f32[512,128]{1,0:T(8,128)S(1)}, f32[512,128]{1,0:T(8,128)}, u32[]{:S(2)}, u32[]{:S(2)}) %collective-permute-start.10) | collective-permute-done | bytes 262176 | tf_op jit(solution)/shard_map/ppermute | solution.py:24
  71.9 2.6 %broadcast_select_fusion.4 = (f32[512,128]{1,0:T(8,128)}, f32[512,128]{1,0:T(8,128)S(1)}) fusion(f32[512,128]{1,0:T(8,128)S(1)} %get-tuple-element.34, pred[]{:T(512)S(6)} %ge.21, f32[512,512]{1,0:T(8,128)S(1)} %maximum_select_fusion.1, f32[512,128]{1,0:T(8,128)} %collective-permute-done.10), kind=kOutput, calls=%fused_computation.69 | convolution fusion | flops 402718720 | bytes 2097153 | tf_op jit(solution)/shard_map/dot_general | solution.py:28
  76.4 6.4 %collective-permute-done.11 = f32[512,128]{1,0:T(8,128)S(1)} collective-permute-done((f32[512,128]{1,0:T(8,128)S(1)}, f32[512,128]{1,0:T(8,128)S(1)}, u32[]{:S(2)}, u32[]{:S(2)}) %collective-permute-start.11) | collective-permute-done | bytes 262176 | tf_op jit(solution)/shard_map/ppermute | solution.py:29
  83.0 1.1 convolution_add_fusion.5
  84.1 1.3 collective-permute-start
  85.4 3.7 %collective-permute-done = f32[64,512]{1,0:T(8,128)S(1)} collective-permute-done((f32[64,512]{1,0:T(8,128)S(1)}, f32[64,512]{1,0:T(8,128)S(1)}, u32[]{:S(2)}, u32[]{:S(2)}) %collective-permute-start) | collective-permute-done | bytes 131104 | tf_op jit(solution)/shard_map/ppermute | solution.py:22
  89.1 1.1 fusion.5
  90.2 1.9 collective-permute-start.1
  92.1 12.4 %collective-permute-start.14 = (f32[512,128]{1,0:T(8,128)}, f32[512,128]{1,0:T(8,128)}, u32[]{:S(2)}, u32[]{:S(2)}) collective-permute-start(f32[512,128]{1,0:T(8,128)} %get-tuple-element.36), channel_id=1, source_target_pairs={{0,64},{8,72},{16,80},{24,88},{32,96},{40,104},{48,112},{56,120},{... | collective-permute-start | bytes 786440 | tf_op jit(solution)/shard_map/ppermute | solution.py:24
  104.5 1.0 pad_maximum_fusion.2
  105.6 2.8 %gather_fusion.3 = f32[4,512,128]{2,1,0:T(8,128)} fusion(f32[4,512,128]{2,1,0:T(8,128)} %pad_maximum_fusion.2, s32[1024]{0:T(1024)S(1)} %pad_clamp_fusion), kind=kCustom, calls=%fused_computation.2.clone | custom fusion | bytes 2097168 | tf_op jit(solution)/shard_map/jit(_take)/gather | solution.py:32
  108.4 1.4 broadcast_select_fusion.1
  110.0 2.3 %collective-permute-done.14 = f32[512,128]{1,0:T(8,128)} collective-permute-done((f32[512,128]{1,0:T(8,128)}, f32[512,128]{1,0:T(8,128)}, u32[]{:S(2)}, u32[]{:S(2)}) %collective-permute-start.14) | collective-permute-done | bytes 262176 | tf_op jit(solution)/shard_map/ppermute | solution.py:24
  112.3 1.9 fusion.28
  115.0 2.0 fusion.4
  117.1 1.9 collective-permute-start.5
  119.0 2.3 %collective-permute-done.15 = f32[512,128]{1,0:T(8,128)S(1)} collective-permute-done((f32[512,128]{1,0:T(8,128)S(1)}, f32[512,128]{1,0:T(8,128)S(1)}, u32[]{:S(2)}, u32[]{:S(2)}) %collective-permute-start.15) | collective-permute-done | bytes 262176 | tf_op jit(solution)/shard_map/ppermute | solution.py:29
  122.2 1.1 fusion.3
  123.3 12.7 %collective-permute-start.9 = (f32[64,512]{1,0:T(8,128)S(1)}, f32[64,512]{1,0:T(8,128)S(1)}, u32[]{:S(2)}, u32[]{:S(2)}) collective-permute-start(f32[64,512]{1,0:T(8,128)S(1)} %fusion.3), channel_id=1, source_target_pairs={{0,64},{8,72},{16,80},{24,88},{32,96},{40,104},{48,112},{56,120},{... | collective-permute-start | bytes 393224 | tf_op jit(solution)/shard_map/ppermute | solution.py:22
  136.1 2.5 %collective-permute-done.9 = f32[64,512]{1,0:T(8,128)S(1)} collective-permute-done((f32[64,512]{1,0:T(8,128)S(1)}, f32[64,512]{1,0:T(8,128)S(1)}, u32[]{:S(2)}, u32[]{:S(2)}) %collective-permute-start.9) | collective-permute-done | bytes 131104 | tf_op jit(solution)/shard_map/ppermute | solution.py:22
  138.6 2.0 fusion.2
  140.6 6.5 %collective-permute-start.13 = (f32[64,512]{1,0:T(8,128)S(1)}, f32[64,512]{1,0:T(8,128)}, u32[]{:S(2)}, u32[]{:S(2)}) collective-permute-start(f32[64,512]{1,0:T(8,128)S(1)} %fusion.2), channel_id=1, source_target_pairs={{0,128},{8,136},{16,144},{24,152},{32,160},{40,168},{48,176},{56,1... | collective-permute-start | bytes 393224 | tf_op jit(solution)/shard_map/ppermute | solution.py:22
  147.1 2.1 pad_maximum_fusion.3
  149.2 1.8 gather_fusion.4
  151.3 2.0 fusion.1
  153.4 1.3 collective-permute-done.17
  154.7 1.1 broadcast_in_dim.30
  155.8 5.4 %all-to-all-start = ((f32[4,1,128,512]{3,2,1,0:T(8,128)}), f32[4,1,128,512]{3,2,1,0:T(8,128)S(1)}, u32[]{:S(2)}, u32[]{:S(2)}) async-start(f32[4,1,128,512]{3,2,1,0:T(8,128)} %broadcast_in_dim.30), calls=%async_computation | async-start | bytes 2097152 | tf_op jit(solution)/shard_map/all_to_all | solution.py:97
  161.2 1.0 copy.14
  162.2 12.3 %all-to-all-done = f32[4,1,128,512]{3,2,1,0:T(8,128)S(1)} async-done(((f32[4,1,128,512]{3,2,1,0:T(8,128)}), f32[4,1,128,512]{3,2,1,0:T(8,128)S(1)}, u32[]{:S(2)}, u32[]{:S(2)}) %all-to-all-start) | async-done | bytes 1048608 | tf_op jit(solution)/shard_map/all_to_all | solution.py:97
  174.5 5.5 %all-to-all-start.1 = ((f32[64,8,256]{2,0,1:T(8,128)}), f32[64,8,256]{2,0,1:T(8,128)S(1)}, u32[]{:S(2)}, u32[]{:S(2)}) async-start(f32[64,8,256]{2,0,1:T(8,128)} %copy.14), calls=%async_computation.1 | async-start | bytes 1048576 | tf_op jit(solution)/shard_map/all_to_all | solution.py:85
  180.2 8.1 %all-to-all-done.1 = f32[64,8,256]{2,0,1:T(8,128)S(1)} async-done(((f32[64,8,256]{2,0,1:T(8,128)}), f32[64,8,256]{2,0,1:T(8,128)S(1)}, u32[]{:S(2)}, u32[]{:S(2)}) %all-to-all-start.1) | async-done | bytes 524320 | tf_op jit(solution)/shard_map/all_to_all | solution.py:85
  188.3 1.9 fusion
  190.2 13.4 %all_to_all.30 = f32[4,128,320]{1,2,0:T(8,128)S(1)} all-to-all(f32[4,128,320]{1,2,0:T(8,128)S(1)} %bitcast.103), channel_id=1, replica_groups={{0,64,128,192},{8,72,136,200},{16,80,144,208},{24,88,152,216},{32,96,16..., dimensions={0} | all-to-all | bytes 1310720 | tf_op jit(solution)/shard_map/all_to_all | solution.py:118
  203.8 12.2 %all_to_all.31 = f32[8,16,320]{2,1,0:T(8,128)S(1)} all-to-all(f32[8,16,320]{2,1,0:T(8,128)S(1)} %bitcast.122), channel_id=1, replica_groups={{0,8,16,24,32,40,48,56},{64,72,80,88,96,104,112,120},{128,136,144,152,1..., dimensions={0} | all-to-all | bytes 327680 | tf_op jit(solution)/shard_map/all_to_all | solution.py:118
  (79 shorter events, 9.9 us)
Async XLA Ops:
  0.6 74.7 %copy-start = (bf16[4,512,256]{2,1,0:T(8,128)(2,1)S(1)}, bf16[4,512,256]{2,1,0:T(8,128)(2,1)}, u32[]{:S(2)}) copy-start(bf16[4,512,256]{2,1,0:T(8,128)(2,1)} %param.10) | copy-start | bytes 3145732
  2.1 11.1 %copy-start.4 = (f32[512,512]{1,0:T(8,128)}, f32[512,512]{1,0:T(8,128)S(1)}, u32[]{:S(2)}) copy-start(f32[512,512]{1,0:T(8,128)S(1)} %bitcast_select_fusion) | copy-start | bytes 3145732
  2.1 9.4 %collective-permute-start.2 = (f32[512,128]{1,0:T(8,128)S(1)}, f32[512,128]{1,0:T(8,128)S(1)}, u32[]{:S(2)}, u32[]{:S(2)}) collective-permute-start(f32[512,128]{1,0:T(8,128)S(1)} %constant_dynamic-slice_fusion.1), channel_id=1, source_target_pairs={{0,8},{8,16},{16,24},{24,32},{32,40},{40,48},{48,56},{56,64},{64,7... | collective-permute-start | bytes 786440 | tf_op jit(solution)/shard_map/ppermute | solution.py:24
  11.5 2.4 %copy-start.1 = (s32[4]{0:T(128)S(1)}, s32[4]{0:T(128)}, u32[]{:S(2)}) copy-start(s32[4]{0:T(128)} %constant.72.clone) | copy-start | bytes 52
  13.2 7.2 %collective-permute-start.3 = (f32[512,128]{1,0:T(8,128)S(1)}, f32[512,128]{1,0:T(8,128)S(1)}, u32[]{:S(2)}, u32[]{:S(2)}) collective-permute-start(f32[512,128]{1,0:T(8,128)S(1)} %get-tuple-element.33), channel_id=1, source_target_pairs={{0,2},{1,3},{2,0},{3,1},{4,6},{5,7},{6,4},{7,5},{8,10},{9,11},{10,... | collective-permute-start | bytes 786440 | tf_op jit(solution)/shard_map/ppermute | solution.py:29
  20.4 6.6 %collective-permute-start.4 = (f32[2,512,128]{2,1,0:T(8,128)S(1)}, f32[2,512,128]{2,1,0:T(8,128)S(1)}, u32[]{:S(2)}, u32[]{:S(2)}) collective-permute-start(f32[2,512,128]{2,1,0:T(8,128)S(1)} %pad_maximum_fusion.4), channel_id=1, source_target_pairs={{0,1},{1,0},{2,3},{3,2},{4,5},{5,4},{6,7},{7,6},{8,9},{9,8},{10,11... | collective-permute-start | bytes 1572872 | tf_op jit(solution)/shard_map/ppermute | solution.py:30
  20.6 17.9 %collective-permute-start.6 = (f32[512,128]{1,0:T(8,128)}, f32[512,128]{1,0:T(8,128)}, u32[]{:S(2)}, u32[]{:S(2)}) collective-permute-start(f32[512,128]{1,0:T(8,128)} %get-tuple-element.32), channel_id=1, source_target_pairs={{0,16},{8,24},{16,32},{24,40},{32,48},{40,56},{48,64},{56,72},{64,... | collective-permute-start | bytes 786440 | tf_op jit(solution)/shard_map/ppermute | solution.py:24
  27.9 1.2 copy-start.6
  40.5 7.9 %collective-permute-start.7 = (f32[512,128]{1,0:T(8,128)S(1)}, f32[512,128]{1,0:T(8,128)S(1)}, u32[]{:S(2)}, u32[]{:S(2)}) collective-permute-start(f32[512,128]{1,0:T(8,128)S(1)} %get-tuple-element.35), channel_id=1, source_target_pairs={{0,2},{1,3},{2,0},{3,1},{4,6},{5,7},{6,4},{7,5},{8,10},{9,11},{10,... | collective-permute-start | bytes 786440 | tf_op jit(solution)/shard_map/ppermute | solution.py:29
  48.5 12.5 %collective-permute-start.8 = (f32[2,512,128]{2,1,0:T(8,128)S(1)}, f32[2,512,128]{2,1,0:T(8,128)}, u32[]{:S(2)}, u32[]{:S(2)}) collective-permute-start(f32[2,512,128]{2,1,0:T(8,128)S(1)} %pad_maximum_fusion.5), channel_id=1, source_target_pairs={{0,1},{1,0},{2,3},{3,2},{4,5},{5,4},{6,7},{7,6},{8,9},{9,8},{10,11... | collective-permute-start | bytes 1572872 | tf_op jit(solution)/shard_map/ppermute | solution.py:30
  49.2 22.7 %collective-permute-start.10 = (f32[512,128]{1,0:T(8,128)S(1)}, f32[512,128]{1,0:T(8,128)}, u32[]{:S(2)}, u32[]{:S(2)}) collective-permute-start(f32[512,128]{1,0:T(8,128)S(1)} %get-tuple-element.34), channel_id=1, source_target_pairs={{0,32},{8,40},{16,48},{24,56},{32,64},{40,72},{48,80},{56,88},{64,... | collective-permute-start | bytes 786440 | tf_op jit(solution)/shard_map/ppermute | solution.py:24
  74.5 8.3 %collective-permute-start.11 = (f32[512,128]{1,0:T(8,128)S(1)}, f32[512,128]{1,0:T(8,128)S(1)}, u32[]{:S(2)}, u32[]{:S(2)}) collective-permute-start(f32[512,128]{1,0:T(8,128)S(1)} %get-tuple-element.37), channel_id=1, source_target_pairs={{0,2},{1,3},{2,0},{3,1},{4,6},{5,7},{6,4},{7,5},{8,10},{9,11},{10,... | collective-permute-start | bytes 786440 | tf_op jit(solution)/shard_map/ppermute | solution.py:29
  75.3 0.9 copy-start.14
  76.2 6.7 %copy-start.7 = (f32[1,512,512]{2,1,0:T(8,128)S(1)}, f32[1,512,512]{2,1,0:T(8,128)}, u32[]{:S(2)}) copy-start(f32[1,512,512]{2,1,0:T(8,128)} %param.9) | copy-start | bytes 3145732
  76.2 6.7 %copy-start.13 = (f32[64,512]{1,0:T(8,128)S(1)}, f32[64,512]{1,0:T(8,128)}, u32[]{:S(2)}) copy-start(f32[64,512]{1,0:T(8,128)} %param.13) | copy-start | bytes 393220
  82.8 6.2 %copy-start.5 = (f32[512,512]{1,0:T(8,128)S(1)}, f32[512,512]{1,0:T(8,128)}, u32[]{:S(2)}) copy-start(f32[512,512]{1,0:T(8,128)} %copy-done.4) | copy-start | bytes 3145732
  82.8 21.7 %collective-permute-start.12 = (f32[2,512,128]{2,1,0:T(8,128)S(1)}, f32[2,512,128]{2,1,0:T(8,128)S(1)}, u32[]{:S(2)}, u32[]{:S(2)}) collective-permute-start(f32[2,512,128]{2,1,0:T(8,128)S(1)} %pad_maximum_fusion.6), channel_id=1, source_target_pairs={{0,1},{1,0},{2,3},{3,2},{4,5},{5,4},{6,7},{7,6},{8,9},{9,8},{10,11... | collective-permute-start | bytes 1572872 | tf_op jit(solution)/shard_map/ppermute | solution.py:30
  84.1 5.0 %collective-permute-start = (f32[64,512]{1,0:T(8,128)S(1)}, f32[64,512]{1,0:T(8,128)S(1)}, u32[]{:S(2)}, u32[]{:S(2)}) collective-permute-start(f32[64,512]{1,0:T(8,128)S(1)} %convolution_add_fusion.5), channel_id=1, source_target_pairs={{0,8},{8,16},{16,24},{24,32},{32,40},{40,48},{48,56},{56,64},{64,7... | collective-permute-start | bytes 393224 | tf_op jit(solution)/shard_map/ppermute | solution.py:22
  90.2 24.9 %collective-permute-start.1 = (f32[64,512]{1,0:T(8,128)S(1)}, f32[64,512]{1,0:T(8,128)}, u32[]{:S(2)}, u32[]{:S(2)}) collective-permute-start(f32[64,512]{1,0:T(8,128)S(1)} %fusion.5), channel_id=1, source_target_pairs={{0,16},{8,24},{16,32},{24,40},{32,48},{40,56},{48,64},{56,72},{64,... | collective-permute-start | bytes 393224 | tf_op jit(solution)/shard_map/ppermute | solution.py:22
  92.1 20.2 %collective-permute-start.14 = (f32[512,128]{1,0:T(8,128)}, f32[512,128]{1,0:T(8,128)}, u32[]{:S(2)}, u32[]{:S(2)}) collective-permute-start(f32[512,128]{1,0:T(8,128)} %get-tuple-element.36), channel_id=1, source_target_pairs={{0,64},{8,72},{16,80},{24,88},{32,96},{40,104},{48,112},{56,120},{... | collective-permute-start | bytes 786440 | tf_op jit(solution)/shard_map/ppermute | solution.py:24
  110.0 7.1 %copy-start.2 = (f32[512,512]{1,0:T(8,128)}, f32[512,512]{1,0:T(8,128)S(1)}, u32[]{:S(2)}) copy-start(f32[512,512]{1,0:T(8,128)S(1)} %maximum_select_fusion.2) | copy-start | bytes 3145732
  114.2 7.1 %collective-permute-start.15 = (f32[512,128]{1,0:T(8,128)S(1)}, f32[512,128]{1,0:T(8,128)S(1)}, u32[]{:S(2)}, u32[]{:S(2)}) collective-permute-start(f32[512,128]{1,0:T(8,128)S(1)} %fusion.28), channel_id=1, source_target_pairs={{0,2},{1,3},{2,0},{3,1},{4,6},{5,7},{6,4},{7,5},{8,10},{9,11},{10,... | collective-permute-start | bytes 786440 | tf_op jit(solution)/shard_map/ppermute | solution.py:29
  117.1 5.1 %collective-permute-start.5 = (f32[64,512]{1,0:T(8,128)S(1)}, f32[64,512]{1,0:T(8,128)S(1)}, u32[]{:S(2)}, u32[]{:S(2)}) collective-permute-start(f32[64,512]{1,0:T(8,128)S(1)} %fusion.4), channel_id=1, source_target_pairs={{0,32},{8,40},{16,48},{24,56},{32,64},{40,72},{48,80},{56,88},{64,... | collective-permute-start | bytes 393224 | tf_op jit(solution)/shard_map/ppermute | solution.py:22
  121.3 0.9 copy-start.8
  121.3 17.2 %copy-start.3 = (f32[512,512]{1,0:T(8,128)S(1)}, f32[512,512]{1,0:T(8,128)}, u32[]{:S(2)}) copy-start(f32[512,512]{1,0:T(8,128)} %copy-done.2) | copy-start | bytes 3145732
  122.2 24.9 %collective-permute-start.16 = (f32[2,512,128]{2,1,0:T(8,128)}, f32[2,512,128]{2,1,0:T(8,128)}, u32[]{:S(2)}, u32[]{:S(2)}) collective-permute-start(f32[2,512,128]{2,1,0:T(8,128)} %pad_maximum_fusion.7), channel_id=1, source_target_pairs={{0,1},{1,0},{2,3},{3,2},{4,5},{5,4},{6,7},{7,6},{8,9},{9,8},{10,11... | collective-permute-start | bytes 1572872 | tf_op jit(solution)/shard_map/ppermute | solution.py:30
  123.3 12.8 %copy-start.11 = (f32[64,512]{1,0:T(8,128)}, f32[64,512]{1,0:T(8,128)S(1)}, u32[]{:S(2)}) copy-start(f32[64,512]{1,0:T(8,128)S(1)} %fusion.3) | copy-start | bytes 393220
  123.3 15.2 %collective-permute-start.9 = (f32[64,512]{1,0:T(8,128)S(1)}, f32[64,512]{1,0:T(8,128)S(1)}, u32[]{:S(2)}, u32[]{:S(2)}) collective-permute-start(f32[64,512]{1,0:T(8,128)S(1)} %fusion.3), channel_id=1, source_target_pairs={{0,64},{8,72},{16,80},{24,88},{32,96},{40,104},{48,112},{56,120},{... | collective-permute-start | bytes 393224 | tf_op jit(solution)/shard_map/ppermute | solution.py:22
  136.1 11.0 %copy-start.9 = (f32[512,128]{1,0:T(8,128)S(1)}, f32[512,128]{1,0:T(8,128)}, u32[]{:S(2)}) copy-start(f32[512,128]{1,0:T(8,128)} %copy-done.8) | copy-start | bytes 786436
  140.6 10.7 %collective-permute-start.13 = (f32[64,512]{1,0:T(8,128)S(1)}, f32[64,512]{1,0:T(8,128)}, u32[]{:S(2)}, u32[]{:S(2)}) collective-permute-start(f32[64,512]{1,0:T(8,128)S(1)} %fusion.2), channel_id=1, source_target_pairs={{0,128},{8,136},{16,144},{24,152},{32,160},{40,168},{48,176},{56,1... | collective-permute-start | bytes 393224 | tf_op jit(solution)/shard_map/ppermute | solution.py:22
  153.3 1.5 copy-start.10
  153.3 1.4 collective-permute-start.17
  155.8 5.4 %copy-start.12 = (bf16[1,64,2048]{2,1,0:T(8,128)(2,1)S(1)}, bf16[1,64,2048]{2,1,0:T(8,128)(2,1)}, u32[]{:S(2)}) copy-start(bf16[1,64,2048]{2,1,0:T(8,128)(2,1)} %param.14) | copy-start | bytes 786436
  155.8 18.7 %all-to-all-start = ((f32[4,1,128,512]{3,2,1,0:T(8,128)}), f32[4,1,128,512]{3,2,1,0:T(8,128)S(1)}, u32[]{:S(2)}, u32[]{:S(2)}) async-start(f32[4,1,128,512]{3,2,1,0:T(8,128)} %broadcast_in_dim.30), calls=%async_computation | async-start | bytes 2097152 | tf_op jit(solution)/shard_map/all_to_all | solution.py:97
  174.5 13.7 %all-to-all-start.1 = ((f32[64,8,256]{2,0,1:T(8,128)}), f32[64,8,256]{2,0,1:T(8,128)S(1)}, u32[]{:S(2)}, u32[]{:S(2)}) async-start(f32[64,8,256]{2,0,1:T(8,128)} %copy.14), calls=%async_computation.1 | async-start | bytes 1048576 | tf_op jit(solution)/shard_map/all_to_all | solution.py:85

commit v11 on v10

--- a/solution.py
+++ b/solution.py
@@ -81,25 +81,18 @@
     sensors = observed.shape[2]
     cross_cols = sensors // scen_shards
     gram_cols = modes // scen_shards
-    readings = observed.astype(jnp.float32).reshape(step_count * local_scen, scen_shards, cross_cols)
-    readings = lax.all_to_all(readings, "scen", 1, 0, tiled=True)
-    readings = readings.reshape(scen_shards, step_count, local_scen, cross_cols)
-    readings = readings.transpose(1, 0, 2, 3).reshape(step_count, scen_shards * local_scen, cross_cols)
-    core = lax.axis_index("scen") % 2
-    partner = lax.ppermute(states, "scen", [(j, j ^ 1) for j in range(scen_shards)])
-    pair = jnp.where(
-        core == 0,
-        jnp.concatenate([states, partner], axis=1),
-        jnp.concatenate([partner, states], axis=1),
+    readings = observed.astype(jnp.float32).reshape(step_count, local_scen, scen_shards, cross_cols)
+    readings = readings.transpose(2, 0, 1, 3)
+    payload = jnp.concatenate(
+        [jnp.broadcast_to(states[None], (scen_shards,) + states.shape), readings], axis=3
     )
-    chips = scen_shards // 2
-    groups = [[c + 2 * k for k in range(chips)] for c in range(2)]
-    every = lax.all_to_all(
-        jnp.broadcast_to(pair[None], (chips,) + pair.shape),
-        "scen", 0, 0, tiled=True, axis_index_groups=groups,
+    received = lax.all_to_all(payload, "scen", 0, 0, tiled=True)
+    received = received.reshape(scen_shards, step_count, local_scen, modes + cross_cols)
+    received = received.transpose(1, 0, 2, 3).reshape(
+        step_count, scen_shards * local_scen, modes + cross_cols
     )
-    every = every.reshape(chips, step_count, 2 * local_scen, modes).transpose(1, 0, 2, 3)
-    every = every.reshape(step_count, scen_shards * local_scen, modes)
+    every = received[:, :, :modes]
+    readings = received[:, :, modes:]
     column = lax.axis_index("scen") * gram_cols
     right = jnp.concatenate(
         [lax.dynamic_slice_in_dim(every, column, gram_cols, axis=2), readings], axis=2

time: 219 us -> 212 us (0.968)
  waiting for transfers between devices: 73 us -> 67.4 us
  starting transfers between devices: 73.3 us -> 68.1 us
  other arithmetic: 9.95 us -> 12.2 us
    all_to_all x2 -> x1, starting transfers between devices: 10.8 us -> 5.23 us  [on_device_body(): received = lax.all_to_all(payload, 'scen', 0, 0, tiled=True)]
    all_to_all x2 -> x1, waiting for transfers between devices: 20.4 us -> 19.5 us  [on_device_body(): received = lax.all_to_all(payload, 'scen', 0, 0, tiled=True)]
  transfers between devices with their start and end apart: 20 -> 18, of which waited for: 13 -> 11; matrix products, arithmetic and copies ran while one was open for 13% -> 15% of each run, Pallas kernels for 0% -> 0%
where the time goes in v11:
time: 212 us; the launch traced here: 210 us
  starting transfers between devices  68.1 us (32%)
  waiting for transfers between devices  67.4 us (32%)
  blocking collectives  25.7 us (12%)
  matrix products  21.4 us (10%)
  local copies, waits for them, and re-layouts  13.1 us (6%)
  other arithmetic  12.2 us (6%)
    ppermute x4, starting transfers between devices, shift_scan(): got_part = lax.ppermute(mine, axis, pairs)  34.5 us
    all_to_all x2, blocking collectives, on_device_body(): lax.all_to_all(pieces, 'tm', 0, 0, tiled=True, axis_index_groups=groups)  25.7 us
    ppermute x5, starting transfers between devices, shift_scan(): got_vector = lax.ppermute(vector, axis, pairs)  24.8 us
    ppermute x4, waiting for transfers between devices, shift_scan(): got_part = lax.ppermute(mine, axis, pairs)  22.7 us
    ppermute x4, waiting for transfers between devices, shift_scan(): far = lax.ppermute(own, pair_axis, across)  20 us
    all_to_all x1, waiting for transfers between devices, on_device_body(): received = lax.all_to_all(payload, 'scen', 0, 0, tiled=True)  19.5 us
    dot_general x5, matrix products, shift_scan(): jnp.einsum('sq,rq->sr', got_vector, matrix, precision=highest) + vector  9.06 us
    dot_general x4, matrix products, shift_scan(): own = jnp.dot(matrix, got_part, precision=highest)  8.28 us
  transfers between devices with their start and end apart: 18, of which 11 were waited for; matrix products, arithmetic and copies ran while one was open for 15% of the time, Pallas kernels for 0%

profile of v11, /device:TPU:24, one launch (start us, length us, event | category | flops | bytes accessed | tf_op | source)
XLA Modules:
  0.0 209.7 jit_solution(3192998741692416555)
XLA Ops:
  0.7 1.4 bitcast_select_fusion
  2.1 3.8 %collective-permute-start.2 = (f32[512,128]{1,0:T(8,128)S(1)}, f32[512,128]{1,0:T(8,128)S(1)}, u32[]{:S(2)}, u32[]{:S(2)}) collective-permute-start(f32[512,128]{1,0:T(8,128)S(1)} %constant_dynamic-slice_fusion.1), channel_id=1, source_target_pairs={{0,8},{8,16},{16,24},{24,32},{32,40},{40,48},{48,56},{56,64},{64,7... | collective-permute-start | bytes 786440 | tf_op jit(solution)/shard_map/ppermute | solution.py:24
  6.0 5.5 %collective-permute-done.2 = f32[512,128]{1,0:T(8,128)S(1)} collective-permute-done((f32[512,128]{1,0:T(8,128)S(1)}, f32[512,128]{1,0:T(8,128)S(1)}, u32[]{:S(2)}, u32[]{:S(2)}) %collective-permute-start.2) | collective-permute-done | bytes 262176 | tf_op jit(solution)/shard_map/ppermute | solution.py:24
  11.5 1.7 broadcast_select_fusion.6
  14.6 5.8 %collective-permute-done.3 = f32[512,128]{1,0:T(8,128)S(1)} collective-permute-done((f32[512,128]{1,0:T(8,128)S(1)}, f32[512,128]{1,0:T(8,128)S(1)}, u32[]{:S(2)}, u32[]{:S(2)}) %collective-permute-start.3) | collective-permute-done | bytes 262176 | tf_op jit(solution)/shard_map/ppermute | solution.py:29
  20.6 6.5 %collective-permute-start.6 = (f32[512,128]{1,0:T(8,128)}, f32[512,128]{1,0:T(8,128)}, u32[]{:S(2)}, u32[]{:S(2)}) collective-permute-start(f32[512,128]{1,0:T(8,128)} %get-tuple-element.32), channel_id=1, source_target_pairs={{0,16},{8,24},{16,32},{24,40},{32,48},{40,56},{48,64},{56,72},{64,... | collective-permute-start | bytes 786440 | tf_op jit(solution)/shard_map/ppermute | solution.py:24
  27.1 1.0 pad_maximum_fusion.1
  28.9 1.1 copy-done.6
  30.2 8.3 %collective-permute-done.6 = f32[512,128]{1,0:T(8,128)} collective-permute-done((f32[512,128]{1,0:T(8,128)}, f32[512,128]{1,0:T(8,128)}, u32[]{:S(2)}, u32[]{:S(2)}) %collective-permute-start.6) | collective-permute-done | bytes 262176 | tf_op jit(solution)/shard_map/ppermute | solution.py:24
  38.5 2.0 broadcast_select_fusion.5
  41.4 7.1 %collective-permute-done.7 = f32[512,128]{1,0:T(8,128)S(1)} collective-permute-done((f32[512,128]{1,0:T(8,128)S(1)}, f32[512,128]{1,0:T(8,128)S(1)}, u32[]{:S(2)}, u32[]{:S(2)}) %collective-permute-start.7) | collective-permute-done | bytes 262176 | tf_op jit(solution)/shard_map/ppermute | solution.py:29
  49.3 11.8 %collective-permute-start.10 = (f32[512,128]{1,0:T(8,128)S(1)}, f32[512,128]{1,0:T(8,128)}, u32[]{:S(2)}, u32[]{:S(2)}) collective-permute-start(f32[512,128]{1,0:T(8,128)S(1)} %get-tuple-element.34), channel_id=1, source_target_pairs={{0,32},{8,40},{16,48},{24,56},{32,64},{40,72},{48,80},{56,88},{64,... | collective-permute-start | bytes 786440 | tf_op jit(solution)/shard_map/ppermute | solution.py:24
  61.1 2.1 pad_maximum_fusion.2
  63.1 1.8 gather_fusion.2
  65.3 6.6 %collective-permute-done.10 = f32[512,128]{1,0:T(8,128)} collective-permute-done((f32[512,128]{1,0:T(8,128)S(1)}, f32[512,128]{1,0:T(8,128)}, u32[]{:S(2)}, u32[]{:S(2)}) %collective-permute-start.10) | collective-permute-done | bytes 262176 | tf_op jit(solution)/shard_map/ppermute | solution.py:24
  71.9 2.6 %broadcast_select_fusion.4 = (f32[512,128]{1,0:T(8,128)}, f32[512,128]{1,0:T(8,128)S(1)}) fusion(f32[512,128]{1,0:T(8,128)S(1)} %get-tuple-element.34, pred[]{:T(512)S(6)} %ge.21, f32[512,512]{1,0:T(8,128)S(1)} %maximum_select_fusion.1, f32[512,128]{1,0:T(8,128)} %collective-permute-done.10), kind=kOutput, calls=%fused_computation.71 | convolution fusion | flops 402718720 | bytes 2097153 | tf_op jit(solution)/shard_map/dot_general | solution.py:28
  75.4 0.9 fusion.14
  76.5 6.4 %collective-permute-done.11 = f32[512,128]{1,0:T(8,128)S(1)} collective-permute-done((f32[512,128]{1,0:T(8,128)S(1)}, f32[512,128]{1,0:T(8,128)S(1)}, u32[]{:S(2)}, u32[]{:S(2)}) %collective-permute-start.11) | collective-permute-done | bytes 262176 | tf_op jit(solution)/shard_map/ppermute | solution.py:29
  83.0 1.1 convolution_add_fusion.5
  84.1 1.3 collective-permute-start
  85.4 3.7 %collective-permute-done = f32[64,512]{1,0:T(8,128)S(1)} collective-permute-done((f32[64,512]{1,0:T(8,128)S(1)}, f32[64,512]{1,0:T(8,128)S(1)}, u32[]{:S(2)}, u32[]{:S(2)}) %collective-permute-start) | collective-permute-done | bytes 131104 | tf_op jit(solution)/shard_map/ppermute | solution.py:22
  89.1 1.1 fusion.5
  90.2 1.9 collective-permute-start.1
  92.2 12.4 %collective-permute-start.14 = (f32[512,128]{1,0:T(8,128)}, f32[512,128]{1,0:T(8,128)}, u32[]{:S(2)}, u32[]{:S(2)}) collective-permute-start(f32[512,128]{1,0:T(8,128)} %get-tuple-element.36), channel_id=1, source_target_pairs={{0,64},{8,72},{16,80},{24,88},{32,96},{40,104},{48,112},{56,120},{... | collective-permute-start | bytes 786440 | tf_op jit(solution)/shard_map/ppermute | solution.py:24
  104.6 1.0 pad_maximum_fusion.3
  105.6 2.8 %gather_fusion.3 = f32[4,512,128]{2,1,0:T(8,128)} fusion(f32[4,512,128]{2,1,0:T(8,128)} %pad_maximum_fusion.3, s32[1024]{0:T(1024)S(1)} %pad_clamp_fusion), kind=kCustom, calls=%fused_computation.2.clone | custom fusion | bytes 2097168 | tf_op jit(solution)/shard_map/jit(_take)/gather | solution.py:32
  108.4 1.4 broadcast_select_fusion.1
  110.0 2.3 %collective-permute-done.14 = f32[512,128]{1,0:T(8,128)} collective-permute-done((f32[512,128]{1,0:T(8,128)}, f32[512,128]{1,0:T(8,128)}, u32[]{:S(2)}, u32[]{:S(2)}) %collective-permute-start.14) | collective-permute-done | bytes 262176 | tf_op jit(solution)/shard_map/ppermute | solution.py:24
  112.3 1.9 fusion.30
  115.1 2.7 %fusion.4 = f32[64,512]{1,0:T(8,128)} fusion(f32[64,512]{1,0:T(8,128)S(1)} %fusion.5, f32[64,512]{1,0:T(8,128)} %collective-permute-done.1, f32[512,512]{1,0:T(8,128)S(1)} %maximum_select_fusion, pred[]{:T(512)S(6)} %ge.22), kind=kOutput, calls=%fused_computation.15 | convolution fusion | flops 201392128 | bytes 1441793 | tf_op jit(solution)/shard_map/sq,rq->sr/dot_general | solution.py:25
  117.8 1.9 collective-permute-start.5
  119.7 1.0 copy.23
  121.5 1.0 pad_maximum_fusion.8
  122.6 2.1 fusion.3
  124.7 13.2 %collective-permute-start.9 = (f32[64,512]{1,0:T(8,128)S(1)}, f32[64,512]{1,0:T(8,128)S(1)}, u32[]{:S(2)}, u32[]{:S(2)}) collective-permute-start(f32[64,512]{1,0:T(8,128)S(1)} %fusion.3), channel_id=1, source_target_pairs={{0,64},{8,72},{16,80},{24,88},{32,96},{40,104},{48,112},{56,120},{... | collective-permute-start | bytes 393224 | tf_op jit(solution)/shard_map/ppermute | solution.py:22
  137.9 1.0 copy.15
  138.9 1.5 collective-permute-done.9
  140.4 1.1 fusion.2
  141.5 6.5 %collective-permute-start.13 = (f32[64,512]{1,0:T(8,128)S(1)}, f32[64,512]{1,0:T(8,128)}, u32[]{:S(2)}, u32[]{:S(2)}) collective-permute-start(f32[64,512]{1,0:T(8,128)S(1)} %fusion.2), channel_id=1, source_target_pairs={{0,128},{8,136},{16,144},{24,152},{32,160},{40,168},{48,176},{56,1... | collective-permute-start | bytes 393224 | tf_op jit(solution)/shard_map/ppermute | solution.py:22
  148.0 2.0 pad_maximum_fusion.4
  150.0 1.8 gather_fusion.4
  152.1 2.0 fusion.1
  154.3 1.3 pad_maximum_fusion
  155.6 5.2 %all-to-all-start = ((f32[8,1,64,768]{3,2,1,0:T(8,128)}), f32[8,1,64,768]{3,2,1,0:T(8,128)S(1)}, u32[]{:S(2)}, u32[]{:S(2)}) async-start(f32[8,1,64,768]{3,2,1,0:T(8,128)} %pad_maximum_fusion), calls=%async_computation | async-start | bytes 3145728 | tf_op jit(solution)/shard_map/all_to_all | solution.py:89
  160.8 19.5 %all-to-all-done = f32[8,1,64,768]{3,2,1,0:T(8,128)S(1)} async-done(((f32[8,1,64,768]{3,2,1,0:T(8,128)}), f32[8,1,64,768]{3,2,1,0:T(8,128)S(1)}, u32[]{:S(2)}, u32[]{:S(2)}) %all-to-all-start) | async-done | bytes 1572896 | tf_op jit(solution)/shard_map/all_to_all | solution.py:89
  180.6 1.9 fusion
  182.5 13.5 %all_to_all.15 = f32[4,128,320]{1,2,0:T(8,128)S(1)} all-to-all(f32[4,128,320]{1,2,0:T(8,128)S(1)} %bitcast.104), channel_id=1, replica_groups={{0,64,128,192},{8,72,136,200},{16,80,144,208},{24,88,152,216},{32,96,16..., dimensions={0} | all-to-all | bytes 1310720 | tf_op jit(solution)/shard_map/all_to_all | solution.py:111
  196.2 12.2 %all_to_all.16 = f32[8,16,320]{2,1,0:T(8,128)S(1)} all-to-all(f32[8,16,320]{2,1,0:T(8,128)S(1)} %bitcast.120), channel_id=1, replica_groups={{0,8,16,24,32,40,48,56},{64,72,80,88,96,104,112,120},{128,136,144,152,1..., dimensions={0} | all-to-all | bytes 327680 | tf_op jit(solution)/shard_map/all_to_all | solution.py:111
  (74 shorter events, 9.1 us)
Async XLA Ops:
  0.6 74.7 %copy-start = (bf16[4,512,256]{2,1,0:T(8,128)(2,1)S(1)}, bf16[4,512,256]{2,1,0:T(8,128)(2,1)}, u32[]{:S(2)}) copy-start(bf16[4,512,256]{2,1,0:T(8,128)(2,1)} %param.10) | copy-start | bytes 3145732
  2.1 12.6 %copy-start.4 = (f32[512,512]{1,0:T(8,128)}, f32[512,512]{1,0:T(8,128)S(1)}, u32[]{:S(2)}) copy-start(f32[512,512]{1,0:T(8,128)S(1)} %bitcast_select_fusion) | copy-start | bytes 3145732
  2.1 11.9 %copy-start.1 = (s32[4]{0:T(128)S(1)}, s32[4]{0:T(128)}, u32[]{:S(2)}) copy-start(s32[4]{0:T(128)} %constant.65.clone) | copy-start | bytes 52
  2.1 9.4 %collective-permute-start.2 = (f32[512,128]{1,0:T(8,128)S(1)}, f32[512,128]{1,0:T(8,128)S(1)}, u32[]{:S(2)}, u32[]{:S(2)}) collective-permute-start(f32[512,128]{1,0:T(8,128)S(1)} %constant_dynamic-slice_fusion.1), channel_id=1, source_target_pairs={{0,8},{8,16},{16,24},{24,32},{32,40},{40,48},{48,56},{56,64},{64,7... | collective-permute-start | bytes 786440 | tf_op jit(solution)/shard_map/ppermute | solution.py:24
  13.2 7.2 %collective-permute-start.3 = (f32[512,128]{1,0:T(8,128)S(1)}, f32[512,128]{1,0:T(8,128)S(1)}, u32[]{:S(2)}, u32[]{:S(2)}) collective-permute-start(f32[512,128]{1,0:T(8,128)S(1)} %get-tuple-element.33), channel_id=1, source_target_pairs={{0,2},{1,3},{2,0},{3,1},{4,6},{5,7},{6,4},{7,5},{8,10},{9,11},{10,... | collective-permute-start | bytes 786440 | tf_op jit(solution)/shard_map/ppermute | solution.py:29
  20.4 6.7 %copy-start.9 = (f32[512,128]{1,0:T(8,128)}, f32[512,128]{1,0:T(8,128)S(1)}, u32[]{:S(2)}) copy-start(f32[512,128]{1,0:T(8,128)S(1)} %collective-permute-done.3) | copy-start | bytes 786436
  20.5 6.6 %collective-permute-start.4 = (f32[2,512,128]{2,1,0:T(8,128)S(1)}, f32[2,512,128]{2,1,0:T(8,128)S(1)}, u32[]{:S(2)}, u32[]{:S(2)}) collective-permute-start(f32[2,512,128]{2,1,0:T(8,128)S(1)} %pad_maximum_fusion.5), channel_id=1, source_target_pairs={{0,1},{1,0},{2,3},{3,2},{4,5},{5,4},{6,7},{7,6},{8,9},{9,8},{10,11... | collective-permute-start | bytes 1572872 | tf_op jit(solution)/shard_map/ppermute | solution.py:30
  20.6 17.9 %collective-permute-start.6 = (f32[512,128]{1,0:T(8,128)}, f32[512,128]{1,0:T(8,128)}, u32[]{:S(2)}, u32[]{:S(2)}) collective-permute-start(f32[512,128]{1,0:T(8,128)} %get-tuple-element.32), channel_id=1, source_target_pairs={{0,16},{8,24},{16,32},{24,40},{32,48},{40,56},{48,64},{56,72},{64,... | collective-permute-start | bytes 786440 | tf_op jit(solution)/shard_map/ppermute | solution.py:24
  28.9 1.2 copy-start.6
  40.6 7.9 %collective-permute-start.7 = (f32[512,128]{1,0:T(8,128)S(1)}, f32[512,128]{1,0:T(8,128)S(1)}, u32[]{:S(2)}, u32[]{:S(2)}) collective-permute-start(f32[512,128]{1,0:T(8,128)S(1)} %get-tuple-element.35), channel_id=1, source_target_pairs={{0,2},{1,3},{2,0},{3,1},{4,6},{5,7},{6,4},{7,5},{8,10},{9,11},{10,... | collective-permute-start | bytes 786440 | tf_op jit(solution)/shard_map/ppermute | solution.py:29
  48.5 12.5 %collective-permute-start.8 = (f32[2,512,128]{2,1,0:T(8,128)S(1)}, f32[2,512,128]{2,1,0:T(8,128)}, u32[]{:S(2)}, u32[]{:S(2)}) collective-permute-start(f32[2,512,128]{2,1,0:T(8,128)S(1)} %pad_maximum_fusion.6), channel_id=1, source_target_pairs={{0,1},{1,0},{2,3},{3,2},{4,5},{5,4},{6,7},{7,6},{8,9},{9,8},{10,11... | collective-permute-start | bytes 1572872 | tf_op jit(solution)/shard_map/ppermute | solution.py:30
  49.3 22.7 %collective-permute-start.10 = (f32[512,128]{1,0:T(8,128)S(1)}, f32[512,128]{1,0:T(8,128)}, u32[]{:S(2)}, u32[]{:S(2)}) collective-permute-start(f32[512,128]{1,0:T(8,128)S(1)} %get-tuple-element.34), channel_id=1, source_target_pairs={{0,32},{8,40},{16,48},{24,56},{32,64},{40,72},{48,80},{56,88},{64,... | collective-permute-start | bytes 786440 | tf_op jit(solution)/shard_map/ppermute | solution.py:24
  74.6 1.7 copy-start.12
  74.6 8.3 %collective-permute-start.11 = (f32[512,128]{1,0:T(8,128)S(1)}, f32[512,128]{1,0:T(8,128)S(1)}, u32[]{:S(2)}, u32[]{:S(2)}) collective-permute-start(f32[512,128]{1,0:T(8,128)S(1)} %get-tuple-element.37), channel_id=1, source_target_pairs={{0,2},{1,3},{2,0},{3,1},{4,6},{5,7},{6,4},{7,5},{8,10},{9,11},{10,... | collective-permute-start | bytes 786440 | tf_op jit(solution)/shard_map/ppermute | solution.py:29
  75.3 7.7 %copy-start.7 = (f32[1,512,512]{2,1,0:T(8,128)S(1)}, f32[1,512,512]{2,1,0:T(8,128)}, u32[]{:S(2)}) copy-start(f32[1,512,512]{2,1,0:T(8,128)} %param.9) | copy-start | bytes 3145732
  75.4 7.7 %copy-start.11 = (f32[64,512]{1,0:T(8,128)S(1)}, f32[64,512]{1,0:T(8,128)}, u32[]{:S(2)}) copy-start(f32[64,512]{1,0:T(8,128)} %param.13) | copy-start | bytes 393220
  76.3 12.8 %copy-start.5 = (f32[512,512]{1,0:T(8,128)S(1)}, f32[512,512]{1,0:T(8,128)}, u32[]{:S(2)}) copy-start(f32[512,512]{1,0:T(8,128)} %copy-done.4) | copy-start | bytes 3145732
  82.9 21.7 %collective-permute-start.12 = (f32[2,512,128]{2,1,0:T(8,128)S(1)}, f32[2,512,128]{2,1,0:T(8,128)S(1)}, u32[]{:S(2)}, u32[]{:S(2)}) collective-permute-start(f32[2,512,128]{2,1,0:T(8,128)S(1)} %pad_maximum_fusion.7), channel_id=1, source_target_pairs={{0,1},{1,0},{2,3},{3,2},{4,5},{5,4},{6,7},{7,6},{8,9},{9,8},{10,11... | collective-permute-start | bytes 1572872 | tf_op jit(solution)/shard_map/ppermute | solution.py:30
  84.1 5.0 %collective-permute-start = (f32[64,512]{1,0:T(8,128)S(1)}, f32[64,512]{1,0:T(8,128)S(1)}, u32[]{:S(2)}, u32[]{:S(2)}) collective-permute-start(f32[64,512]{1,0:T(8,128)S(1)} %convolution_add_fusion.5), channel_id=1, source_target_pairs={{0,8},{8,16},{16,24},{24,32},{32,40},{40,48},{48,56},{56,64},{64,7... | collective-permute-start | bytes 393224 | tf_op jit(solution)/shard_map/ppermute | solution.py:22
  90.2 24.9 %collective-permute-start.1 = (f32[64,512]{1,0:T(8,128)S(1)}, f32[64,512]{1,0:T(8,128)}, u32[]{:S(2)}, u32[]{:S(2)}) collective-permute-start(f32[64,512]{1,0:T(8,128)S(1)} %fusion.5), channel_id=1, source_target_pairs={{0,16},{8,24},{16,32},{24,40},{32,48},{40,56},{48,64},{56,72},{64,... | collective-permute-start | bytes 393224 | tf_op jit(solution)/shard_map/ppermute | solution.py:22
  92.2 20.1 %collective-permute-start.14 = (f32[512,128]{1,0:T(8,128)}, f32[512,128]{1,0:T(8,128)}, u32[]{:S(2)}, u32[]{:S(2)}) collective-permute-start(f32[512,128]{1,0:T(8,128)} %get-tuple-element.36), channel_id=1, source_target_pairs={{0,64},{8,72},{16,80},{24,88},{32,96},{40,104},{48,112},{56,120},{... | collective-permute-start | bytes 786440 | tf_op jit(solution)/shard_map/ppermute | solution.py:24
  110.0 7.7 %copy-start.2 = (f32[512,512]{1,0:T(8,128)}, f32[512,512]{1,0:T(8,128)S(1)}, u32[]{:S(2)}) copy-start(f32[512,512]{1,0:T(8,128)S(1)} %maximum_select_fusion.2) | copy-start | bytes 3145732
  114.3 7.2 %collective-permute-start.15 = (f32[512,128]{1,0:T(8,128)S(1)}, f32[512,128]{1,0:T(8,128)}, u32[]{:S(2)}, u32[]{:S(2)}) collective-permute-start(f32[512,128]{1,0:T(8,128)S(1)} %fusion.30), channel_id=1, source_target_pairs={{0,2},{1,3},{2,0},{3,1},{4,6},{5,7},{6,4},{7,5},{8,10},{9,11},{10,... | collective-permute-start | bytes 786440 | tf_op jit(solution)/shard_map/ppermute | solution.py:29
  117.8 4.8 %collective-permute-start.5 = (f32[64,512]{1,0:T(8,128)}, f32[64,512]{1,0:T(8,128)S(1)}, u32[]{:S(2)}, u32[]{:S(2)}) collective-permute-start(f32[64,512]{1,0:T(8,128)} %fusion.4), channel_id=1, source_target_pairs={{0,32},{8,40},{16,48},{24,56},{32,64},{40,72},{48,80},{56,88},{64,... | collective-permute-start | bytes 393224 | tf_op jit(solution)/shard_map/ppermute | solution.py:22
  122.5 17.9 %copy-start.3 = (f32[512,512]{1,0:T(8,128)S(1)}, f32[512,512]{1,0:T(8,128)}, u32[]{:S(2)}) copy-start(f32[512,512]{1,0:T(8,128)} %copy-done.2) | copy-start | bytes 3145732
  122.5 25.5 %collective-permute-start.16 = (f32[2,512,128]{2,1,0:T(8,128)S(1)}, f32[2,512,128]{2,1,0:T(8,128)S(1)}, u32[]{:S(2)}, u32[]{:S(2)}) collective-permute-start(f32[2,512,128]{2,1,0:T(8,128)S(1)} %pad_maximum_fusion.8), channel_id=1, source_target_pairs={{0,1},{1,0},{2,3},{3,2},{4,5},{5,4},{6,7},{7,6},{8,9},{9,8},{10,11... | collective-permute-start | bytes 1572872 | tf_op jit(solution)/shard_map/ppermute | solution.py:30
  124.7 15.7 %collective-permute-start.9 = (f32[64,512]{1,0:T(8,128)S(1)}, f32[64,512]{1,0:T(8,128)S(1)}, u32[]{:S(2)}, u32[]{:S(2)}) collective-permute-start(f32[64,512]{1,0:T(8,128)S(1)} %fusion.3), channel_id=1, source_target_pairs={{0,64},{8,72},{16,80},{24,88},{32,96},{40,104},{48,112},{56,120},{... | collective-permute-start | bytes 393224 | tf_op jit(solution)/shard_map/ppermute | solution.py:22
  141.5 10.6 %collective-permute-start.13 = (f32[64,512]{1,0:T(8,128)S(1)}, f32[64,512]{1,0:T(8,128)}, u32[]{:S(2)}, u32[]{:S(2)}) collective-permute-start(f32[64,512]{1,0:T(8,128)S(1)} %fusion.2), channel_id=1, source_target_pairs={{0,128},{8,136},{16,144},{24,152},{32,160},{40,168},{48,176},{56,1... | collective-permute-start | bytes 393224 | tf_op jit(solution)/shard_map/ppermute | solution.py:22
  152.1 2.2 %copy-start.8 = (f32[8,1,64,256]{3,2,1,0:T(8,128)S(1)}, f32[8,1,64,256]{3,2,1,0:T(8,128)}, u32[]{:S(2)}) copy-start(f32[8,1,64,256]{3,2,1,0:T(8,128)} %copy.15) | copy-start | bytes 1572868
  154.1 1.4 copy-start.10
  155.6 24.7 %all-to-all-start = ((f32[8,1,64,768]{3,2,1,0:T(8,128)}), f32[8,1,64,768]{3,2,1,0:T(8,128)S(1)}, u32[]{:S(2)}, u32[]{:S(2)}) async-start(f32[8,1,64,768]{3,2,1,0:T(8,128)} %pad_maximum_fusion), calls=%async_computation | async-start | bytes 3145728 | tf_op jit(solution)/shard_map/all_to_all | solution.py:89

commit v12 on v11

--- a/solution.py
+++ b/solution.py
@@ -6,33 +6,35 @@
 
 def shift_scan(matrix, vector, axis, pair_axis):
     highest = lax.Precision.HIGHEST
-    count, index = (lax.axis_size(axis), lax.axis_index(axis))
+    count = lax.axis_size(axis)
     pair_count = lax.axis_size(pair_axis)
     part = lax.axis_index(pair_axis) % 4
     width = matrix.shape[1] // 4
     across = [(j, j ^ 2) for j in range(pair_count)]
     swap = [(j, j ^ 1) for j in range(pair_count)]
-    place = jnp.array([0, 2, 1, 3], jnp.int32)[part ^ jnp.arange(4, dtype=jnp.int32)]
-    mine = lax.dynamic_slice_in_dim(matrix, part * width, width, axis=1)
+    quarters = [part, part ^ 2, part ^ 1, part ^ 3]
+    pieces = [lax.dynamic_slice_in_dim(matrix, k * width, width, axis=1) for k in quarters]
     distance = 1
     while distance < count:
         pairs = [(j, j + distance) for j in range(count - distance)]
         last = 2 * distance >= count
-        has = index >= distance
         got_vector = lax.ppermute(vector, axis, pairs)
         if not last:
-            got_part = lax.ppermute(mine, axis, pairs)
-        newer = jnp.einsum("sq,rq->sr", got_vector, matrix, precision=highest) + vector
-        vector = jnp.where(has, newer, vector)
+            got_part = lax.ppermute(pieces[0], axis, pairs)
+        newer = vector
+        for piece, k in zip(pieces, quarters):
+            front = lax.dynamic_slice_in_dim(got_vector, k * width, width, axis=1)
+            newer = newer + jnp.einsum("sq,rq->sr", front, piece, precision=highest)
+        vector = newer
         if not last:
-            own = jnp.dot(matrix, got_part, precision=highest)
+            own = None
+            for piece, k in zip(pieces, quarters):
+                block = lax.dynamic_slice_in_dim(got_part, k * width, width, axis=0)
+                term = jnp.dot(piece, block, precision=highest)
+                own = term if own is None else own + term
             far = lax.ppermute(own, pair_axis, across)
             near = lax.ppermute(jnp.stack([own, far]), pair_axis, swap)
-            pieces = jnp.concatenate([jnp.stack([own, far]), near], axis=0)
-            ordered = jnp.take(pieces, place, axis=0)
-            joined = jnp.concatenate([ordered[k] for k in range(4)], axis=1)
-            matrix = jnp.where(has, joined, matrix)
-            mine = jnp.where(has, own, mine)
+            pieces = [own, far, near[0], near[1]]
         distance = distance * 2
     return vector
 
@@ -98,17 +100,18 @@
         [lax.dynamic_slice_in_dim(every, column, gram_cols, axis=2), readings], axis=2
     )
     joined = jnp.einsum("tsr,tso->ro", every, right, precision=highest) * normalize
-    mine = joined
-    stride = time_shards
-    for size in tm_groups:
-        stride //= size
-        groups = [
-            [base + k * stride for k in range(size)]
-            for base in range(time_shards)
-            if (base // stride) % size == 0
-        ]
-        pieces = mine.reshape(size, mine.shape[0] // size, mine.shape[1])
-        mine = lax.all_to_all(pieces, "tm", 0, 0, tiled=True, axis_index_groups=groups).sum(axis=0)
+    outer, inner = tm_groups if len(tm_groups) == 2 else (1, time_shards)
+    block = modes // time_shards
+    pieces = joined.reshape(outer, inner, block, joined.shape[1]).transpose(1, 0, 2, 3)
+    near_groups = [[base * inner + k for k in range(inner)] for base in range(outer)]
+    pieces = lax.all_to_all(pieces, "tm", 0, 0, tiled=True, axis_index_groups=near_groups)
+    mine = pieces.reshape(inner, outer, block, joined.shape[1]).sum(axis=0)
+    if outer > 1:
+        far_groups = [[k * inner + base for k in range(outer)] for base in range(inner)]
+        mine = lax.all_to_all(mine, "tm", 0, 0, tiled=True, axis_index_groups=far_groups)
+        mine = mine.sum(axis=0)
+    else:
+        mine = mine[0]
     return (states, mine[:, :gram_cols], mine[:, gram_cols:])
 
 

time: 212 us -> 188 us (0.89)
  blocking collectives: 25.7 us -> 37.2 us
  other arithmetic: 12.2 us -> 1.58 us
  local copies, waits for them, and re-layouts: 13.1 us -> 2.77 us
  waiting for transfers between devices: 67.4 us -> 61.8 us
  starting transfers between devices: 68.1 us -> 63.9 us
  matrix products: 21.4 us -> 17.8 us
    ppermute x4, waiting for transfers between devices: 20 us -> 6.15 us  [shift_scan(): far = lax.ppermute(own, pair_axis, across)]
    ppermute x4, starting transfers between devices: 34.5 us -> 22 us  [shift_scan(): got_part = lax.ppermute(pieces[0], axis, pairs)]
    all_to_all x2, blocking collectives: 25.7 us -> 37.2 us  [the longest x1 26.3 us: on_device_body(): lax.all_to_all(pieces, 'tm', 0, 0, tiled=True, axis_index_groups=near_gro...]
    ppermute x4, waiting for transfers between devices: 22.7 us -> 33 us  [shift_scan(): got_part = lax.ppermute(pieces[0], axis, pairs)]
    gather x5 -> x0, local copies, waits for them, and re-layouts: 7.73 us -> none  [the longest x4 7.09 us: shift_scan(): ordered = jnp.take(pieces, place, axis=0)]
    ppermute x5, starting transfers between devices: 24.8 us -> 31.9 us  [shift_scan(): got_vector = lax.ppermute(vector, axis, pairs)]
    concatenate x4 -> x0, other arithmetic: 6.13 us -> none  [shift_scan(): pieces = jnp.concatenate([jnp.stack([own, far]), near], axis=0)]
    dot_general x9 -> x36, matrix products: 17.3 us -> 13.7 us  [the longest x20 7.76 us: shift_scan(): newer = newer + jnp.einsum('sq,rq->sr', front, piece, precision=highest)]
  transfers between devices with their start and end apart: 18 -> 18, of which waited for: 11 -> 7; matrix products, arithmetic and copies ran while one was open for 15% -> 4% of each run, Pallas kernels for 0% -> 0%
where the time goes in v12:
time: 188 us; the launch traced here: 187 us
  starting transfers between devices  63.9 us (34%)
  waiting for transfers between devices  61.8 us (33%)
  blocking collectives  37.2 us (20%)
  matrix products  17.8 us (9%)
  local copies, waits for them, and re-layouts  2.77 us (1%)
  between operations  2.11 us (1%)
    ppermute x4, waiting for transfers between devices, shift_scan(): got_part = lax.ppermute(pieces[0], axis, pairs)  33 us
    ppermute x5, starting transfers between devices, shift_scan(): got_vector = lax.ppermute(vector, axis, pairs)  31.9 us
    all_to_all x1, blocking collectives, on_device_body(): lax.all_to_all(pieces, 'tm', 0, 0, tiled=True, axis_index_groups=near_gro...  26.3 us
    ppermute x4, starting transfers between devices, shift_scan(): got_part = lax.ppermute(pieces[0], axis, pairs)  22 us
    all_to_all x1, waiting for transfers between devices, on_device_body(): received = lax.all_to_all(payload, 'scen', 0, 0, tiled=True)  19.5 us
    all_to_all x1, blocking collectives, on_device_body(): lax.all_to_all(mine, 'tm', 0, 0, tiled=True, axis_index_groups=far_groups)  10.9 us
    dot_general x20, matrix products, shift_scan(): newer = newer + jnp.einsum('sq,rq->sr', front, piece, precision=highest)  7.76 us
    ppermute x4, waiting for transfers between devices, shift_scan(): far = lax.ppermute(own, pair_axis, across)  6.15 us
  transfers between devices with their start and end apart: 18, of which 7 were waited for; matrix products, arithmetic and copies ran while one was open for 4% of the time, Pallas kernels for 0%

profile of v12, /device:TPU:24, one launch (start us, length us, event | category | flops | bytes accessed | tf_op | source)
XLA Modules:
  0.0 187.1 jit_solution(11602533535758977326)
XLA Ops:
  1.5 0.4 copy-done
  1.9 0.9 fusion.25
  3.0 1.1 convolution_add_fusion.4
  4.1 3.8 %collective-permute-start = (f32[64,512]{1,0:T(8,128)S(1)}, f32[64,512]{1,0:T(8,128)S(1)}, u32[]{:S(2)}, u32[]{:S(2)}) collective-permute-start(f32[64,512]{1,0:T(8,128)S(1)} %convolution_add_fusion.4), channel_id=1, source_target_pairs={{0,8},{8,16},{16,24},{24,32},{32,40},{40,48},{48,56},{56,64},{64,7... | collective-permute-start | bytes 393224 | tf_op jit(solution)/shard_map/ppermute | solution.py:21
  8.1 3.8 %collective-permute-start.2 = (f32[512,128]{1,0:T(8,128)S(1)}, f32[512,128]{1,0:T(8,128)S(1)}, u32[]{:S(2)}, u32[]{:S(2)}) collective-permute-start(f32[512,128]{1,0:T(8,128)S(1)} %constant_dynamic-slice_fusion.1), channel_id=1, source_target_pairs={{0,8},{8,16},{16,24},{24,32},{32,40},{40,48},{48,56},{56,64},{64,7... | collective-permute-start | bytes 786440 | tf_op jit(solution)/shard_map/ppermute | solution.py:23
  12.0 0.4 fusion.45
  12.4 0.4 fusion.49
  12.8 4.4 %collective-permute-done.2 = f32[512,128]{1,0:T(8,128)S(1)} collective-permute-done((f32[512,128]{1,0:T(8,128)S(1)}, f32[512,128]{1,0:T(8,128)S(1)}, u32[]{:S(2)}, u32[]{:S(2)}) %collective-permute-start.2) | collective-permute-done | bytes 262176 | tf_op jit(solution)/shard_map/ppermute | solution.py:23
  18.8 0.8 collective-permute-start.3
  19.6 0.4 fusion.53
  20.0 0.4 fusion.22
  20.4 6.4 %collective-permute-start.1 = (f32[64,512]{1,0:T(8,128)S(1)}, f32[64,512]{1,0:T(8,128)S(1)}, u32[]{:S(2)}, u32[]{:S(2)}) collective-permute-start(f32[64,512]{1,0:T(8,128)S(1)} %fusion.22), channel_id=1, source_target_pairs={{0,16},{8,24},{16,32},{24,40},{32,48},{40,56},{48,64},{56,72},{64,... | collective-permute-start | bytes 393224 | tf_op jit(solution)/shard_map/ppermute | solution.py:21
  26.9 6.1 %collective-permute-start.6 = (f32[512,128]{1,0:T(8,128)S(1)}, f32[512,128]{1,0:T(8,128)S(1)}, u32[]{:S(2)}, u32[]{:S(2)}) collective-permute-start(f32[512,128]{1,0:T(8,128)S(1)} %fusion.7), channel_id=1, source_target_pairs={{0,16},{8,24},{16,32},{24,40},{32,48},{40,56},{48,64},{56,72},{64,... | collective-permute-start | bytes 786440 | tf_op jit(solution)/shard_map/ppermute | solution.py:23
  33.0 0.4 fusion.95
  33.4 11.4 %collective-permute-done.6 = f32[512,128]{1,0:T(8,128)S(1)} collective-permute-done((f32[512,128]{1,0:T(8,128)S(1)}, f32[512,128]{1,0:T(8,128)S(1)}, u32[]{:S(2)}, u32[]{:S(2)}) %collective-permute-start.6) | collective-permute-done | bytes 262176 | tf_op jit(solution)/shard_map/ppermute | solution.py:23
  46.4 1.4 collective-permute-start.7
  48.2 0.4 fusion.34
  48.6 0.4 fusion.19
  49.0 8.5 %collective-permute-start.5 = (f32[64,512]{1,0:T(8,128)S(1)}, f32[64,512]{1,0:T(8,128)S(1)}, u32[]{:S(2)}, u32[]{:S(2)}) collective-permute-start(f32[64,512]{1,0:T(8,128)S(1)} %fusion.19), channel_id=1, source_target_pairs={{0,32},{8,40},{16,48},{24,56},{32,64},{40,72},{48,80},{56,88},{64,... | collective-permute-start | bytes 393224 | tf_op jit(solution)/shard_map/ppermute | solution.py:21
  57.6 6.3 %collective-permute-start.10 = (f32[512,128]{1,0:T(8,128)S(1)}, f32[512,128]{1,0:T(8,128)S(1)}, u32[]{:S(2)}, u32[]{:S(2)}) collective-permute-start(f32[512,128]{1,0:T(8,128)S(1)} %fusion.5), channel_id=1, source_target_pairs={{0,32},{8,40},{16,48},{24,56},{32,64},{40,72},{48,80},{56,88},{64,... | collective-permute-start | bytes 786440 | tf_op jit(solution)/shard_map/ppermute | solution.py:23
  63.9 0.4 fusion.90
  64.3 11.4 %collective-permute-done.10 = f32[512,128]{1,0:T(8,128)S(1)} collective-permute-done((f32[512,128]{1,0:T(8,128)S(1)}, f32[512,128]{1,0:T(8,128)S(1)}, u32[]{:S(2)}, u32[]{:S(2)}) %collective-permute-start.10) | collective-permute-done | bytes 262176 | tf_op jit(solution)/shard_map/ppermute | solution.py:23
  77.2 1.5 collective-permute-start.11
  79.1 0.4 fusion.38
  79.5 0.4 fusion.16
  79.9 7.3 %collective-permute-start.9 = (f32[64,512]{1,0:T(8,128)S(1)}, f32[64,512]{1,0:T(8,128)S(1)}, u32[]{:S(2)}, u32[]{:S(2)}) collective-permute-start(f32[64,512]{1,0:T(8,128)S(1)} %fusion.16), channel_id=1, source_target_pairs={{0,64},{8,72},{16,80},{24,88},{32,96},{40,104},{48,112},{56,120},{... | collective-permute-start | bytes 393224 | tf_op jit(solution)/shard_map/ppermute | solution.py:21
  87.3 5.9 %collective-permute-start.14 = (f32[512,128]{1,0:T(8,128)S(1)}, f32[512,128]{1,0:T(8,128)S(1)}, u32[]{:S(2)}, u32[]{:S(2)}) collective-permute-start(f32[512,128]{1,0:T(8,128)S(1)} %fusion.3), channel_id=1, source_target_pairs={{0,64},{8,72},{16,80},{24,88},{32,96},{40,104},{48,112},{56,120},{... | collective-permute-start | bytes 786440 | tf_op jit(solution)/shard_map/ppermute | solution.py:23
  93.3 0.4 fusion.85
  93.7 5.7 %collective-permute-done.14 = f32[512,128]{1,0:T(8,128)S(1)} collective-permute-done((f32[512,128]{1,0:T(8,128)S(1)}, f32[512,128]{1,0:T(8,128)S(1)}, u32[]{:S(2)}, u32[]{:S(2)}) %collective-permute-start.14) | collective-permute-done | bytes 262176 | tf_op jit(solution)/shard_map/ppermute | solution.py:23
  100.9 1.0 collective-permute-start.15
  101.9 0.4 fusion.40
  102.3 0.4 fusion.42
  102.7 6.1 %collective-permute-done.15 = f32[512,128]{1,0:T(8,128)S(1)} collective-permute-done((f32[512,128]{1,0:T(8,128)S(1)}, f32[512,128]{1,0:T(8,128)S(1)}, u32[]{:S(2)}, u32[]{:S(2)}) %collective-permute-start.15) | collective-permute-done | bytes 262176 | tf_op jit(solution)/shard_map/ppermute | solution.py:35
  109.0 0.4 fusion.13
  109.4 5.9 %collective-permute-start.13 = (f32[64,512]{1,0:T(8,128)S(1)}, f32[64,512]{1,0:T(8,128)S(1)}, u32[]{:S(2)}, u32[]{:S(2)}) collective-permute-start(f32[64,512]{1,0:T(8,128)S(1)} %fusion.13), channel_id=1, source_target_pairs={{0,128},{8,136},{16,144},{24,152},{32,160},{40,168},{48,176},{56,1... | collective-permute-start | bytes 393224 | tf_op jit(solution)/shard_map/ppermute | solution.py:21
  115.5 3.2 %collective-permute-done.13 = f32[64,512]{1,0:T(8,128)S(1)} collective-permute-done((f32[64,512]{1,0:T(8,128)S(1)}, f32[64,512]{1,0:T(8,128)S(1)}, u32[]{:S(2)}, u32[]{:S(2)}) %collective-permute-start.13) | collective-permute-done | bytes 131104 | tf_op jit(solution)/shard_map/ppermute | solution.py:21
  118.7 0.4 fusion.80
  119.1 0.4 fusion.30
  119.5 0.4 fusion.29
  119.9 0.4 fusion.10
  120.4 1.3 pad_maximum_fusion
  121.7 4.8 %all-to-all-start = ((f32[8,1,64,768]{3,2,1,0:T(8,128)}), f32[8,1,64,768]{3,2,1,0:T(8,128)S(1)}, u32[]{:S(2)}, u32[]{:S(2)}) async-start(f32[8,1,64,768]{3,2,1,0:T(8,128)} %pad_maximum_fusion), calls=%async_computation | async-start | bytes 3145728 | tf_op jit(solution)/shard_map/all_to_all | solution.py:91
  126.5 19.5 %all-to-all-done = f32[8,1,64,768]{3,2,1,0:T(8,128)S(1)} async-done(((f32[8,1,64,768]{3,2,1,0:T(8,128)}), f32[8,1,64,768]{3,2,1,0:T(8,128)S(1)}, u32[]{:S(2)}, u32[]{:S(2)}) %all-to-all-start) | async-done | bytes 1572896 | tf_op jit(solution)/shard_map/all_to_all | solution.py:91
  146.3 1.9 convolution_multiply_fusion
  148.5 26.3 %all_to_all.15 = f32[8,4,16,320]{3,2,1,0:T(8,128)S(1)} all-to-all(f32[8,4,16,320]{3,2,1,0:T(8,128)S(1)} %copy.17), channel_id=1, replica_groups={{0,8,16,24,32,40,48,56},{64,72,80,88,96,104,112,120},{128,136,144,152,1..., dimensions={0} | all-to-all | bytes 1310720 | tf_op jit(solution)/shard_map/all_to_all | solution.py:107
  174.9 10.9 %all_to_all.16 = f32[4,16,320]{2,1,0:T(8,128)S(1)} all-to-all(f32[4,16,320]{2,1,0:T(8,128)S(1)} %reduce_sum.18), channel_id=1, replica_groups={{0,64,128,192},{8,72,136,200},{16,80,144,208},{24,88,152,216},{32,96,16..., dimensions={0} | all-to-all | bytes 163840 | tf_op jit(solution)/shard_map/all_to_all | solution.py:111
  185.8 0.7 slice.59
  186.5 0.6 slice.58
  (62 shorter events, 8.7 us)
Async XLA Ops:
  0.6 1.2 copy-start
  0.6 2.1 %copy-start.5 = (bf16[1,64,256]{2,1,0:T(8,128)(2,1)S(1)}, bf16[1,64,256]{2,1,0:T(8,128)(2,1)}, u32[]{:S(2)}) copy-start(bf16[1,64,256]{2,1,0:T(8,128)(2,1)} %param.9) | copy-start | bytes 98308
  0.7 2.3 %copy-start.1 = (f32[1,512,512]{2,1,0:T(8,128)S(1)}, f32[1,512,512]{2,1,0:T(8,128)}, u32[]{:S(2)}) copy-start(f32[1,512,512]{2,1,0:T(8,128)} %param.6) | copy-start | bytes 3145732
  0.7 2.3 %copy-start.4 = (f32[64,512]{1,0:T(8,128)S(1)}, f32[64,512]{1,0:T(8,128)}, u32[]{:S(2)}) copy-start(f32[64,512]{1,0:T(8,128)} %param.10) | copy-start | bytes 393220
  4.1 7.9 %collective-permute-start = (f32[64,512]{1,0:T(8,128)S(1)}, f32[64,512]{1,0:T(8,128)S(1)}, u32[]{:S(2)}, u32[]{:S(2)}) collective-permute-start(f32[64,512]{1,0:T(8,128)S(1)} %convolution_add_fusion.4), channel_id=1, source_target_pairs={{0,8},{8,16},{16,24},{24,32},{32,40},{40,48},{48,56},{56,64},{64,7... | collective-permute-start | bytes 393224 | tf_op jit(solution)/shard_map/ppermute | solution.py:21
  8.1 9.1 %collective-permute-start.2 = (f32[512,128]{1,0:T(8,128)S(1)}, f32[512,128]{1,0:T(8,128)S(1)}, u32[]{:S(2)}, u32[]{:S(2)}) collective-permute-start(f32[512,128]{1,0:T(8,128)S(1)} %constant_dynamic-slice_fusion.1), channel_id=1, source_target_pairs={{0,8},{8,16},{16,24},{24,32},{32,40},{40,48},{48,56},{56,64},{64,7... | collective-permute-start | bytes 786440 | tf_op jit(solution)/shard_map/ppermute | solution.py:23
  18.8 8.0 %collective-permute-start.3 = (f32[512,128]{1,0:T(8,128)S(1)}, f32[512,128]{1,0:T(8,128)S(1)}, u32[]{:S(2)}, u32[]{:S(2)}) collective-permute-start(f32[512,128]{1,0:T(8,128)S(1)} %fusion.7), channel_id=1, source_target_pairs={{0,2},{1,3},{2,0},{3,1},{4,6},{5,7},{6,4},{7,5},{8,10},{9,11},{10,... | collective-permute-start | bytes 786440 | tf_op jit(solution)/shard_map/ppermute | solution.py:35
  20.4 12.6 %collective-permute-start.1 = (f32[64,512]{1,0:T(8,128)S(1)}, f32[64,512]{1,0:T(8,128)S(1)}, u32[]{:S(2)}, u32[]{:S(2)}) collective-permute-start(f32[64,512]{1,0:T(8,128)S(1)} %fusion.22), channel_id=1, source_target_pairs={{0,16},{8,24},{16,32},{24,40},{32,48},{40,56},{48,64},{56,72},{64,... | collective-permute-start | bytes 393224 | tf_op jit(solution)/shard_map/ppermute | solution.py:21
  26.8 18.4 %collective-permute-start.4 = (f32[2,512,128]{2,1,0:T(8,128)S(1)}, f32[2,512,128]{2,1,0:T(8,128)S(1)}, u32[]{:S(2)}, u32[]{:S(2)}) collective-permute-start(f32[2,512,128]{2,1,0:T(8,128)S(1)} %pad_maximum_fusion.1), channel_id=1, source_target_pairs={{0,1},{1,0},{2,3},{3,2},{4,5},{5,4},{6,7},{7,6},{8,9},{9,8},{10,11... | collective-permute-start | bytes 1572872 | tf_op jit(solution)/shard_map/ppermute | solution.py:36
  26.9 17.9 %collective-permute-start.6 = (f32[512,128]{1,0:T(8,128)S(1)}, f32[512,128]{1,0:T(8,128)S(1)}, u32[]{:S(2)}, u32[]{:S(2)}) collective-permute-start(f32[512,128]{1,0:T(8,128)S(1)} %fusion.7), channel_id=1, source_target_pairs={{0,16},{8,24},{16,32},{24,40},{32,48},{40,56},{48,64},{56,72},{64,... | collective-permute-start | bytes 786440 | tf_op jit(solution)/shard_map/ppermute | solution.py:23
  46.4 11.1 %collective-permute-start.7 = (f32[512,128]{1,0:T(8,128)S(1)}, f32[512,128]{1,0:T(8,128)S(1)}, u32[]{:S(2)}, u32[]{:S(2)}) collective-permute-start(f32[512,128]{1,0:T(8,128)S(1)} %fusion.5), channel_id=1, source_target_pairs={{0,2},{1,3},{2,0},{3,1},{4,6},{5,7},{6,4},{7,5},{8,10},{9,11},{10,... | collective-permute-start | bytes 786440 | tf_op jit(solution)/shard_map/ppermute | solution.py:35
  49.0 14.9 %collective-permute-start.5 = (f32[64,512]{1,0:T(8,128)S(1)}, f32[64,512]{1,0:T(8,128)S(1)}, u32[]{:S(2)}, u32[]{:S(2)}) collective-permute-start(f32[64,512]{1,0:T(8,128)S(1)} %fusion.19), channel_id=1, source_target_pairs={{0,32},{8,40},{16,48},{24,56},{32,64},{40,72},{48,80},{56,88},{64,... | collective-permute-start | bytes 393224 | tf_op jit(solution)/shard_map/ppermute | solution.py:21
  57.5 18.5 %collective-permute-start.8 = (f32[2,512,128]{2,1,0:T(8,128)S(1)}, f32[2,512,128]{2,1,0:T(8,128)S(1)}, u32[]{:S(2)}, u32[]{:S(2)}) collective-permute-start(f32[2,512,128]{2,1,0:T(8,128)S(1)} %pad_maximum_fusion.2), channel_id=1, source_target_pairs={{0,1},{1,0},{2,3},{3,2},{4,5},{5,4},{6,7},{7,6},{8,9},{9,8},{10,11... | collective-permute-start | bytes 1572872 | tf_op jit(solution)/shard_map/ppermute | solution.py:36
  57.6 18.0 %collective-permute-start.10 = (f32[512,128]{1,0:T(8,128)S(1)}, f32[512,128]{1,0:T(8,128)S(1)}, u32[]{:S(2)}, u32[]{:S(2)}) collective-permute-start(f32[512,128]{1,0:T(8,128)S(1)} %fusion.5), channel_id=1, source_target_pairs={{0,32},{8,40},{16,48},{24,56},{32,64},{40,72},{48,80},{56,88},{64,... | collective-permute-start | bytes 786440 | tf_op jit(solution)/shard_map/ppermute | solution.py:23
  77.2 16.0 %copy-start.3 = (bf16[1,64,2048]{2,1,0:T(8,128)(2,1)S(1)}, bf16[1,64,2048]{2,1,0:T(8,128)(2,1)}, u32[]{:S(2)}) copy-start(bf16[1,64,2048]{2,1,0:T(8,128)(2,1)} %param.11) | copy-start | bytes 786436
  77.2 9.9 %collective-permute-start.11 = (f32[512,128]{1,0:T(8,128)S(1)}, f32[512,128]{1,0:T(8,128)S(1)}, u32[]{:S(2)}, u32[]{:S(2)}) collective-permute-start(f32[512,128]{1,0:T(8,128)S(1)} %fusion.3), channel_id=1, source_target_pairs={{0,2},{1,3},{2,0},{3,1},{4,6},{5,7},{6,4},{7,5},{8,10},{9,11},{10,... | collective-permute-start | bytes 786440 | tf_op jit(solution)/shard_map/ppermute | solution.py:35
  79.9 13.4 %collective-permute-start.9 = (f32[64,512]{1,0:T(8,128)S(1)}, f32[64,512]{1,0:T(8,128)S(1)}, u32[]{:S(2)}, u32[]{:S(2)}) collective-permute-start(f32[64,512]{1,0:T(8,128)S(1)} %fusion.16), channel_id=1, source_target_pairs={{0,64},{8,72},{16,80},{24,88},{32,96},{40,104},{48,112},{56,120},{... | collective-permute-start | bytes 393224 | tf_op jit(solution)/shard_map/ppermute | solution.py:21
  87.2 12.6 %collective-permute-start.12 = (f32[2,512,128]{2,1,0:T(8,128)S(1)}, f32[2,512,128]{2,1,0:T(8,128)S(1)}, u32[]{:S(2)}, u32[]{:S(2)}) collective-permute-start(f32[2,512,128]{2,1,0:T(8,128)S(1)} %pad_maximum_fusion.3), channel_id=1, source_target_pairs={{0,1},{1,0},{2,3},{3,2},{4,5},{5,4},{6,7},{7,6},{8,9},{9,8},{10,11... | collective-permute-start | bytes 1572872 | tf_op jit(solution)/shard_map/ppermute | solution.py:36
  87.3 12.1 %collective-permute-start.14 = (f32[512,128]{1,0:T(8,128)S(1)}, f32[512,128]{1,0:T(8,128)S(1)}, u32[]{:S(2)}, u32[]{:S(2)}) collective-permute-start(f32[512,128]{1,0:T(8,128)S(1)} %fusion.3), channel_id=1, source_target_pairs={{0,64},{8,72},{16,80},{24,88},{32,96},{40,104},{48,112},{56,120},{... | collective-permute-start | bytes 786440 | tf_op jit(solution)/shard_map/ppermute | solution.py:23
  100.9 7.9 %collective-permute-start.15 = (f32[512,128]{1,0:T(8,128)S(1)}, f32[512,128]{1,0:T(8,128)S(1)}, u32[]{:S(2)}, u32[]{:S(2)}) collective-permute-start(f32[512,128]{1,0:T(8,128)S(1)} %fusion.1), channel_id=1, source_target_pairs={{0,2},{1,3},{2,0},{3,1},{4,6},{5,7},{6,4},{7,5},{8,10},{9,11},{10,... | collective-permute-start | bytes 786440 | tf_op jit(solution)/shard_map/ppermute | solution.py:35
  108.9 10.2 %collective-permute-start.16 = (f32[2,512,128]{2,1,0:T(8,128)S(1)}, f32[2,512,128]{2,1,0:T(8,128)S(1)}, u32[]{:S(2)}, u32[]{:S(2)}) collective-permute-start(f32[2,512,128]{2,1,0:T(8,128)S(1)} %pad_maximum_fusion.4), channel_id=1, source_target_pairs={{0,1},{1,0},{2,3},{3,2},{4,5},{5,4},{6,7},{7,6},{8,9},{9,8},{10,11... | collective-permute-start | bytes 1572872 | tf_op jit(solution)/shard_map/ppermute | solution.py:36
  109.4 9.3 %collective-permute-start.13 = (f32[64,512]{1,0:T(8,128)S(1)}, f32[64,512]{1,0:T(8,128)S(1)}, u32[]{:S(2)}, u32[]{:S(2)}) collective-permute-start(f32[64,512]{1,0:T(8,128)S(1)} %fusion.13), channel_id=1, source_target_pairs={{0,128},{8,136},{16,144},{24,152},{32,160},{40,168},{48,176},{56,1... | collective-permute-start | bytes 393224 | tf_op jit(solution)/shard_map/ppermute | solution.py:21
  120.3 1.4 copy-start.2
  121.7 24.3 %all-to-all-start = ((f32[8,1,64,768]{3,2,1,0:T(8,128)}), f32[8,1,64,768]{3,2,1,0:T(8,128)S(1)}, u32[]{:S(2)}, u32[]{:S(2)}) async-start(f32[8,1,64,768]{3,2,1,0:T(8,128)} %pad_maximum_fusion), calls=%async_computation | async-start | bytes 3145728 | tf_op jit(solution)/shard_map/all_to_all | solution.py:91

commit v13 on v8

--- a/solution.py
+++ b/solution.py
@@ -5,33 +5,36 @@
 
 
 def shift_scan(matrix, vector, axis, pair_axis):
-    highest = lax.Precision.HIGH
-    count, index = (lax.axis_size(axis), lax.axis_index(axis))
+    highest = lax.Precision.HIGHEST
+    count = lax.axis_size(axis)
     pair_count = lax.axis_size(pair_axis)
-    side = lax.axis_index(pair_axis) % 2
-    width = matrix.shape[1] // 2
+    part = lax.axis_index(pair_axis) % 4
+    width = matrix.shape[1] // 4
+    across = [(j, j ^ 2) for j in range(pair_count)]
     swap = [(j, j ^ 1) for j in range(pair_count)]
-    mine = lax.dynamic_slice_in_dim(matrix, side * width, width, axis=1)
+    quarters = [part, part ^ 2, part ^ 1, part ^ 3]
+    pieces = [lax.dynamic_slice_in_dim(matrix, k * width, width, axis=1) for k in quarters]
     distance = 1
     while distance < count:
         pairs = [(j, j + distance) for j in range(count - distance)]
         last = 2 * distance >= count
-        has = index >= distance
         got_vector = lax.ppermute(vector, axis, pairs)
         if not last:
-            got_half = lax.ppermute(mine, axis, pairs)
-        newer = jnp.einsum("sq,rq->sr", got_vector, matrix, precision=highest) + vector
-        vector = jnp.where(has, newer, vector)
+            got_part = lax.ppermute(pieces[0], axis, pairs)
+        newer = vector
+        for piece, k in zip(pieces, quarters):
+            front = lax.dynamic_slice_in_dim(got_vector, k * width, width, axis=1)
+            newer = newer + jnp.einsum("sq,rq->sr", front, piece, precision=highest)
+        vector = newer
         if not last:
-            own = jnp.dot(matrix, got_half, precision=highest)
-            other = lax.ppermute(own, pair_axis, swap)
-            joined = jnp.where(
-                side == 0,
-                jnp.concatenate([own, other], axis=1),
-                jnp.concatenate([other, own], axis=1),
-            )
-            matrix = jnp.where(has, joined, matrix)
-            mine = jnp.where(has, own, mine)
+            own = None
+            for piece, k in zip(pieces, quarters):
+                block = lax.dynamic_slice_in_dim(got_part, k * width, width, axis=0)
+                term = jnp.dot(piece, block, precision=highest)
+                own = term if own is None else own + term
+            far = lax.ppermute(own, pair_axis, across)
+            near = lax.ppermute(jnp.stack([own, far]), pair_axis, swap)
+            pieces = [own, far, near[0], near[1]]
         distance = distance * 2
     return vector
 

time: 202 us -> 189 us (0.936)
  waiting for transfers between devices: 81.6 us -> 63.6 us
  starting transfers between devices: 63.3 us -> 69.5 us
  other arithmetic: 4.46 us -> 0.28 us
  matrix products: 14 us -> 17.8 us
    ppermute x8 -> x12, waiting for transfers between devices: 52.7 us -> 39.2 us  [the longest x4 33 us: shift_scan(): got_part = lax.ppermute(pieces[0], axis, pairs)]
    ppermute x5, starting transfers between devices: 26.7 us -> 31.9 us  [shift_scan(): got_vector = lax.ppermute(vector, axis, pairs)]
    ppermute x5, waiting for transfers between devices: 7.99 us -> 3.39 us  [shift_scan(): got_vector = lax.ppermute(vector, axis, pairs)]
    select_n x3 -> x0, other arithmetic: 4.32 us -> none  [shift_scan(): matrix = jnp.where(has, joined, matrix)]
    dot_general x9 -> x36, matrix products: 9.95 us -> 13.7 us  [the longest x20 7.78 us: shift_scan(): newer = newer + jnp.einsum('sq,rq->sr', front, piece, precision=highest)]
    ppermute x8 -> x12, starting transfers between devices: 26.3 us -> 27.1 us  [the longest x4 22 us: shift_scan(): got_part = lax.ppermute(pieces[0], axis, pairs)]
  transfers between devices with their start and end apart: 15 -> 19, of which waited for: 10 -> 8; matrix products, arithmetic and copies ran while one was open for 6% -> 5% of each run, Pallas kernels for 0% -> 0%
where the time goes in v13:
time: 189 us; the launch traced here: 187 us
  starting transfers between devices  69.5 us (37%)
  waiting for transfers between devices  63.6 us (34%)
  blocking collectives  29 us (15%)
  matrix products  17.8 us (9%)
  local copies, waits for them, and re-layouts  5.04 us (3%)
  between operations  1.95 us (1%)
    ppermute x4, waiting for transfers between devices, shift_scan(): got_part = lax.ppermute(pieces[0], axis, pairs)  33 us
    ppermute x5, starting transfers between devices, shift_scan(): got_vector = lax.ppermute(vector, axis, pairs)  31.9 us
    all_to_all x2, blocking collectives, on_device_body(): lax.all_to_all(pieces, 'tm', 0, 0, tiled=True, axis_index_groups=groups)  29 us
    ppermute x4, starting transfers between devices, shift_scan(): got_part = lax.ppermute(pieces[0], axis, pairs)  22 us
    all_to_all x1, waiting for transfers between devices, on_device_body(): lax.all_to_all(jnp.broadcast_to(states[None], (scen_shards,) + states.sha...  12.8 us
    all_to_all x1, waiting for transfers between devices, on_device_body(): readings = lax.all_to_all(readings, 'scen', 1, 0, tiled=True)  8.09 us
    dot_general x20, matrix products, shift_scan(): newer = newer + jnp.einsum('sq,rq->sr', front, piece, precision=highest)  7.78 us
    ppermute x4, waiting for transfers between devices, shift_scan(): far = lax.ppermute(own, pair_axis, across)  6.18 us
  transfers between devices with their start and end apart: 19, of which 8 were waited for; matrix products, arithmetic and copies ran while one was open for 5% of the time, Pallas kernels for 0%

profile of v13, /device:TPU:24, one launch (start us, length us, event | category | flops | bytes accessed | tf_op | source)
XLA Modules:
  0.0 187.1 jit_solution(17540077060063953102)
XLA Ops:
  1.4 0.5 copy-done
  1.9 0.9 fusion.25
  3.1 0.7 copy-done.4
  3.8 1.1 convolution_add_fusion.4
  4.9 3.8 %collective-permute-start = (f32[64,512]{1,0:T(8,128)S(1)}, f32[64,512]{1,0:T(8,128)S(1)}, u32[]{:S(2)}, u32[]{:S(2)}) collective-permute-start(f32[64,512]{1,0:T(8,128)S(1)} %convolution_add_fusion.4), channel_id=1, source_target_pairs={{0,8},{8,16},{16,24},{24,32},{32,40},{40,48},{48,56},{56,64},{64,7... | collective-permute-start | bytes 393224 | tf_op jit(solution)/shard_map/ppermute | solution.py:21
  8.9 3.8 %collective-permute-start.2 = (f32[512,128]{1,0:T(8,128)S(1)}, f32[512,128]{1,0:T(8,128)S(1)}, u32[]{:S(2)}, u32[]{:S(2)}) collective-permute-start(f32[512,128]{1,0:T(8,128)S(1)} %constant_dynamic-slice_fusion.1), channel_id=1, source_target_pairs={{0,8},{8,16},{16,24},{24,32},{32,40},{40,48},{48,56},{56,64},{64,7... | collective-permute-start | bytes 786440 | tf_op jit(solution)/shard_map/ppermute | solution.py:23
  12.8 0.4 fusion.45
  13.2 0.4 fusion.49
  13.6 4.4 %collective-permute-done.2 = f32[512,128]{1,0:T(8,128)S(1)} collective-permute-done((f32[512,128]{1,0:T(8,128)S(1)}, f32[512,128]{1,0:T(8,128)S(1)}, u32[]{:S(2)}, u32[]{:S(2)}) %collective-permute-start.2) | collective-permute-done | bytes 262176 | tf_op jit(solution)/shard_map/ppermute | solution.py:23
  19.5 0.8 collective-permute-start.3
  20.4 0.4 fusion.53
  20.7 0.4 fusion.23
  21.2 6.4 %collective-permute-start.1 = (f32[64,512]{1,0:T(8,128)S(1)}, f32[64,512]{1,0:T(8,128)S(1)}, u32[]{:S(2)}, u32[]{:S(2)}) collective-permute-start(f32[64,512]{1,0:T(8,128)S(1)} %fusion.23), channel_id=1, source_target_pairs={{0,16},{8,24},{16,32},{24,40},{32,48},{40,56},{48,64},{56,72},{64,... | collective-permute-start | bytes 393224 | tf_op jit(solution)/shard_map/ppermute | solution.py:21
  27.7 6.1 %collective-permute-start.6 = (f32[512,128]{1,0:T(8,128)S(1)}, f32[512,128]{1,0:T(8,128)S(1)}, u32[]{:S(2)}, u32[]{:S(2)}) collective-permute-start(f32[512,128]{1,0:T(8,128)S(1)} %fusion.8), channel_id=1, source_target_pairs={{0,16},{8,24},{16,32},{24,40},{32,48},{40,56},{48,64},{56,72},{64,... | collective-permute-start | bytes 786440 | tf_op jit(solution)/shard_map/ppermute | solution.py:23
  33.8 0.4 fusion.95
  34.2 11.4 %collective-permute-done.6 = f32[512,128]{1,0:T(8,128)S(1)} collective-permute-done((f32[512,128]{1,0:T(8,128)S(1)}, f32[512,128]{1,0:T(8,128)S(1)}, u32[]{:S(2)}, u32[]{:S(2)}) %collective-permute-start.6) | collective-permute-done | bytes 262176 | tf_op jit(solution)/shard_map/ppermute | solution.py:23
  47.1 1.4 collective-permute-start.7
  48.5 0.4 fusion.32
  48.9 0.4 fusion.34
  49.3 0.4 fusion.20
  49.7 8.5 %collective-permute-start.5 = (f32[64,512]{1,0:T(8,128)S(1)}, f32[64,512]{1,0:T(8,128)S(1)}, u32[]{:S(2)}, u32[]{:S(2)}) collective-permute-start(f32[64,512]{1,0:T(8,128)S(1)} %fusion.20), channel_id=1, source_target_pairs={{0,32},{8,40},{16,48},{24,56},{32,64},{40,72},{48,80},{56,88},{64,... | collective-permute-start | bytes 393224 | tf_op jit(solution)/shard_map/ppermute | solution.py:21
  58.4 6.2 %collective-permute-start.10 = (f32[512,128]{1,0:T(8,128)S(1)}, f32[512,128]{1,0:T(8,128)S(1)}, u32[]{:S(2)}, u32[]{:S(2)}) collective-permute-start(f32[512,128]{1,0:T(8,128)S(1)} %fusion.6), channel_id=1, source_target_pairs={{0,32},{8,40},{16,48},{24,56},{32,64},{40,72},{48,80},{56,88},{64,... | collective-permute-start | bytes 786440 | tf_op jit(solution)/shard_map/ppermute | solution.py:23
  65.0 11.4 %collective-permute-done.10 = f32[512,128]{1,0:T(8,128)S(1)} collective-permute-done((f32[512,128]{1,0:T(8,128)S(1)}, f32[512,128]{1,0:T(8,128)S(1)}, u32[]{:S(2)}, u32[]{:S(2)}) %collective-permute-start.10) | collective-permute-done | bytes 262176 | tf_op jit(solution)/shard_map/ppermute | solution.py:23
  77.9 1.5 collective-permute-start.11
  79.9 0.4 fusion.38
  80.2 0.4 fusion.17
  80.7 7.2 %collective-permute-start.9 = (f32[64,512]{1,0:T(8,128)S(1)}, f32[64,512]{1,0:T(8,128)S(1)}, u32[]{:S(2)}, u32[]{:S(2)}) collective-permute-start(f32[64,512]{1,0:T(8,128)S(1)} %fusion.17), channel_id=1, source_target_pairs={{0,64},{8,72},{16,80},{24,88},{32,96},{40,104},{48,112},{56,120},{... | collective-permute-start | bytes 393224 | tf_op jit(solution)/shard_map/ppermute | solution.py:21
  88.0 5.9 %collective-permute-start.14 = (f32[512,128]{1,0:T(8,128)S(1)}, f32[512,128]{1,0:T(8,128)S(1)}, u32[]{:S(2)}, u32[]{:S(2)}) collective-permute-start(f32[512,128]{1,0:T(8,128)S(1)} %fusion.4), channel_id=1, source_target_pairs={{0,64},{8,72},{16,80},{24,88},{32,96},{40,104},{48,112},{56,120},{... | collective-permute-start | bytes 786440 | tf_op jit(solution)/shard_map/ppermute | solution.py:23
  94.3 5.8 %collective-permute-done.14 = f32[512,128]{1,0:T(8,128)S(1)} collective-permute-done((f32[512,128]{1,0:T(8,128)S(1)}, f32[512,128]{1,0:T(8,128)S(1)}, u32[]{:S(2)}, u32[]{:S(2)}) %collective-permute-start.14) | collective-permute-done | bytes 262176 | tf_op jit(solution)/shard_map/ppermute | solution.py:23
  101.6 1.0 collective-permute-start.15
  103.0 0.4 fusion.42
  103.4 6.2 %collective-permute-done.15 = f32[512,128]{1,0:T(8,128)S(1)} collective-permute-done((f32[512,128]{1,0:T(8,128)S(1)}, f32[512,128]{1,0:T(8,128)S(1)}, u32[]{:S(2)}, u32[]{:S(2)}) %collective-permute-start.15) | collective-permute-done | bytes 262176 | tf_op jit(solution)/shard_map/ppermute | solution.py:35
  109.7 0.4 fusion.14
  110.1 5.9 %collective-permute-start.13 = (f32[64,512]{1,0:T(8,128)S(1)}, f32[64,512]{1,0:T(8,128)S(1)}, u32[]{:S(2)}, u32[]{:S(2)}) collective-permute-start(f32[64,512]{1,0:T(8,128)S(1)} %fusion.14), channel_id=1, source_target_pairs={{0,128},{8,136},{16,144},{24,152},{32,160},{40,168},{48,176},{56,1... | collective-permute-start | bytes 393224 | tf_op jit(solution)/shard_map/ppermute | solution.py:21
  116.0 3.4 %collective-permute-done.13 = f32[64,512]{1,0:T(8,128)S(1)} collective-permute-done((f32[64,512]{1,0:T(8,128)S(1)}, f32[64,512]{1,0:T(8,128)S(1)}, u32[]{:S(2)}, u32[]{:S(2)}) %collective-permute-start.13) | collective-permute-done | bytes 131104 | tf_op jit(solution)/shard_map/ppermute | solution.py:21
  120.2 0.4 fusion.29
  120.6 0.4 fusion.11
  121.0 1.1 broadcast_in_dim.19
  122.1 5.0 %all-to-all-start = ((f32[8,1,64,512]{3,2,1,0:T(8,128)}), f32[8,1,64,512]{3,2,1,0:T(8,128)S(1)}, u32[]{:S(2)}, u32[]{:S(2)}) async-start(f32[8,1,64,512]{3,2,1,0:T(8,128)} %broadcast_in_dim.19), calls=%async_computation | async-start | bytes 2097152 | tf_op jit(solution)/shard_map/all_to_all | solution.py:90
  127.2 1.0 copy.13
  128.1 12.8 %all-to-all-done = f32[8,1,64,512]{3,2,1,0:T(8,128)S(1)} async-done(((f32[8,1,64,512]{3,2,1,0:T(8,128)}), f32[8,1,64,512]{3,2,1,0:T(8,128)S(1)}, u32[]{:S(2)}, u32[]{:S(2)}) %all-to-all-start) | async-done | bytes 1048608 | tf_op jit(solution)/shard_map/all_to_all | solution.py:90
  141.0 5.5 %all-to-all-start.1 = ((f32[64,8,256]{2,0,1:T(8,128)}), f32[64,8,256]{2,0,1:T(8,128)S(1)}, u32[]{:S(2)}, u32[]{:S(2)}) async-start(f32[64,8,256]{2,0,1:T(8,128)} %copy.13), calls=%async_computation.1 | async-start | bytes 1048576 | tf_op jit(solution)/shard_map/all_to_all | solution.py:87
  146.6 8.1 %all-to-all-done.1 = f32[64,8,256]{2,0,1:T(8,128)S(1)} async-done(((f32[64,8,256]{2,0,1:T(8,128)}), f32[64,8,256]{2,0,1:T(8,128)S(1)}, u32[]{:S(2)}, u32[]{:S(2)}) %all-to-all-start.1) | async-done | bytes 524320 | tf_op jit(solution)/shard_map/all_to_all | solution.py:87
  154.7 1.9 fusion
  156.6 15.8 %all_to_all.30 = f32[4,128,320]{1,2,0:T(8,128)S(1)} all-to-all(f32[4,128,320]{1,2,0:T(8,128)S(1)} %bitcast.96), channel_id=1, replica_groups={{0,64,128,192},{8,72,136,200},{16,80,144,208},{24,88,152,216},{32,96,16..., dimensions={0} | all-to-all | bytes 1310720 | tf_op jit(solution)/shard_map/all_to_all | solution.py:110
  172.6 13.2 %all_to_all.31 = f32[8,16,320]{2,1,0:T(8,128)S(1)} all-to-all(f32[8,16,320]{2,1,0:T(8,128)S(1)} %bitcast.104), channel_id=1, replica_groups={{0,8,16,24,32,40,48,56},{64,72,80,88,96,104,112,120},{128,136,144,152,1..., dimensions={0} | all-to-all | bytes 327680 | tf_op jit(solution)/shard_map/all_to_all | solution.py:110
  185.8 0.7 slice.49
  186.5 0.6 slice.48
  (60 shorter events, 9.6 us)
Async XLA Ops:
  0.6 1.2 copy-start
  1.9 0.9 copy-start.5
  1.9 1.2 copy-start.1
  2.8 1.0 copy-start.4
  4.9 7.9 %collective-permute-start = (f32[64,512]{1,0:T(8,128)S(1)}, f32[64,512]{1,0:T(8,128)S(1)}, u32[]{:S(2)}, u32[]{:S(2)}) collective-permute-start(f32[64,512]{1,0:T(8,128)S(1)} %convolution_add_fusion.4), channel_id=1, source_target_pairs={{0,8},{8,16},{16,24},{24,32},{32,40},{40,48},{48,56},{56,64},{64,7... | collective-permute-start | bytes 393224 | tf_op jit(solution)/shard_map/ppermute | solution.py:21
  8.9 9.1 %collective-permute-start.2 = (f32[512,128]{1,0:T(8,128)S(1)}, f32[512,128]{1,0:T(8,128)S(1)}, u32[]{:S(2)}, u32[]{:S(2)}) collective-permute-start(f32[512,128]{1,0:T(8,128)S(1)} %constant_dynamic-slice_fusion.1), channel_id=1, source_target_pairs={{0,8},{8,16},{16,24},{24,32},{32,40},{40,48},{48,56},{56,64},{64,7... | collective-permute-start | bytes 786440 | tf_op jit(solution)/shard_map/ppermute | solution.py:23
  19.5 8.0 %collective-permute-start.3 = (f32[512,128]{1,0:T(8,128)S(1)}, f32[512,128]{1,0:T(8,128)S(1)}, u32[]{:S(2)}, u32[]{:S(2)}) collective-permute-start(f32[512,128]{1,0:T(8,128)S(1)} %fusion.8), channel_id=1, source_target_pairs={{0,2},{1,3},{2,0},{3,1},{4,6},{5,7},{6,4},{7,5},{8,10},{9,11},{10,... | collective-permute-start | bytes 786440 | tf_op jit(solution)/shard_map/ppermute | solution.py:35
  21.2 12.6 %collective-permute-start.1 = (f32[64,512]{1,0:T(8,128)S(1)}, f32[64,512]{1,0:T(8,128)S(1)}, u32[]{:S(2)}, u32[]{:S(2)}) collective-permute-start(f32[64,512]{1,0:T(8,128)S(1)} %fusion.23), channel_id=1, source_target_pairs={{0,16},{8,24},{16,32},{24,40},{32,48},{40,56},{48,64},{56,72},{64,... | collective-permute-start | bytes 393224 | tf_op jit(solution)/shard_map/ppermute | solution.py:21
  27.6 18.4 %collective-permute-start.4 = (f32[2,512,128]{2,1,0:T(8,128)S(1)}, f32[2,512,128]{2,1,0:T(8,128)S(1)}, u32[]{:S(2)}, u32[]{:S(2)}) collective-permute-start(f32[2,512,128]{2,1,0:T(8,128)S(1)} %pad_maximum_fusion), channel_id=1, source_target_pairs={{0,1},{1,0},{2,3},{3,2},{4,5},{5,4},{6,7},{7,6},{8,9},{9,8},{10,11... | collective-permute-start | bytes 1572872 | tf_op jit(solution)/shard_map/ppermute | solution.py:36
  27.7 17.9 %collective-permute-start.6 = (f32[512,128]{1,0:T(8,128)S(1)}, f32[512,128]{1,0:T(8,128)S(1)}, u32[]{:S(2)}, u32[]{:S(2)}) collective-permute-start(f32[512,128]{1,0:T(8,128)S(1)} %fusion.8), channel_id=1, source_target_pairs={{0,16},{8,24},{16,32},{24,40},{32,48},{40,56},{48,64},{56,72},{64,... | collective-permute-start | bytes 786440 | tf_op jit(solution)/shard_map/ppermute | solution.py:23
  47.1 11.1 %collective-permute-start.7 = (f32[512,128]{1,0:T(8,128)S(1)}, f32[512,128]{1,0:T(8,128)S(1)}, u32[]{:S(2)}, u32[]{:S(2)}) collective-permute-start(f32[512,128]{1,0:T(8,128)S(1)} %fusion.6), channel_id=1, source_target_pairs={{0,2},{1,3},{2,0},{3,1},{4,6},{5,7},{6,4},{7,5},{8,10},{9,11},{10,... | collective-permute-start | bytes 786440 | tf_op jit(solution)/shard_map/ppermute | solution.py:35
  49.7 14.9 %collective-permute-start.5 = (f32[64,512]{1,0:T(8,128)S(1)}, f32[64,512]{1,0:T(8,128)S(1)}, u32[]{:S(2)}, u32[]{:S(2)}) collective-permute-start(f32[64,512]{1,0:T(8,128)S(1)} %fusion.20), channel_id=1, source_target_pairs={{0,32},{8,40},{16,48},{24,56},{32,64},{40,72},{48,80},{56,88},{64,... | collective-permute-start | bytes 393224 | tf_op jit(solution)/shard_map/ppermute | solution.py:21
  58.3 18.5 %collective-permute-start.8 = (f32[2,512,128]{2,1,0:T(8,128)S(1)}, f32[2,512,128]{2,1,0:T(8,128)S(1)}, u32[]{:S(2)}, u32[]{:S(2)}) collective-permute-start(f32[2,512,128]{2,1,0:T(8,128)S(1)} %pad_maximum_fusion.1), channel_id=1, source_target_pairs={{0,1},{1,0},{2,3},{3,2},{4,5},{5,4},{6,7},{7,6},{8,9},{9,8},{10,11... | collective-permute-start | bytes 1572872 | tf_op jit(solution)/shard_map/ppermute | solution.py:36
  58.4 18.0 %collective-permute-start.10 = (f32[512,128]{1,0:T(8,128)S(1)}, f32[512,128]{1,0:T(8,128)S(1)}, u32[]{:S(2)}, u32[]{:S(2)}) collective-permute-start(f32[512,128]{1,0:T(8,128)S(1)} %fusion.6), channel_id=1, source_target_pairs={{0,32},{8,40},{16,48},{24,56},{32,64},{40,72},{48,80},{56,88},{64,... | collective-permute-start | bytes 786440 | tf_op jit(solution)/shard_map/ppermute | solution.py:23
  77.9 9.9 %collective-permute-start.11 = (f32[512,128]{1,0:T(8,128)S(1)}, f32[512,128]{1,0:T(8,128)S(1)}, u32[]{:S(2)}, u32[]{:S(2)}) collective-permute-start(f32[512,128]{1,0:T(8,128)S(1)} %fusion.4), channel_id=1, source_target_pairs={{0,2},{1,3},{2,0},{3,1},{4,6},{5,7},{6,4},{7,5},{8,10},{9,11},{10,... | collective-permute-start | bytes 786440 | tf_op jit(solution)/shard_map/ppermute | solution.py:35
  80.7 13.3 %collective-permute-start.9 = (f32[64,512]{1,0:T(8,128)S(1)}, f32[64,512]{1,0:T(8,128)S(1)}, u32[]{:S(2)}, u32[]{:S(2)}) collective-permute-start(f32[64,512]{1,0:T(8,128)S(1)} %fusion.17), channel_id=1, source_target_pairs={{0,64},{8,72},{16,80},{24,88},{32,96},{40,104},{48,112},{56,120},{... | collective-permute-start | bytes 393224 | tf_op jit(solution)/shard_map/ppermute | solution.py:21
  87.9 12.6 %collective-permute-start.12 = (f32[2,512,128]{2,1,0:T(8,128)S(1)}, f32[2,512,128]{2,1,0:T(8,128)S(1)}, u32[]{:S(2)}, u32[]{:S(2)}) collective-permute-start(f32[2,512,128]{2,1,0:T(8,128)S(1)} %pad_maximum_fusion.2), channel_id=1, source_target_pairs={{0,1},{1,0},{2,3},{3,2},{4,5},{5,4},{6,7},{7,6},{8,9},{9,8},{10,11... | collective-permute-start | bytes 1572872 | tf_op jit(solution)/shard_map/ppermute | solution.py:36
  88.0 12.1 %collective-permute-start.14 = (f32[512,128]{1,0:T(8,128)S(1)}, f32[512,128]{1,0:T(8,128)S(1)}, u32[]{:S(2)}, u32[]{:S(2)}) collective-permute-start(f32[512,128]{1,0:T(8,128)S(1)} %fusion.4), channel_id=1, source_target_pairs={{0,64},{8,72},{16,80},{24,88},{32,96},{40,104},{48,112},{56,120},{... | collective-permute-start | bytes 786440 | tf_op jit(solution)/shard_map/ppermute | solution.py:23
  101.6 7.9 %collective-permute-start.15 = (f32[512,128]{1,0:T(8,128)S(1)}, f32[512,128]{1,0:T(8,128)S(1)}, u32[]{:S(2)}, u32[]{:S(2)}) collective-permute-start(f32[512,128]{1,0:T(8,128)S(1)} %fusion.2), channel_id=1, source_target_pairs={{0,2},{1,3},{2,0},{3,1},{4,6},{5,7},{6,4},{7,5},{8,10},{9,11},{10,... | collective-permute-start | bytes 786440 | tf_op jit(solution)/shard_map/ppermute | solution.py:35
  109.6 10.2 %collective-permute-start.16 = (f32[2,512,128]{2,1,0:T(8,128)S(1)}, f32[2,512,128]{2,1,0:T(8,128)S(1)}, u32[]{:S(2)}, u32[]{:S(2)}) collective-permute-start(f32[2,512,128]{2,1,0:T(8,128)S(1)} %pad_maximum_fusion.3), channel_id=1, source_target_pairs={{0,1},{1,0},{2,3},{3,2},{4,5},{5,4},{6,7},{7,6},{8,9},{9,8},{10,11... | collective-permute-start | bytes 1572872 | tf_op jit(solution)/shard_map/ppermute | solution.py:36
  110.1 9.3 %collective-permute-start.13 = (f32[64,512]{1,0:T(8,128)S(1)}, f32[64,512]{1,0:T(8,128)S(1)}, u32[]{:S(2)}, u32[]{:S(2)}) collective-permute-start(f32[64,512]{1,0:T(8,128)S(1)} %fusion.14), channel_id=1, source_target_pairs={{0,128},{8,136},{16,144},{24,152},{32,160},{40,168},{48,176},{56,1... | collective-permute-start | bytes 393224 | tf_op jit(solution)/shard_map/ppermute | solution.py:21
  121.0 1.1 copy-start.2
  122.1 5.0 %copy-start.3 = (bf16[1,64,2048]{2,1,0:T(8,128)(2,1)S(1)}, bf16[1,64,2048]{2,1,0:T(8,128)(2,1)}, u32[]{:S(2)}) copy-start(bf16[1,64,2048]{2,1,0:T(8,128)(2,1)} %param.11) | copy-start | bytes 786436
  122.1 18.8 %all-to-all-start = ((f32[8,1,64,512]{3,2,1,0:T(8,128)}), f32[8,1,64,512]{3,2,1,0:T(8,128)S(1)}, u32[]{:S(2)}, u32[]{:S(2)}) async-start(f32[8,1,64,512]{3,2,1,0:T(8,128)} %broadcast_in_dim.19), calls=%async_computation | async-start | bytes 2097152 | tf_op jit(solution)/shard_map/all_to_all | solution.py:90
  141.0 13.7 %all-to-all-start.1 = ((f32[64,8,256]{2,0,1:T(8,128)}), f32[64,8,256]{2,0,1:T(8,128)S(1)}, u32[]{:S(2)}, u32[]{:S(2)}) async-start(f32[64,8,256]{2,0,1:T(8,128)} %copy.13), calls=%async_computation.1 | async-start | bytes 1048576 | tf_op jit(solution)/shard_map/all_to_all | solution.py:87

commit v14 on v13

--- a/solution.py
+++ b/solution.py
@@ -30,7 +30,7 @@
             own = None
             for piece, k in zip(pieces, quarters):
                 block = lax.dynamic_slice_in_dim(got_part, k * width, width, axis=0)
-                term = jnp.dot(piece, block, precision=highest)
+                term = jnp.dot(piece, block, precision=lax.Precision.HIGH)
                 own = term if own is None else own + term
             far = lax.ppermute(own, pair_axis, across)
             near = lax.ppermute(jnp.stack([own, far]), pair_axis, swap)
@@ -83,15 +83,18 @@
     sensors = observed.shape[2]
     cross_cols = sensors // scen_shards
     gram_cols = modes // scen_shards
-    readings = observed.astype(jnp.float32).reshape(step_count * local_scen, scen_shards, cross_cols)
-    readings = lax.all_to_all(readings, "scen", 1, 0, tiled=True)
-    readings = readings.reshape(scen_shards, step_count, local_scen, cross_cols)
-    readings = readings.transpose(1, 0, 2, 3).reshape(step_count, scen_shards * local_scen, cross_cols)
-    every = lax.all_to_all(
-        jnp.broadcast_to(states[None], (scen_shards,) + states.shape), "scen", 0, 0, tiled=True
+    readings = observed.astype(jnp.float32).reshape(step_count, local_scen, scen_shards, cross_cols)
+    readings = readings.transpose(2, 0, 1, 3)
+    payload = jnp.concatenate(
+        [jnp.broadcast_to(states[None], (scen_shards,) + states.shape), readings], axis=3
     )
-    every = every.reshape(scen_shards, step_count, local_scen, modes).transpose(1, 0, 2, 3)
-    every = every.reshape(step_count, scen_shards * local_scen, modes)
+    received = lax.all_to_all(payload, "scen", 0, 0, tiled=True)
+    received = received.reshape(scen_shards, step_count, local_scen, modes + cross_cols)
+    received = received.transpose(1, 0, 2, 3).reshape(
+        step_count, scen_shards * local_scen, modes + cross_cols
+    )
+    every = received[:, :, :modes]
+    readings = received[:, :, modes:]
     column = lax.axis_index("scen") * gram_cols
     right = jnp.concatenate(
         [lax.dynamic_slice_in_dim(every, column, gram_cols, axis=2), readings], axis=2

time: 189 us -> 178 us (0.942)
  starting transfers between devices: 69.5 us -> 63.9 us
  local copies, waits for them, and re-layouts: 5.04 us -> 2.62 us
  waiting for transfers between devices: 63.6 us -> 61.6 us
    all_to_all x2 -> x1, starting transfers between devices: 10.5 us -> 4.88 us  [on_device_body(): received = lax.all_to_all(payload, 'scen', 0, 0, tiled=True)]
    all_to_all x2 -> x1, waiting for transfers between devices: 20.9 us -> 19.5 us  [on_device_body(): received = lax.all_to_all(payload, 'scen', 0, 0, tiled=True)]
  transfers between devices with their start and end apart: 19 -> 18, of which waited for: 8 -> 7; matrix products, arithmetic and copies ran while one was open for 5% -> 4% of each run, Pallas kernels for 0% -> 0%
where the time goes in v14:
time: 178 us; the launch traced here: 177 us
  starting transfers between devices  63.9 us (36%)
  waiting for transfers between devices  61.6 us (35%)
  blocking collectives  28.9 us (16%)
  matrix products  16 us (9%)
  local copies, waits for them, and re-layouts  2.62 us (1%)
  between operations  2.1 us (1%)
    ppermute x4, waiting for transfers between devices, shift_scan(): got_part = lax.ppermute(pieces[0], axis, pairs)  32.8 us
    ppermute x5, starting transfers between devices, shift_scan(): got_vector = lax.ppermute(vector, axis, pairs)  31.9 us
    all_to_all x2, blocking collectives, on_device_body(): lax.all_to_all(pieces, 'tm', 0, 0, tiled=True, axis_index_groups=groups)  28.9 us
    ppermute x4, starting transfers between devices, shift_scan(): got_part = lax.ppermute(pieces[0], axis, pairs)  22.2 us
    all_to_all x1, waiting for transfers between devices, on_device_body(): received = lax.all_to_all(payload, 'scen', 0, 0, tiled=True)  19.5 us
    dot_general x20, matrix products, shift_scan(): newer = newer + jnp.einsum('sq,rq->sr', front, piece, precision=highest)  7.78 us
    ppermute x4, waiting for transfers between devices, shift_scan(): far = lax.ppermute(own, pair_axis, across)  6.17 us
    all_to_all x1, starting transfers between devices, on_device_body(): received = lax.all_to_all(payload, 'scen', 0, 0, tiled=True)  4.88 us
  transfers between devices with their start and end apart: 18, of which 7 were waited for; matrix products, arithmetic and copies ran while one was open for 4% of the time, Pallas kernels for 0%

profile of v14, /device:TPU:24, one launch (start us, length us, event | category | flops | bytes accessed | tf_op | source)
XLA Modules:
  0.0 176.8 jit_solution(8049998448418766138)
XLA Ops:
  1.5 0.4 copy-done
  1.9 0.9 fusion.26
  3.0 1.1 convolution_add_fusion.4
  4.1 3.8 %collective-permute-start = (f32[64,512]{1,0:T(8,128)S(1)}, f32[64,512]{1,0:T(8,128)S(1)}, u32[]{:S(2)}, u32[]{:S(2)}) collective-permute-start(f32[64,512]{1,0:T(8,128)S(1)} %convolution_add_fusion.4), channel_id=1, source_target_pairs={{0,8},{8,16},{16,24},{24,32},{32,40},{40,48},{48,56},{56,64},{64,7... | collective-permute-start | bytes 393224 | tf_op jit(solution)/shard_map/ppermute | solution.py:21
  8.1 3.8 %collective-permute-start.2 = (f32[512,128]{1,0:T(8,128)S(1)}, f32[512,128]{1,0:T(8,128)S(1)}, u32[]{:S(2)}, u32[]{:S(2)}) collective-permute-start(f32[512,128]{1,0:T(8,128)S(1)} %constant_dynamic-slice_fusion.1), channel_id=1, source_target_pairs={{0,8},{8,16},{16,24},{24,32},{32,40},{40,48},{48,56},{56,64},{64,7... | collective-permute-start | bytes 786440 | tf_op jit(solution)/shard_map/ppermute | solution.py:23
  12.0 0.4 fusion.46
  12.4 0.4 fusion.50
  12.8 4.4 %collective-permute-done.2 = f32[512,128]{1,0:T(8,128)S(1)} collective-permute-done((f32[512,128]{1,0:T(8,128)S(1)}, f32[512,128]{1,0:T(8,128)S(1)}, u32[]{:S(2)}, u32[]{:S(2)}) %collective-permute-start.2) | collective-permute-done | bytes 262176 | tf_op jit(solution)/shard_map/ppermute | solution.py:23
  18.3 0.8 collective-permute-start.3
  19.1 0.4 fusion.54
  19.5 0.4 fusion.23
  19.9 6.4 %collective-permute-start.1 = (f32[64,512]{1,0:T(8,128)S(1)}, f32[64,512]{1,0:T(8,128)S(1)}, u32[]{:S(2)}, u32[]{:S(2)}) collective-permute-start(f32[64,512]{1,0:T(8,128)S(1)} %fusion.23), channel_id=1, source_target_pairs={{0,16},{8,24},{16,32},{24,40},{32,48},{40,56},{48,64},{56,72},{64,... | collective-permute-start | bytes 393224 | tf_op jit(solution)/shard_map/ppermute | solution.py:21
  26.5 6.1 %collective-permute-start.6 = (f32[512,128]{1,0:T(8,128)S(1)}, f32[512,128]{1,0:T(8,128)S(1)}, u32[]{:S(2)}, u32[]{:S(2)}) collective-permute-start(f32[512,128]{1,0:T(8,128)S(1)} %fusion.8), channel_id=1, source_target_pairs={{0,16},{8,24},{16,32},{24,40},{32,48},{40,56},{48,64},{56,72},{64,... | collective-permute-start | bytes 786440 | tf_op jit(solution)/shard_map/ppermute | solution.py:23
  32.6 0.4 fusion.96
  33.0 11.4 %collective-permute-done.6 = f32[512,128]{1,0:T(8,128)S(1)} collective-permute-done((f32[512,128]{1,0:T(8,128)S(1)}, f32[512,128]{1,0:T(8,128)S(1)}, u32[]{:S(2)}, u32[]{:S(2)}) %collective-permute-start.6) | collective-permute-done | bytes 262176 | tf_op jit(solution)/shard_map/ppermute | solution.py:23
  45.5 1.4 collective-permute-start.7
  46.9 0.4 fusion.33
  47.3 0.4 fusion.35
  47.7 0.4 fusion.20
  48.1 8.5 %collective-permute-start.5 = (f32[64,512]{1,0:T(8,128)S(1)}, f32[64,512]{1,0:T(8,128)S(1)}, u32[]{:S(2)}, u32[]{:S(2)}) collective-permute-start(f32[64,512]{1,0:T(8,128)S(1)} %fusion.20), channel_id=1, source_target_pairs={{0,32},{8,40},{16,48},{24,56},{32,64},{40,72},{48,80},{56,88},{64,... | collective-permute-start | bytes 393224 | tf_op jit(solution)/shard_map/ppermute | solution.py:21
  56.8 6.2 %collective-permute-start.10 = (f32[512,128]{1,0:T(8,128)S(1)}, f32[512,128]{1,0:T(8,128)S(1)}, u32[]{:S(2)}, u32[]{:S(2)}) collective-permute-start(f32[512,128]{1,0:T(8,128)S(1)} %fusion.6), channel_id=1, source_target_pairs={{0,32},{8,40},{16,48},{24,56},{32,64},{40,72},{48,80},{56,88},{64,... | collective-permute-start | bytes 786440 | tf_op jit(solution)/shard_map/ppermute | solution.py:23
  63.0 0.4 fusion.91
  63.4 11.4 %collective-permute-done.10 = f32[512,128]{1,0:T(8,128)S(1)} collective-permute-done((f32[512,128]{1,0:T(8,128)S(1)}, f32[512,128]{1,0:T(8,128)S(1)}, u32[]{:S(2)}, u32[]{:S(2)}) %collective-permute-start.10) | collective-permute-done | bytes 262176 | tf_op jit(solution)/shard_map/ppermute | solution.py:23
  75.9 1.3 collective-permute-start.11
  77.2 0.4 fusion.37
  77.6 0.4 fusion.39
  78.0 0.4 fusion.17
  78.4 7.2 %collective-permute-start.9 = (f32[64,512]{1,0:T(8,128)S(1)}, f32[64,512]{1,0:T(8,128)S(1)}, u32[]{:S(2)}, u32[]{:S(2)}) collective-permute-start(f32[64,512]{1,0:T(8,128)S(1)} %fusion.17), channel_id=1, source_target_pairs={{0,64},{8,72},{16,80},{24,88},{32,96},{40,104},{48,112},{56,120},{... | collective-permute-start | bytes 393224 | tf_op jit(solution)/shard_map/ppermute | solution.py:21
  85.8 6.1 %collective-permute-start.14 = (f32[512,128]{1,0:T(8,128)S(1)}, f32[512,128]{1,0:T(8,128)S(1)}, u32[]{:S(2)}, u32[]{:S(2)}) collective-permute-start(f32[512,128]{1,0:T(8,128)S(1)} %fusion.4), channel_id=1, source_target_pairs={{0,64},{8,72},{16,80},{24,88},{32,96},{40,104},{48,112},{56,120},{... | collective-permute-start | bytes 786440 | tf_op jit(solution)/shard_map/ppermute | solution.py:23
  92.0 0.4 fusion.86
  92.4 5.5 %collective-permute-done.14 = f32[512,128]{1,0:T(8,128)S(1)} collective-permute-done((f32[512,128]{1,0:T(8,128)S(1)}, f32[512,128]{1,0:T(8,128)S(1)}, u32[]{:S(2)}, u32[]{:S(2)}) %collective-permute-start.14) | collective-permute-done | bytes 262176 | tf_op jit(solution)/shard_map/ppermute | solution.py:23
  99.0 1.0 collective-permute-start.15
  100.3 0.4 fusion.43
  100.7 6.2 %collective-permute-done.15 = f32[512,128]{1,0:T(8,128)S(1)} collective-permute-done((f32[512,128]{1,0:T(8,128)S(1)}, f32[512,128]{1,0:T(8,128)S(1)}, u32[]{:S(2)}, u32[]{:S(2)}) %collective-permute-start.15) | collective-permute-done | bytes 262176 | tf_op jit(solution)/shard_map/ppermute | solution.py:35
  107.0 0.4 fusion.14
  107.4 5.9 %collective-permute-start.13 = (f32[64,512]{1,0:T(8,128)S(1)}, f32[64,512]{1,0:T(8,128)S(1)}, u32[]{:S(2)}, u32[]{:S(2)}) collective-permute-start(f32[64,512]{1,0:T(8,128)S(1)} %fusion.14), channel_id=1, source_target_pairs={{0,128},{8,136},{16,144},{24,152},{32,160},{40,168},{48,176},{56,1... | collective-permute-start | bytes 393224 | tf_op jit(solution)/shard_map/ppermute | solution.py:21
  113.6 3.2 %collective-permute-done.13 = f32[64,512]{1,0:T(8,128)S(1)} collective-permute-done((f32[64,512]{1,0:T(8,128)S(1)}, f32[64,512]{1,0:T(8,128)S(1)}, u32[]{:S(2)}, u32[]{:S(2)}) %collective-permute-start.13) | collective-permute-done | bytes 131104 | tf_op jit(solution)/shard_map/ppermute | solution.py:21
  117.1 0.4 fusion.31
  117.5 0.4 fusion.30
  117.9 0.4 fusion.11
  118.5 1.3 pad_maximum_fusion
  119.7 4.9 %all-to-all-start = ((f32[8,1,64,768]{3,2,1,0:T(8,128)}), f32[8,1,64,768]{3,2,1,0:T(8,128)S(1)}, u32[]{:S(2)}, u32[]{:S(2)}) async-start(f32[8,1,64,768]{3,2,1,0:T(8,128)} %pad_maximum_fusion), calls=%async_computation | async-start | bytes 3145728 | tf_op jit(solution)/shard_map/all_to_all | solution.py:91
  124.6 19.5 %all-to-all-done = f32[8,1,64,768]{3,2,1,0:T(8,128)S(1)} async-done(((f32[8,1,64,768]{3,2,1,0:T(8,128)}), f32[8,1,64,768]{3,2,1,0:T(8,128)S(1)}, u32[]{:S(2)}, u32[]{:S(2)}) %all-to-all-start) | async-done | bytes 1572896 | tf_op jit(solution)/shard_map/all_to_all | solution.py:91
  144.4 1.9 %fusion = f32[40,4,8,128]{3,2,1,0:T(8,128)S(1)} fusion(f32[1,512,256]{2,1,0:T(8,128)S(1)} %slice.57, f32[1,512,64]{2,1,0:T(8,128)S(1)} %constant_dynamic-slice_fusion, f32[1,512,768]{2,1,0:T(8,128)S(1)} %bitcast.94), kind=kOutput, calls=%fused_computation.2 | convolution fusion | flops 1006960640 | bytes 2490368 | tf_op jit(solution)/shard_map/tsr,tso->ro/dot_general | solution.py:102
  146.4 15.7 %all_to_all.15 = f32[4,128,320]{1,2,0:T(8,128)S(1)} all-to-all(f32[4,128,320]{1,2,0:T(8,128)S(1)} %bitcast.98), channel_id=1, replica_groups={{0,64,128,192},{8,72,136,200},{16,80,144,208},{24,88,152,216},{32,96,16..., dimensions={0} | all-to-all | bytes 1310720 | tf_op jit(solution)/shard_map/all_to_all | solution.py:113
  162.3 13.2 %all_to_all.16 = f32[8,16,320]{2,1,0:T(8,128)S(1)} all-to-all(f32[8,16,320]{2,1,0:T(8,128)S(1)} %bitcast.105), channel_id=1, replica_groups={{0,8,16,24,32,40,48,56},{64,72,80,88,96,104,112,120},{128,136,144,152,1..., dimensions={0} | all-to-all | bytes 327680 | tf_op jit(solution)/shard_map/all_to_all | solution.py:113
  175.5 0.7 slice.59
  176.2 0.6 slice.58
  (62 shorter events, 6.7 us)
Async XLA Ops:
  0.6 1.2 copy-start
  0.6 2.1 %copy-start.5 = (bf16[1,64,256]{2,1,0:T(8,128)(2,1)S(1)}, bf16[1,64,256]{2,1,0:T(8,128)(2,1)}, u32[]{:S(2)}) copy-start(bf16[1,64,256]{2,1,0:T(8,128)(2,1)} %param.9) | copy-start | bytes 98308
  0.7 2.3 %copy-start.1 = (f32[1,512,512]{2,1,0:T(8,128)S(1)}, f32[1,512,512]{2,1,0:T(8,128)}, u32[]{:S(2)}) copy-start(f32[1,512,512]{2,1,0:T(8,128)} %param.6) | copy-start | bytes 3145732
  0.7 2.3 %copy-start.4 = (f32[64,512]{1,0:T(8,128)S(1)}, f32[64,512]{1,0:T(8,128)}, u32[]{:S(2)}) copy-start(f32[64,512]{1,0:T(8,128)} %param.10) | copy-start | bytes 393220
  4.1 7.9 %collective-permute-start = (f32[64,512]{1,0:T(8,128)S(1)}, f32[64,512]{1,0:T(8,128)S(1)}, u32[]{:S(2)}, u32[]{:S(2)}) collective-permute-start(f32[64,512]{1,0:T(8,128)S(1)} %convolution_add_fusion.4), channel_id=1, source_target_pairs={{0,8},{8,16},{16,24},{24,32},{32,40},{40,48},{48,56},{56,64},{64,7... | collective-permute-start | bytes 393224 | tf_op jit(solution)/shard_map/ppermute | solution.py:21
  8.1 9.1 %collective-permute-start.2 = (f32[512,128]{1,0:T(8,128)S(1)}, f32[512,128]{1,0:T(8,128)S(1)}, u32[]{:S(2)}, u32[]{:S(2)}) collective-permute-start(f32[512,128]{1,0:T(8,128)S(1)} %constant_dynamic-slice_fusion.1), channel_id=1, source_target_pairs={{0,8},{8,16},{16,24},{24,32},{32,40},{40,48},{48,56},{56,64},{64,7... | collective-permute-start | bytes 786440 | tf_op jit(solution)/shard_map/ppermute | solution.py:23
  18.3 8.0 %collective-permute-start.3 = (f32[512,128]{1,0:T(8,128)S(1)}, f32[512,128]{1,0:T(8,128)S(1)}, u32[]{:S(2)}, u32[]{:S(2)}) collective-permute-start(f32[512,128]{1,0:T(8,128)S(1)} %fusion.8), channel_id=1, source_target_pairs={{0,2},{1,3},{2,0},{3,1},{4,6},{5,7},{6,4},{7,5},{8,10},{9,11},{10,... | collective-permute-start | bytes 786440 | tf_op jit(solution)/shard_map/ppermute | solution.py:35
  19.9 12.6 %collective-permute-start.1 = (f32[64,512]{1,0:T(8,128)S(1)}, f32[64,512]{1,0:T(8,128)S(1)}, u32[]{:S(2)}, u32[]{:S(2)}) collective-permute-start(f32[64,512]{1,0:T(8,128)S(1)} %fusion.23), channel_id=1, source_target_pairs={{0,16},{8,24},{16,32},{24,40},{32,48},{40,56},{48,64},{56,72},{64,... | collective-permute-start | bytes 393224 | tf_op jit(solution)/shard_map/ppermute | solution.py:21
  26.4 18.3 %collective-permute-start.4 = (f32[2,512,128]{2,1,0:T(8,128)S(1)}, f32[2,512,128]{2,1,0:T(8,128)S(1)}, u32[]{:S(2)}, u32[]{:S(2)}) collective-permute-start(f32[2,512,128]{2,1,0:T(8,128)S(1)} %pad_maximum_fusion.1), channel_id=1, source_target_pairs={{0,1},{1,0},{2,3},{3,2},{4,5},{5,4},{6,7},{7,6},{8,9},{9,8},{10,11... | collective-permute-start | bytes 1572872 | tf_op jit(solution)/shard_map/ppermute | solution.py:36
  26.5 17.9 %collective-permute-start.6 = (f32[512,128]{1,0:T(8,128)S(1)}, f32[512,128]{1,0:T(8,128)S(1)}, u32[]{:S(2)}, u32[]{:S(2)}) collective-permute-start(f32[512,128]{1,0:T(8,128)S(1)} %fusion.8), channel_id=1, source_target_pairs={{0,16},{8,24},{16,32},{24,40},{32,48},{40,56},{48,64},{56,72},{64,... | collective-permute-start | bytes 786440 | tf_op jit(solution)/shard_map/ppermute | solution.py:23
  45.5 11.1 %collective-permute-start.7 = (f32[512,128]{1,0:T(8,128)S(1)}, f32[512,128]{1,0:T(8,128)S(1)}, u32[]{:S(2)}, u32[]{:S(2)}) collective-permute-start(f32[512,128]{1,0:T(8,128)S(1)} %fusion.6), channel_id=1, source_target_pairs={{0,2},{1,3},{2,0},{3,1},{4,6},{5,7},{6,4},{7,5},{8,10},{9,11},{10,... | collective-permute-start | bytes 786440 | tf_op jit(solution)/shard_map/ppermute | solution.py:35
  48.1 14.9 %collective-permute-start.5 = (f32[64,512]{1,0:T(8,128)S(1)}, f32[64,512]{1,0:T(8,128)S(1)}, u32[]{:S(2)}, u32[]{:S(2)}) collective-permute-start(f32[64,512]{1,0:T(8,128)S(1)} %fusion.20), channel_id=1, source_target_pairs={{0,32},{8,40},{16,48},{24,56},{32,64},{40,72},{48,80},{56,88},{64,... | collective-permute-start | bytes 393224 | tf_op jit(solution)/shard_map/ppermute | solution.py:21
  56.7 18.4 %collective-permute-start.8 = (f32[2,512,128]{2,1,0:T(8,128)S(1)}, f32[2,512,128]{2,1,0:T(8,128)S(1)}, u32[]{:S(2)}, u32[]{:S(2)}) collective-permute-start(f32[2,512,128]{2,1,0:T(8,128)S(1)} %pad_maximum_fusion.2), channel_id=1, source_target_pairs={{0,1},{1,0},{2,3},{3,2},{4,5},{5,4},{6,7},{7,6},{8,9},{9,8},{10,11... | collective-permute-start | bytes 1572872 | tf_op jit(solution)/shard_map/ppermute | solution.py:36
  56.8 18.0 %collective-permute-start.10 = (f32[512,128]{1,0:T(8,128)S(1)}, f32[512,128]{1,0:T(8,128)S(1)}, u32[]{:S(2)}, u32[]{:S(2)}) collective-permute-start(f32[512,128]{1,0:T(8,128)S(1)} %fusion.6), channel_id=1, source_target_pairs={{0,32},{8,40},{16,48},{24,56},{32,64},{40,72},{48,80},{56,88},{64,... | collective-permute-start | bytes 786440 | tf_op jit(solution)/shard_map/ppermute | solution.py:23
  75.9 16.0 %copy-start.3 = (bf16[1,64,2048]{2,1,0:T(8,128)(2,1)S(1)}, bf16[1,64,2048]{2,1,0:T(8,128)(2,1)}, u32[]{:S(2)}) copy-start(bf16[1,64,2048]{2,1,0:T(8,128)(2,1)} %param.11) | copy-start | bytes 786436
  75.9 9.8 %collective-permute-start.11 = (f32[512,128]{1,0:T(8,128)S(1)}, f32[512,128]{1,0:T(8,128)S(1)}, u32[]{:S(2)}, u32[]{:S(2)}) collective-permute-start(f32[512,128]{1,0:T(8,128)S(1)} %fusion.4), channel_id=1, source_target_pairs={{0,2},{1,3},{2,0},{3,1},{4,6},{5,7},{6,4},{7,5},{8,10},{9,11},{10,... | collective-permute-start | bytes 786440 | tf_op jit(solution)/shard_map/ppermute | solution.py:35
  78.4 13.6 %collective-permute-start.9 = (f32[64,512]{1,0:T(8,128)S(1)}, f32[64,512]{1,0:T(8,128)S(1)}, u32[]{:S(2)}, u32[]{:S(2)}) collective-permute-start(f32[64,512]{1,0:T(8,128)S(1)} %fusion.17), channel_id=1, source_target_pairs={{0,64},{8,72},{16,80},{24,88},{32,96},{40,104},{48,112},{56,120},{... | collective-permute-start | bytes 393224 | tf_op jit(solution)/shard_map/ppermute | solution.py:21
  85.7 12.5 %collective-permute-start.12 = (f32[2,512,128]{2,1,0:T(8,128)S(1)}, f32[2,512,128]{2,1,0:T(8,128)S(1)}, u32[]{:S(2)}, u32[]{:S(2)}) collective-permute-start(f32[2,512,128]{2,1,0:T(8,128)S(1)} %pad_maximum_fusion.3), channel_id=1, source_target_pairs={{0,1},{1,0},{2,3},{3,2},{4,5},{5,4},{6,7},{7,6},{8,9},{9,8},{10,11... | collective-permute-start | bytes 1572872 | tf_op jit(solution)/shard_map/ppermute | solution.py:36
  85.8 12.1 %collective-permute-start.14 = (f32[512,128]{1,0:T(8,128)S(1)}, f32[512,128]{1,0:T(8,128)S(1)}, u32[]{:S(2)}, u32[]{:S(2)}) collective-permute-start(f32[512,128]{1,0:T(8,128)S(1)} %fusion.4), channel_id=1, source_target_pairs={{0,64},{8,72},{16,80},{24,88},{32,96},{40,104},{48,112},{56,120},{... | collective-permute-start | bytes 786440 | tf_op jit(solution)/shard_map/ppermute | solution.py:23
  99.0 7.9 %collective-permute-start.15 = (f32[512,128]{1,0:T(8,128)S(1)}, f32[512,128]{1,0:T(8,128)S(1)}, u32[]{:S(2)}, u32[]{:S(2)}) collective-permute-start(f32[512,128]{1,0:T(8,128)S(1)} %fusion.2), channel_id=1, source_target_pairs={{0,2},{1,3},{2,0},{3,1},{4,6},{5,7},{6,4},{7,5},{8,10},{9,11},{10,... | collective-permute-start | bytes 786440 | tf_op jit(solution)/shard_map/ppermute | solution.py:35
  106.9 10.2 %collective-permute-start.16 = (f32[2,512,128]{2,1,0:T(8,128)S(1)}, f32[2,512,128]{2,1,0:T(8,128)S(1)}, u32[]{:S(2)}, u32[]{:S(2)}) collective-permute-start(f32[2,512,128]{2,1,0:T(8,128)S(1)} %pad_maximum_fusion.4), channel_id=1, source_target_pairs={{0,1},{1,0},{2,3},{3,2},{4,5},{5,4},{6,7},{7,6},{8,9},{9,8},{10,11... | collective-permute-start | bytes 1572872 | tf_op jit(solution)/shard_map/ppermute | solution.py:36
  107.4 9.3 %collective-permute-start.13 = (f32[64,512]{1,0:T(8,128)S(1)}, f32[64,512]{1,0:T(8,128)S(1)}, u32[]{:S(2)}, u32[]{:S(2)}) collective-permute-start(f32[64,512]{1,0:T(8,128)S(1)} %fusion.14), channel_id=1, source_target_pairs={{0,128},{8,136},{16,144},{24,152},{32,160},{40,168},{48,176},{56,1... | collective-permute-start | bytes 393224 | tf_op jit(solution)/shard_map/ppermute | solution.py:21
  118.3 1.4 copy-start.2
  119.7 24.4 %all-to-all-start = ((f32[8,1,64,768]{3,2,1,0:T(8,128)}), f32[8,1,64,768]{3,2,1,0:T(8,128)S(1)}, u32[]{:S(2)}, u32[]{:S(2)}) async-start(f32[8,1,64,768]{3,2,1,0:T(8,128)} %pad_maximum_fusion), calls=%async_computation | async-start | bytes 3145728 | tf_op jit(solution)/shard_map/all_to_all | solution.py:91
